TPU v7x, 128 devices: a whole 4x4x4 slice. The times are simulated.
128 devices in a mesh: req: 8 (over x, core), kv: 16 (over y, z).
Axes of the slice: x: 4, y: 4, z: 4, core: 2. Of those that a mesh axis runs over, the one named last changes fastest.
Arguments:
- x_steps: bfloat16 [4, 1024, 1536], P(None, ('req', 'kv')), may hold values from -6 to 6
- lengths: int32 [128], replicated, may hold values from 16 to 8192
- perm: int32 [128], replicated, may hold values from 0 to 127, as said below
- parents: int32 [4, 1024], replicated, may hold values from 0 to 7
- table: int32 [1024, 9], P(('req', 'kv')), may hold values from 0 to 9215, as said below
- pool: bfloat16 [9216, 128, 256], P(('req', 'kv')), may hold values from -900 to 900
- norm_attn: float32 [1536], replicated, may hold values from 0.1 to 1.9
- w_query: bfloat16 [1536, 1536], replicated, may hold values from -0.15625 to 0.15625
- w_keyval: bfloat16 [1536, 256], replicated, may hold values from -0.15625 to 0.15625
- w_out: bfloat16 [1536, 1536], replicated, may hold values from -0.15625 to 0.15625
- norm_mlp: float32 [1536], replicated, may hold values from 0.1 to 1.9
- w_gate: bfloat16 [1536, 4608], P(None, 'kv'), may hold values from -0.15625 to 0.15625
- w_up: bfloat16 [1536, 4608], P(None, 'kv'), may hold values from -0.15625 to 0.15625
- w_down: bfloat16 [4608, 1536], P('kv'), may hold values from -0.09375 to 0.09375
Outputs:
- outputs: bfloat16 [4, 1024, 1536], P(None, ('req', 'kv'))
Inputs may be any that keep to these rules, and one draw needn't show every extreme that they name: perm is a permutation with perm[s] % 16 == s % 16; among the 8 slots s with one s // 16 and one s % 16 // 8, every req index occurs as perm[s] // 16 exactly once. The entries of row b lie in [(b // 8) * 72, (b // 8 + 1) * 72); no page appears twice in the table.
All inputs are finite; a program needn't handle non-finite values.
Results may differ from a plain program's by a relative error of at most 0.02.
Values may be sent and summed in bfloat16 or wider, within the bound.
No kernel may reach another device: no remote copies, remote signals or barrier semaphores. Data moves between devices by JAX's collectives and lax.ppermute only.
A program may use at most 192 MiB of HBM per device.

v0:
```python
import jax
import jax.numpy as jnp
from jax import lax
from jax.sharding import PartitionSpec as P

WINDOW = 1024
PAGE = 128
BEAMS = 8


EPSILON = 1e-06
NEGATIVE = -1e30


def merged_2(array, axis, combine):
    everything = jax.tree.map(lambda part: lax.all_gather(part, axis), array)
    first = jax.tree.map(lambda part: part[0], everything)

    def turn(k, so_far):
        return combine(so_far, jax.tree.map(lambda part: part[k], everything))

    return lax.fori_loop(1, lax.axis_size(axis), turn, first)


def member_of(beam_index, half_index, halves):
    return beam_index % 2 + 2 * half_index + 2 * halves * (beam_index // 2)


def rms_round(values, gain):
    wide = values.astype(jnp.float32)
    mean_square = jnp.mean(wide * wide, axis=-1, keepdims=True)
    return (wide * lax.rsqrt(mean_square + EPSILON) * gain).astype(jnp.bfloat16)


def page_partial(queries, pages, key_pos, length, step_index):
    head_dim = queries.shape[-1]
    keys = pages[:, :, :head_dim]
    values = pages[:, :, head_dim:]
    scores = jnp.einsum(
        "jrhd,rkd->jrhk", queries, keys, preferred_element_type=jnp.float32
    ) * head_dim ** (-0.5)
    allowed = (key_pos < length[:, None]) & (key_pos > length[:, None] + step_index - WINDOW)
    scores = jnp.where(allowed[None, :, None, :], scores, NEGATIVE)
    highest = jnp.max(scores, axis=-1)
    weights = jnp.exp(scores - highest[..., None]).astype(jnp.bfloat16)
    totals = jnp.sum(weights.astype(jnp.float32), axis=-1)
    weighted = jnp.einsum("jrhk,rkd->jrhd", weights, values, preferred_element_type=jnp.float32)
    return (highest, totals, weighted)


def fresh_partial(queries, entries, count):
    head_dim = queries.shape[-1]
    keys = entries[..., :count, :head_dim]
    values = entries[..., :count, head_dim:]
    scores = jnp.einsum(
        "...hd,...kd->...hk", queries, keys, preferred_element_type=jnp.float32
    ) * head_dim ** (-0.5)
    highest = jnp.max(scores, axis=-1)
    weights = jnp.exp(scores - highest[..., None]).astype(jnp.bfloat16)
    totals = jnp.sum(weights.astype(jnp.float32), axis=-1)
    weighted = jnp.einsum("...hk,...kd->...hd", weights, values, preferred_element_type=jnp.float32)
    return (highest, totals, weighted)


def join_parts(first, second):
    highest = jnp.maximum(first[0], second[0])
    scale_first = jnp.exp(first[0] - highest)
    scale_second = jnp.exp(second[0] - highest)
    totals = first[1] * scale_first + second[1] * scale_second
    weighted = first[2] * scale_first[..., None] + second[2] * scale_second[..., None]
    return (highest, totals, weighted)


def feed_forward(mlp_in, w_gate, w_up, w_down):
    gate = jnp.dot(mlp_in, w_gate, preferred_element_type=jnp.float32)
    upward = jnp.dot(mlp_in, w_up, preferred_element_type=jnp.float32)
    hidden = (jax.nn.gelu(gate, approximate=True) * upward).astype(jnp.bfloat16)
    return jnp.dot(hidden, w_down, preferred_element_type=jnp.float32)


def rank_within(labels, offsets):
    earlier = (labels[None, :] == labels[:, None]) & (offsets[None, :] < offsets[:, None])
    return jnp.sum(earlier.astype(jnp.int32), axis=1)


def pick_half(array, halves, half):
    shaped = array.reshape((BEAMS // 2, halves, 2) + array.shape[1:])
    picked = lax.dynamic_index_in_dim(shaped, half, 1, keepdims=False)
    return picked.reshape((BEAMS,) + array.shape[1:])


def place_block(block, filler, halves, half):
    whole = jnp.full((BEAMS // 2, halves, 2) + block.shape[1:], filler, block.dtype)
    placed = lax.dynamic_update_slice_in_dim(
        whole, block.reshape((BEAMS // 2, 1, 2) + block.shape[1:]), half, 1
    )
    return placed.reshape((BEAMS * halves,) + block.shape[1:])


def on_device(
    x_steps,
    lengths,
    perm,
    parents,
    table,
    pool,
    norm_attn,
    w_query,
    w_keyval,
    w_out,
    norm_mlp,
    w_gate,
    w_up,
    w_down,
):
    steps, rows, width = x_steps.shape
    head_dim = pool.shape[2] // 2
    heads = w_query.shape[1] // head_dim
    span = table.shape[1] * pool.shape[1]
    req_count = lax.axis_size("req")
    kv_count = lax.axis_size("kv")
    group = lax.axis_index("req")
    member = lax.axis_index("kv")
    halves = kv_count // BEAMS
    half = member // 2 % halves
    beam = member % 2 + 2 * (member // (2 * halves))
    per_group = halves * rows
    group_rows = kv_count * rows
    quota = rows // req_count
    offsets = jnp.arange(rows, dtype=jnp.int32)
    slot_ids = group * per_group + half * rows + offsets
    placed = lax.dynamic_slice_in_dim(perm.reshape(req_count, per_group), half * rows, rows, 1)
    serving = lax.dynamic_index_in_dim(placed, group, 0, keepdims=False)
    target = jnp.sum(
        jnp.where(placed == slot_ids[None, :], jnp.arange(req_count, dtype=jnp.int32)[:, None], 0),
        axis=0,
    )
    anchor = serving // per_group
    send_order = jnp.argsort(target * rows + offsets)
    outgoing = x_steps[:, send_order].reshape(steps, req_count, quota, width)
    arrived = lax.all_to_all(outgoing, "req", split_axis=1, concat_axis=1, tiled=True).reshape(
        steps, rows, width
    )
    inputs = arrived[:, anchor * quota + rank_within(anchor, offsets)]
    length = lengths[serving]
    first_page = jnp.maximum(length - WINDOW + 1, 0) // PAGE
    key_pos = first_page[:, None] * PAGE + jnp.arange(span, dtype=jnp.int32)[None, :]
    device = group * kv_count + member
    pages = pool[table - device * pool.shape[0]].reshape(rows, span, 2 * head_dim)
    family = lax.dynamic_slice_in_dim(parents, group * group_rows, group_rows, 1)
    row_ids = jnp.arange(group_rows, dtype=jnp.int32)
    row_member = row_ids // rows
    row_half = row_member // 2 % halves
    within = row_ids % rows
    ancestor = row_member % 2 + 2 * (row_member // (2 * halves))
    recent = jnp.zeros((group_rows, steps, 2 * head_dim), jnp.bfloat16)
    results = []
    for step_index in range(steps):
        parent_rows = member_of(family[step_index], row_half, halves) * rows + within
        ancestor = ancestor[parent_rows]
        recent = recent[parent_rows]
        current = inputs[step_index]
        normed = rms_round(current, norm_attn)
        query = jnp.dot(normed, w_query, preferred_element_type=jnp.float32).astype(jnp.bfloat16)
        fresh = jnp.dot(normed, w_keyval, preferred_element_type=jnp.float32).astype(jnp.bfloat16)
        query_all, fresh_all = (
            lax.all_gather(query, "kv", axis=0, tiled=True),
            lax.all_gather(fresh, "kv", axis=0, tiled=True),
        )
        recent = recent.at[:, step_index].set(fresh_all)
        query_block = pick_half(query_all.reshape(kv_count, rows, heads, head_dim), halves, half)
        held = pick_half(ancestor.reshape(kv_count, rows), halves, half) == beam
        page = page_partial(query_block, pages, key_pos, length, step_index)
        held_heads = held[..., None]
        highest = place_block(jnp.where(held_heads, page[0], NEGATIVE), NEGATIVE, halves, half)
        totals = place_block(jnp.where(held_heads, page[1], 0.0), 0.0, halves, half)
        weighted = place_block(jnp.where(held_heads[..., None], page[2], 0.0), 0.0, halves, half)
        merged = merged_2((highest, totals, weighted), "kv", join_parts)
        page_own = tuple(
            (
                lax.dynamic_index_in_dim(member_part, member, 0, keepdims=False)
                for member_part in merged
            )
        )
        own_entries = lax.dynamic_slice_in_dim(recent, member * rows, rows, 0)
        joined = join_parts(
            page_own,
            fresh_partial(query.reshape(rows, heads, head_dim), own_entries, step_index + 1),
        )
        attended = (
            (joined[2] / joined[1][..., None]).astype(jnp.bfloat16).reshape(rows, heads * head_dim)
        )
        residual = (
            current.astype(jnp.float32)
            + jnp.dot(attended, w_out, preferred_element_type=jnp.float32)
        ).astype(jnp.bfloat16)
        terms = feed_forward(
            lax.all_gather(rms_round(residual, norm_mlp), "kv", axis=0, tiled=True),
            w_gate,
            w_up,
            w_down,
        )
        summed = lax.psum_scatter(
            terms.astype(jnp.bfloat16), "kv", scatter_dimension=0, tiled=True
        ).astype(jnp.float32)
        results.append((residual.astype(jnp.float32) + summed).astype(jnp.bfloat16))
    finished = jnp.stack(results)
    back_order = jnp.argsort(anchor * rows + offsets)
    leaving = finished[:, back_order].reshape(steps, req_count, quota, width)
    returned = lax.all_to_all(leaving, "req", split_axis=1, concat_axis=1, tiled=True).reshape(
        steps, rows, width
    )
    return returned[:, target * quota + rank_within(target, offsets)]


def solution(mesh):
    in_specs = (
        P(None, ("req", "kv"), None),
        P(),
        P(),
        P(),
        P(("req", "kv"), None),
        P(("req", "kv"), None, None),
        P(),
        P(),
        P(),
        P(),
        P(),
        P(None, "kv"),
        P(None, "kv"),
        P("kv", None),
    )
    out_specs = P(None, ("req", "kv"), None)
    return jax.shard_map(
        on_device, mesh=mesh, in_specs=in_specs, out_specs=out_specs, check_vma=False
    )
```

profile of v0, /device:TPU:1, one launch (start us, length us, event | category | flops | bytes accessed | tf_op | source)
XLA Modules:
  0.0 938.9 jit_solution(8522241222401222963)
XLA Ops:
  39.0 20.2 %all_gather.90 = bf16[128,1536]{1,0:T(8,128)(2,1)S(1)} all-gather(bf16[8,1536]{1,0:T(8,128)(2,1)S(1)} %convolution_convert_fusion.4), channel_id=1, replica_groups=mesh['req'=8,'kv'=16] {'kv'}, dimensions={0}, use_global_device_ids=true | all-gather | bytes 417792 | tf_op jit(solution)/shard_map/all_gather | solution.py:167
  67.1 19.5 %all_gather.72 = bf16[128,1536]{1,0:T(8,128)(2,1)S(1)} all-gather(bf16[8,1536]{1,0:T(8,128)(2,1)S(1)} %convolution_convert_fusion.7), channel_id=1, replica_groups=mesh['req'=8,'kv'=16] {'kv'}, dimensions={0}, use_global_device_ids=true | all-gather | bytes 417792 | tf_op jit(solution)/shard_map/all_gather | solution.py:167
  96.3 17.8 %all_gather.78 = bf16[128,1536]{1,0:T(8,128)(2,1)S(1)} all-gather(bf16[8,1536]{1,0:T(8,128)(2,1)S(1)} %convolution_convert_fusion.6), channel_id=1, replica_groups=mesh['req'=8,'kv'=16] {'kv'}, dimensions={0}, use_global_device_ids=true | all-gather | bytes 417792 | tf_op jit(solution)/shard_map/all_gather | solution.py:167
  125.7 20.9 %all_gather.76 = bf16[128,256]{1,0:T(8,128)(2,1)S(1)} all-gather(bf16[8,256]{1,0:T(8,128)(2,1)S(1)} %convolution_convert_fusion.11), channel_id=1, replica_groups=mesh['req'=8,'kv'=16] {'kv'}, dimensions={0}, use_global_device_ids=true | all-gather | bytes 69632 | tf_op jit(solution)/shard_map/all_gather | solution.py:168
  149.5 16.4 %all_gather.82 = bf16[128,256]{1,0:T(8,128)(2,1)S(1)} all-gather(bf16[8,256]{1,0:T(8,128)(2,1)S(1)} %convolution_convert_fusion.10), channel_id=1, replica_groups=mesh['req'=8,'kv'=16] {'kv'}, dimensions={0}, use_global_device_ids=true | all-gather | bytes 69632 | tf_op jit(solution)/shard_map/all_gather | solution.py:168
  168.9 19.8 %all_gather.88 = bf16[128,256]{1,0:T(8,128)(2,1)S(1)} all-gather(bf16[8,256]{1,0:T(8,128)(2,1)S(1)} %convolution_convert_fusion.9), channel_id=1, replica_groups=mesh['req'=8,'kv'=16] {'kv'}, dimensions={0}, use_global_device_ids=true | all-gather | bytes 69632 | tf_op jit(solution)/shard_map/all_gather | solution.py:168
  191.6 16.4 %all_gather.94 = bf16[128,256]{1,0:T(8,128)(2,1)S(1)} all-gather(bf16[8,256]{1,0:T(8,128)(2,1)S(1)} %convolution_convert_fusion.8), channel_id=1, replica_groups=mesh['req'=8,'kv'=16] {'kv'}, dimensions={0}, use_global_device_ids=true | all-gather | bytes 69632 | tf_op jit(solution)/shard_map/all_gather | solution.py:168
  219.0 21.9 %all_gather.84 = bf16[128,1536]{1,0:T(8,128)(2,1)S(1)} all-gather(bf16[8,1536]{1,0:T(8,128)(2,1)S(1)} %convolution_convert_fusion.5), channel_id=1, replica_groups=mesh['req'=8,'kv'=16] {'kv'}, dimensions={0}, use_global_device_ids=true | all-gather | bytes 417792 | tf_op jit(solution)/shard_map/all_gather | solution.py:167
  248.8 20.1 %all_gather.91 = f32[16,16,8,12]{1,2,3,0:T(8,128)} all-gather(f32[1,16,8,12]{1,2,3,0:T(8,128)S(1)} %copy.375), channel_id=1, replica_groups=mesh['req'=8,'kv'=16] {'kv'}, dimensions={0}, use_global_device_ids=true | all-gather | bytes 104448 | tf_op jit(solution)/shard_map/all_gather | solution.py:16
  268.8 22.3 %all_gather.92 = f32[16,16,8,12]{1,2,3,0:T(8,128)} all-gather(f32[1,16,8,12]{1,2,3,0:T(8,128)S(1)} %copy.378), channel_id=1, replica_groups=mesh['req'=8,'kv'=16] {'kv'}, dimensions={0}, use_global_device_ids=true | all-gather | bytes 104448 | tf_op jit(solution)/shard_map/all_gather | solution.py:16
  291.2 20.8 %all_gather.73 = f32[16,16,8,12]{1,2,3,0:T(8,128)S(1)} all-gather(f32[1,16,8,12]{1,2,3,0:T(8,128)S(1)} %copy.320), channel_id=1, replica_groups=mesh['req'=8,'kv'=16] {'kv'}, dimensions={0}, use_global_device_ids=true | all-gather | bytes 104448 | tf_op jit(solution)/shard_map/all_gather | solution.py:16
  312.0 22.7 %all_gather.74 = f32[16,16,8,12]{1,2,3,0:T(8,128)S(1)} all-gather(f32[1,16,8,12]{1,2,3,0:T(8,128)S(1)} %copy.323), channel_id=1, replica_groups=mesh['req'=8,'kv'=16] {'kv'}, dimensions={0}, use_global_device_ids=true | all-gather | bytes 104448 | tf_op jit(solution)/shard_map/all_gather | solution.py:16
  334.7 21.6 %all_gather.79 = f32[16,16,8,12]{1,2,3,0:T(8,128)S(1)} all-gather(f32[1,16,8,12]{1,2,3,0:T(8,128)S(1)} %copy.341), channel_id=1, replica_groups=mesh['req'=8,'kv'=16] {'kv'}, dimensions={0}, use_global_device_ids=true | all-gather | bytes 104448 | tf_op jit(solution)/shard_map/all_gather | solution.py:16
  356.3 18.0 %all_gather.80 = f32[16,16,8,12]{1,2,3,0:T(8,128)S(1)} all-gather(f32[1,16,8,12]{1,2,3,0:T(8,128)S(1)} %copy.344), channel_id=1, replica_groups=mesh['req'=8,'kv'=16] {'kv'}, dimensions={0}, use_global_device_ids=true | all-gather | bytes 104448 | tf_op jit(solution)/shard_map/all_gather | solution.py:16
  374.3 19.4 %all_gather.85 = f32[16,16,8,12]{1,2,3,0:T(8,128)} all-gather(f32[1,16,8,12]{1,2,3,0:T(8,128)S(1)} %copy.358), channel_id=1, replica_groups=mesh['req'=8,'kv'=16] {'kv'}, dimensions={0}, use_global_device_ids=true | all-gather | bytes 104448 | tf_op jit(solution)/shard_map/all_gather | solution.py:16
  393.7 20.4 %all_gather.86 = f32[16,16,8,12]{1,2,3,0:T(8,128)} all-gather(f32[1,16,8,12]{1,2,3,0:T(8,128)S(1)} %copy.361), channel_id=1, replica_groups=mesh['req'=8,'kv'=16] {'kv'}, dimensions={0}, use_global_device_ids=true | all-gather | bytes 104448 | tf_op jit(solution)/shard_map/all_gather | solution.py:16
  426.8 46.2 %while.83 = (s32[]{:T(128)}, f32[16,8,12]{0,1,2:T(8,128)S(1)}, f32[16,8,12]{0,1,2:T(8,128)S(1)}, f32[16,8,12,128]{3,2,1,0:T(8,128)S(1)}, f32[16,16,8,12]{1,2,3,0...) while((s32[]{:T(128)}, f32[16,8,12]{0,1,2:T(8,128)S(1)}, ...), condition=%wide.region_32.33_spmd, body=%wide.region_31.32_spmd.sunk | while | flops 599045 | bytes 4018327 | solution.py:22
  475.3 46.3 %while.80 = (s32[]{:T(128)}, f32[16,8,12]{0,1,2:T(8,128)S(1)}, f32[16,8,12]{0,1,2:T(8,128)S(1)}, f32[16,8,12,128]{3,2,1,0:T(8,128)S(1)}, f32[16,16,8,12]{1,2,3,0...) while((s32[]{:T(128)}, f32[16,8,12]{0,1,2:T(8,128)S(1)}, ...), condition=%wide.region_7.8_spmd, body=%wide.region_6.7_spmd.sunk | while | flops 599045 | bytes 4018327 | solution.py:22
  524.6 73.6 %while.81 = (s32[]{:T(128)}, f32[16,8,12]{0,1,2:T(8,128)S(1)}, f32[16,8,12]{0,1,2:T(8,128)S(1)}, f32[16,8,12,128]{3,2,1,0:T(8,128)}, f32[16,16,8,12]{1,2,3,0:T(8...) while((s32[]{:T(128)}, f32[16,8,12]{0,1,2:T(8,128)S(1)}, ...), condition=%wide.region_14.15_spmd, body=%wide.region_13.14_spmd.sunk | while | flops 599045 | bytes 4018327 | solution.py:22
  610.4 46.2 %while.82 = (s32[]{:T(128)}, f32[16,8,12]{0,1,2:T(8,128)S(1)}, f32[16,8,12]{0,1,2:T(8,128)S(1)}, f32[16,8,12,128]{3,2,1,0:T(8,128)S(1)}, f32[16,16,8,12]{1,2,3,0...) while((s32[]{:T(128)}, f32[16,8,12]{0,1,2:T(8,128)S(1)}, ...), condition=%wide.region_23.24_spmd, body=%wide.region_22.23_spmd.sunk | while | flops 599045 | bytes 4018327 | solution.py:22
  661.9 16.4 %all_gather.95 = bf16[128,1536]{1,0:T(8,128)(2,1)S(1)} all-gather(bf16[8,1536]{1,0:T(8,128)(2,1)S(1)} %get-tuple-element.991), channel_id=1, replica_groups=mesh['req'=8,'kv'=16] {'kv'}, dimensions={0}, use_global_device_ids=true | all-gather | bytes 417792 | tf_op jit(solution)/shard_map/all_gather | solution.py:198
  678.3 17.8 %all_gather.89 = bf16[128,1536]{1,0:T(8,128)(2,1)S(1)} all-gather(bf16[8,1536]{1,0:T(8,128)(2,1)S(1)} %get-tuple-element.990), channel_id=1, replica_groups=mesh['req'=8,'kv'=16] {'kv'}, dimensions={0}, use_global_device_ids=true | all-gather | bytes 417792 | tf_op jit(solution)/shard_map/all_gather | solution.py:198
  722.7 17.9 %all_gather.77 = bf16[128,1536]{1,0:T(8,128)(2,1)S(1)} all-gather(bf16[8,1536]{1,0:T(8,128)(2,1)S(1)} %copy-done.28), channel_id=1, replica_groups=mesh['req'=8,'kv'=16] {'kv'}, dimensions={0}, use_global_device_ids=true | all-gather | bytes 417792 | tf_op jit(solution)/shard_map/all_gather | solution.py:198
  744.2 170.9 %all-reduce.7.cloned.1.call-done = (bf16[128,1536]{1,0:T(8,128)(2,1)}, bf16[128,1536]{1,0:T(8,128)(2,1)}, bf16[128,1536]{1,0:T(8,128)(2,1)}, bf16[128,1536]{1,0:T(8,128)(2,1)}) async-done(((bf16[128,1536]{1,0:T(8,128)(2,1)}, bf16[128,1536]{1,0:T(8,128)(2,1)}, bf16[128,1536]{1,0:T(8,128)(2,1)}, bf16[128,1536]{1,0:T(8,128)(2,1)}), (bf16[128,1536]{1,0:T(8,128)(2,1)}, bf16[128,1536]{1,0:T(8,128)(2,1)}, ...) | async-done | bytes 1572880
  (636 shorter events, 380.3 us)
Async XLA Ops:
  6.5 691.7 %copy-start = (bf16[288,1536]{1,0:T(8,128)(2,1)S(1)}, bf16[288,1536]{1,0:T(8,128)(2,1)}, u32[]{:S(2)}) copy-start(bf16[288,1536]{1,0:T(8,128)(2,1)} %param.43) | copy-start | bytes 2654212
  12.4 22.5 %all-to-all-start = ((bf16[4,8,1,1536]{3,0,2,1:T(4,128)(2,1)}), bf16[4,8,1,1536]{3,0,2,1:T(4,128)(2,1)S(1)}, u32[]{:S(2)}, u32[]{:S(2)}) async-start(bf16[4,8,1,1536]{3,0,2,1:T(4,128)(2,1)} %copy.313), calls=%async_computation | async-start | bytes 196608 | tf_op jit(solution)/shard_map/all_to_all | solution.py:141
  18.2 407.2 %all-gather.11.cloned.1.call-start = ((), (), s32[]{:S(2)}) async-start(), calls=%async_computation.5 | async-start | bytes 13369344 | tf_op jit(solution)/shard_map/all_gather | solution.py:16
  63.7 409.5 %all-gather.5.cloned.1.call-start = ((), (), s32[]{:S(2)}) async-start(), calls=%async_computation.2 | async-start | bytes 13369344 | tf_op jit(solution)/shard_map/all_gather | solution.py:16
  92.9 429.3 %all-gather.7.cloned.1.call-start = ((), (), s32[]{:S(2)}) async-start(), calls=%async_computation.3 | async-start | bytes 13369344 | tf_op jit(solution)/shard_map/all_gather | solution.py:16
  120.4 488.6 %all-gather.9.cloned.1.call-start = ((), (), s32[]{:S(2)}) async-start(), calls=%async_computation.4 | async-start | bytes 13369344 | tf_op jit(solution)/shard_map/all_gather | solution.py:16
  167.8 247.0 %copy-start.21 = (bf16[128,4,256]{2,1,0:T(4,128)(2,1)}, bf16[128,4,256]{2,1,0:T(4,128)(2,1)S(1)}, u32[]{:S(2)}) copy-start(bf16[128,4,256]{2,1,0:T(4,128)(2,1)S(1)} %scatter.15) | copy-start | bytes 786436
  190.5 226.5 %copy-start.20 = (bf16[128,4,256]{2,1,0:T(4,128)(2,1)}, bf16[128,4,256]{2,1,0:T(4,128)(2,1)S(1)}, u32[]{:S(2)}) copy-start(bf16[128,4,256]{2,1,0:T(4,128)(2,1)S(1)} %scatter.16) | copy-start | bytes 786436
  248.7 169.3 %copy-start.27 = (bf16[128,4,256]{2,1,0:T(4,128)(2,1)}, bf16[128,4,256]{2,1,0:T(4,128)(2,1)S(1)}, u32[]{:S(2)}) copy-start(bf16[128,4,256]{2,1,0:T(4,128)(2,1)S(1)} %scatter.19) | copy-start | bytes 786436
  248.8 171.8 %copy-start.11 = (f32[8,1152,8,12]{1,3,2,0:T(8,128)S(1)}, f32[8,1152,8,12]{1,3,2,0:T(8,128)}, u32[]{:S(2)}) copy-start(f32[8,1152,8,12]{1,3,2,0:T(8,128)} %copy-done.10) | copy-start | bytes 10616836
  312.0 107.7 %copy-start.18 = (f32[16,16,8,12]{1,2,3,0:T(8,128)}, f32[16,16,8,12]{1,2,3,0:T(8,128)S(1)}, u32[]{:S(2)}) copy-start(f32[16,16,8,12]{1,2,3,0:T(8,128)S(1)} %all_gather.73) | copy-start | bytes 294916
  334.7 85.0 %copy-start.19 = (f32[16,16,8,12]{1,2,3,0:T(8,128)}, f32[16,16,8,12]{1,2,3,0:T(8,128)S(1)}, u32[]{:S(2)}) copy-start(f32[16,16,8,12]{1,2,3,0:T(8,128)S(1)} %all_gather.74) | copy-start | bytes 294916
  356.3 62.6 %copy-start.16 = (f32[16,16,8,12]{1,2,3,0:T(8,128)}, f32[16,16,8,12]{1,2,3,0:T(8,128)S(1)}, u32[]{:S(2)}) copy-start(f32[16,16,8,12]{1,2,3,0:T(8,128)S(1)} %all_gather.79) | copy-start | bytes 294916
  424.5 490.5 %all-reduce.7.cloned.1.call-start = ((), (), s32[]{:S(2)}) async-start(), calls=%async_computation.6 | async-start | bytes 3145728
  475.3 46.6 %copy-start.40 = (f32[8,1,12]{2,1,0:T(1,128)S(1)}, f32[8,1,12]{2,1,0:T(1,128)}, u32[]{:S(2)}) copy-start(f32[8,1,12]{2,1,0:T(1,128)} %fusion.132) | copy-start | bytes 1156
  524.6 73.9 %copy-start.34 = (f32[8,12]{1,0:T(8,128)S(1)}, f32[8,12]{1,0:T(8,128)}, u32[]{:S(2)}) copy-start(f32[8,12]{1,0:T(8,128)} %copy-done.33) | copy-start | bytes 1156
  524.6 73.9 %copy-start.35 = (f32[8,12]{1,0:T(8,128)S(1)}, f32[8,12]{1,0:T(8,128)}, u32[]{:S(2)}) copy-start(f32[8,12]{1,0:T(8,128)} %convert_reduce_fusion.6) | copy-start | bytes 1156
  608.9 52.2 %copy-start.23 = (f32[8,1536]{1,0:T(8,128)}, f32[8,1536]{1,0:T(8,128)S(1)}, u32[]{:S(2)}) copy-start(f32[8,1536]{1,0:T(8,128)S(1)} %get-tuple-element.1037) | copy-start | bytes 147460
  610.3 46.5 %copy-start.30 = (f32[8,12]{1,0:T(8,128)S(1)}, f32[8,12]{1,0:T(8,128)}, u32[]{:S(2)}) copy-start(f32[8,12]{1,0:T(8,128)} %copy-done.29) | copy-start | bytes 1156
  610.3 46.5 %copy-start.31 = (f32[8,12]{1,0:T(8,128)S(1)}, f32[8,12]{1,0:T(8,128)}, u32[]{:S(2)}) copy-start(f32[8,12]{1,0:T(8,128)} %convert_reduce_fusion.5) | copy-start | bytes 1156
  661.9 58.5 %copy-start.3 = (bf16[1536,288]{0,1:T(8,128)(2,1)S(1)}, bf16[1536,288]{0,1:T(8,128)(2,1)}, u32[]{:S(2)}) copy-start(bf16[1536,288]{0,1:T(8,128)(2,1)} %param.41) | copy-start | bytes 2654212
  720.8 194.2 %copy-start.24 = (f32[8,1536]{1,0:T(8,128)S(1)}, f32[8,1536]{1,0:T(8,128)}, u32[]{:S(2)}) copy-start(f32[8,1536]{1,0:T(8,128)} %copy-done.23) | copy-start | bytes 147460
  720.8 195.0 %copy-start.26 = (f32[8,1536]{1,0:T(8,128)S(1)}, f32[8,1536]{1,0:T(8,128)}, u32[]{:S(2)}) copy-start(f32[8,1536]{1,0:T(8,128)} %copy-done.25) | copy-start | bytes 147460
  919.4 11.4 %all-to-all-start.1 = ((bf16[4,8,1,1536]{3,0,2,1:T(4,128)(2,1)}), bf16[4,8,1,1536]{3,0,2,1:T(4,128)(2,1)S(1)}, u32[]{:S(2)}, u32[]{:S(2)}) async-start(bf16[4,8,1,1536]{3,0,2,1:T(4,128)(2,1)} %bitcast.140), calls=%async_computation.1 | async-start | bytes 196608 | tf_op jit(solution)/shard_map/all_to_all | solution.py:210
  (33 other events, 423.7 us)
Sparse Core Ops, SparseCore 0:
  63.8 97.4 all-gather.10
  163.5 91.9 all-gather.4
  257.7 102.1 all-gather.6
  424.6 152.7 all-gather.8
  743.0 172.0 all-reduce.6
where the time goes:
time: 955 us; the launch traced here: 939 us
  blocking collectives  387 us (41%)
  waiting for transfers between devices  176 us (18%)
  other arithmetic  146 us (15%)
  local copies, waits for them, and re-layouts  144 us (15%)
  matrix products  56.8 us (6%)
  between operations  15.5 us (2%)
  starting transfers between devices  12.6 us (1%)
    unnamed x6, waiting for transfers between devices  171 us
    all_gather x8, blocking collectives, merged_2(): everything = jax.tree.map(lambda part: lax.all_gather(part, axis), array)  165 us
    all_gather x4, blocking collectives, on_device(): lax.all_gather(query, 'kv', axis=0, tiled=True)  79.3 us
    all_gather x4, blocking collectives, on_device(): lax.all_gather(fresh, 'kv', axis=0, tiled=True)  73.6 us
    dynamic_slice x60, local copies, waits for them, and re-layouts, turn(): return combine(so_far, jax.tree.map(lambda part: part[k], everything))  71.7 us
    add x60, other arithmetic, join_parts(): first[2] * scale_first[..., None] + second[2] * scale_second[..., None]  70.3 us
    all_gather x4, blocking collectives, on_device(): lax.all_gather(rms_round(residual, norm_mlp), 'kv', axis=0, tiled=True)  68.5 us
    add x64, other arithmetic, join_parts(): totals = first[1] * scale_first + second[1] * scale_second  53.4 us
  transfers between devices with their start and end apart: 7, of which 2 were waited for; matrix products, arithmetic and copies ran while one was open for 27% of the time, Pallas kernels for 0%

commit v1 on v0

v1 whole, which is shorter than its diff:
```python
import jax
import jax.numpy as jnp
from jax import lax
from jax.sharding import PartitionSpec as P

WINDOW = 1024
PAGE = 128
BEAMS = 8


EPSILON = 1e-06
NEGATIVE = -1e30


def member_of(beam_index, half_index, halves):
    return beam_index % 2 + 2 * half_index + 2 * halves * (beam_index // 2)


def rms_round(values, gain):
    wide = values.astype(jnp.float32)
    mean_square = jnp.mean(wide * wide, axis=-1, keepdims=True)
    return (wide * lax.rsqrt(mean_square + EPSILON) * gain).astype(jnp.bfloat16)


def rank_within(labels, offsets):
    earlier = (labels[None, :] == labels[:, None]) & (offsets[None, :] < offsets[:, None])
    return jnp.sum(earlier.astype(jnp.int32), axis=1)


def follow(index, table):
    picks = index[:, None, :] == jnp.arange(BEAMS, dtype=jnp.int32)[None, :, None]
    return jnp.sum(jnp.where(picks, table[None, :, :], 0), axis=1)


def pick_rows(index, table):
    picks = index[:, None, :] == jnp.arange(BEAMS, dtype=jnp.int32)[None, :, None]
    return jnp.sum(jnp.where(picks[..., None], table[None, :, :, :], 0), axis=1).astype(table.dtype)


def on_device(
    x_steps,
    lengths,
    perm,
    parents,
    table,
    pool,
    norm_attn,
    w_query,
    w_keyval,
    w_out,
    norm_mlp,
    w_gate,
    w_up,
    w_down,
):
    steps, rows, width = x_steps.shape
    head_dim = pool.shape[2] // 2
    heads = w_query.shape[1] // head_dim
    qwidth = heads * head_dim
    span = table.shape[1] * pool.shape[1]
    req_count = lax.axis_size("req")
    kv_count = lax.axis_size("kv")
    group = lax.axis_index("req")
    member = lax.axis_index("kv")
    halves = kv_count // BEAMS
    half = member // 2 % halves
    beam = member % 2 + 2 * (member // (2 * halves))
    per_group = halves * rows
    group_rows = kv_count * rows
    quota = rows // req_count

    offsets = jnp.arange(rows, dtype=jnp.int32)
    slot_ids = group * per_group + half * rows + offsets
    placed = lax.dynamic_slice_in_dim(perm.reshape(req_count, per_group), half * rows, rows, 1)
    serving = lax.dynamic_index_in_dim(placed, group, 0, keepdims=False)
    target = jnp.sum(
        jnp.where(placed == slot_ids[None, :], jnp.arange(req_count, dtype=jnp.int32)[:, None], 0),
        axis=0,
    )
    anchor = serving // per_group
    send_order = jnp.argsort(target * rows + offsets)
    outgoing = x_steps[:, send_order].reshape(steps, req_count, quota, width)
    arrived = lax.all_to_all(outgoing, "req", split_axis=1, concat_axis=1, tiled=True).reshape(
        steps, rows, width
    )
    inputs = arrived[:, anchor * quota + rank_within(anchor, offsets)]

    normed = rms_round(inputs.reshape(steps * rows, width), norm_attn)
    query = jnp.dot(normed, w_query, preferred_element_type=jnp.float32).astype(jnp.bfloat16)
    fresh = jnp.dot(normed, w_keyval, preferred_element_type=jnp.float32).astype(jnp.bfloat16)
    packed = jnp.concatenate([query, fresh], axis=-1).reshape(steps, rows, qwidth + 2 * head_dim)
    gathered = lax.all_gather(packed, "kv", axis=0)
    mine = gathered.reshape((BEAMS // 2, halves, 2) + packed.shape)
    mine = lax.dynamic_index_in_dim(mine, half, 1, keepdims=False).reshape((BEAMS,) + packed.shape)
    queries = mine[..., :qwidth].reshape(BEAMS, steps, rows, heads, head_dim)
    entries = mine[..., qwidth:]

    family = lax.dynamic_slice_in_dim(parents, group * group_rows, group_rows, 1).reshape(
        (steps, BEAMS // 2, halves, 2, rows)
    )
    family = lax.dynamic_index_in_dim(family, half, 2, keepdims=False).reshape(steps, BEAMS, rows)
    own = jnp.broadcast_to(jnp.arange(BEAMS, dtype=jnp.int32)[:, None], (BEAMS, rows))
    cache_beam = own
    sources = []
    cache_beams = []
    listed = []
    for step_index in range(steps):
        cache_beam = follow(family[step_index], cache_beam)
        sources = [follow(family[step_index], source) for source in sources] + [own]
        cache_beams.append(cache_beam)
        picked = [pick_rows(source, entries[:, s]) for s, source in enumerate(sources)]
        picked += [jnp.zeros_like(picked[0])] * (steps - 1 - step_index)
        listed.append(jnp.stack(picked))
    held = jnp.stack(cache_beams, axis=1) == beam
    listed = jnp.stack(listed)

    length = lengths[serving]
    first_page = jnp.maximum(length - WINDOW + 1, 0) // PAGE
    key_pos = first_page[:, None] * PAGE + jnp.arange(span, dtype=jnp.int32)[None, :]
    device = group * kv_count + member
    pages = pool[table - device * pool.shape[0]].reshape(rows, span, 2 * head_dim)
    keys = pages[:, :, :head_dim]
    values = pages[:, :, head_dim:]
    scale = head_dim ** (-0.5)
    scores = jnp.einsum(
        "jtrhd,rkd->jtrhk", queries, keys, preferred_element_type=jnp.float32
    ) * scale
    step_ids = jnp.arange(steps, dtype=jnp.int32)
    allowed = (key_pos[None, :, :] < length[None, :, None]) & (
        key_pos[None, :, :] > length[None, :, None] + step_ids[:, None, None] - WINDOW
    )
    scores = jnp.where(allowed[None, :, :, None, :], scores, NEGATIVE)
    high_c = jnp.max(scores, axis=-1)
    weights = jnp.exp(scores - high_c[..., None]).astype(jnp.bfloat16)
    total_c = jnp.sum(weights.astype(jnp.float32), axis=-1)
    sum_c = jnp.einsum("jtrhk,rkd->jtrhd", weights, values, preferred_element_type=jnp.float32)

    new_keys = listed[..., :head_dim]
    new_values = listed[..., head_dim:]
    fresh_scores = jnp.einsum(
        "jtrhd,tsjrd->jtrhs", queries, new_keys, preferred_element_type=jnp.float32
    ) * scale
    counted = step_ids[None, :] <= step_ids[:, None]
    fresh_scores = jnp.where(counted[None, :, None, None, :], fresh_scores, NEGATIVE)
    high_n = jnp.max(fresh_scores, axis=-1)
    fresh_weights = jnp.exp(fresh_scores - high_n[..., None]).astype(jnp.bfloat16)
    fresh_weights = jnp.where(counted[None, :, None, None, :], fresh_weights, 0)
    total_n = jnp.sum(fresh_weights.astype(jnp.float32), axis=-1)
    sum_n = jnp.einsum(
        "jtrhs,tsjrd->jtrhd", fresh_weights, new_values, preferred_element_type=jnp.float32
    )

    highest = jnp.maximum(high_c, high_n)
    scale_c = jnp.exp(high_c - highest)
    scale_n = jnp.exp(high_n - highest)
    totals = total_c * scale_c + total_n * scale_n
    weighted = sum_c * scale_c[..., None] + sum_n * scale_n[..., None]
    attended = (weighted / totals[..., None]).astype(jnp.bfloat16).reshape(
        BEAMS, steps, rows, qwidth
    )
    attended = jnp.where(held[..., None], attended, jnp.zeros_like(attended))

    spread = attended.reshape(BEAMS // 2, 1, 2, steps, rows, qwidth)
    in_half = (jnp.arange(halves, dtype=jnp.int32) == half)[None, :, None, None, None, None]
    outgoing_att = jnp.where(in_half, spread, jnp.zeros_like(spread)).reshape(
        kv_count, steps, rows, qwidth
    )
    received = lax.all_to_all(outgoing_att, "kv", split_axis=0, concat_axis=0, tiled=True)
    attended_own = jnp.sum(received.astype(jnp.float32), axis=0).astype(jnp.bfloat16)

    current = inputs.reshape(steps * rows, width)
    residual = (
        current.astype(jnp.float32)
        + jnp.dot(attended_own.reshape(steps * rows, qwidth), w_out, preferred_element_type=jnp.float32)
    ).astype(jnp.bfloat16)
    mlp_in = lax.all_gather(rms_round(residual, norm_mlp), "kv", axis=0, tiled=True)
    gate = jnp.dot(mlp_in, w_gate, preferred_element_type=jnp.float32)
    upward = jnp.dot(mlp_in, w_up, preferred_element_type=jnp.float32)
    hidden = (jax.nn.gelu(gate, approximate=True) * upward).astype(jnp.bfloat16)
    terms = jnp.dot(hidden, w_down, preferred_element_type=jnp.float32).astype(jnp.bfloat16)
    terms = terms.reshape(kv_count, steps * rows, width)
    partial = lax.all_to_all(terms, "kv", split_axis=0, concat_axis=0, tiled=True)
    summed = jnp.sum(partial.astype(jnp.float32), axis=0)
    finished = (residual.astype(jnp.float32) + summed).astype(jnp.bfloat16).reshape(
        steps, rows, width
    )

    back_order = jnp.argsort(anchor * rows + offsets)
    leaving = finished[:, back_order].reshape(steps, req_count, quota, width)
    returned = lax.all_to_all(leaving, "req", split_axis=1, concat_axis=1, tiled=True).reshape(
        steps, rows, width
    )
    return returned[:, target * quota + rank_within(target, offsets)]


def solution(mesh):
    in_specs = (
        P(None, ("req", "kv"), None),
        P(),
        P(),
        P(),
        P(("req", "kv"), None),
        P(("req", "kv"), None, None),
        P(),
        P(),
        P(),
        P(),
        P(),
        P(None, "kv"),
        P(None, "kv"),
        P("kv", None),
    )
    out_specs = P(None, ("req", "kv"), None)
    return jax.shard_map(
        on_device, mesh=mesh, in_specs=in_specs, out_specs=out_specs, check_vma=False
    )
```

time: 955 us -> 239 us (0.25); the launches traced: 939 us -> 238 us
  blocking collectives: 387 us -> 24.9 us
  other arithmetic: 146 us -> 20 us
  local copies, waits for them, and re-layouts: 144 us -> 20 us
  waiting for transfers between devices: 176 us -> 105 us
  matrix products: 56.8 us -> 35.3 us
    all_gather x20 -> x0, blocking collectives: 387 us -> none  [the longest x8 165 us: merged_2(): everything = jax.tree.map(lambda part: lax.all_gather(part, axis), array)]
    unnamed x6 -> x2, waiting for transfers between devices: 171 us -> 0.03 us
    add x125 -> x2, other arithmetic: 124 us -> 0.25 us  [the longest x1 0.18 us: on_device(): totals = total_c * scale_c + total_n * scale_n]
    all_gather x4 -> x2, waiting for transfers between devices: 0.04 us -> 79.4 us  [the longest x1 43.8 us: on_device(): lax.all_gather(rms_round(residual, norm_mlp), 'kv', axis=0, tiled=True)]
    dynamic_slice x69 -> x1, local copies, waits for them, and re-layouts: 71.9 us -> 1.39 us  [on_device(): lax.dynamic_index_in_dim(mine, half, 1, keepdims=False)]
    all_to_all x0 -> x1, blocking collectives: none -> 24.9 us  [on_device(): lax.all_to_all(outgoing_att, 'kv', split_axis=0, concat_axis=0, tiled=True)]
    all_to_all x0 -> x1, waiting for transfers between devices: none -> 19.2 us  [on_device(): lax.all_to_all(terms, 'kv', split_axis=0, concat_axis=0, tiled=True)]
    exp x122 -> x2, local copies, waits for them, and re-layouts: 16.1 us -> 0.07 us  [the longest x1 0.04 us: on_device(): scale_n = jnp.exp(high_n - highest)]
  transfers between devices with their start and end apart: 7 -> 5, of which waited for: 2 -> 5; matrix products, arithmetic and copies ran while one was open for 27% -> 5% of each run, Pallas kernels for 0% -> 0%
where the time goes in v1:
time: 239 us; the launch traced here: 238 us
  waiting for transfers between devices  105 us (44%)
  matrix products  35.3 us (15%)
  blocking collectives  24.9 us (10%)
  local copies, waits for them, and re-layouts  20 us (8%)
  other arithmetic  20 us (8%)
  starting transfers between devices  19.1 us (8%)
  between operations  14 us (6%)
    all_gather x1, waiting for transfers between devices, on_device(): lax.all_gather(rms_round(residual, norm_mlp), 'kv', axis=0, tiled=True)  43.8 us
    all_gather x1, waiting for transfers between devices, on_device(): gathered = lax.all_gather(packed, 'kv', axis=0)  35.6 us
    all_to_all x1, blocking collectives, on_device(): lax.all_to_all(outgoing_att, 'kv', split_axis=0, concat_axis=0, tiled=True)  24.9 us
    all_to_all x1, waiting for transfers between devices, on_device(): lax.all_to_all(terms, 'kv', split_axis=0, concat_axis=0, tiled=True)  19.2 us
    reduce_sum x1, other arithmetic, on_device(): total_c = jnp.sum(weights.astype(jnp.float32), axis=-1)  11 us
    dot_general x1, matrix products, on_device(): jnp.einsum('jtrhk,rkd->jtrhd', weights, values, preferred_element_type=jn...  9.68 us
    all_to_all x1, starting transfers between devices, on_device(): lax.all_to_all(leaving, 'req', split_axis=1, concat_axis=1, tiled=True)  8.59 us
    dot_general x1, matrix products, on_device(): jnp.einsum('jtrhd,rkd->jtrhk', queries, keys, preferred_element_type=jnp....  8.53 us
  transfers between devices with their start and end apart: 5, of which 5 were waited for; matrix products, arithmetic and copies ran while one was open for 5% of the time, Pallas kernels for 0%

profile of v1, /device:TPU:1, one launch (start us, length us, event | category | flops | bytes accessed | tf_op | source)
XLA Modules:
  0.0 238.4 jit_solution(9731133063465071926)
XLA Ops:
  8.5 1.7 gather_fusion
  10.9 5.8 %all-to-all-start = ((bf16[4,8,1,1536]{3,0,2,1:T(4,128)(2,1)}), bf16[4,8,1,1536]{3,0,2,1:T(4,128)(2,1)S(1)}, u32[]{:S(2)}, u32[]{:S(2)}) async-start(bf16[4,8,1,1536]{3,0,2,1:T(4,128)(2,1)} %copy.127), calls=%async_computation | async-start | bytes 196608 | tf_op jit(solution)/shard_map/all_to_all | solution.py:83
  18.8 1.3 gather_fusion.3
  20.2 1.6 all-to-all-done
  22.7 1.4 convolution_convert_fusion.2
  24.1 3.3 %convolution_convert_fusion.1 = bf16[32,1536]{1,0:T(8,128)(2,1)S(1)} fusion(bf16[1536,1536]{1,0:T(8,128)(2,1)} %param.21, f32[4,8,1536]{2,0,1:T(4,128)S(1)} %convert_bitcast_fusion, f32[1536]{0:T(1024)} %param.20, f32[32]{0:T(128)S(1)} %rsqrt.20), kind=kOutput, calls=%fused_computation.19 | convolution fusion | flops 151191552 | bytes 5019776 | tf_op jit(solution)/shard_map/dot_general | solution.py:89
  28.2 7.8 %gather_fusion.2 = bf16[72,128,256]{2,1,0:T(8,128)(2,1)} fusion(bf16[72,128,256]{2,1,0:T(8,128)(2,1)} %param.19, s32[1024]{0:T(1024)S(1)} %pad_clamp_fusion.3), kind=kCustom, calls=%fused_computation.2 | custom fusion | bytes 9437472 | tf_op jit(solution)/shard_map/gather | solution.py:121
  36.7 35.6 %all-gather.3.cloned.1.call-done = bf16[16,4,8,1792]{3,2,1,0:T(8,128)(2,1)} async-done(((bf16[1,4,8,1792]{3,2,1,0:T(8,128)(2,1)}), bf16[16,4,8,1792]{3,2,1,0:T(8,128)(2,1)}) %all-gather.3.cloned.1.call-update) | async-done | bytes 1835024 | tf_op jit(solution)/shard_map/all_gather | solution.py:92
  72.3 1.4 constant_dynamic-slice_fusion.1
  77.9 1.9 fusion.25
  79.8 8.5 %fusion = (f32[8,4,8,12]{3,1,0,2:T(4,128)S(1)}, f32[8,1152,8,4,12]{1,4,3,2,0:T(8,128)}) fusion(pred[4,8,1152]{2,0,1:T(4,128)(4,1)S(1)} %compare_and_fusion, bf16[8,4,8,12,128]{4,2,3,1,0:T(8,128)(2,1)S(1)} %slice_bitcast_fusion.6, bf16[8,1152,256]{2,1,0:T(8,128)(2,1)S(1)} %bitcast.164), kind=kOutput, calls=%fused_computation.10 | convolution fusion | flops 916583424 | bytes 17350656 | tf_op jit(solution)/shard_map/jtrhd,rkd->jtrhk/dot_general | solution.py:125
  88.3 11.0 %convert_reduce_fusion = f32[8,4,8,12]{3,1,0,2:T(4,128)S(1)} fusion(f32[8,4,8,12]{3,1,0,2:T(4,128)S(1)} %get-tuple-element.56, f32[8,1152,8,4,12]{1,4,3,2,0:T(8,128)} %get-tuple-element.57, pred[4,8,1152]{2,0,1:T(4,128)(4,1)S(1)} %compare_and_fusion), kind=kLoop, calls=%fused_computation.8 | loop fusion | flops 17691648 | bytes 14217216 | tf_op jit(solution)/shard_map/reduce_sum | solution.py:135
  99.6 9.7 %fusion.6 = bf16[8,4,8,12,128]{4,3,1,0,2:T(8,128)(2,1)S(1)} fusion(f32[8,4,8,12,128]{4,3,1,0,2:T(8,128)} %fusion.25, bf16[8,1152,256]{2,1,0:T(8,128)(2,1)} %bitcast.161, f32[8,1152,8,4,12]{1,4,3,2,0:T(8,128)} %get-tuple-element.57, f32[8,4,8,12]{3,1,0,2:T(4,128)S(1)} %get-tuple-element.56, pred[4,8,1152]{2,0,1:T(4,128)(4,1)S(1)} %compare_and_fusion, ...), kind=kOutput, calls=%fused_computation.23 | convolution fusion | flops 918552576 | bytes 24203264 | tf_op jit(solution)/shard_map/jtrhk,rkd->jtrhd/dot_general | solution.py:136
  110.6 24.9 %all_to_all.20 = bf16[16,4,8,1536]{3,2,1,0:T(8,128)(2,1)S(1)} all-to-all(bf16[16,4,8,1536]{3,2,1,0:T(8,128)(2,1)S(1)} %bitcast_select_fusion.1), channel_id=1, replica_groups=mesh['req'=8,'kv'=16] {'kv'}, dimensions={0} | all-to-all | bytes 3145728 | tf_op jit(solution)/shard_map/all_to_all | solution.py:168
  135.7 3.4 %multiply_reduce_fusion = (f32[32]{0:T(128)S(1)}, f32[32,1536]{1,0:T(8,128)S(1)}) fusion(bf16[1536,1536]{1,0:T(8,128)(2,1)} %param.23, bf16[4,8,1536]{2,1,0:T(8,128)(2,1)S(1)} %reduce_sum.322, f32[4,8,1536]{2,0,1:T(4,128)S(1)} %convert_bitcast_fusion), kind=kOutput, calls=%fused_computation.70 | convolution fusion | flops 151240672 | bytes 5210240 | tf_op jit(solution)/shard_map/dot_general | solution.py:174
  139.9 43.8 %all-gather.5.cloned.1.call-done = bf16[512,1536]{1,0:T(8,128)(2,1)} async-done(((bf16[32,1536]{1,0:T(8,128)(2,1)}), bf16[512,1536]{1,0:T(8,128)(2,1)}) %all-gather.5.cloned.1.call-update) | async-done | bytes 1572880 | tf_op jit(solution)/shard_map/all_gather | solution.py:176
  183.8 2.1 fusion.53
  185.8 4.2 %convolution_convert_fusion = bf16[512,1536]{1,0:T(8,128)(2,1)} fusion(bf16[288,1536]{1,0:T(8,128)(2,1)S(1)} %copy-done, bf16[512,1536]{1,0:T(8,128)(2,1)} %all-gather.5.cloned.1.call-done, bf16[1536,288]{0,1:T(8,128)(2,1)S(1)} %copy-done.3, f32[512,288]{0,1:T(8,128)S(1)} %fusion.53), kind=kOutput, calls=%fused_computation.12 | convolution fusion | flops 908230656 | bytes 5505024 | tf_op jit(solution)/shard_map/dot_general | solution.py:180
  190.1 4.7 %all-to-all-start.2 = ((bf16[16,32,1536]{2,1,0:T(8,128)(2,1)}), bf16[16,32,1536]{2,1,0:T(8,128)(2,1)S(1)}, u32[]{:S(2)}, u32[]{:S(2)}) async-start(bf16[16,32,1536]{2,1,0:T(8,128)(2,1)} %bitcast.168), calls=%async_computation.2 | async-start | bytes 3145728 | tf_op jit(solution)/shard_map/all_to_all | solution.py:182
  194.8 1.0 sort.32
  195.9 19.2 %all-to-all-done.2 = bf16[16,32,1536]{2,1,0:T(8,128)(2,1)S(1)} async-done(((bf16[16,32,1536]{2,1,0:T(8,128)(2,1)}), bf16[16,32,1536]{2,1,0:T(8,128)(2,1)S(1)}, u32[]{:S(2)}, u32[]{:S(2)}) %all-to-all-start.2) | async-done | bytes 1572896 | tf_op jit(solution)/shard_map/all_to_all | solution.py:182
  215.4 1.3 gather_fusion.4
  216.7 8.6 %all-to-all-start.3 = ((bf16[4,8,1,1536]{3,0,2,1:T(4,128)(2,1)}), bf16[4,8,1,1536]{3,0,2,1:T(4,128)(2,1)S(1)}, u32[]{:S(2)}, u32[]{:S(2)}) async-start(bf16[4,8,1,1536]{3,0,2,1:T(4,128)(2,1)} %bitcast.60), calls=%async_computation.3 | async-start | bytes 196608 | tf_op jit(solution)/shard_map/all_to_all | solution.py:190
  225.3 5.0 %all-to-all-done.3 = bf16[4,8,1,1536]{3,0,2,1:T(4,128)(2,1)S(1)} async-done(((bf16[4,8,1,1536]{3,0,2,1:T(4,128)(2,1)}), bf16[4,8,1,1536]{3,0,2,1:T(4,128)(2,1)S(1)}, u32[]{:S(2)}, u32[]{:S(2)}) %all-to-all-start.3) | async-done | bytes 98336 | tf_op jit(solution)/shard_map/all_to_all | solution.py:190
  (104 shorter events, 15.3 us)
Async XLA Ops:
  6.5 179.3 %copy-start = (bf16[288,1536]{1,0:T(8,128)(2,1)S(1)}, bf16[288,1536]{1,0:T(8,128)(2,1)}, u32[]{:S(2)}) copy-start(bf16[288,1536]{1,0:T(8,128)(2,1)} %param.27) | copy-start | bytes 2654212
  10.9 10.8 %all-to-all-start = ((bf16[4,8,1,1536]{3,0,2,1:T(4,128)(2,1)}), bf16[4,8,1,1536]{3,0,2,1:T(4,128)(2,1)S(1)}, u32[]{:S(2)}, u32[]{:S(2)}) async-start(bf16[4,8,1,1536]{3,0,2,1:T(4,128)(2,1)} %copy.127), calls=%async_computation | async-start | bytes 196608 | tf_op jit(solution)/shard_map/all_to_all | solution.py:83
  16.7 55.6 %all-gather.3.cloned.1.call-start = ((), (), s32[]{:S(2)}) async-start(), calls=%async_computation.4 | async-start | bytes 1949696 | tf_op jit(solution)/shard_map/all_gather | solution.py:92
  28.1 155.6 %all-gather.5.cloned.1.call-start = ((), (), s32[]{:S(2)}) async-start(), calls=%async_computation.5 | async-start | bytes 1671168 | tf_op jit(solution)/shard_map/all_gather | solution.py:176
  72.3 7.5 %slice-start = ((s8[4718592]{0:T(1024)(128)(4,1)}), s8[4194304]{0:T(1024)(128)(4,1)S(1)}, s32[]{:S(2)}) async-start(s8[4718592]{0:T(1024)(128)(4,1)} %bitcast.162), calls=%async_computation.6 | async-start | bytes 8388608
  76.2 3.6 %slice-start.1 = ((s8[4718592]{0:T(1024)(128)(4,1)}), s8[524288]{0:T(1024)(128)(4,1)S(1)}, s32[]{:S(2)}) async-start(s8[4718592]{0:T(1024)(128)(4,1)} %bitcast.162), calls=%async_computation.7 | async-start | bytes 1048576
  110.6 28.6 %copy-start.1 = (f32[1536]{0:T(1024)S(1)}, f32[1536]{0:T(1024)}, u32[]{:S(2)}) copy-start(f32[1536]{0:T(1024)} %param.24) | copy-start | bytes 18436
  135.7 48.1 %copy-start.2 = (bf16[1536,288]{0,1:T(8,128)(2,1)S(1)}, bf16[1536,288]{0,1:T(8,128)(2,1)}, u32[]{:S(2)}) copy-start(bf16[1536,288]{0,1:T(8,128)(2,1)} %param.25) | copy-start | bytes 2654212
  139.2 46.7 %copy-start.3 = (bf16[1536,288]{0,1:T(8,128)(2,1)S(1)}, bf16[1536,288]{0,1:T(8,128)(2,1)}, u32[]{:S(2)}) copy-start(bf16[1536,288]{0,1:T(8,128)(2,1)} %param.26) | copy-start | bytes 2654212
  190.1 25.0 %all-to-all-start.2 = ((bf16[16,32,1536]{2,1,0:T(8,128)(2,1)}), bf16[16,32,1536]{2,1,0:T(8,128)(2,1)S(1)}, u32[]{:S(2)}, u32[]{:S(2)}) async-start(bf16[16,32,1536]{2,1,0:T(8,128)(2,1)} %bitcast.168), calls=%async_computation.2 | async-start | bytes 3145728 | tf_op jit(solution)/shard_map/all_to_all | solution.py:182
  216.7 13.6 %all-to-all-start.3 = ((bf16[4,8,1,1536]{3,0,2,1:T(4,128)(2,1)}), bf16[4,8,1,1536]{3,0,2,1:T(4,128)(2,1)S(1)}, u32[]{:S(2)}, u32[]{:S(2)}) async-start(bf16[4,8,1,1536]{3,0,2,1:T(4,128)(2,1)} %bitcast.60), calls=%async_computation.3 | async-start | bytes 196608 | tf_op jit(solution)/shard_map/all_to_all | solution.py:190
Sparse Core Ops, SparseCore 0:
  28.3 44.0 all-gather.2
  140.1 43.6 all-gather.4

commit v2 on v1

--- a/solution.py
+++ b/solution.py
@@ -89,7 +89,9 @@
     query = jnp.dot(normed, w_query, preferred_element_type=jnp.float32).astype(jnp.bfloat16)
     fresh = jnp.dot(normed, w_keyval, preferred_element_type=jnp.float32).astype(jnp.bfloat16)
     packed = jnp.concatenate([query, fresh], axis=-1).reshape(steps, rows, qwidth + 2 * head_dim)
-    gathered = lax.all_gather(packed, "kv", axis=0)
+    gathered = lax.all_to_all(
+        jnp.broadcast_to(packed[None], (kv_count,) + packed.shape), "kv", 0, 0, tiled=True
+    )
     mine = gathered.reshape((BEAMS // 2, halves, 2) + packed.shape)
     mine = lax.dynamic_index_in_dim(mine, half, 1, keepdims=False).reshape((BEAMS,) + packed.shape)
     queries = mine[..., :qwidth].reshape(BEAMS, steps, rows, heads, head_dim)
@@ -173,24 +175,38 @@
         current.astype(jnp.float32)
         + jnp.dot(attended_own.reshape(steps * rows, qwidth), w_out, preferred_element_type=jnp.float32)
     ).astype(jnp.bfloat16)
-    mlp_in = lax.all_gather(rms_round(residual, norm_mlp), "kv", axis=0, tiled=True)
+    mlp_own = rms_round(residual, norm_mlp)
+    mlp_in = lax.all_to_all(
+        jnp.broadcast_to(mlp_own[None], (kv_count,) + mlp_own.shape), "kv", 0, 0, tiled=True
+    ).reshape(kv_count * steps * rows, width)
     gate = jnp.dot(mlp_in, w_gate, preferred_element_type=jnp.float32)
     upward = jnp.dot(mlp_in, w_up, preferred_element_type=jnp.float32)
     hidden = (jax.nn.gelu(gate, approximate=True) * upward).astype(jnp.bfloat16)
-    terms = jnp.dot(hidden, w_down, preferred_element_type=jnp.float32).astype(jnp.bfloat16)
-    terms = terms.reshape(kv_count, steps * rows, width)
-    partial = lax.all_to_all(terms, "kv", split_axis=0, concat_axis=0, tiled=True)
-    summed = jnp.sum(partial.astype(jnp.float32), axis=0)
-    finished = (residual.astype(jnp.float32) + summed).astype(jnp.bfloat16).reshape(
-        steps, rows, width
-    )
-
-    back_order = jnp.argsort(anchor * rows + offsets)
-    leaving = finished[:, back_order].reshape(steps, req_count, quota, width)
-    returned = lax.all_to_all(leaving, "req", split_axis=1, concat_axis=1, tiled=True).reshape(
-        steps, rows, width
-    )
-    return returned[:, target * quota + rank_within(target, offsets)]
+    terms = jnp.dot(hidden, w_down, preferred_element_type=jnp.float32)
+    terms = terms.reshape(kv_count, steps, rows, width)
+    is_own = (jnp.arange(kv_count, dtype=jnp.int32) == member)[:, None, None, None]
+    terms = terms + jnp.where(is_own, residual.astype(jnp.float32).reshape(steps, rows, width)[None], 0.0)
+    terms = terms.astype(jnp.bfloat16)
+
+    slot_req = perm.reshape(req_count, halves, rows) // (halves * rows)
+    mine_req = lax.dynamic_index_in_dim(slot_req, group, 0, keepdims=False)
+    member_half = jnp.arange(kv_count, dtype=jnp.int32) // 2 % halves
+    req_ids = jnp.arange(req_count, dtype=jnp.int32)
+    row_of = mine_req[member_half]
+    choose = row_of[:, None, :] == req_ids[None, :, None]
+    leaving = jnp.sum(
+        jnp.where(choose[:, :, None, :, None], terms[:, None].astype(jnp.float32), 0.0), axis=3
+    ).astype(jnp.bfloat16)
+    leaving = jnp.swapaxes(leaving, 0, 1).reshape(req_count * kv_count, steps, width)
+    arrived_sums = lax.all_to_all(leaving, ("req", "kv"), 0, 0, tiled=True).reshape(
+        req_count, kv_count, steps, width
+    )
+    per_group_sum = jnp.sum(arrived_sums.astype(jnp.float32), axis=1)
+    served_by = slot_req[:, half, :] == group
+    finished = jnp.sum(
+        jnp.where(served_by[:, None, :, None], per_group_sum[:, :, None, :], 0.0), axis=0
+    )
+    return finished.astype(jnp.bfloat16)
 
 
 def solution(mesh):

time: 239 us -> 201 us (0.84)
  waiting for transfers between devices: 105 us -> 56.9 us
  between operations: 14 us -> 0.66 us
  other arithmetic: 20 us -> 32 us
  starting transfers between devices: 19.1 us -> 29.4 us
  local copies, waits for them, and re-layouts: 20 us -> 24.2 us
  matrix products: 35.3 us -> 32.8 us
    all_gather x2 -> x0, waiting for transfers between devices: 79.4 us -> none  [the longest x1 43.8 us: on_device(): lax.all_gather(rms_round(residual, norm_mlp), 'kv', axis=0, tiled=True)]
    all_to_all x2 -> x3, waiting for transfers between devices: 24.1 us -> 55.5 us  [the longest x1 23.9 us: on_device(): lax.all_to_all(leaving, ('req', 'kv'), 0, 0, tiled=True)]
    reduce_sum x1 -> x3, other arithmetic: 0.22 us -> 11.5 us  [the longest x1 10.1 us: on_device(): jnp.sum(jnp.where(choose[:, :, None, :, None], terms[:, None].astype(jnp....]
    all_to_all x2 -> x3, starting transfers between devices: 13.2 us -> 23.6 us  [the longest x1 11.4 us: on_device(): lax.all_to_all(leaving, ('req', 'kv'), 0, 0, tiled=True)]
    broadcast_in_dim x0 -> x2, local copies, waits for them, and re-layouts: none -> 2.75 us  [the longest x1 1.44 us: on_device(): jnp.broadcast_to(packed[None], (kv_count,) + packed.shape)]
    convert_element_type x0 -> x1, other arithmetic: none -> 2.5 us  [on_device(): terms[:, None].astype(jnp.float32)]
    reshape x1 -> x2, local copies, waits for them, and re-layouts: 0.05 us -> 2.46 us  [the longest x1 2.37 us: on_device(): jnp.swapaxes(leaving, 0, 1).reshape(req_count * kv_count, steps, width)]
  transfers between devices with their start and end apart: 5 -> 4, of which waited for: 5 -> 4; matrix products, arithmetic and copies ran while one was open for 5% -> 7% of each run, Pallas kernels for 0% -> 0%
where the time goes in v2:
time: 201 us; the launch traced here: 200 us
  waiting for transfers between devices  56.9 us (28%)
  matrix products  32.8 us (16%)
  other arithmetic  32 us (16%)
  starting transfers between devices  29.4 us (15%)
  local copies, waits for them, and re-layouts  24.2 us (12%)
  blocking collectives  23.9 us (12%)
    all_to_all x1, blocking collectives, on_device(): lax.all_to_all(outgoing_att, 'kv', split_axis=0, concat_axis=0, tiled=True)  23.9 us
    all_to_all x1, waiting for transfers between devices, on_device(): lax.all_to_all(leaving, ('req', 'kv'), 0, 0, tiled=True)  23.9 us
    all_to_all x1, waiting for transfers between devices, on_device(): lax.all_to_all(jnp.broadcast_to(mlp_own[None], (kv_count,) + mlp_own.shap...  16.8 us
    all_to_all x1, waiting for transfers between devices, on_device(): lax.all_to_all(jnp.broadcast_to(packed[None], (kv_count,) + packed.shape)...  14.8 us
    all_to_all x1, starting transfers between devices, on_device(): lax.all_to_all(leaving, ('req', 'kv'), 0, 0, tiled=True)  11.4 us
    reduce_sum x1, other arithmetic, on_device(): total_c = jnp.sum(weights.astype(jnp.float32), axis=-1)  11 us
    reduce_sum x1, other arithmetic, on_device(): jnp.sum(jnp.where(choose[:, :, None, :, None], terms[:, None].astype(jnp....  10.1 us
    dot_general x1, matrix products, on_device(): jnp.einsum('jtrhk,rkd->jtrhd', weights, values, preferred_element_type=jn...  9.14 us
  transfers between devices with their start and end apart: 4, of which 4 were waited for; matrix products, arithmetic and copies ran while one was open for 7% of the time, Pallas kernels for 0%

profile of v2, /device:TPU:1, one launch (start us, length us, event | category | flops | bytes accessed | tf_op | source)
XLA Modules:
  0.0 199.9 jit_solution(9365579530968788228)
XLA Ops:
  2.0 1.7 gather_fusion.1
  4.4 5.8 %all-to-all-start = ((bf16[4,8,1,1536]{3,0,2,1:T(4,128)(2,1)}), bf16[4,8,1,1536]{3,0,2,1:T(4,128)(2,1)S(1)}, u32[]{:S(2)}, u32[]{:S(2)}) async-start(bf16[4,8,1,1536]{3,0,2,1:T(4,128)(2,1)} %copy.121), calls=%async_computation | async-start | bytes 196608 | tf_op jit(solution)/shard_map/all_to_all | solution.py:83
  10.3 1.4 gather_fusion.4
  13.8 1.4 all-to-all-done
  16.2 3.3 %convolution_convert_fusion = bf16[32,1536]{1,0:T(8,128)(2,1)S(1)} fusion(bf16[1536,1536]{1,0:T(8,128)(2,1)} %param.21, f32[4,8,1536]{2,0,1:T(4,128)S(1)} %convert_bitcast_fusion.1, f32[1536]{0:T(1024)} %param.20, f32[32]{0:T(128)S(1)} %rsqrt.20), kind=kOutput, calls=%fused_computation.19 | convolution fusion | flops 151191552 | bytes 5019776 | tf_op jit(solution)/shard_map/dot_general | solution.py:89
  19.8 1.4 broadcast_in_dim.454
  21.3 7.8 %all-to-all-start.1 = ((bf16[16,4,8,1792]{3,2,1,0:T(8,128)(2,1)}), bf16[16,4,8,1792]{3,2,1,0:T(8,128)(2,1)S(1)}, u32[]{:S(2)}, u32[]{:S(2)}) async-start(bf16[16,4,8,1792]{3,2,1,0:T(8,128)(2,1)} %broadcast_in_dim.454), calls=%async_computation.1 | async-start | bytes 3670016 | tf_op jit(solution)/shard_map/all_to_all | solution.py:92
  29.2 7.8 %gather_fusion.3 = bf16[72,128,256]{2,1,0:T(8,128)(2,1)} fusion(bf16[72,128,256]{2,1,0:T(8,128)(2,1)} %param.19, s32[1024]{0:T(1024)S(1)} %pad_clamp_fusion.1), kind=kCustom, calls=%fused_computation.3 | custom fusion | bytes 9437472 | tf_op jit(solution)/shard_map/gather | solution.py:123
  37.5 14.8 %all-to-all-done.1 = bf16[16,4,8,1792]{3,2,1,0:T(8,128)(2,1)S(1)} async-done(((bf16[16,4,8,1792]{3,2,1,0:T(8,128)(2,1)}), bf16[16,4,8,1792]{3,2,1,0:T(8,128)(2,1)S(1)}, u32[]{:S(2)}, u32[]{:S(2)}) %all-to-all-start.1) | async-done | bytes 1835040 | tf_op jit(solution)/shard_map/all_to_all | solution.py:92
  54.6 8.5 %fusion = (f32[8,4,8,12]{3,1,0,2:T(4,128)S(1)}, f32[8,1152,8,4,12]{1,4,3,2,0:T(8,128)}) fusion(pred[4,8,1152]{2,0,1:T(4,128)(4,1)S(1)} %compare_and_fusion, bf16[8,4,8,12,128]{4,2,3,1,0:T(8,128)(2,1)S(1)} %slice_bitcast_fusion.6, bf16[8,1152,256]{2,1,0:T(8,128)(2,1)S(1)} %bitcast.162), kind=kOutput, calls=%fused_computation.10 | convolution fusion | flops 916583424 | bytes 17350656 | tf_op jit(solution)/shard_map/jtrhd,rkd->jtrhk/dot_general | solution.py:127
  63.1 11.0 %convert_reduce_fusion = f32[8,4,8,12]{3,1,0,2:T(4,128)S(1)} fusion(f32[8,4,8,12]{3,1,0,2:T(4,128)S(1)} %get-tuple-element.51, f32[8,1152,8,4,12]{1,4,3,2,0:T(8,128)} %get-tuple-element.52, pred[4,8,1152]{2,0,1:T(4,128)(4,1)S(1)} %compare_and_fusion), kind=kLoop, calls=%fused_computation.8 | loop fusion | flops 17691648 | bytes 14217216 | tf_op jit(solution)/shard_map/reduce_sum | solution.py:137
  77.6 9.1 %fusion.6 = bf16[8,4,8,12,128]{4,3,1,0,2:T(8,128)(2,1)S(1)} fusion(f32[8,4,8,12,128]{4,3,1,0,2:T(8,128)S(1)} %fusion.27, bf16[8,1152,256]{2,1,0:T(8,128)(2,1)} %bitcast.161, f32[8,1152,8,4,12]{1,4,3,2,0:T(8,128)} %get-tuple-element.52, f32[8,4,8,12]{3,1,0,2:T(4,128)S(1)} %get-tuple-element.51, pred[4,8,1152]{2,0,1:T(4,128)(4,1)S(1)} %compare_and_fusion, ...), kind=kOutput, calls=%fused_computation.23 | convolution fusion | flops 918552576 | bytes 23678976 | tf_op jit(solution)/shard_map/jtrhk,rkd->jtrhd/dot_general | solution.py:138
  88.0 23.9 %all_to_all.25 = bf16[16,4,8,1536]{3,2,1,0:T(8,128)(2,1)S(1)} all-to-all(bf16[16,4,8,1536]{3,2,1,0:T(8,128)(2,1)S(1)} %bitcast_select_fusion.1), channel_id=1, replica_groups=mesh['req'=8,'kv'=16] {'kv'}, dimensions={0} | all-to-all | bytes 3145728 | tf_op jit(solution)/shard_map/all_to_all | solution.py:170
  112.2 3.4 %multiply_reduce_fusion = (f32[32]{0:T(128)S(1)}, f32[32,1536]{1,0:T(8,128)S(1)}) fusion(bf16[1536,1536]{1,0:T(8,128)(2,1)} %param.23, bf16[4,8,1536]{2,1,0:T(8,128)(2,1)S(1)} %reduce_sum.331, f32[4,8,1536]{2,0,1:T(4,128)S(1)} %convert_bitcast_fusion.1), kind=kOutput, calls=%fused_computation.73 | convolution fusion | flops 151240672 | bytes 5210240 | tf_op jit(solution)/shard_map/dot_general | solution.py:176
  115.7 1.3 broadcast_in_dim.485
  117.0 4.4 %all-to-all-start.3 = ((bf16[16,32,1536]{2,1,0:T(8,128)(2,1)}), bf16[16,32,1536]{2,1,0:T(8,128)(2,1)S(1)}, u32[]{:S(2)}, u32[]{:S(2)}) async-start(bf16[16,32,1536]{2,1,0:T(8,128)(2,1)} %broadcast_in_dim.485), calls=%async_computation.3 | async-start | bytes 3145728 | tf_op jit(solution)/shard_map/all_to_all | solution.py:179
  123.4 16.8 %all-to-all-done.3 = bf16[16,32,1536]{2,1,0:T(8,128)(2,1)S(1)} async-done(((bf16[16,32,1536]{2,1,0:T(8,128)(2,1)}), bf16[16,32,1536]{2,1,0:T(8,128)(2,1)S(1)}, u32[]{:S(2)}, u32[]{:S(2)}) %all-to-all-start.3) | async-done | bytes 1572896 | tf_op jit(solution)/shard_map/all_to_all | solution.py:179
  140.2 2.6 %fusion.55 = f32[512,288]{0,1:T(8,128)} fusion(bf16[512,1536]{1,0:T(8,128)(2,1)S(1)} %bitcast.164, bf16[1536,288]{0,1:T(8,128)(2,1)} %param.25), kind=kOutput, calls=%fused_computation.189 | convolution fusion | flops 452984832 | bytes 3047424 | tf_op jit(solution)/shard_map/dot_general | solution.py:182
  142.8 4.4 %fusion.10 = f32[512,1536]{1,0:T(8,128)} fusion(bf16[288,1536]{1,0:T(8,128)(2,1)S(1)} %copy-done, bf16[512,1536]{1,0:T(8,128)(2,1)S(1)} %bitcast.165, bf16[1536,288]{0,1:T(8,128)(2,1)S(1)} %copy-done.2, f32[512,288]{0,1:T(8,128)} %fusion.55), kind=kOutput, calls=%fused_computation.32 | convolution fusion | flops 907444224 | bytes 7077888 | tf_op jit(solution)/shard_map/dot_general | solution.py:185
  147.2 2.5 %fusion.7 = f32[16,4,8,1536]{3,2,1,0:T(8,128)S(1)} fusion(f32[16,4,8,1536]{3,2,1,0:T(8,128)} %bitcast.163, f32[4,8,1536]{2,1,0:T(8,128)S(1)} %bitcast.172, pred[16]{0:T(512)(128)(4,1)S(1)} %iota_compare_fusion.14), kind=kLoop, calls=%fused_computation.24 | loop fusion | flops 3145728 | bytes 6488080 | tf_op jit(solution)/shard_map/convert_element_type | solution.py:198
  149.7 10.1 %select_reduce_fusion = bf16[16,8,4,1536]{3,2,1,0:T(4,128)(2,1)S(1)} fusion(f32[16,4,8,1536]{3,2,1,0:T(8,128)S(1)} %fusion.7, pred[16,8,8]{2,1,0:T(8,128)(4,1)S(1)} %copy-done.4), kind=kLoop, calls=%fused_computation.5 | loop fusion | flops 11796480 | bytes 4719616 | tf_op jit(solution)/shard_map/reduce_sum | solution.py:197
  160.7 2.4 %copy.150 = bf16[128,4,1536]{2,1,0:T(4,128)(2,1)} copy(bf16[128,4,1536]{2,0,1:T(8,128)(2,1)S(1)} %bitcast.166) | data formatting | bytes 3145728 | tf_op jit(solution)/shard_map/reshape | solution.py:200
  163.1 11.4 %all-to-all-start.4 = ((bf16[128,4,1536]{2,1,0:T(4,128)(2,1)}), bf16[128,4,1536]{2,1,0:T(4,128)(2,1)S(1)}, u32[]{:S(2)}, u32[]{:S(2)}) async-start(bf16[128,4,1536]{2,1,0:T(4,128)(2,1)} %copy.150), calls=%async_computation.4 | async-start | bytes 3145728 | tf_op jit(solution)/shard_map/all_to_all | solution.py:201
  174.6 23.9 %all-to-all-done.4 = bf16[128,4,1536]{2,1,0:T(4,128)(2,1)S(1)} async-done(((bf16[128,4,1536]{2,1,0:T(4,128)(2,1)}), bf16[128,4,1536]{2,1,0:T(4,128)(2,1)S(1)}, u32[]{:S(2)}, u32[]{:S(2)}) %all-to-all-start.4) | async-done | bytes 1572896 | tf_op jit(solution)/shard_map/all_to_all | solution.py:201
  (113 shorter events, 18.0 us)
Async XLA Ops:
  0.0 142.8 %copy-start = (bf16[288,1536]{1,0:T(8,128)(2,1)S(1)}, bf16[288,1536]{1,0:T(8,128)(2,1)}, u32[]{:S(2)}) copy-start(bf16[288,1536]{1,0:T(8,128)(2,1)} %param.27) | copy-start | bytes 2654212
  4.4 10.8 %all-to-all-start = ((bf16[4,8,1,1536]{3,0,2,1:T(4,128)(2,1)}), bf16[4,8,1,1536]{3,0,2,1:T(4,128)(2,1)S(1)}, u32[]{:S(2)}, u32[]{:S(2)}) async-start(bf16[4,8,1,1536]{3,0,2,1:T(4,128)(2,1)} %copy.121), calls=%async_computation | async-start | bytes 196608 | tf_op jit(solution)/shard_map/all_to_all | solution.py:83
  10.2 9.3 %copy-start.3 = (bf16[1536,256]{1,0:T(8,128)(2,1)S(1)}, bf16[1536,256]{1,0:T(8,128)(2,1)}, u32[]{:S(2)}) copy-start(bf16[1536,256]{1,0:T(8,128)(2,1)} %param.22) | copy-start | bytes 2359300
  10.3 9.2 %copy-start.5 = (f32[1536]{0:T(1024)S(1)}, f32[1536]{0:T(1024)}, u32[]{:S(2)}) copy-start(f32[1536]{0:T(1024)} %param.20) | copy-start | bytes 18436
  21.3 31.0 %all-to-all-start.1 = ((bf16[16,4,8,1792]{3,2,1,0:T(8,128)(2,1)}), bf16[16,4,8,1792]{3,2,1,0:T(8,128)(2,1)S(1)}, u32[]{:S(2)}, u32[]{:S(2)}) async-start(bf16[16,4,8,1792]{3,2,1,0:T(8,128)(2,1)} %broadcast_in_dim.454), calls=%async_computation.1 | async-start | bytes 3670016 | tf_op jit(solution)/shard_map/all_to_all | solution.py:92
  52.3 2.3 %copy-start.1 = (bf16[72,128,256]{2,1,0:T(8,128)(2,1)S(1)}, bf16[72,128,256]{2,1,0:T(8,128)(2,1)}, u32[]{:S(2)}) copy-start(bf16[72,128,256]{2,1,0:T(8,128)(2,1)} %gather_fusion.3) | copy-start | bytes 14155780
  111.9 3.6 %copy-start.8 = (f32[1536]{0:T(1024)S(1)}, f32[1536]{0:T(1024)}, u32[]{:S(2)}) copy-start(f32[1536]{0:T(1024)} %param.24) | copy-start | bytes 18436
  115.6 5.8 %copy-start.9 = (s32[128]{0:T(128)S(1)}, s32[128]{0:T(128)}, u32[]{:S(2)}) copy-start(s32[128]{0:T(128)} %param.16) | copy-start | bytes 1540
  117.0 23.2 %all-to-all-start.3 = ((bf16[16,32,1536]{2,1,0:T(8,128)(2,1)}), bf16[16,32,1536]{2,1,0:T(8,128)(2,1)S(1)}, u32[]{:S(2)}, u32[]{:S(2)}) async-start(bf16[16,32,1536]{2,1,0:T(8,128)(2,1)} %broadcast_in_dim.485), calls=%async_computation.3 | async-start | bytes 3145728 | tf_op jit(solution)/shard_map/all_to_all | solution.py:179
  121.4 21.4 %copy-start.2 = (bf16[1536,288]{0,1:T(8,128)(2,1)S(1)}, bf16[1536,288]{0,1:T(8,128)(2,1)}, u32[]{:S(2)}) copy-start(bf16[1536,288]{0,1:T(8,128)(2,1)} %param.26) | copy-start | bytes 2654212
  121.6 0.6 copy-start.6
  147.2 2.5 %copy-start.4 = (pred[16,8,8]{2,1,0:T(8,128)(4,1)S(1)}, pred[16,8,8]{2,1,0:T(8,128)(4,1)}, u32[]{:S(2)}) copy-start(pred[16,8,8]{2,1,0:T(8,128)(4,1)} %iota_compare_fusion) | copy-start | bytes 3076
  160.7 13.8 %copy-start.7 = (s32[8,2,8]{2,1,0:T(2,128)S(1)}, s32[8,2,8]{2,1,0:T(2,128)}, u32[]{:S(2)}) copy-start(s32[8,2,8]{2,1,0:T(2,128)} %copy-done.6) | copy-start | bytes 1540
  163.1 35.4 %all-to-all-start.4 = ((bf16[128,4,1536]{2,1,0:T(4,128)(2,1)}), bf16[128,4,1536]{2,1,0:T(4,128)(2,1)S(1)}, u32[]{:S(2)}, u32[]{:S(2)}) async-start(bf16[128,4,1536]{2,1,0:T(4,128)(2,1)} %copy.150), calls=%async_computation.4 | async-start | bytes 3145728 | tf_op jit(solution)/shard_map/all_to_all | solution.py:201

commit v3 on v2

--- a/solution.py
+++ b/solution.py
@@ -83,7 +83,12 @@
     arrived = lax.all_to_all(outgoing, "req", split_axis=1, concat_axis=1, tiled=True).reshape(
         steps, rows, width
     )
-    inputs = arrived[:, anchor * quota + rank_within(anchor, offsets)]
+    slot_req = perm.reshape(req_count, halves, rows) // (halves * rows)
+    mine_req = slot_req[:, half, :][group]
+    offset_of = jnp.sum(
+        jnp.where(mine_req[None, :] == offsets[:, None], offsets[None, :], 0), axis=1
+    )
+    inputs = arrived
 
     normed = rms_round(inputs.reshape(steps * rows, width), norm_attn)
     query = jnp.dot(normed, w_query, preferred_element_type=jnp.float32).astype(jnp.bfloat16)
@@ -101,6 +106,7 @@
         (steps, BEAMS // 2, halves, 2, rows)
     )
     family = lax.dynamic_index_in_dim(family, half, 2, keepdims=False).reshape(steps, BEAMS, rows)
+    family = family[:, :, offset_of]
     own = jnp.broadcast_to(jnp.arange(BEAMS, dtype=jnp.int32)[:, None], (BEAMS, rows))
     cache_beam = own
     sources = []
@@ -116,11 +122,11 @@
     held = jnp.stack(cache_beams, axis=1) == beam
     listed = jnp.stack(listed)
 
-    length = lengths[serving]
+    length = lengths[serving[offset_of]]
     first_page = jnp.maximum(length - WINDOW + 1, 0) // PAGE
     key_pos = first_page[:, None] * PAGE + jnp.arange(span, dtype=jnp.int32)[None, :]
     device = group * kv_count + member
-    pages = pool[table - device * pool.shape[0]].reshape(rows, span, 2 * head_dim)
+    pages = pool[table[offset_of] - device * pool.shape[0]].reshape(rows, span, 2 * head_dim)
     keys = pages[:, :, :head_dim]
     values = pages[:, :, head_dim:]
     scale = head_dim ** (-0.5)
@@ -188,16 +194,7 @@
     terms = terms + jnp.where(is_own, residual.astype(jnp.float32).reshape(steps, rows, width)[None], 0.0)
     terms = terms.astype(jnp.bfloat16)
 
-    slot_req = perm.reshape(req_count, halves, rows) // (halves * rows)
-    mine_req = lax.dynamic_index_in_dim(slot_req, group, 0, keepdims=False)
-    member_half = jnp.arange(kv_count, dtype=jnp.int32) // 2 % halves
-    req_ids = jnp.arange(req_count, dtype=jnp.int32)
-    row_of = mine_req[member_half]
-    choose = row_of[:, None, :] == req_ids[None, :, None]
-    leaving = jnp.sum(
-        jnp.where(choose[:, :, None, :, None], terms[:, None].astype(jnp.float32), 0.0), axis=3
-    ).astype(jnp.bfloat16)
-    leaving = jnp.swapaxes(leaving, 0, 1).reshape(req_count * kv_count, steps, width)
+    leaving = jnp.transpose(terms, (2, 0, 1, 3)).reshape(req_count * kv_count, steps, width)
     arrived_sums = lax.all_to_all(leaving, ("req", "kv"), 0, 0, tiled=True).reshape(
         req_count, kv_count, steps, width
     )

time: 201 us -> 195 us (0.970)
  other arithmetic: 32 us -> 21.8 us
  waiting for transfers between devices: 56.9 us -> 59 us
    reduce_sum x2 -> x1, other arithmetic: 10.3 us -> 0.12 us  [on_device(): jnp.sum(jnp.where(mine_req[None, :] == offsets[:, None], offsets[None, :]...]
    gather x4 -> x5, local copies, waits for them, and re-layouts: 10.4 us -> 11.6 us  [the longest x1 7.85 us: on_device(): pool[table[offset_of] - device * pool.shape[0]]]
  transfers between devices with their start and end apart: 4 -> 4, of which waited for: 4 -> 4; matrix products, arithmetic and copies ran while one was open for 7% -> 6% of each run, Pallas kernels for 0% -> 0%
where the time goes in v3:
time: 195 us; the launch traced here: 194 us
  waiting for transfers between devices  59 us (30%)
  matrix products  34.7 us (18%)
  starting transfers between devices  29.5 us (15%)
  local copies, waits for them, and re-layouts  24.3 us (12%)
  blocking collectives  23.9 us (12%)
  other arithmetic  21.8 us (11%)
    all_to_all x1, blocking collectives, on_device(): lax.all_to_all(outgoing_att, 'kv', split_axis=0, concat_axis=0, tiled=True)  23.9 us
    all_to_all x1, waiting for transfers between devices, on_device(): lax.all_to_all(leaving, ('req', 'kv'), 0, 0, tiled=True)  23.9 us
    all_to_all x1, waiting for transfers between devices, on_device(): lax.all_to_all(jnp.broadcast_to(mlp_own[None], (kv_count,) + mlp_own.shap...  18.8 us
    all_to_all x1, waiting for transfers between devices, on_device(): lax.all_to_all(jnp.broadcast_to(packed[None], (kv_count,) + packed.shape)...  14.8 us
    all_to_all x1, starting transfers between devices, on_device(): lax.all_to_all(leaving, ('req', 'kv'), 0, 0, tiled=True)  11.3 us
    reduce_sum x1, other arithmetic, on_device(): total_c = jnp.sum(weights.astype(jnp.float32), axis=-1)  11 us
    dot_general x1, matrix products, on_device(): jnp.einsum('jtrhk,rkd->jtrhd', weights, values, preferred_element_type=jn...  9.63 us
    dot_general x1, matrix products, on_device(): jnp.einsum('jtrhd,rkd->jtrhk', queries, keys, preferred_element_type=jnp....  8.53 us
  transfers between devices with their start and end apart: 4, of which 4 were waited for; matrix products, arithmetic and copies ran while one was open for 6% of the time, Pallas kernels for 0%

profile of v3, /device:TPU:1, one launch (start us, length us, event | category | flops | bytes accessed | tf_op | source)
XLA Modules:
  0.0 193.8 jit_solution(14602089501223062517)
XLA Ops:
  3.7 1.3 gather_fusion.5
  5.0 1.7 gather_fusion
  7.4 5.8 %all-to-all-start = ((bf16[4,8,1,1536]{3,0,2,1:T(4,128)(2,1)}), bf16[4,8,1,1536]{3,0,2,1:T(4,128)(2,1)S(1)}, u32[]{:S(2)}, u32[]{:S(2)}) async-start(bf16[4,8,1,1536]{3,0,2,1:T(4,128)(2,1)} %copy.163), calls=%async_computation | async-start | bytes 196608 | tf_op jit(solution)/shard_map/all_to_all | solution.py:83
  16.7 1.5 all-to-all-done
  18.9 3.3 %convolution_convert_fusion = bf16[32,1536]{1,0:T(8,128)(2,1)S(1)} fusion(bf16[1536,1536]{1,0:T(8,128)(2,1)} %param.21, f32[4,8,1,1536]{3,0,2,1:T(4,128)S(1)} %convert_element_type.113, f32[1536]{0:T(1024)S(1)} %copy-done.3, f32[32]{0:T(128)S(1)} %rsqrt.20), kind=kOutput, calls=%fused_computation.20 | convolution fusion | flops 151191552 | bytes 5019776 | tf_op jit(solution)/shard_map/dot_general | solution.py:94
  22.2 1.4 broadcast_in_dim.436
  23.6 7.8 %all-to-all-start.1 = ((bf16[16,4,8,1792]{3,2,1,0:T(8,128)(2,1)}), bf16[16,4,8,1792]{3,2,1,0:T(8,128)(2,1)S(1)}, u32[]{:S(2)}, u32[]{:S(2)}) async-start(bf16[16,4,8,1792]{3,2,1,0:T(8,128)(2,1)} %broadcast_in_dim.436), calls=%async_computation.1 | async-start | bytes 3670016 | tf_op jit(solution)/shard_map/all_to_all | solution.py:97
  31.7 7.9 %gather_fusion.3 = bf16[72,128,256]{2,1,0:T(8,128)(2,1)} fusion(bf16[72,128,256]{2,1,0:T(8,128)(2,1)} %param.19, s32[1024]{0:T(1024)S(1)} %pad_clamp_fusion.1), kind=kCustom, calls=%fused_computation.3 | custom fusion | bytes 9437472 | tf_op jit(solution)/shard_map/gather | solution.py:129
  39.8 14.8 %all-to-all-done.1 = bf16[16,4,8,1792]{3,2,1,0:T(8,128)(2,1)S(1)} async-done(((bf16[16,4,8,1792]{3,2,1,0:T(8,128)(2,1)}), bf16[16,4,8,1792]{3,2,1,0:T(8,128)(2,1)S(1)}, u32[]{:S(2)}, u32[]{:S(2)}) %all-to-all-start.1) | async-done | bytes 1835040 | tf_op jit(solution)/shard_map/all_to_all | solution.py:97
  58.8 1.9 fusion.27
  60.8 8.5 %fusion = (f32[8,4,8,12]{3,1,0,2:T(4,128)S(1)}, f32[8,1152,8,4,12]{1,4,3,2,0:T(8,128)}) fusion(pred[4,8,1152]{2,0,1:T(4,128)(4,1)S(1)} %compare_and_fusion, bf16[8,4,8,12,128]{4,2,3,1,0:T(8,128)(2,1)S(1)} %slice_bitcast_fusion.6, bf16[8,1152,256]{2,1,0:T(8,128)(2,1)S(1)} %bitcast.143), kind=kOutput, calls=%fused_computation.10 | convolution fusion | flops 916583424 | bytes 17350656 | tf_op jit(solution)/shard_map/jtrhd,rkd->jtrhk/dot_general | solution.py:133
  69.3 11.0 %convert_reduce_fusion = f32[8,4,8,12]{3,1,0,2:T(4,128)S(1)} fusion(f32[8,4,8,12]{3,1,0,2:T(4,128)S(1)} %get-tuple-element.49, f32[8,1152,8,4,12]{1,4,3,2,0:T(8,128)} %get-tuple-element.50, pred[4,8,1152]{2,0,1:T(4,128)(4,1)S(1)} %compare_and_fusion), kind=kLoop, calls=%fused_computation.8 | loop fusion | flops 17691648 | bytes 14217216 | tf_op jit(solution)/shard_map/reduce_sum | solution.py:143
  80.6 9.6 %fusion.7 = bf16[8,4,8,12,128]{4,3,1,0,2:T(8,128)(2,1)S(1)} fusion(f32[8,4,8,12,128]{4,3,1,0,2:T(8,128)} %fusion.27, bf16[8,1152,256]{2,1,0:T(8,128)(2,1)} %bitcast.140, f32[8,1152,8,4,12]{1,4,3,2,0:T(8,128)} %get-tuple-element.50, f32[8,4,8,12]{3,1,0,2:T(4,128)S(1)} %get-tuple-element.49, pred[4,8,1152]{2,0,1:T(4,128)(4,1)S(1)} %compare_and_fusion, ...), kind=kOutput, calls=%fused_computation.24 | convolution fusion | flops 918552576 | bytes 24203264 | tf_op jit(solution)/shard_map/jtrhk,rkd->jtrhd/dot_general | solution.py:144
  91.5 23.9 %all_to_all.25 = bf16[16,4,8,1536]{3,2,1,0:T(8,128)(2,1)S(1)} all-to-all(bf16[16,4,8,1536]{3,2,1,0:T(8,128)(2,1)S(1)} %bitcast_select_fusion.1), channel_id=1, replica_groups=mesh['req'=8,'kv'=16] {'kv'}, dimensions={0} | all-to-all | bytes 3145728 | tf_op jit(solution)/shard_map/all_to_all | solution.py:176
  115.7 3.4 %multiply_reduce_fusion = (f32[32]{0:T(128)S(1)}, f32[32,1536]{1,0:T(8,128)S(1)}) fusion(bf16[1536,1536]{1,0:T(8,128)(2,1)} %param.23, bf16[4,8,1536]{2,1,0:T(8,128)(2,1)S(1)} %reduce_sum.322, f32[4,8,1,1536]{3,0,2,1:T(4,128)S(1)} %convert_element_type.113), kind=kOutput, calls=%fused_computation.71 | convolution fusion | flops 151240672 | bytes 5210240 | tf_op jit(solution)/shard_map/dot_general | solution.py:182
  119.2 1.3 broadcast_in_dim.467
  120.5 4.6 %all-to-all-start.3 = ((bf16[16,32,1536]{2,1,0:T(8,128)(2,1)}), bf16[16,32,1536]{2,1,0:T(8,128)(2,1)S(1)}, u32[]{:S(2)}, u32[]{:S(2)}) async-start(bf16[16,32,1536]{2,1,0:T(8,128)(2,1)} %broadcast_in_dim.467), calls=%async_computation.3 | async-start | bytes 3145728 | tf_op jit(solution)/shard_map/all_to_all | solution.py:185
  125.0 18.8 %all-to-all-done.3 = bf16[16,32,1536]{2,1,0:T(8,128)(2,1)S(1)} async-done(((bf16[16,32,1536]{2,1,0:T(8,128)(2,1)}), bf16[16,32,1536]{2,1,0:T(8,128)(2,1)S(1)}, u32[]{:S(2)}, u32[]{:S(2)}) %all-to-all-start.3) | async-done | bytes 1572896 | tf_op jit(solution)/shard_map/all_to_all | solution.py:185
  143.8 2.6 %fusion.52 = f32[512,288]{0,1:T(8,128)} fusion(bf16[512,1536]{1,0:T(8,128)(2,1)S(1)} %bitcast.145, bf16[1536,288]{0,1:T(8,128)(2,1)} %param.25), kind=kOutput, calls=%fused_computation.157 | convolution fusion | flops 452984832 | bytes 3047424 | tf_op jit(solution)/shard_map/dot_general | solution.py:188
  146.5 4.4 %fusion.10 = f32[512,1536]{1,0:T(8,128)} fusion(bf16[288,1536]{1,0:T(8,128)(2,1)S(1)} %copy-done, bf16[512,1536]{1,0:T(8,128)(2,1)S(1)} %bitcast.146, bf16[1536,288]{0,1:T(8,128)(2,1)S(1)} %copy-done.1, f32[512,288]{0,1:T(8,128)} %fusion.52), kind=kOutput, calls=%fused_computation.31 | convolution fusion | flops 907444224 | bytes 7077888 | tf_op jit(solution)/shard_map/dot_general | solution.py:191
  150.9 3.8 %fusion.1 = bf16[16,4,8,1536]{3,0,2,1:T(8,128)(2,1)S(1)} fusion(f32[16,4,8,1536]{3,2,1,0:T(8,128)} %bitcast.144, f32[4,8,1536]{2,1,0:T(8,128)S(1)} %bitcast.152, pred[16]{0:T(512)(128)(4,1)S(1)} %iota_compare_fusion.13), kind=kLoop, calls=%fused_computation.13 | loop fusion | flops 2359296 | bytes 4915216 | tf_op jit(solution)/shard_map/convert_element_type | solution.py:195
  154.7 2.4 %copy.197 = bf16[128,4,1536]{2,1,0:T(4,128)(2,1)} copy(bf16[128,4,1536]{2,0,1:T(8,128)(2,1)S(1)} %bitcast.147) | data formatting | bytes 3145728 | tf_op jit(solution)/shard_map/reshape | solution.py:197
  157.1 11.3 %all-to-all-start.4 = ((bf16[128,4,1536]{2,1,0:T(4,128)(2,1)}), bf16[128,4,1536]{2,1,0:T(4,128)(2,1)S(1)}, u32[]{:S(2)}, u32[]{:S(2)}) async-start(bf16[128,4,1536]{2,1,0:T(4,128)(2,1)} %copy.197), calls=%async_computation.4 | async-start | bytes 3145728 | tf_op jit(solution)/shard_map/all_to_all | solution.py:198
  168.5 23.9 %all-to-all-done.4 = bf16[128,4,1536]{2,1,0:T(4,128)(2,1)S(1)} async-done(((bf16[128,4,1536]{2,1,0:T(4,128)(2,1)}), bf16[128,4,1536]{2,1,0:T(4,128)(2,1)S(1)}, u32[]{:S(2)}, u32[]{:S(2)}) %all-to-all-start.4) | async-done | bytes 1572896 | tf_op jit(solution)/shard_map/all_to_all | solution.py:198
  (109 shorter events, 16.2 us)
Async XLA Ops:
  0.0 146.5 %copy-start = (bf16[288,1536]{1,0:T(8,128)(2,1)S(1)}, bf16[288,1536]{1,0:T(8,128)(2,1)}, u32[]{:S(2)}) copy-start(bf16[288,1536]{1,0:T(8,128)(2,1)} %param.27) | copy-start | bytes 2654212
  0.0 18.6 %copy-start.3 = (f32[1536]{0:T(1024)S(1)}, f32[1536]{0:T(1024)}, u32[]{:S(2)}) copy-start(f32[1536]{0:T(1024)} %param.20) | copy-start | bytes 18436
  0.0 18.6 %copy-start.2 = (bf16[1536,256]{1,0:T(8,128)(2,1)S(1)}, bf16[1536,256]{1,0:T(8,128)(2,1)}, u32[]{:S(2)}) copy-start(bf16[1536,256]{1,0:T(8,128)(2,1)} %param.22) | copy-start | bytes 2359300
  7.4 10.8 %all-to-all-start = ((bf16[4,8,1,1536]{3,0,2,1:T(4,128)(2,1)}), bf16[4,8,1,1536]{3,0,2,1:T(4,128)(2,1)S(1)}, u32[]{:S(2)}, u32[]{:S(2)}) async-start(bf16[4,8,1,1536]{3,0,2,1:T(4,128)(2,1)} %copy.163), calls=%async_computation | async-start | bytes 196608 | tf_op jit(solution)/shard_map/all_to_all | solution.py:83
  23.6 31.0 %all-to-all-start.1 = ((bf16[16,4,8,1792]{3,2,1,0:T(8,128)(2,1)}), bf16[16,4,8,1792]{3,2,1,0:T(8,128)(2,1)S(1)}, u32[]{:S(2)}, u32[]{:S(2)}) async-start(bf16[16,4,8,1792]{3,2,1,0:T(8,128)(2,1)} %broadcast_in_dim.436), calls=%async_computation.1 | async-start | bytes 3670016 | tf_op jit(solution)/shard_map/all_to_all | solution.py:97
  54.6 6.1 %slice-start = ((s8[4718592]{0:T(1024)(128)(4,1)}), s8[4194304]{0:T(1024)(128)(4,1)S(1)}, s32[]{:S(2)}) async-start(s8[4718592]{0:T(1024)(128)(4,1)} %bitcast.141), calls=%async_computation.5 | async-start | bytes 8388608
  57.2 3.6 %slice-start.1 = ((s8[4718592]{0:T(1024)(128)(4,1)}), s8[524288]{0:T(1024)(128)(4,1)S(1)}, s32[]{:S(2)}) async-start(s8[4718592]{0:T(1024)(128)(4,1)} %bitcast.141), calls=%async_computation.6 | async-start | bytes 1048576
  115.4 3.6 %copy-start.4 = (f32[1536]{0:T(1024)S(1)}, f32[1536]{0:T(1024)}, u32[]{:S(2)}) copy-start(f32[1536]{0:T(1024)} %param.24) | copy-start | bytes 18436
  120.5 26.0 %copy-start.1 = (bf16[1536,288]{0,1:T(8,128)(2,1)S(1)}, bf16[1536,288]{0,1:T(8,128)(2,1)}, u32[]{:S(2)}) copy-start(bf16[1536,288]{0,1:T(8,128)(2,1)} %param.26) | copy-start | bytes 2654212
  120.5 23.4 %all-to-all-start.3 = ((bf16[16,32,1536]{2,1,0:T(8,128)(2,1)}), bf16[16,32,1536]{2,1,0:T(8,128)(2,1)S(1)}, u32[]{:S(2)}, u32[]{:S(2)}) async-start(bf16[16,32,1536]{2,1,0:T(8,128)(2,1)} %broadcast_in_dim.467), calls=%async_computation.3 | async-start | bytes 3145728 | tf_op jit(solution)/shard_map/all_to_all | solution.py:185
  157.1 35.3 %all-to-all-start.4 = ((bf16[128,4,1536]{2,1,0:T(4,128)(2,1)}), bf16[128,4,1536]{2,1,0:T(4,128)(2,1)S(1)}, u32[]{:S(2)}, u32[]{:S(2)}) async-start(bf16[128,4,1536]{2,1,0:T(4,128)(2,1)} %copy.197), calls=%async_computation.4 | async-start | bytes 3145728 | tf_op jit(solution)/shard_map/all_to_all | solution.py:198

commit v4 on v3

--- a/solution.py
+++ b/solution.py
@@ -2,6 +2,8 @@
 import jax.numpy as jnp
 from jax import lax
 from jax.sharding import PartitionSpec as P
+from jax.experimental import pallas as pl
+from jax.experimental.pallas import tpu as pltpu
 
 WINDOW = 1024
 PAGE = 128
@@ -35,6 +37,60 @@
 def pick_rows(index, table):
     picks = index[:, None, :] == jnp.arange(BEAMS, dtype=jnp.int32)[None, :, None]
     return jnp.sum(jnp.where(picks[..., None], table[None, :, :, :], 0), axis=1).astype(table.dtype)
+
+
+def cache_kernel(bounds_ref, q_ref, kv_ref, high_ref, total_ref, sum_ref):
+    r = pl.program_id(0)
+    steps = q_ref.shape[1]
+    head_dim = q_ref.shape[3]
+    keys = kv_ref[0, :, :head_dim]
+    values = kv_ref[0, :, head_dim:]
+    pos = lax.broadcasted_iota(jnp.int32, (1, kv_ref.shape[1]), 1)
+    for t in range(steps):
+        lo = bounds_ref[(r * steps + t) * 2]
+        hi = bounds_ref[(r * steps + t) * 2 + 1]
+        scores = lax.dot_general(
+            q_ref[0, t], keys, (((1,), (1,)), ((), ())), preferred_element_type=jnp.float32
+        ) * (head_dim ** (-0.5))
+        allowed = (pos > lo) & (pos < hi)
+        scores = jnp.where(allowed, scores, NEGATIVE)
+        high = jnp.max(scores, axis=1, keepdims=True)
+        weights = jnp.exp(scores - high).astype(jnp.bfloat16)
+        high_ref[0, t] = high
+        total_ref[0, t] = jnp.sum(weights.astype(jnp.float32), axis=1, keepdims=True)
+        sum_ref[0, t] = jnp.dot(weights, values, preferred_element_type=jnp.float32)
+
+
+def cache_part(bounds, queries, pages):
+    rows, steps, count, head_dim = queries.shape
+    span = pages.shape[1]
+    flops = 4 * rows * steps * count * span * head_dim
+    return pl.pallas_call(
+        cache_kernel,
+        grid_spec=pltpu.PrefetchScalarGridSpec(
+            num_scalar_prefetch=1,
+            grid=(rows,),
+            in_specs=[
+                pl.BlockSpec((1, steps, count, head_dim), lambda r, b: (r, 0, 0, 0)),
+                pl.BlockSpec((1, span, pages.shape[2]), lambda r, b: (r, 0, 0)),
+            ],
+            out_specs=[
+                pl.BlockSpec((1, steps, count, 1), lambda r, b: (r, 0, 0, 0)),
+                pl.BlockSpec((1, steps, count, 1), lambda r, b: (r, 0, 0, 0)),
+                pl.BlockSpec((1, steps, count, head_dim), lambda r, b: (r, 0, 0, 0)),
+            ],
+        ),
+        out_shape=[
+            jax.ShapeDtypeStruct((rows, steps, count, 1), jnp.float32),
+            jax.ShapeDtypeStruct((rows, steps, count, 1), jnp.float32),
+            jax.ShapeDtypeStruct((rows, steps, count, head_dim), jnp.float32),
+        ],
+        cost_estimate=pl.CostEstimate(
+            flops=flops,
+            transcendentals=rows * steps * count * span,
+            bytes_accessed=pages.size * 2 + queries.size * 2 + rows * steps * count * (head_dim + 2) * 4,
+        ),
+    )(bounds, queries, pages)
 
 
 def on_device(
@@ -124,24 +180,19 @@
 
     length = lengths[serving[offset_of]]
     first_page = jnp.maximum(length - WINDOW + 1, 0) // PAGE
-    key_pos = first_page[:, None] * PAGE + jnp.arange(span, dtype=jnp.int32)[None, :]
     device = group * kv_count + member
     pages = pool[table[offset_of] - device * pool.shape[0]].reshape(rows, span, 2 * head_dim)
-    keys = pages[:, :, :head_dim]
-    values = pages[:, :, head_dim:]
     scale = head_dim ** (-0.5)
-    scores = jnp.einsum(
-        "jtrhd,rkd->jtrhk", queries, keys, preferred_element_type=jnp.float32
-    ) * scale
     step_ids = jnp.arange(steps, dtype=jnp.int32)
-    allowed = (key_pos[None, :, :] < length[None, :, None]) & (
-        key_pos[None, :, :] > length[None, :, None] + step_ids[:, None, None] - WINDOW
-    )
-    scores = jnp.where(allowed[None, :, :, None, :], scores, NEGATIVE)
-    high_c = jnp.max(scores, axis=-1)
-    weights = jnp.exp(scores - high_c[..., None]).astype(jnp.bfloat16)
-    total_c = jnp.sum(weights.astype(jnp.float32), axis=-1)
-    sum_c = jnp.einsum("jtrhk,rkd->jtrhd", weights, values, preferred_element_type=jnp.float32)
+    base = first_page * PAGE
+    lo = length[:, None] + step_ids[None, :] - WINDOW - base[:, None]
+    hi = jnp.broadcast_to((length - base)[:, None], (rows, steps))
+    bounds = jnp.stack([lo, hi], axis=-1).reshape(rows * steps * 2)
+    by_row = jnp.transpose(queries, (2, 1, 0, 3, 4)).reshape(rows, steps, BEAMS * heads, head_dim)
+    high_c, total_c, sum_c = cache_part(bounds, by_row, pages)
+    high_c = jnp.transpose(high_c.reshape(rows, steps, BEAMS, heads), (2, 1, 0, 3))
+    total_c = jnp.transpose(total_c.reshape(rows, steps, BEAMS, heads), (2, 1, 0, 3))
+    sum_c = jnp.transpose(sum_c.reshape(rows, steps, BEAMS, heads, head_dim), (2, 1, 0, 3, 4))
 
     new_keys = listed[..., :head_dim]
     new_values = listed[..., head_dim:]

time: 195 us -> 194 us (level)
  Pallas kernels: 0 us -> 15.9 us
  matrix products: 34.7 us -> 19.3 us
  other arithmetic: 21.8 us -> 15.8 us
  local copies, waits for them, and re-layouts: 24.3 us -> 30.3 us
    dot_general x2 -> x0, matrix products: 18.2 us -> none  [the longest x1 9.63 us: on_device(): jnp.einsum('jtrhk,rkd->jtrhd', weights, values, preferred_element_type=jn...]
    pallas_call x0 -> x1, Pallas kernels: none -> 15.9 us  [cache_part(): pl.pallas_call(cache_kernel, grid_spec=pltpu.PrefetchScalarGridSpec(num_s...]
    reduce_sum x1 -> x0, other arithmetic: 11 us -> none  [on_device(): total_c = jnp.sum(weights.astype(jnp.float32), axis=-1)]
    pallas_call x0 -> x2, other arithmetic: none -> 4.05 us  [cache_part(): pl.pallas_call(cache_kernel, grid_spec=pltpu.PrefetchScalarGridSpec(num_s...]
    reshape x0 -> x5, local copies, waits for them, and re-layouts: none -> 3.55 us  [the longest x1 1.66 us: on_device(): (weighted / totals[..., None]).astype(jnp.bfloat16)]
    pallas_call x0 -> x1, local copies, waits for them, and re-layouts: none -> 2.32 us  [cache_part(): pl.pallas_call(cache_kernel, grid_spec=pltpu.PrefetchScalarGridSpec(num_s...]
where the time goes in v4:
time: 194 us; the launch traced here: 193 us
  waiting for transfers between devices  58.9 us (30%)
  local copies, waits for them, and re-layouts  30.3 us (16%)
  starting transfers between devices  28.1 us (14%)
  blocking collectives  24 us (12%)
  matrix products  19.3 us (10%)
  Pallas kernels  15.9 us (8%)
  other arithmetic  15.8 us (8%)
    all_to_all x1, blocking collectives, on_device(): lax.all_to_all(outgoing_att, 'kv', split_axis=0, concat_axis=0, tiled=True)  24 us
    all_to_all x1, waiting for transfers between devices, on_device(): lax.all_to_all(leaving, ('req', 'kv'), 0, 0, tiled=True)  23.9 us
    all_to_all x1, waiting for transfers between devices, on_device(): lax.all_to_all(jnp.broadcast_to(mlp_own[None], (kv_count,) + mlp_own.shap...  18.8 us
    pallas_call x1, Pallas kernels, cache_part(): pl.pallas_call(cache_kernel, grid_spec=pltpu.PrefetchScalarGridSpec(num_s...  15.9 us
    all_to_all x1, waiting for transfers between devices, on_device(): lax.all_to_all(jnp.broadcast_to(packed[None], (kv_count,) + packed.shape)...  14.3 us
    all_to_all x1, starting transfers between devices, on_device(): lax.all_to_all(leaving, ('req', 'kv'), 0, 0, tiled=True)  10.2 us
    gather x1, local copies, waits for them, and re-layouts, on_device(): pool[table[offset_of] - device * pool.shape[0]]  7.81 us
    all_to_all x1, starting transfers between devices, on_device(): lax.all_to_all(jnp.broadcast_to(packed[None], (kv_count,) + packed.shape)...  7.78 us
  transfers between devices with their start and end apart: 4, of which 4 were waited for; matrix products, arithmetic and copies ran while one was open for 6% of the time, Pallas kernels for 0%

profile of v4, /device:TPU:1, one launch (start us, length us, event | category | flops | bytes accessed | tf_op | source)
XLA Modules:
  0.0 192.9 jit_solution(2630385049576042424)
XLA Ops:
  5.0 1.7 gather_fusion
  7.4 5.8 %all-to-all-start = ((bf16[4,8,1,1536]{3,0,2,1:T(4,128)(2,1)}), bf16[4,8,1,1536]{3,0,2,1:T(4,128)(2,1)S(1)}, u32[]{:S(2)}, u32[]{:S(2)}) async-start(bf16[4,8,1,1536]{3,0,2,1:T(4,128)(2,1)} %copy.181), calls=%async_computation | async-start | bytes 196608 | tf_op jit(solution)/shard_map/all_to_all | solution.py:139
  16.3 1.9 all-to-all-done
  18.9 3.3 %convolution_convert_fusion = bf16[32,1536]{1,0:T(8,128)(2,1)S(1)} fusion(bf16[1536,1536]{1,0:T(8,128)(2,1)} %param.21, f32[4,8,1,1536]{3,0,2,1:T(4,128)S(1)} %convert_element_type.105, f32[1536]{0:T(1024)S(1)} %copy-done.4, f32[32]{0:T(128)S(1)} %rsqrt.20), kind=kOutput, calls=%fused_computation.12 | convolution fusion | flops 151191552 | bytes 5019776 | tf_op jit(solution)/shard_map/dot_general | solution.py:150
  23.6 7.8 %all-to-all-start.1 = ((bf16[16,4,8,1792]{3,2,1,0:T(8,128)(2,1)}), bf16[16,4,8,1792]{3,2,1,0:T(8,128)(2,1)S(1)}, u32[]{:S(2)}, u32[]{:S(2)}) async-start(bf16[16,4,8,1792]{3,2,1,0:T(8,128)(2,1)} %broadcast_in_dim.418), calls=%async_computation.1 | async-start | bytes 3670016 | tf_op jit(solution)/shard_map/all_to_all | solution.py:153
  31.8 7.8 %gather_fusion.5 = bf16[72,128,256]{2,1,0:T(8,128)(2,1)} fusion(bf16[72,128,256]{2,1,0:T(8,128)(2,1)} %param.19, s32[1024]{0:T(1024)S(1)} %pad_clamp_fusion), kind=kCustom, calls=%fused_computation.5 | custom fusion | bytes 9437472 | tf_op jit(solution)/shard_map/gather | solution.py:184
  40.4 14.3 %all-to-all-done.1 = bf16[16,4,8,1792]{3,2,1,0:T(8,128)(2,1)S(1)} async-done(((bf16[16,4,8,1792]{3,2,1,0:T(8,128)(2,1)}), bf16[16,4,8,1792]{3,2,1,0:T(8,128)(2,1)S(1)}, u32[]{:S(2)}, u32[]{:S(2)}) %all-to-all-start.1) | async-done | bytes 1835040 | tf_op jit(solution)/shard_map/all_to_all | solution.py:153
  59.0 15.9 %shard_map.136 = (f32[8,4,96,1]{3,2,1,0:T(8,128)}, f32[8,4,96,1]{3,2,1,0:T(8,128)}, f32[8,4,96,128]{3,2,1,0:T(8,128)}) custom-call(s32[64]{0:T(128)} %reshape.346.bounds_ref, bf16[8,4,96,128]{3,2,1,0:T(8,128)(2,1)} %copy.195.q_ref, bf16[8,1152,256]{2,1,0:T(8,128)(2,1)} %bitcast.134), custom_call_target="tpu_custom_call" | custom-call | flops 1811939328 | bytes 7102464 | tf_op jit(solution)/shard_map/pallas_call | solution.py:68
  75.0 2.3 %copy.196 = f32[8,4,96,128]{3,0,2,1:T(8,128)S(1)} copy(f32[8,4,96,128]{3,2,1,0:T(8,128)} %get-tuple-element.10) | data formatting | bytes 3145728 | tf_op jit(solution)/shard_map/pallas_call | solution.py:68
  77.3 2.0 %reduce.12 = f32[8,4,96]{2,1,0:T(4,128)S(1)} reduce(f32[8,4,96,1]{3,2,1,0:T(8,128)} %get-tuple-element.11, f32[]{:T(128)} %constant.180), dimensions={3}, to_apply=%get-tuple-element.11.reduce_sub_computation | reduce | bytes 24580 | tf_op jit(solution)/shard_map/pallas_call | solution.py:68
  79.3 2.0 %reduce.13 = f32[8,4,96]{2,1,0:T(4,128)S(1)} reduce(f32[8,4,96,1]{3,2,1,0:T(8,128)} %get-tuple-element.12, f32[]{:T(128)} %constant.180), dimensions={3}, to_apply=%get-tuple-element.12.reduce_sub_computation | reduce | bytes 24580 | tf_op jit(solution)/shard_map/pallas_call | solution.py:68
  83.8 1.8 fusion.47
  86.3 3.5 %fusion.5 = bf16[8,4,8,12,128]{4,3,2,1,0:T(8,128)(2,1)} fusion(f32[8,4,8,12,128]{4,0,3,2,1:T(8,128)S(1)} %bitcast.140, f32[8,4,8,12]{3,2,1,0:T(8,128)S(1)} %get-tuple-element.37, f32[8,4,8,12]{3,2,1,0:T(8,128)S(1)} %get-tuple-element.38, f32[8,4,8,12]{3,2,1,0:T(8,128)S(1)} %get-tuple-element.39, bf16[4,4,8,8,256]{4,1,3,0,2:T(4,128)(2,1)S(1)} %pad_maximum_fusion, ...), kind=kOutput, calls=%fused_computation.16 | convolution fusion | flops 5148672 | bytes 3670528 | tf_op jit(solution)/shard_map/jtrhs,tsjrd->jtrhd/dot_general | solution.py:208
  89.8 1.7 reshape.355
  91.8 24.0 %all_to_all.25 = bf16[16,4,8,1536]{3,2,1,0:T(8,128)(2,1)S(1)} all-to-all(bf16[16,4,8,1536]{3,2,1,0:T(8,128)(2,1)S(1)} %bitcast_select_fusion), channel_id=1, replica_groups=mesh['req'=8,'kv'=16] {'kv'}, dimensions={0} | all-to-all | bytes 3145728 | tf_op jit(solution)/shard_map/all_to_all | solution.py:227
  116.0 3.4 %multiply_reduce_fusion = (f32[32]{0:T(128)S(1)}, f32[32,1536]{1,0:T(8,128)S(1)}) fusion(bf16[1536,1536]{1,0:T(8,128)(2,1)} %param.23, bf16[4,8,1536]{2,1,0:T(8,128)(2,1)S(1)} %reduce_sum.312, f32[4,8,1,1536]{3,0,2,1:T(4,128)S(1)} %convert_element_type.105), kind=kOutput, calls=%fused_computation.61 | convolution fusion | flops 151240672 | bytes 5210240 | tf_op jit(solution)/shard_map/dot_general | solution.py:233
  120.8 4.4 %all-to-all-start.3 = ((bf16[16,32,1536]{2,1,0:T(8,128)(2,1)}), bf16[16,32,1536]{2,1,0:T(8,128)(2,1)S(1)}, u32[]{:S(2)}, u32[]{:S(2)}) async-start(bf16[16,32,1536]{2,1,0:T(8,128)(2,1)} %broadcast_in_dim.448), calls=%async_computation.3 | async-start | bytes 3145728 | tf_op jit(solution)/shard_map/all_to_all | solution.py:236
  125.2 18.8 %all-to-all-done.3 = bf16[16,32,1536]{2,1,0:T(8,128)(2,1)S(1)} async-done(((bf16[16,32,1536]{2,1,0:T(8,128)(2,1)}), bf16[16,32,1536]{2,1,0:T(8,128)(2,1)S(1)}, u32[]{:S(2)}, u32[]{:S(2)}) %all-to-all-start.3) | async-done | bytes 1572896 | tf_op jit(solution)/shard_map/all_to_all | solution.py:236
  144.0 2.7 %fusion.48 = f32[512,288]{0,1:T(8,128)} fusion(bf16[512,1536]{1,0:T(8,128)(2,1)S(1)} %bitcast.131, bf16[1536,288]{0,1:T(8,128)(2,1)} %param.25), kind=kOutput, calls=%fused_computation.145 | convolution fusion | flops 452984832 | bytes 3047424 | tf_op jit(solution)/shard_map/dot_general | solution.py:239
  146.7 4.4 %fusion.8 = f32[512,1536]{1,0:T(8,128)} fusion(bf16[288,1536]{1,0:T(8,128)(2,1)S(1)} %copy-done, bf16[512,1536]{1,0:T(8,128)(2,1)S(1)} %bitcast.132, bf16[1536,288]{0,1:T(8,128)(2,1)S(1)} %copy-done.1, f32[512,288]{0,1:T(8,128)} %fusion.48), kind=kOutput, calls=%fused_computation.23 | convolution fusion | flops 907444224 | bytes 7077888 | tf_op jit(solution)/shard_map/dot_general | solution.py:242
  151.1 3.8 %fusion = bf16[16,4,8,1536]{3,0,2,1:T(8,128)(2,1)S(1)} fusion(f32[16,4,8,1536]{3,2,1,0:T(8,128)} %bitcast.130, f32[4,8,1536]{2,1,0:T(8,128)S(1)} %bitcast.139, pred[16]{0:T(512)(128)(4,1)S(1)} %iota_compare_fusion.13), kind=kLoop, calls=%fused_computation.8 | loop fusion | flops 2359296 | bytes 4915216 | tf_op jit(solution)/shard_map/convert_element_type | solution.py:246
  155.0 2.4 %copy.215 = bf16[128,4,1536]{2,1,0:T(4,128)(2,1)} copy(bf16[128,4,1536]{2,0,1:T(8,128)(2,1)S(1)} %bitcast.133) | data formatting | bytes 3145728 | tf_op jit(solution)/shard_map/reshape | solution.py:248
  157.3 10.2 %all-to-all-start.4 = ((bf16[128,4,1536]{2,1,0:T(4,128)(2,1)}), bf16[128,4,1536]{2,1,0:T(4,128)(2,1)S(1)}, u32[]{:S(2)}, u32[]{:S(2)}) async-start(bf16[128,4,1536]{2,1,0:T(4,128)(2,1)} %copy.215), calls=%async_computation.4 | async-start | bytes 3145728 | tf_op jit(solution)/shard_map/all_to_all | solution.py:249
  167.6 23.9 %all-to-all-done.4 = bf16[128,4,1536]{2,1,0:T(4,128)(2,1)S(1)} async-done(((bf16[128,4,1536]{2,1,0:T(4,128)(2,1)}), bf16[128,4,1536]{2,1,0:T(4,128)(2,1)S(1)}, u32[]{:S(2)}, u32[]{:S(2)}) %all-to-all-start.4) | async-done | bytes 1572896 | tf_op jit(solution)/shard_map/all_to_all | solution.py:249
  (111 shorter events, 22.6 us)
Async XLA Ops:
  0.0 146.7 %copy-start = (bf16[288,1536]{1,0:T(8,128)(2,1)S(1)}, bf16[288,1536]{1,0:T(8,128)(2,1)}, u32[]{:S(2)}) copy-start(bf16[288,1536]{1,0:T(8,128)(2,1)} %param.27) | copy-start | bytes 2654212
  0.0 13.4 %copy-start.3 = (s32[8,9]{1,0:T(8,128)S(1)}, s32[8,9]{1,0:T(8,128)}, u32[]{:S(2)}) copy-start(s32[8,9]{1,0:T(8,128)} %param.18) | copy-start | bytes 868
  0.0 18.6 %copy-start.4 = (f32[1536]{0:T(1024)S(1)}, f32[1536]{0:T(1024)}, u32[]{:S(2)}) copy-start(f32[1536]{0:T(1024)} %param.20) | copy-start | bytes 18436
  0.0 18.6 %copy-start.2 = (bf16[1536,256]{1,0:T(8,128)(2,1)S(1)}, bf16[1536,256]{1,0:T(8,128)(2,1)}, u32[]{:S(2)}) copy-start(bf16[1536,256]{1,0:T(8,128)(2,1)} %param.22) | copy-start | bytes 2359300
  7.4 10.8 %all-to-all-start = ((bf16[4,8,1,1536]{3,0,2,1:T(4,128)(2,1)}), bf16[4,8,1,1536]{3,0,2,1:T(4,128)(2,1)S(1)}, u32[]{:S(2)}, u32[]{:S(2)}) async-start(bf16[4,8,1,1536]{3,0,2,1:T(4,128)(2,1)} %copy.181), calls=%async_computation | async-start | bytes 196608 | tf_op jit(solution)/shard_map/all_to_all | solution.py:139
  23.6 31.0 %all-to-all-start.1 = ((bf16[16,4,8,1792]{3,2,1,0:T(8,128)(2,1)}), bf16[16,4,8,1792]{3,2,1,0:T(8,128)(2,1)S(1)}, u32[]{:S(2)}, u32[]{:S(2)}) async-start(bf16[16,4,8,1792]{3,2,1,0:T(8,128)(2,1)} %broadcast_in_dim.418), calls=%async_computation.1 | async-start | bytes 3670016 | tf_op jit(solution)/shard_map/all_to_all | solution.py:153
  79.3 4.5 %copy-start.6 = (pred[4,4]{1,0:T(4,128)(4,1)S(1)}, pred[4,4]{1,0:T(4,128)(4,1)}, u32[]{:S(2)}) copy-start(pred[4,4]{1,0:T(4,128)(4,1)} %iota_compare_fusion.12) | copy-start | bytes 52
  116.0 3.4 %copy-start.5 = (f32[1536]{0:T(1024)S(1)}, f32[1536]{0:T(1024)}, u32[]{:S(2)}) copy-start(f32[1536]{0:T(1024)} %param.24) | copy-start | bytes 18436
  120.8 23.2 %all-to-all-start.3 = ((bf16[16,32,1536]{2,1,0:T(8,128)(2,1)}), bf16[16,32,1536]{2,1,0:T(8,128)(2,1)S(1)}, u32[]{:S(2)}, u32[]{:S(2)}) async-start(bf16[16,32,1536]{2,1,0:T(8,128)(2,1)} %broadcast_in_dim.448), calls=%async_computation.3 | async-start | bytes 3145728 | tf_op jit(solution)/shard_map/all_to_all | solution.py:236
  144.0 2.7 %copy-start.1 = (bf16[1536,288]{0,1:T(8,128)(2,1)S(1)}, bf16[1536,288]{0,1:T(8,128)(2,1)}, u32[]{:S(2)}) copy-start(bf16[1536,288]{0,1:T(8,128)(2,1)} %param.26) | copy-start | bytes 2654212
  157.3 34.1 %all-to-all-start.4 = ((bf16[128,4,1536]{2,1,0:T(4,128)(2,1)}), bf16[128,4,1536]{2,1,0:T(4,128)(2,1)S(1)}, u32[]{:S(2)}, u32[]{:S(2)}) async-start(bf16[128,4,1536]{2,1,0:T(4,128)(2,1)} %copy.215), calls=%async_computation.4 | async-start | bytes 3145728 | tf_op jit(solution)/shard_map/all_to_all | solution.py:249

commit v5 on v4

--- a/solution.py
+++ b/solution.py
@@ -39,58 +39,88 @@
     return jnp.sum(jnp.where(picks[..., None], table[None, :, :, :], 0), axis=1).astype(table.dtype)
 
 
-def cache_kernel(bounds_ref, q_ref, kv_ref, high_ref, total_ref, sum_ref):
+def attend_kernel(bounds_ref, held_ref, q_ref, kv_ref, new_ref, out_ref):
     r = pl.program_id(0)
     steps = q_ref.shape[1]
-    head_dim = q_ref.shape[3]
+    beams = q_ref.shape[2]
+    head_dim = q_ref.shape[4]
+    scale = head_dim ** (-0.5)
     keys = kv_ref[0, :, :head_dim]
     values = kv_ref[0, :, head_dim:]
     pos = lax.broadcasted_iota(jnp.int32, (1, kv_ref.shape[1]), 1)
     for t in range(steps):
         lo = bounds_ref[(r * steps + t) * 2]
         hi = bounds_ref[(r * steps + t) * 2 + 1]
-        scores = lax.dot_general(
-            q_ref[0, t], keys, (((1,), (1,)), ((), ())), preferred_element_type=jnp.float32
-        ) * (head_dim ** (-0.5))
         allowed = (pos > lo) & (pos < hi)
-        scores = jnp.where(allowed, scores, NEGATIVE)
-        high = jnp.max(scores, axis=1, keepdims=True)
-        weights = jnp.exp(scores - high).astype(jnp.bfloat16)
-        high_ref[0, t] = high
-        total_ref[0, t] = jnp.sum(weights.astype(jnp.float32), axis=1, keepdims=True)
-        sum_ref[0, t] = jnp.dot(weights, values, preferred_element_type=jnp.float32)
-
-
-def cache_part(bounds, queries, pages):
-    rows, steps, count, head_dim = queries.shape
+
+        def one_beam(j, carry, t=t, allowed=allowed):
+            flag = held_ref[(r * steps + t) * beams + j]
+
+            @pl.when(flag != 0)
+            def _():
+                query = q_ref[0, t, j]
+                scores = lax.dot_general(
+                    query, keys, (((1,), (1,)), ((), ())), preferred_element_type=jnp.float32
+                ) * scale
+                scores = jnp.where(allowed, scores, NEGATIVE)
+                high_c = jnp.max(scores, axis=1, keepdims=True)
+                weights = jnp.exp(scores - high_c).astype(jnp.bfloat16)
+                total_c = jnp.sum(weights.astype(jnp.float32), axis=1, keepdims=True)
+                sum_c = jnp.dot(weights, values, preferred_element_type=jnp.float32)
+                wide = query.astype(jnp.float32)
+                entries = new_ref[0, t, j].astype(jnp.float32)
+                fresh = [
+                    jnp.sum(wide * entries[s : s + 1, :head_dim], axis=1, keepdims=True) * scale
+                    for s in range(t + 1)
+                ]
+                high_n = fresh[0]
+                for one in fresh[1:]:
+                    high_n = jnp.maximum(high_n, one)
+                fresh_w = [jnp.exp(one - high_n).astype(jnp.bfloat16).astype(jnp.float32) for one in fresh]
+                total_n = fresh_w[0]
+                sum_n = fresh_w[0] * entries[0:1, head_dim:]
+                for s in range(1, t + 1):
+                    total_n = total_n + fresh_w[s]
+                    sum_n = sum_n + fresh_w[s] * entries[s : s + 1, head_dim:]
+                highest = jnp.maximum(high_c, high_n)
+                scale_c = jnp.exp(high_c - highest)
+                scale_n = jnp.exp(high_n - highest)
+                totals = total_c * scale_c + total_n * scale_n
+                weighted = sum_c * scale_c + sum_n * scale_n
+                out_ref[0, t, j] = (weighted / totals).astype(out_ref.dtype)
+
+            @pl.when(flag == 0)
+            def _():
+                out_ref[0, t, j] = jnp.zeros(out_ref.shape[3:], out_ref.dtype)
+
+            return carry
+
+        lax.fori_loop(0, beams, one_beam, 0)
+
+
+def attend(bounds, held, queries, pages, listed):
+    rows, steps, beams, padded, head_dim = queries.shape
     span = pages.shape[1]
-    flops = 4 * rows * steps * count * span * head_dim
+    flops = 4 * rows * steps * padded * span * head_dim
     return pl.pallas_call(
-        cache_kernel,
+        attend_kernel,
         grid_spec=pltpu.PrefetchScalarGridSpec(
-            num_scalar_prefetch=1,
+            num_scalar_prefetch=2,
             grid=(rows,),
             in_specs=[
-                pl.BlockSpec((1, steps, count, head_dim), lambda r, b: (r, 0, 0, 0)),
-                pl.BlockSpec((1, span, pages.shape[2]), lambda r, b: (r, 0, 0)),
+                pl.BlockSpec((1, steps, beams, padded, head_dim), lambda r, b, h: (r, 0, 0, 0, 0)),
+                pl.BlockSpec((1, span, pages.shape[2]), lambda r, b, h: (r, 0, 0)),
+                pl.BlockSpec((1,) + listed.shape[1:], lambda r, b, h: (r, 0, 0, 0, 0)),
             ],
-            out_specs=[
-                pl.BlockSpec((1, steps, count, 1), lambda r, b: (r, 0, 0, 0)),
-                pl.BlockSpec((1, steps, count, 1), lambda r, b: (r, 0, 0, 0)),
-                pl.BlockSpec((1, steps, count, head_dim), lambda r, b: (r, 0, 0, 0)),
-            ],
+            out_specs=pl.BlockSpec((1, steps, beams, padded, head_dim), lambda r, b, h: (r, 0, 0, 0, 0)),
         ),
-        out_shape=[
-            jax.ShapeDtypeStruct((rows, steps, count, 1), jnp.float32),
-            jax.ShapeDtypeStruct((rows, steps, count, 1), jnp.float32),
-            jax.ShapeDtypeStruct((rows, steps, count, head_dim), jnp.float32),
-        ],
+        out_shape=jax.ShapeDtypeStruct(queries.shape, jnp.bfloat16),
         cost_estimate=pl.CostEstimate(
             flops=flops,
-            transcendentals=rows * steps * count * span,
-            bytes_accessed=pages.size * 2 + queries.size * 2 + rows * steps * count * (head_dim + 2) * 4,
+            transcendentals=rows * steps * padded * span,
+            bytes_accessed=pages.size * 2 + queries.size * 4 + listed.size * 2,
         ),
-    )(bounds, queries, pages)
+    )(bounds, held, queries, pages, listed)
 
 
 def on_device(
@@ -188,36 +218,12 @@
     lo = length[:, None] + step_ids[None, :] - WINDOW - base[:, None]
     hi = jnp.broadcast_to((length - base)[:, None], (rows, steps))
     bounds = jnp.stack([lo, hi], axis=-1).reshape(rows * steps * 2)
-    by_row = jnp.transpose(queries, (2, 1, 0, 3, 4)).reshape(rows, steps, BEAMS * heads, head_dim)
-    high_c, total_c, sum_c = cache_part(bounds, by_row, pages)
-    high_c = jnp.transpose(high_c.reshape(rows, steps, BEAMS, heads), (2, 1, 0, 3))
-    total_c = jnp.transpose(total_c.reshape(rows, steps, BEAMS, heads), (2, 1, 0, 3))
-    sum_c = jnp.transpose(sum_c.reshape(rows, steps, BEAMS, heads, head_dim), (2, 1, 0, 3, 4))
-
-    new_keys = listed[..., :head_dim]
-    new_values = listed[..., head_dim:]
-    fresh_scores = jnp.einsum(
-        "jtrhd,tsjrd->jtrhs", queries, new_keys, preferred_element_type=jnp.float32
-    ) * scale
-    counted = step_ids[None, :] <= step_ids[:, None]
-    fresh_scores = jnp.where(counted[None, :, None, None, :], fresh_scores, NEGATIVE)
-    high_n = jnp.max(fresh_scores, axis=-1)
-    fresh_weights = jnp.exp(fresh_scores - high_n[..., None]).astype(jnp.bfloat16)
-    fresh_weights = jnp.where(counted[None, :, None, None, :], fresh_weights, 0)
-    total_n = jnp.sum(fresh_weights.astype(jnp.float32), axis=-1)
-    sum_n = jnp.einsum(
-        "jtrhs,tsjrd->jtrhd", fresh_weights, new_values, preferred_element_type=jnp.float32
-    )
-
-    highest = jnp.maximum(high_c, high_n)
-    scale_c = jnp.exp(high_c - highest)
-    scale_n = jnp.exp(high_n - highest)
-    totals = total_c * scale_c + total_n * scale_n
-    weighted = sum_c * scale_c[..., None] + sum_n * scale_n[..., None]
-    attended = (weighted / totals[..., None]).astype(jnp.bfloat16).reshape(
-        BEAMS, steps, rows, qwidth
-    )
-    attended = jnp.where(held[..., None], attended, jnp.zeros_like(attended))
+    padded = jnp.pad(queries, ((0, 0), (0, 0), (0, 0), (0, 16 - heads), (0, 0)))
+    by_row = jnp.transpose(padded, (2, 1, 0, 3, 4))
+    held_flags = jnp.transpose(held, (2, 1, 0)).astype(jnp.int32).reshape(rows * steps * BEAMS)
+    listed_by_row = jnp.transpose(listed, (3, 0, 2, 1, 4))
+    attended = attend(bounds, held_flags, by_row, pages, listed_by_row)[:, :, :, :heads]
+    attended = jnp.transpose(attended, (2, 1, 0, 3, 4)).reshape(BEAMS, steps, rows, qwidth)
 
     spread = attended.reshape(BEAMS // 2, 1, 2, steps, rows, qwidth)
     in_half = (jnp.arange(halves, dtype=jnp.int32) == half)[None, :, None, None, None, None]

time: 194 us -> 206 us (1.062); the launches traced: 193 us -> 208 us
  blocking collectives: 24 us -> 50.4 us
  starting transfers between devices: 28.1 us -> 22.6 us
  other arithmetic: 15.8 us -> 10.4 us
  matrix products: 19.3 us -> 14.1 us
  waiting for transfers between devices: 58.9 us -> 63.5 us
  Pallas kernels: 15.9 us -> 18.7 us
  local copies, waits for them, and re-layouts: 30.3 us -> 27.9 us
    all_to_all x1, blocking collectives: 24 us -> 50.4 us  [on_device(): lax.all_to_all(outgoing_att, 'kv', split_axis=0, concat_axis=0, tiled=True)]
    dot_general x2 -> x0, matrix products: 5.27 us -> none  [the longest x1 3.46 us: on_device(): jnp.einsum('jtrhs,tsjrd->jtrhd', fresh_weights, new_values, preferred_ele...]
    all_to_all x1, starting transfers between devices: 10.2 us -> 5.13 us  [on_device(): lax.all_to_all(leaving, ('req', 'kv'), 0, 0, tiled=True)]
    all_to_all x1, waiting for transfers between devices: 18.8 us -> 23.6 us  [on_device(): lax.all_to_all(jnp.broadcast_to(mlp_own[None], (kv_count,) + mlp_own.shap...]
    pallas_call x2 -> x0, other arithmetic: 4.05 us -> none  [cache_part(): pl.pallas_call(cache_kernel, grid_spec=pltpu.PrefetchScalarGridSpec(num_s...]
    transpose x1 -> x3, local copies, waits for them, and re-layouts: 0.06 us -> 3.58 us  [the longest x2 2.32 us: on_device(): jnp.transpose(attended, (2, 1, 0, 3, 4)).reshape(BEAMS, steps, rows, qwidth)]
    pallas_call x1, Pallas kernels: 15.9 us -> 18.7 us  [attend(): pl.pallas_call(attend_kernel, grid_spec=pltpu.PrefetchScalarGridSpec(num_...]
    pallas_call x1 -> x0, local copies, waits for them, and re-layouts: 2.32 us -> none  [cache_part(): pl.pallas_call(cache_kernel, grid_spec=pltpu.PrefetchScalarGridSpec(num_s...]
where the time goes in v5:
time: 206 us; the launch traced here: 208 us
  waiting for transfers between devices  63.5 us (31%)
  blocking collectives  50.4 us (24%)
  local copies, waits for them, and re-layouts  27.9 us (14%)
  starting transfers between devices  22.6 us (11%)
  Pallas kernels  18.7 us (9%)
  matrix products  14.1 us (7%)
  other arithmetic  10.4 us (5%)
    all_to_all x1, blocking collectives, on_device(): lax.all_to_all(outgoing_att, 'kv', split_axis=0, concat_axis=0, tiled=True)  50.4 us
    all_to_all x1, waiting for transfers between devices, on_device(): lax.all_to_all(leaving, ('req', 'kv'), 0, 0, tiled=True)  24.1 us
    all_to_all x1, waiting for transfers between devices, on_device(): lax.all_to_all(jnp.broadcast_to(mlp_own[None], (kv_count,) + mlp_own.shap...  23.6 us
    pallas_call x1, Pallas kernels, attend(): pl.pallas_call(attend_kernel, grid_spec=pltpu.PrefetchScalarGridSpec(num_...  18.7 us
    all_to_all x1, waiting for transfers between devices, on_device(): lax.all_to_all(jnp.broadcast_to(packed[None], (kv_count,) + packed.shape)...  12.3 us
    gather x1, local copies, waits for them, and re-layouts, on_device(): pool[table[offset_of] - device * pool.shape[0]]  7.81 us
    all_to_all x1, starting transfers between devices, on_device(): lax.all_to_all(jnp.broadcast_to(packed[None], (kv_count,) + packed.shape)...  7.77 us
    all_to_all x1, starting transfers between devices, on_device(): lax.all_to_all(outgoing, 'req', split_axis=1, concat_axis=1, tiled=True)  5.8 us
  transfers between devices with their start and end apart: 4, of which 4 were waited for; matrix products, arithmetic and copies ran while one was open for 6% of the time, Pallas kernels for 0%

profile of v5, /device:TPU:1, one launch (start us, length us, event | category | flops | bytes accessed | tf_op | source)
XLA Modules:
  0.0 208.2 jit_solution(12939282456563321696)
XLA Ops:
  3.7 1.3 gather_fusion.2
  5.0 1.7 gather_fusion
  7.4 5.8 %all-to-all-start = ((bf16[4,8,1,1536]{3,0,2,1:T(4,128)(2,1)}), bf16[4,8,1,1536]{3,0,2,1:T(4,128)(2,1)S(1)}, u32[]{:S(2)}, u32[]{:S(2)}) async-start(bf16[4,8,1,1536]{3,0,2,1:T(4,128)(2,1)} %copy.113), calls=%async_computation | async-start | bytes 196608 | tf_op jit(solution)/shard_map/all_to_all | solution.py:169
  14.7 3.5 %all-to-all-done = bf16[4,8,1,1536]{3,0,2,1:T(4,128)(2,1)S(1)} async-done(((bf16[4,8,1,1536]{3,0,2,1:T(4,128)(2,1)}), bf16[4,8,1,1536]{3,0,2,1:T(4,128)(2,1)S(1)}, u32[]{:S(2)}, u32[]{:S(2)}) %all-to-all-start) | async-done | bytes 98336 | tf_op jit(solution)/shard_map/all_to_all | solution.py:169
  18.9 3.3 %convolution_convert_fusion = bf16[32,1536]{1,0:T(8,128)(2,1)S(1)} fusion(bf16[1536,1536]{1,0:T(8,128)(2,1)} %param.21, f32[4,8,1,1536]{3,0,2,1:T(4,128)S(1)} %convert_element_type.98, f32[1536]{0:T(1024)S(1)} %copy-done.4, f32[32]{0:T(128)S(1)} %rsqrt.20), kind=kOutput, calls=%fused_computation.12 | convolution fusion | flops 151191552 | bytes 5019776 | tf_op jit(solution)/shard_map/dot_general | solution.py:180
  22.2 1.5 broadcast_in_dim.375
  23.6 7.8 %all-to-all-start.1 = ((bf16[16,4,8,1792]{3,2,1,0:T(8,128)(2,1)}), bf16[16,4,8,1792]{3,2,1,0:T(8,128)(2,1)S(1)}, u32[]{:S(2)}, u32[]{:S(2)}) async-start(bf16[16,4,8,1792]{3,2,1,0:T(8,128)(2,1)} %broadcast_in_dim.375), calls=%async_computation.1 | async-start | bytes 3670016 | tf_op jit(solution)/shard_map/all_to_all | solution.py:183
  34.5 7.8 %gather_fusion.5 = bf16[72,128,256]{2,1,0:T(8,128)(2,1)} fusion(bf16[72,128,256]{2,1,0:T(8,128)(2,1)} %param.19, s32[1024]{0:T(1024)S(1)} %pad_clamp_fusion), kind=kCustom, calls=%fused_computation.5 | custom fusion | bytes 9437472 | tf_op jit(solution)/shard_map/gather | solution.py:214
  42.4 12.3 %all-to-all-done.1 = bf16[16,4,8,1792]{3,2,1,0:T(8,128)(2,1)S(1)} async-done(((bf16[16,4,8,1792]{3,2,1,0:T(8,128)(2,1)}), bf16[16,4,8,1792]{3,2,1,0:T(8,128)(2,1)S(1)}, u32[]{:S(2)}, u32[]{:S(2)}) %all-to-all-start.1) | async-done | bytes 1835040 | tf_op jit(solution)/shard_map/all_to_all | solution.py:183
  56.4 1.3 pad_bitcast_fusion.q_ref
  58.7 1.2 maximum_bitcast_fusion.new_ref
  59.9 18.7 %shard_map.136 = bf16[8,4,8,16,128]{4,3,2,1,0:T(8,128)(2,1)} custom-call(s32[64]{0:T(128)} %reshape.276.bounds_ref, s32[256]{0:T(256)} %reshape.291.held_ref, bf16[8,4,8,16,128]{4,3,2,1,0:T(8,128)(2,1)} %pad_bitcast_fusion.q_ref, bf16[8,1152,256]{2,1,0:T(8,128)(2,1)} %bitcast.109, bf16[8,4,8,4,256]{4,3,2,1,0:T(4,128)(2,1)} %maximum_bitcast_fusion.new_ref), custom_call_target="tpu_custom_call" | custom-call | flops 301989888 | bytes 7340032 | tf_op jit(solution)/shard_map/pallas_call | solution.py:105
  78.6 1.4 slice_bitcast_fusion
  81.1 50.4 %all_to_all.25 = bf16[16,4,8,1536]{3,2,1,0:T(8,128)(2,1)S(1)} all-to-all(bf16[16,4,8,1536]{3,2,1,0:T(8,128)(2,1)S(1)} %bitcast_select_fusion), channel_id=1, replica_groups=mesh['req'=8,'kv'=16] {'kv'}, dimensions={0} | all-to-all | bytes 3145728 | tf_op jit(solution)/shard_map/all_to_all | solution.py:233
  131.8 3.4 %multiply_reduce_fusion = (f32[32]{0:T(128)S(1)}, f32[32,1536]{1,0:T(8,128)S(1)}) fusion(bf16[1536,1536]{1,0:T(8,128)(2,1)} %param.23, bf16[4,8,1536]{2,1,0:T(8,128)(2,1)S(1)} %reduce_sum.302, f32[4,8,1,1536]{3,0,2,1:T(4,128)S(1)} %convert_element_type.98), kind=kOutput, calls=%fused_computation.49 | convolution fusion | flops 151240672 | bytes 5210240 | tf_op jit(solution)/shard_map/dot_general | solution.py:239
  135.3 1.3 broadcast_in_dim.402
  136.6 3.9 %all-to-all-start.3 = ((bf16[16,32,1536]{2,1,0:T(8,128)(2,1)}), bf16[16,32,1536]{2,1,0:T(8,128)(2,1)S(1)}, u32[]{:S(2)}, u32[]{:S(2)}) async-start(bf16[16,32,1536]{2,1,0:T(8,128)(2,1)} %broadcast_in_dim.402), calls=%async_computation.3 | async-start | bytes 3145728 | tf_op jit(solution)/shard_map/all_to_all | solution.py:242
  140.5 23.6 %all-to-all-done.3 = bf16[16,32,1536]{2,1,0:T(8,128)(2,1)S(1)} async-done(((bf16[16,32,1536]{2,1,0:T(8,128)(2,1)}), bf16[16,32,1536]{2,1,0:T(8,128)(2,1)S(1)}, u32[]{:S(2)}, u32[]{:S(2)}) %all-to-all-start.3) | async-done | bytes 1572896 | tf_op jit(solution)/shard_map/all_to_all | solution.py:242
  164.2 2.7 %fusion.33 = f32[512,288]{0,1:T(8,128)} fusion(bf16[512,1536]{1,0:T(8,128)(2,1)S(1)} %bitcast.111, bf16[1536,288]{0,1:T(8,128)(2,1)} %param.25), kind=kOutput, calls=%fused_computation.126 | convolution fusion | flops 452984832 | bytes 3047424 | tf_op jit(solution)/shard_map/dot_general | solution.py:245
  166.9 4.4 %fusion.4 = f32[512,1536]{1,0:T(8,128)} fusion(bf16[288,1536]{1,0:T(8,128)(2,1)S(1)} %copy-done, bf16[512,1536]{1,0:T(8,128)(2,1)S(1)} %bitcast.112, bf16[1536,288]{0,1:T(8,128)(2,1)S(1)} %copy-done.1, f32[512,288]{0,1:T(8,128)} %fusion.33), kind=kOutput, calls=%fused_computation.17 | convolution fusion | flops 907444224 | bytes 7077888 | tf_op jit(solution)/shard_map/dot_general | solution.py:248
  171.3 3.8 %fusion = bf16[16,4,8,1536]{3,0,2,1:T(8,128)(2,1)S(1)} fusion(f32[16,4,8,1536]{3,2,1,0:T(8,128)} %bitcast.110, f32[4,8,1536]{2,1,0:T(8,128)S(1)} %bitcast.118, pred[16]{0:T(512)(128)(4,1)S(1)} %iota_compare_fusion.12), kind=kLoop, calls=%fused_computation.8 | loop fusion | flops 2359296 | bytes 4915216 | tf_op jit(solution)/shard_map/convert_element_type | solution.py:252
  175.1 2.4 %copy.137 = bf16[128,4,1536]{2,1,0:T(4,128)(2,1)} copy(bf16[128,4,1536]{2,0,1:T(8,128)(2,1)S(1)} %bitcast.113) | data formatting | bytes 3145728 | tf_op jit(solution)/shard_map/reshape | solution.py:254
  177.5 5.1 %all-to-all-start.4 = ((bf16[128,4,1536]{2,1,0:T(4,128)(2,1)}), bf16[128,4,1536]{2,1,0:T(4,128)(2,1)S(1)}, u32[]{:S(2)}, u32[]{:S(2)}) async-start(bf16[128,4,1536]{2,1,0:T(4,128)(2,1)} %copy.137), calls=%async_computation.4 | async-start | bytes 3145728 | tf_op jit(solution)/shard_map/all_to_all | solution.py:255
  182.7 24.1 %all-to-all-done.4 = bf16[128,4,1536]{2,1,0:T(4,128)(2,1)S(1)} async-done(((bf16[128,4,1536]{2,1,0:T(4,128)(2,1)}), bf16[128,4,1536]{2,1,0:T(4,128)(2,1)S(1)}, u32[]{:S(2)}, u32[]{:S(2)}) %all-to-all-start.4) | async-done | bytes 1572896 | tf_op jit(solution)/shard_map/all_to_all | solution.py:255
  (101 shorter events, 14.9 us)
Async XLA Ops:
  0.0 166.9 %copy-start = (bf16[288,1536]{1,0:T(8,128)(2,1)S(1)}, bf16[288,1536]{1,0:T(8,128)(2,1)}, u32[]{:S(2)}) copy-start(bf16[288,1536]{1,0:T(8,128)(2,1)} %param.27) | copy-start | bytes 2654212
  0.0 13.2 %copy-start.3 = (s32[8,9]{1,0:T(8,128)S(1)}, s32[8,9]{1,0:T(8,128)}, u32[]{:S(2)}) copy-start(s32[8,9]{1,0:T(8,128)} %param.18) | copy-start | bytes 868
  0.0 18.6 %copy-start.4 = (f32[1536]{0:T(1024)S(1)}, f32[1536]{0:T(1024)}, u32[]{:S(2)}) copy-start(f32[1536]{0:T(1024)} %param.20) | copy-start | bytes 18436
  0.0 18.6 %copy-start.2 = (bf16[1536,256]{1,0:T(8,128)(2,1)S(1)}, bf16[1536,256]{1,0:T(8,128)(2,1)}, u32[]{:S(2)}) copy-start(bf16[1536,256]{1,0:T(8,128)(2,1)} %param.22) | copy-start | bytes 2359300
  7.4 10.8 %all-to-all-start = ((bf16[4,8,1,1536]{3,0,2,1:T(4,128)(2,1)}), bf16[4,8,1,1536]{3,0,2,1:T(4,128)(2,1)S(1)}, u32[]{:S(2)}, u32[]{:S(2)}) async-start(bf16[4,8,1,1536]{3,0,2,1:T(4,128)(2,1)} %copy.113), calls=%async_computation | async-start | bytes 196608 | tf_op jit(solution)/shard_map/all_to_all | solution.py:169
  23.6 31.0 %all-to-all-start.1 = ((bf16[16,4,8,1792]{3,2,1,0:T(8,128)(2,1)}), bf16[16,4,8,1792]{3,2,1,0:T(8,128)(2,1)S(1)}, u32[]{:S(2)}, u32[]{:S(2)}) async-start(bf16[16,4,8,1792]{3,2,1,0:T(8,128)(2,1)} %broadcast_in_dim.375), calls=%async_computation.1 | async-start | bytes 3670016 | tf_op jit(solution)/shard_map/all_to_all | solution.py:183
  131.8 3.4 %copy-start.5 = (f32[1536]{0:T(1024)S(1)}, f32[1536]{0:T(1024)}, u32[]{:S(2)}) copy-start(f32[1536]{0:T(1024)} %param.24) | copy-start | bytes 18436
  136.6 27.6 %all-to-all-start.3 = ((bf16[16,32,1536]{2,1,0:T(8,128)(2,1)}), bf16[16,32,1536]{2,1,0:T(8,128)(2,1)S(1)}, u32[]{:S(2)}, u32[]{:S(2)}) async-start(bf16[16,32,1536]{2,1,0:T(8,128)(2,1)} %broadcast_in_dim.402), calls=%async_computation.3 | async-start | bytes 3145728 | tf_op jit(solution)/shard_map/all_to_all | solution.py:242
  164.2 2.7 %copy-start.1 = (bf16[1536,288]{0,1:T(8,128)(2,1)S(1)}, bf16[1536,288]{0,1:T(8,128)(2,1)}, u32[]{:S(2)}) copy-start(bf16[1536,288]{0,1:T(8,128)(2,1)} %param.26) | copy-start | bytes 2654212
  177.5 29.2 %all-to-all-start.4 = ((bf16[128,4,1536]{2,1,0:T(4,128)(2,1)}), bf16[128,4,1536]{2,1,0:T(4,128)(2,1)S(1)}, u32[]{:S(2)}, u32[]{:S(2)}) async-start(bf16[128,4,1536]{2,1,0:T(4,128)(2,1)} %copy.137), calls=%async_computation.4 | async-start | bytes 3145728 | tf_op jit(solution)/shard_map/all_to_all | solution.py:255

commit v6 on v4

--- a/solution.py
+++ b/solution.py
@@ -1,7 +1,7 @@
 import jax
 import jax.numpy as jnp
 from jax import lax
-from jax.sharding import PartitionSpec as P
+from jax.sharding import Mesh, PartitionSpec as P
 from jax.experimental import pallas as pl
 from jax.experimental.pallas import tpu as pltpu
 
@@ -11,6 +11,8 @@
 
 
 EPSILON = 1e-06
+KV = ("y", "zhi", "zlo")
+HALF = ("y", "zlo")
 NEGATIVE = -1e30
 
 
@@ -115,12 +117,12 @@
     qwidth = heads * head_dim
     span = table.shape[1] * pool.shape[1]
     req_count = lax.axis_size("req")
-    kv_count = lax.axis_size("kv")
+    kv_count = lax.axis_size(KV)
     group = lax.axis_index("req")
-    member = lax.axis_index("kv")
-    halves = kv_count // BEAMS
-    half = member // 2 % halves
-    beam = member % 2 + 2 * (member // (2 * halves))
+    halves = lax.axis_size("zhi")
+    half = lax.axis_index("zhi")
+    beam = lax.axis_index("y") * 2 + lax.axis_index("zlo")
+    member = member_of(beam, half, halves)
     per_group = halves * rows
     group_rows = kv_count * rows
     quota = rows // req_count
@@ -150,11 +152,9 @@
     query = jnp.dot(normed, w_query, preferred_element_type=jnp.float32).astype(jnp.bfloat16)
     fresh = jnp.dot(normed, w_keyval, preferred_element_type=jnp.float32).astype(jnp.bfloat16)
     packed = jnp.concatenate([query, fresh], axis=-1).reshape(steps, rows, qwidth + 2 * head_dim)
-    gathered = lax.all_to_all(
-        jnp.broadcast_to(packed[None], (kv_count,) + packed.shape), "kv", 0, 0, tiled=True
-    )
-    mine = gathered.reshape((BEAMS // 2, halves, 2) + packed.shape)
-    mine = lax.dynamic_index_in_dim(mine, half, 1, keepdims=False).reshape((BEAMS,) + packed.shape)
+    mine = lax.all_to_all(
+        jnp.broadcast_to(packed[None], (BEAMS,) + packed.shape), HALF, 0, 0, tiled=True
+    )
     queries = mine[..., :qwidth].reshape(BEAMS, steps, rows, heads, head_dim)
     entries = mine[..., qwidth:]
 
@@ -219,12 +219,7 @@
     )
     attended = jnp.where(held[..., None], attended, jnp.zeros_like(attended))
 
-    spread = attended.reshape(BEAMS // 2, 1, 2, steps, rows, qwidth)
-    in_half = (jnp.arange(halves, dtype=jnp.int32) == half)[None, :, None, None, None, None]
-    outgoing_att = jnp.where(in_half, spread, jnp.zeros_like(spread)).reshape(
-        kv_count, steps, rows, qwidth
-    )
-    received = lax.all_to_all(outgoing_att, "kv", split_axis=0, concat_axis=0, tiled=True)
+    received = lax.all_to_all(attended, HALF, split_axis=0, concat_axis=0, tiled=True)
     attended_own = jnp.sum(received.astype(jnp.float32), axis=0).astype(jnp.bfloat16)
 
     current = inputs.reshape(steps * rows, width)
@@ -234,7 +229,7 @@
     ).astype(jnp.bfloat16)
     mlp_own = rms_round(residual, norm_mlp)
     mlp_in = lax.all_to_all(
-        jnp.broadcast_to(mlp_own[None], (kv_count,) + mlp_own.shape), "kv", 0, 0, tiled=True
+        jnp.broadcast_to(mlp_own[None], (kv_count,) + mlp_own.shape), KV, 0, 0, tiled=True
     ).reshape(kv_count * steps * rows, width)
     gate = jnp.dot(mlp_in, w_gate, preferred_element_type=jnp.float32)
     upward = jnp.dot(mlp_in, w_up, preferred_element_type=jnp.float32)
@@ -246,7 +241,7 @@
     terms = terms.astype(jnp.bfloat16)
 
     leaving = jnp.transpose(terms, (2, 0, 1, 3)).reshape(req_count * kv_count, steps, width)
-    arrived_sums = lax.all_to_all(leaving, ("req", "kv"), 0, 0, tiled=True).reshape(
+    arrived_sums = lax.all_to_all(leaving, ("req",) + KV, 0, 0, tiled=True).reshape(
         req_count, kv_count, steps, width
     )
     per_group_sum = jnp.sum(arrived_sums.astype(jnp.float32), axis=1)
@@ -258,23 +253,30 @@
 
 
 def solution(mesh):
+    req_count, kv_count = mesh.devices.shape
+    halves = kv_count // BEAMS
+    split = Mesh(
+        mesh.devices.reshape(req_count, BEAMS // 2, halves, 2), ("req",) + KV
+    )
+    mesh = split
+    ROWS = ("req",) + KV
     in_specs = (
-        P(None, ("req", "kv"), None),
-        P(),
-        P(),
-        P(),
-        P(("req", "kv"), None),
-        P(("req", "kv"), None, None),
-        P(),
-        P(),
-        P(),
-        P(),
-        P(),
-        P(None, "kv"),
-        P(None, "kv"),
-        P("kv", None),
-    )
-    out_specs = P(None, ("req", "kv"), None)
+        P(None, ROWS, None),
+        P(),
+        P(),
+        P(),
+        P(ROWS, None),
+        P(ROWS, None, None),
+        P(),
+        P(),
+        P(),
+        P(),
+        P(),
+        P(None, KV),
+        P(None, KV),
+        P(KV, None),
+    )
+    out_specs = P(None, ROWS, None)
     return jax.shard_map(
         on_device, mesh=mesh, in_specs=in_specs, out_specs=out_specs, check_vma=False
     )

time: 194 us -> 167 us (0.86)
  blocking collectives: 24 us -> 14 us
  waiting for transfers between devices: 58.9 us -> 50.6 us
  starting transfers between devices: 28.1 us -> 25.4 us
  local copies, waits for them, and re-layouts: 30.3 us -> 28.1 us
    all_to_all x1, blocking collectives: 24 us -> 14 us  [on_device(): lax.all_to_all(attended, HALF, split_axis=0, concat_axis=0, tiled=True)]
    all_to_all x2, waiting for transfers between devices: 38.2 us -> 28.4 us  [the longest x1 23.9 us: on_device(): lax.all_to_all(leaving, ('req',) + KV, 0, 0, tiled=True)]
    all_to_all x2, starting transfers between devices: 17.9 us -> 13.8 us  [the longest x1 8.3 us: on_device(): lax.all_to_all(leaving, ('req',) + KV, 0, 0, tiled=True)]
  transfers between devices with their start and end apart: 4 -> 4, of which waited for: 4 -> 4; matrix products, arithmetic and copies ran while one was open for 6% -> 7% of each run, Pallas kernels for 0% -> 0%
where the time goes in v6:
time: 167 us; the launch traced here: 166 us
  waiting for transfers between devices  50.6 us (30%)
  local copies, waits for them, and re-layouts  28.1 us (17%)
  starting transfers between devices  25.4 us (15%)
  matrix products  17.5 us (10%)
  Pallas kernels  15.9 us (10%)
  other arithmetic  14.1 us (8%)
  blocking collectives  14 us (8%)
    all_to_all x1, waiting for transfers between devices, on_device(): lax.all_to_all(leaving, ('req',) + KV, 0, 0, tiled=True)  23.9 us
    all_to_all x1, waiting for transfers between devices, on_device(): lax.all_to_all(jnp.broadcast_to(mlp_own[None], (kv_count,) + mlp_own.shap...  19.9 us
    pallas_call x1, Pallas kernels, cache_part(): pl.pallas_call(cache_kernel, grid_spec=pltpu.PrefetchScalarGridSpec(num_s...  15.9 us
    all_to_all x1, blocking collectives, on_device(): lax.all_to_all(attended, HALF, split_axis=0, concat_axis=0, tiled=True)  14 us
    all_to_all x1, starting transfers between devices, on_device(): lax.all_to_all(leaving, ('req',) + KV, 0, 0, tiled=True)  8.3 us
    gather x1, local copies, waits for them, and re-layouts, on_device(): pool[table[offset_of] - device * pool.shape[0]]  7.81 us
    all_to_all x1, starting transfers between devices, on_device(): lax.all_to_all(outgoing, 'req', split_axis=1, concat_axis=1, tiled=True)  5.8 us
    all_to_all x1, starting transfers between devices, on_device(): lax.all_to_all(jnp.broadcast_to(mlp_own[None], (kv_count,) + mlp_own.shap...  5.72 us
  transfers between devices with their start and end apart: 4, of which 4 were waited for; matrix products, arithmetic and copies ran while one was open for 7% of the time, Pallas kernels for 0%

profile of v6, /device:TPU:1, one launch (start us, length us, event | category | flops | bytes accessed | tf_op | source)
XLA Modules:
  0.0 166.2 jit_solution(9511730403665706123)
XLA Ops:
  3.6 1.3 gather_fusion.3
  5.0 1.7 %gather_fusion = bf16[8,4,1536]{2,0,1:T(8,128)(2,1)S(1)} fusion(bf16[4,8,1536]{2,1,0:T(8,128)(2,1)} %param.14, s32[1024]{0:T(1024)S(1)} %pad_clamp_fusion.3), kind=kCustom, calls=%fused_computation | custom fusion | bytes 196640 | tf_op jit(solution)/shard_map/gather | solution.py:140
  7.4 5.8 %all-to-all-start = ((bf16[4,8,1,1536]{3,0,2,1:T(4,128)(2,1)}), bf16[4,8,1,1536]{3,0,2,1:T(4,128)(2,1)S(1)}, u32[]{:S(2)}, u32[]{:S(2)}) async-start(bf16[4,8,1,1536]{3,0,2,1:T(4,128)(2,1)} %copy.147), calls=%async_computation | async-start | bytes 196608 | tf_op jit(solution)/shard_map/all_to_all | solution.py:141
  15.9 2.3 %all-to-all-done = bf16[4,8,1,1536]{3,0,2,1:T(4,128)(2,1)S(1)} async-done(((bf16[4,8,1,1536]{3,0,2,1:T(4,128)(2,1)}), bf16[4,8,1,1536]{3,0,2,1:T(4,128)(2,1)S(1)}, u32[]{:S(2)}, u32[]{:S(2)}) %all-to-all-start) | async-done | bytes 98336 | tf_op jit(solution)/shard_map/all_to_all | solution.py:141
  18.8 3.3 %convolution_convert_fusion = bf16[32,1536]{1,0:T(8,128)(2,1)S(1)} fusion(bf16[1536,1536]{1,0:T(8,128)(2,1)} %param.21, f32[4,8,1,1536]{3,0,2,1:T(4,128)S(1)} %convert_element_type.105, f32[1536]{0:T(1024)S(1)} %copy-done.5, f32[32]{0:T(128)S(1)} %rsqrt.20), kind=kOutput, calls=%fused_computation.12 | convolution fusion | flops 151191552 | bytes 5019776 | tf_op jit(solution)/shard_map/dot_general | solution.py:152
  23.2 5.5 %all-to-all-start.1 = ((bf16[8,4,8,1792]{3,2,1,0:T(8,128)(2,1)}), bf16[8,4,8,1792]{3,2,1,0:T(8,128)(2,1)S(1)}, u32[]{:S(2)}, u32[]{:S(2)}) async-start(bf16[8,4,8,1792]{3,2,1,0:T(8,128)(2,1)} %broadcast_in_dim.383), calls=%async_computation.1 | async-start | bytes 1835008 | tf_op jit(solution)/shard_map/all_to_all | solution.py:155
  29.5 7.8 %gather_fusion.5 = bf16[72,128,256]{2,1,0:T(8,128)(2,1)} fusion(bf16[72,128,256]{2,1,0:T(8,128)(2,1)} %param.19, s32[1024]{0:T(1024)S(1)} %pad_clamp_fusion), kind=kCustom, calls=%fused_computation.5 | custom fusion | bytes 9437472 | tf_op jit(solution)/shard_map/gather | solution.py:184
  37.4 4.5 %all-to-all-done.1 = bf16[8,4,8,1792]{3,2,1,0:T(8,128)(2,1)S(1)} async-done(((bf16[8,4,8,1792]{3,2,1,0:T(8,128)(2,1)}), bf16[8,4,8,1792]{3,2,1,0:T(8,128)(2,1)S(1)}, u32[]{:S(2)}, u32[]{:S(2)}) %all-to-all-start.1) | async-done | bytes 917536 | tf_op jit(solution)/shard_map/all_to_all | solution.py:155
  44.8 15.9 %shard_map.136 = (f32[8,4,96,1]{3,2,1,0:T(8,128)}, f32[8,4,96,1]{3,2,1,0:T(8,128)}, f32[8,4,96,128]{3,2,1,0:T(8,128)}) custom-call(s32[64]{0:T(128)} %reshape.321.bounds_ref, bf16[8,4,96,128]{3,2,1,0:T(8,128)(2,1)} %copy.158.q_ref, bf16[8,1152,256]{2,1,0:T(8,128)(2,1)} %bitcast.122), custom_call_target="tpu_custom_call" | custom-call | flops 1811939328 | bytes 7102464 | tf_op jit(solution)/shard_map/pallas_call | solution.py:70
  60.7 3.5 %copy.159 = f32[8,4,96,128]{3,0,2,1:T(8,128)} copy(f32[8,4,96,128]{3,2,1,0:T(8,128)} %get-tuple-element.10) | data formatting | bytes 3145728 | tf_op jit(solution)/shard_map/pallas_call | solution.py:70
  64.1 2.0 %reduce.12 = f32[8,4,96]{2,1,0:T(4,128)S(1)} reduce(f32[8,4,96,1]{3,2,1,0:T(8,128)} %get-tuple-element.11, f32[]{:T(128)} %constant.170), dimensions={3}, to_apply=%get-tuple-element.11.reduce_sub_computation | reduce | bytes 24580 | tf_op jit(solution)/shard_map/pallas_call | solution.py:70
  66.2 2.0 %reduce.13 = f32[8,4,96]{2,1,0:T(4,128)S(1)} reduce(f32[8,4,96,1]{3,2,1,0:T(8,128)} %get-tuple-element.12, f32[]{:T(128)} %constant.170), dimensions={3}, to_apply=%get-tuple-element.12.reduce_sub_computation | reduce | bytes 24580 | tf_op jit(solution)/shard_map/pallas_call | solution.py:70
  71.2 2.7 %fusion.5 = bf16[8,4,8,12,128]{4,3,2,1,0:T(8,128)(2,1)S(1)} fusion(f32[8,4,8,12,128]{4,0,3,2,1:T(8,128)S(1)} %bitcast.125, f32[8,4,8,12]{3,2,1,0:T(8,128)S(1)} %get-tuple-element.37, f32[8,4,8,12]{3,2,1,0:T(8,128)S(1)} %get-tuple-element.38, f32[8,4,8,12]{3,2,1,0:T(8,128)S(1)} %get-tuple-element.39, bf16[4,4,8,8,256]{4,1,3,0,2:T(4,128)(2,1)S(1)} %pad_maximum_fusion, ...), kind=kOutput, calls=%fused_computation.16 | convolution fusion | flops 5148672 | bytes 3670528 | tf_op jit(solution)/shard_map/jtrhs,tsjrd->jtrhd/dot_general | solution.py:208
  74.6 14.0 %all_to_all.25 = bf16[8,4,8,1536]{3,2,1,0:T(8,128)(2,1)S(1)} all-to-all(bf16[8,4,8,1536]{3,2,1,0:T(8,128)(2,1)S(1)} %broadcast_select_fusion), channel_id=1, replica_groups=mesh['req'=8,'y'=4,'zhi'=2,'zlo'=2] {'y','zlo'}, dimensions={0} | all-to-all | bytes 1572864 | tf_op jit(solution)/shard_map/all_to_all | solution.py:222
  88.8 3.4 %multiply_reduce_fusion = (f32[32]{0:T(128)S(1)}, f32[32,1536]{1,0:T(8,128)S(1)}) fusion(bf16[1536,1536]{1,0:T(8,128)(2,1)} %param.23, bf16[4,8,1536]{2,1,0:T(8,128)(2,1)S(1)} %reduce_sum.312, f32[4,8,1,1536]{3,0,2,1:T(4,128)S(1)} %convert_element_type.105), kind=kOutput, calls=%fused_computation.60 | convolution fusion | flops 151240672 | bytes 5210240 | tf_op jit(solution)/shard_map/dot_general | solution.py:228
  92.2 1.3 broadcast_in_dim.410
  93.5 5.7 %all-to-all-start.3 = ((bf16[16,32,1536]{2,1,0:T(8,128)(2,1)}), bf16[16,32,1536]{2,1,0:T(8,128)(2,1)S(1)}, u32[]{:S(2)}, u32[]{:S(2)}) async-start(bf16[16,32,1536]{2,1,0:T(8,128)(2,1)} %broadcast_in_dim.410), calls=%async_computation.3 | async-start | bytes 3145728 | tf_op jit(solution)/shard_map/all_to_all | solution.py:231
  99.3 19.9 %all-to-all-done.3 = bf16[16,32,1536]{2,1,0:T(8,128)(2,1)S(1)} async-done(((bf16[16,32,1536]{2,1,0:T(8,128)(2,1)}), bf16[16,32,1536]{2,1,0:T(8,128)(2,1)S(1)}, u32[]{:S(2)}, u32[]{:S(2)}) %all-to-all-start.3) | async-done | bytes 1572896 | tf_op jit(solution)/shard_map/all_to_all | solution.py:231
  119.2 2.7 %fusion.48 = f32[512,288]{0,1:T(8,128)} fusion(bf16[512,1536]{1,0:T(8,128)(2,1)S(1)} %bitcast.119, bf16[1536,288]{0,1:T(8,128)(2,1)} %param.25), kind=kOutput, calls=%fused_computation.142 | convolution fusion | flops 452984832 | bytes 3047424 | tf_op jit(solution)/shard_map/dot_general | solution.py:234
  121.9 4.4 %fusion.8 = f32[512,1536]{1,0:T(8,128)} fusion(bf16[288,1536]{1,0:T(8,128)(2,1)S(1)} %copy-done, bf16[512,1536]{1,0:T(8,128)(2,1)S(1)} %bitcast.120, bf16[1536,288]{0,1:T(8,128)(2,1)S(1)} %copy-done.2, f32[512,288]{0,1:T(8,128)} %fusion.48), kind=kOutput, calls=%fused_computation.22 | convolution fusion | flops 907444224 | bytes 7077888 | tf_op jit(solution)/shard_map/dot_general | solution.py:237
  126.3 3.8 %fusion = bf16[16,4,8,1536]{3,0,2,1:T(8,128)(2,1)S(1)} fusion(f32[16,4,8,1536]{3,2,1,0:T(8,128)} %bitcast.118, f32[4,8,1536]{2,1,0:T(8,128)S(1)} %bitcast.124, pred[16]{0:T(512)(128)(4,1)S(1)} %iota_compare_fusion.13), kind=kLoop, calls=%fused_computation.8 | loop fusion | flops 2359296 | bytes 4915216 | tf_op jit(solution)/shard_map/convert_element_type | solution.py:241
  130.1 2.4 %copy.178 = bf16[128,4,1536]{2,1,0:T(4,128)(2,1)} copy(bf16[128,4,1536]{2,0,1:T(8,128)(2,1)S(1)} %bitcast.121) | data formatting | bytes 3145728 | tf_op jit(solution)/shard_map/reshape | solution.py:243
  132.5 8.3 %all-to-all-start.4 = ((bf16[128,4,1536]{2,1,0:T(4,128)(2,1)}), bf16[128,4,1536]{2,1,0:T(4,128)(2,1)S(1)}, u32[]{:S(2)}, u32[]{:S(2)}) async-start(bf16[128,4,1536]{2,1,0:T(4,128)(2,1)} %copy.178), calls=%async_computation.4 | async-start | bytes 3145728 | tf_op jit(solution)/shard_map/all_to_all | solution.py:244
  140.8 23.9 %all-to-all-done.4 = bf16[128,4,1536]{2,1,0:T(4,128)(2,1)S(1)} async-done(((bf16[128,4,1536]{2,1,0:T(4,128)(2,1)}), bf16[128,4,1536]{2,1,0:T(4,128)(2,1)S(1)}, u32[]{:S(2)}, u32[]{:S(2)}) %all-to-all-start.4) | async-done | bytes 1572896 | tf_op jit(solution)/shard_map/all_to_all | solution.py:244
  (107 shorter events, 17.4 us)
Async XLA Ops:
  0.0 121.9 %copy-start = (bf16[288,1536]{1,0:T(8,128)(2,1)S(1)}, bf16[288,1536]{1,0:T(8,128)(2,1)}, u32[]{:S(2)}) copy-start(bf16[288,1536]{1,0:T(8,128)(2,1)} %param.27) | copy-start | bytes 2654212
  0.0 13.2 %copy-start.4 = (s32[8,9]{1,0:T(8,128)S(1)}, s32[8,9]{1,0:T(8,128)}, u32[]{:S(2)}) copy-start(s32[8,9]{1,0:T(8,128)} %param.18) | copy-start | bytes 868
  0.0 18.5 %copy-start.5 = (f32[1536]{0:T(1024)S(1)}, f32[1536]{0:T(1024)}, u32[]{:S(2)}) copy-start(f32[1536]{0:T(1024)} %param.20) | copy-start | bytes 18436
  0.0 18.5 %copy-start.3 = (bf16[1536,256]{1,0:T(8,128)(2,1)S(1)}, bf16[1536,256]{1,0:T(8,128)(2,1)}, u32[]{:S(2)}) copy-start(bf16[1536,256]{1,0:T(8,128)(2,1)} %param.22) | copy-start | bytes 2359300
  7.4 10.8 %all-to-all-start = ((bf16[4,8,1,1536]{3,0,2,1:T(4,128)(2,1)}), bf16[4,8,1,1536]{3,0,2,1:T(4,128)(2,1)S(1)}, u32[]{:S(2)}, u32[]{:S(2)}) async-start(bf16[4,8,1,1536]{3,0,2,1:T(4,128)(2,1)} %copy.147), calls=%async_computation | async-start | bytes 196608 | tf_op jit(solution)/shard_map/all_to_all | solution.py:141
  23.2 18.8 %all-to-all-start.1 = ((bf16[8,4,8,1792]{3,2,1,0:T(8,128)(2,1)}), bf16[8,4,8,1792]{3,2,1,0:T(8,128)(2,1)S(1)}, u32[]{:S(2)}, u32[]{:S(2)}) async-start(bf16[8,4,8,1792]{3,2,1,0:T(8,128)(2,1)} %broadcast_in_dim.383), calls=%async_computation.1 | async-start | bytes 1835008 | tf_op jit(solution)/shard_map/all_to_all | solution.py:155
  69.8 1.4 copy-start.1
  88.7 3.4 %copy-start.6 = (f32[1536]{0:T(1024)S(1)}, f32[1536]{0:T(1024)}, u32[]{:S(2)}) copy-start(f32[1536]{0:T(1024)} %param.24) | copy-start | bytes 18436
  93.5 25.6 %all-to-all-start.3 = ((bf16[16,32,1536]{2,1,0:T(8,128)(2,1)}), bf16[16,32,1536]{2,1,0:T(8,128)(2,1)S(1)}, u32[]{:S(2)}, u32[]{:S(2)}) async-start(bf16[16,32,1536]{2,1,0:T(8,128)(2,1)} %broadcast_in_dim.410), calls=%async_computation.3 | async-start | bytes 3145728 | tf_op jit(solution)/shard_map/all_to_all | solution.py:231
  119.2 2.7 %copy-start.2 = (bf16[1536,288]{0,1:T(8,128)(2,1)S(1)}, bf16[1536,288]{0,1:T(8,128)(2,1)}, u32[]{:S(2)}) copy-start(bf16[1536,288]{0,1:T(8,128)(2,1)} %param.26) | copy-start | bytes 2654212
  132.5 32.3 %all-to-all-start.4 = ((bf16[128,4,1536]{2,1,0:T(4,128)(2,1)}), bf16[128,4,1536]{2,1,0:T(4,128)(2,1)S(1)}, u32[]{:S(2)}, u32[]{:S(2)}) async-start(bf16[128,4,1536]{2,1,0:T(4,128)(2,1)} %copy.178), calls=%async_computation.4 | async-start | bytes 3145728 | tf_op jit(solution)/shard_map/all_to_all | solution.py:244

commit v7 on v6

--- a/solution.py
+++ b/solution.py
@@ -41,58 +41,67 @@
     return jnp.sum(jnp.where(picks[..., None], table[None, :, :, :], 0), axis=1).astype(table.dtype)
 
 
-def cache_kernel(bounds_ref, q_ref, kv_ref, high_ref, total_ref, sum_ref):
+def attend_kernel(bounds_ref, q_ref, kv_ref, new_ref, pick_ref, out_ref):
     r = pl.program_id(0)
     steps = q_ref.shape[1]
     head_dim = q_ref.shape[3]
+    scale = head_dim ** (-0.5)
     keys = kv_ref[0, :, :head_dim]
     values = kv_ref[0, :, head_dim:]
     pos = lax.broadcasted_iota(jnp.int32, (1, kv_ref.shape[1]), 1)
+    contract = (((1,), (1,)), ((), ()))
     for t in range(steps):
         lo = bounds_ref[(r * steps + t) * 2]
         hi = bounds_ref[(r * steps + t) * 2 + 1]
-        scores = lax.dot_general(
-            q_ref[0, t], keys, (((1,), (1,)), ((), ())), preferred_element_type=jnp.float32
-        ) * (head_dim ** (-0.5))
+        query = q_ref[0, t]
+        scores = lax.dot_general(query, keys, contract, preferred_element_type=jnp.float32) * scale
         allowed = (pos > lo) & (pos < hi)
         scores = jnp.where(allowed, scores, NEGATIVE)
-        high = jnp.max(scores, axis=1, keepdims=True)
-        weights = jnp.exp(scores - high).astype(jnp.bfloat16)
-        high_ref[0, t] = high
-        total_ref[0, t] = jnp.sum(weights.astype(jnp.float32), axis=1, keepdims=True)
-        sum_ref[0, t] = jnp.dot(weights, values, preferred_element_type=jnp.float32)
-
-
-def cache_part(bounds, queries, pages):
+        high_c = jnp.max(scores, axis=1, keepdims=True)
+        weights = jnp.exp(scores - high_c).astype(jnp.bfloat16)
+        total_c = jnp.sum(weights.astype(jnp.float32), axis=1, keepdims=True)
+        sum_c = jnp.dot(weights, values, preferred_element_type=jnp.float32)
+        entries = new_ref[0, t]
+        fresh = lax.dot_general(
+            query, entries[:, :head_dim], contract, preferred_element_type=jnp.float32
+        ) * scale
+        fresh = jnp.where(pick_ref[t] > 0, fresh, NEGATIVE)
+        high_n = jnp.max(fresh, axis=1, keepdims=True)
+        fresh_w = jnp.exp(fresh - high_n).astype(jnp.bfloat16)
+        total_n = jnp.sum(fresh_w.astype(jnp.float32), axis=1, keepdims=True)
+        sum_n = jnp.dot(fresh_w, entries[:, head_dim:], preferred_element_type=jnp.float32)
+        highest = jnp.maximum(high_c, high_n)
+        scale_c = jnp.exp(high_c - highest)
+        scale_n = jnp.exp(high_n - highest)
+        totals = total_c * scale_c + total_n * scale_n
+        weighted = sum_c * scale_c + sum_n * scale_n
+        out_ref[0, t] = (weighted / totals).astype(out_ref.dtype)
+
+
+def attend(bounds, queries, pages, entries, pick):
     rows, steps, count, head_dim = queries.shape
     span = pages.shape[1]
-    flops = 4 * rows * steps * count * span * head_dim
+    flops = 4 * rows * steps * count * (span + entries.shape[2]) * head_dim
     return pl.pallas_call(
-        cache_kernel,
+        attend_kernel,
         grid_spec=pltpu.PrefetchScalarGridSpec(
             num_scalar_prefetch=1,
             grid=(rows,),
             in_specs=[
                 pl.BlockSpec((1, steps, count, head_dim), lambda r, b: (r, 0, 0, 0)),
                 pl.BlockSpec((1, span, pages.shape[2]), lambda r, b: (r, 0, 0)),
+                pl.BlockSpec((1,) + entries.shape[1:], lambda r, b: (r, 0, 0, 0)),
+                pl.BlockSpec(pick.shape, lambda r, b: (0, 0, 0)),
             ],
-            out_specs=[
-                pl.BlockSpec((1, steps, count, 1), lambda r, b: (r, 0, 0, 0)),
-                pl.BlockSpec((1, steps, count, 1), lambda r, b: (r, 0, 0, 0)),
-                pl.BlockSpec((1, steps, count, head_dim), lambda r, b: (r, 0, 0, 0)),
-            ],
+            out_specs=pl.BlockSpec((1, steps, count, head_dim), lambda r, b: (r, 0, 0, 0)),
         ),
-        out_shape=[
-            jax.ShapeDtypeStruct((rows, steps, count, 1), jnp.float32),
-            jax.ShapeDtypeStruct((rows, steps, count, 1), jnp.float32),
-            jax.ShapeDtypeStruct((rows, steps, count, head_dim), jnp.float32),
-        ],
+        out_shape=jax.ShapeDtypeStruct(queries.shape, jnp.bfloat16),
         cost_estimate=pl.CostEstimate(
             flops=flops,
             transcendentals=rows * steps * count * span,
-            bytes_accessed=pages.size * 2 + queries.size * 2 + rows * steps * count * (head_dim + 2) * 4,
+            bytes_accessed=pages.size * 2 + queries.size * 4 + entries.size * 2,
         ),
-    )(bounds, queries, pages)
+    )(bounds, queries, pages, entries, pick)
 
 
 def on_device(
@@ -189,34 +198,17 @@
     hi = jnp.broadcast_to((length - base)[:, None], (rows, steps))
     bounds = jnp.stack([lo, hi], axis=-1).reshape(rows * steps * 2)
     by_row = jnp.transpose(queries, (2, 1, 0, 3, 4)).reshape(rows, steps, BEAMS * heads, head_dim)
-    high_c, total_c, sum_c = cache_part(bounds, by_row, pages)
-    high_c = jnp.transpose(high_c.reshape(rows, steps, BEAMS, heads), (2, 1, 0, 3))
-    total_c = jnp.transpose(total_c.reshape(rows, steps, BEAMS, heads), (2, 1, 0, 3))
-    sum_c = jnp.transpose(sum_c.reshape(rows, steps, BEAMS, heads, head_dim), (2, 1, 0, 3, 4))
-
-    new_keys = listed[..., :head_dim]
-    new_values = listed[..., head_dim:]
-    fresh_scores = jnp.einsum(
-        "jtrhd,tsjrd->jtrhs", queries, new_keys, preferred_element_type=jnp.float32
-    ) * scale
-    counted = step_ids[None, :] <= step_ids[:, None]
-    fresh_scores = jnp.where(counted[None, :, None, None, :], fresh_scores, NEGATIVE)
-    high_n = jnp.max(fresh_scores, axis=-1)
-    fresh_weights = jnp.exp(fresh_scores - high_n[..., None]).astype(jnp.bfloat16)
-    fresh_weights = jnp.where(counted[None, :, None, None, :], fresh_weights, 0)
-    total_n = jnp.sum(fresh_weights.astype(jnp.float32), axis=-1)
-    sum_n = jnp.einsum(
-        "jtrhs,tsjrd->jtrhd", fresh_weights, new_values, preferred_element_type=jnp.float32
-    )
-
-    highest = jnp.maximum(high_c, high_n)
-    scale_c = jnp.exp(high_c - highest)
-    scale_n = jnp.exp(high_n - highest)
-    totals = total_c * scale_c + total_n * scale_n
-    weighted = sum_c * scale_c[..., None] + sum_n * scale_n[..., None]
-    attended = (weighted / totals[..., None]).astype(jnp.bfloat16).reshape(
-        BEAMS, steps, rows, qwidth
-    )
+    entries_by_row = jnp.transpose(listed, (3, 0, 1, 2, 4)).reshape(
+        rows, steps, steps * BEAMS, 2 * head_dim
+    )
+    row_beam = jnp.arange(BEAMS * heads, dtype=jnp.int32) // heads
+    column = jnp.arange(steps * BEAMS, dtype=jnp.int32)
+    pick = (
+        (column[None, None, :] % BEAMS == row_beam[None, :, None])
+        & (column[None, None, :] // BEAMS <= step_ids[:, None, None])
+    ).astype(jnp.float32)
+    attended = attend(bounds, by_row, pages, entries_by_row, pick)
+    attended = jnp.transpose(attended.reshape(rows, steps, BEAMS, qwidth), (2, 1, 0, 3))
     attended = jnp.where(held[..., None], attended, jnp.zeros_like(attended))
 
     received = lax.all_to_all(attended, HALF, split_axis=0, concat_axis=0, tiled=True)
@@ -227,7 +219,7 @@
         current.astype(jnp.float32)
         + jnp.dot(attended_own.reshape(steps * rows, qwidth), w_out, preferred_element_type=jnp.float32)
     ).astype(jnp.bfloat16)
-    mlp_own = rms_round(residual, norm_mlp)
+    mlp_own = jnp.swapaxes(rms_round(residual, norm_mlp).reshape(steps, rows, width), 0, 1)
     mlp_in = lax.all_to_all(
         jnp.broadcast_to(mlp_own[None], (kv_count,) + mlp_own.shape), KV, 0, 0, tiled=True
     ).reshape(kv_count * steps * rows, width)
@@ -235,16 +227,16 @@
     upward = jnp.dot(mlp_in, w_up, preferred_element_type=jnp.float32)
     hidden = (jax.nn.gelu(gate, approximate=True) * upward).astype(jnp.bfloat16)
     terms = jnp.dot(hidden, w_down, preferred_element_type=jnp.float32)
-    terms = terms.reshape(kv_count, steps, rows, width)
-    is_own = (jnp.arange(kv_count, dtype=jnp.int32) == member)[:, None, None, None]
-    terms = terms + jnp.where(is_own, residual.astype(jnp.float32).reshape(steps, rows, width)[None], 0.0)
-    terms = terms.astype(jnp.bfloat16)
-
-    leaving = jnp.transpose(terms, (2, 0, 1, 3)).reshape(req_count * kv_count, steps, width)
-    arrived_sums = lax.all_to_all(leaving, ("req",) + KV, 0, 0, tiled=True).reshape(
-        req_count, kv_count, steps, width
-    )
-    per_group_sum = jnp.sum(arrived_sums.astype(jnp.float32), axis=1)
+    terms = terms.reshape(kv_count, rows, steps, width)
+    own_rows = jnp.swapaxes(residual.astype(jnp.float32).reshape(steps, rows, width), 0, 1)
+    own_rows = lax.dynamic_index_in_dim(terms, member, 0, keepdims=False) + own_rows
+    terms = lax.dynamic_update_index_in_dim(terms, own_rows, member, 0).astype(jnp.bfloat16)
+
+    leaving = terms.reshape(kv_count * req_count, steps, width)
+    arrived_sums = lax.all_to_all(leaving, KV + ("req",), 0, 0, tiled=True).reshape(
+        kv_count, req_count, steps, width
+    )
+    per_group_sum = jnp.sum(arrived_sums.astype(jnp.float32), axis=0)
     served_by = slot_req[:, half, :] == group
     finished = jnp.sum(
         jnp.where(served_by[:, None, :, None], per_group_sum[:, :, None, :], 0.0), axis=0

time: 167 us -> 171 us (1.024)
  Pallas kernels: 15.9 us -> 22.6 us
  local copies, waits for them, and re-layouts: 28.1 us -> 32.9 us
  other arithmetic: 14.1 us -> 9.86 us
  matrix products: 17.5 us -> 14.5 us
    pallas_call x1, Pallas kernels: 15.9 us -> 22.6 us  [attend(): pl.pallas_call(attend_kernel, grid_spec=pltpu.PrefetchScalarGridSpec(num_...]
    reshape x5 -> x3, local copies, waits for them, and re-layouts: 3.4 us -> 8.16 us  [the longest x1 4.82 us: on_device(): terms = terms.reshape(kv_count, rows, steps, width)]
    pallas_call x2 -> x0, other arithmetic: 4.05 us -> none  [cache_part(): pl.pallas_call(cache_kernel, grid_spec=pltpu.PrefetchScalarGridSpec(num_s...]
    pallas_call x1 -> x0, local copies, waits for them, and re-layouts: 3.47 us -> none  [cache_part(): pl.pallas_call(cache_kernel, grid_spec=pltpu.PrefetchScalarGridSpec(num_s...]
    dot_general x2 -> x0, matrix products: 3.42 us -> none  [the longest x1 2.75 us: on_device(): jnp.einsum('jtrhs,tsjrd->jtrhd', fresh_weights, new_values, preferred_ele...]
  transfers between devices with their start and end apart: 4 -> 4, of which waited for: 4 -> 4; matrix products, arithmetic and copies ran while one was open for 7% -> 8% of each run, Pallas kernels for 0% -> 0%
where the time goes in v7:
time: 171 us; the launch traced here: 170 us
  waiting for transfers between devices  49.9 us (29%)
  local copies, waits for them, and re-layouts  32.9 us (19%)
  starting transfers between devices  25.9 us (15%)
  Pallas kernels  22.6 us (13%)
  matrix products  14.5 us (8%)
  blocking collectives  13.9 us (8%)
  other arithmetic  9.86 us (6%)
    all_to_all x1, waiting for transfers between devices, on_device(): lax.all_to_all(leaving, KV + ('req',), 0, 0, tiled=True)  24.9 us
    pallas_call x1, Pallas kernels, attend(): pl.pallas_call(attend_kernel, grid_spec=pltpu.PrefetchScalarGridSpec(num_...  22.6 us
    all_to_all x1, waiting for transfers between devices, on_device(): lax.all_to_all(jnp.broadcast_to(mlp_own[None], (kv_count,) + mlp_own.shap...  19.9 us
    all_to_all x1, blocking collectives, on_device(): lax.all_to_all(attended, HALF, split_axis=0, concat_axis=0, tiled=True)  13.9 us
    all_to_all x1, starting transfers between devices, on_device(): lax.all_to_all(leaving, KV + ('req',), 0, 0, tiled=True)  8.85 us
    gather x1, local copies, waits for them, and re-layouts, on_device(): pool[table[offset_of] - device * pool.shape[0]]  7.81 us
    all_to_all x1, starting transfers between devices, on_device(): lax.all_to_all(outgoing, 'req', split_axis=1, concat_axis=1, tiled=True)  5.8 us
    all_to_all x1, starting transfers between devices, on_device(): lax.all_to_all(jnp.broadcast_to(mlp_own[None], (kv_count,) + mlp_own.shap...  5.7 us
  transfers between devices with their start and end apart: 4, of which 4 were waited for; matrix products, arithmetic and copies ran while one was open for 8% of the time, Pallas kernels for 0%

profile of v7, /device:TPU:1, one launch (start us, length us, event | category | flops | bytes accessed | tf_op | source)
XLA Modules:
  0.0 170.1 jit_solution(5979244320560120087)
XLA Ops:
  3.6 1.3 gather_fusion.3
  5.0 1.7 %gather_fusion = bf16[8,4,1536]{2,0,1:T(8,128)(2,1)S(1)} fusion(bf16[4,8,1536]{2,1,0:T(8,128)(2,1)} %param.14, s32[1024]{0:T(1024)S(1)} %pad_clamp_fusion.3), kind=kCustom, calls=%fused_computation | custom fusion | bytes 196640 | tf_op jit(solution)/shard_map/gather | solution.py:149
  7.4 5.8 %all-to-all-start = ((bf16[4,8,1,1536]{3,0,2,1:T(4,128)(2,1)}), bf16[4,8,1,1536]{3,0,2,1:T(4,128)(2,1)S(1)}, u32[]{:S(2)}, u32[]{:S(2)}) async-start(bf16[4,8,1,1536]{3,0,2,1:T(4,128)(2,1)} %copy.102), calls=%async_computation | async-start | bytes 196608 | tf_op jit(solution)/shard_map/all_to_all | solution.py:150
  13.3 1.2 gather_fusion.4
  16.7 1.5 all-to-all-done
  18.8 3.3 %convolution_convert_fusion = bf16[32,1536]{1,0:T(8,128)(2,1)S(1)} fusion(bf16[1536,1536]{1,0:T(8,128)(2,1)} %param.21, f32[4,8,1,1536]{3,0,2,1:T(4,128)S(1)} %convert_element_type.95, f32[1536]{0:T(1024)S(1)} %copy-done.4, f32[32]{0:T(128)S(1)} %rsqrt.20), kind=kOutput, calls=%fused_computation.10 | convolution fusion | flops 151191552 | bytes 5019776 | tf_op jit(solution)/shard_map/dot_general | solution.py:161
  23.2 5.5 %all-to-all-start.1 = ((bf16[8,4,8,1792]{3,2,1,0:T(8,128)(2,1)}), bf16[8,4,8,1792]{3,2,1,0:T(8,128)(2,1)S(1)}, u32[]{:S(2)}, u32[]{:S(2)}) async-start(bf16[8,4,8,1792]{3,2,1,0:T(8,128)(2,1)} %broadcast_in_dim.336), calls=%async_computation.1 | async-start | bytes 1835008 | tf_op jit(solution)/shard_map/all_to_all | solution.py:164
  29.7 7.8 %gather_fusion.5 = bf16[72,128,256]{2,1,0:T(8,128)(2,1)} fusion(bf16[72,128,256]{2,1,0:T(8,128)(2,1)} %param.19, s32[1024]{0:T(1024)S(1)} %pad_clamp_fusion), kind=kCustom, calls=%fused_computation.5 | custom fusion | bytes 9437472 | tf_op jit(solution)/shard_map/gather | solution.py:193
  38.2 3.7 %all-to-all-done.1 = bf16[8,4,8,1792]{3,2,1,0:T(8,128)(2,1)S(1)} async-done(((bf16[8,4,8,1792]{3,2,1,0:T(8,128)(2,1)}), bf16[8,4,8,1792]{3,2,1,0:T(8,128)(2,1)S(1)}, u32[]{:S(2)}, u32[]{:S(2)}) %all-to-all-start.1) | async-done | bytes 917536 | tf_op jit(solution)/shard_map/all_to_all | solution.py:164
  42.1 1.0 copy.114.q_ref
  45.0 22.6 %shard_map.136 = bf16[8,4,96,128]{3,2,1,0:T(8,128)(2,1)} custom-call(s32[64]{0:T(128)} %reshape.419.bounds_ref, bf16[8,4,96,128]{3,2,1,0:T(8,128)(2,1)} %copy.114.q_ref, bf16[8,1152,256]{2,1,0:T(8,128)(2,1)} %bitcast.114, bf16[8,4,32,256]{3,2,1,0:T(8,128)(2,1)} %bitcast.118, f32[4,96,32]{2,1,0:T(8,128)} %and_convert_fusion.pick_ref), custom_call_target="tpu_custom_call" | custom-call | flops 1862270976 | bytes 6815744 | tf_op jit(solution)/shard_map/pallas_call | solution.py:85
  67.6 2.0 %reshape.424 = bf16[8,4,8,1536]{3,2,1,0:T(8,128)(2,1)S(1)} reshape(bf16[8,4,96,128]{3,2,1,0:T(8,128)(2,1)} %shard_map.136) | data formatting | bytes 1572864 | tf_op jit(solution)/shard_map/reshape | solution.py:211
  70.3 13.9 %all_to_all.25 = bf16[8,4,8,1536]{3,1,2,0:T(4,128)(2,1)S(1)} all-to-all(bf16[8,4,8,1536]{3,1,2,0:T(4,128)(2,1)S(1)} %bitcast_select_fusion), channel_id=1, replica_groups=mesh['req'=8,'y'=4,'zhi'=2,'zlo'=2] {'y','zlo'}, dimensions={0} | all-to-all | bytes 1572864 | tf_op jit(solution)/shard_map/all_to_all | solution.py:214
  84.6 3.3 %multiply_reduce_fusion = (f32[32]{0:T(128)S(1)}, f32[32,1536]{1,0:T(8,128)S(1)}) fusion(bf16[1536,1536]{1,0:T(8,128)(2,1)} %param.23, bf16[4,8,1536]{2,0,1:T(4,128)(2,1)S(1)} %reduce_sum.302, f32[4,8,1,1536]{3,0,2,1:T(4,128)S(1)} %convert_element_type.95), kind=kOutput, calls=%fused_computation.49 | convolution fusion | flops 151240672 | bytes 5210240 | tf_op jit(solution)/shard_map/dot_general | solution.py:220
  88.1 1.8 %broadcast_in_dim.360 = bf16[16,8,4,1536]{3,2,1,0:T(4,128)(2,1)} broadcast(bf16[8,4,1536]{2,1,0:T(4,128)(2,1)S(1)} %copy.118), dimensions={1,2,3} | broadcast | bytes 1671168 | tf_op jit(solution)/shard_map/broadcast_in_dim | solution.py:224
  89.9 5.7 %all-to-all-start.3 = ((bf16[16,8,4,1536]{3,2,1,0:T(4,128)(2,1)}), bf16[16,8,4,1536]{3,2,1,0:T(4,128)(2,1)S(1)}, u32[]{:S(2)}, u32[]{:S(2)}) async-start(bf16[16,8,4,1536]{3,2,1,0:T(4,128)(2,1)} %broadcast_in_dim.360), calls=%async_computation.3 | async-start | bytes 3145728 | tf_op jit(solution)/shard_map/all_to_all | solution.py:223
  95.6 19.9 %all-to-all-done.3 = bf16[16,8,4,1536]{3,2,1,0:T(4,128)(2,1)S(1)} async-done(((bf16[16,8,4,1536]{3,2,1,0:T(4,128)(2,1)}), bf16[16,8,4,1536]{3,2,1,0:T(4,128)(2,1)S(1)}, u32[]{:S(2)}, u32[]{:S(2)}) %all-to-all-start.3) | async-done | bytes 1572896 | tf_op jit(solution)/shard_map/all_to_all | solution.py:223
  115.5 1.3 reshape.427
  116.9 3.2 %fusion.35 = f32[512,288]{0,1:T(8,128)} fusion(bf16[512,1536]{1,0:T(8,128)(2,1)} %reshape.427, bf16[1536,288]{0,1:T(8,128)(2,1)} %param.25), kind=kOutput, calls=%fused_computation.137 | convolution fusion | flops 452984832 | bytes 3047424 | tf_op jit(solution)/shard_map/dot_general | solution.py:226
  120.1 4.4 %fusion.3 = f32[512,1536]{1,0:T(8,128)} fusion(bf16[288,1536]{1,0:T(8,128)(2,1)S(1)} %copy-done, bf16[512,1536]{1,0:T(8,128)(2,1)S(1)} %copy-done.1, bf16[1536,288]{0,1:T(8,128)(2,1)S(1)} %copy-done.2, f32[512,288]{0,1:T(8,128)} %fusion.35), kind=kOutput, calls=%fused_computation.14 | convolution fusion | flops 907444224 | bytes 7077888 | tf_op jit(solution)/shard_map/dot_general | solution.py:229
  124.5 4.8 %reshape.428 = f32[16,8,4,1536]{3,2,1,0:T(4,128)} reshape(f32[512,1536]{1,0:T(8,128)} %fusion.3) | data formatting | bytes 6291456 | tf_op jit(solution)/shard_map/reshape | solution.py:230
  131.1 3.7 %convert_element_type.91 = bf16[16,8,4,1536]{3,2,1,0:T(4,128)(2,1)} convert(f32[16,8,4,1536]{3,2,1,0:T(4,128)} %copy_dynamic-update-slice_fusion) | non-fusion elementwise | flops 786432 | bytes 4718592 | tf_op jit(solution)/shard_map/convert_element_type | solution.py:233
  134.9 8.8 %all-to-all-start.4 = ((bf16[128,4,1536]{2,1,0:T(4,128)(2,1)}), bf16[128,4,1536]{2,1,0:T(4,128)(2,1)S(1)}, u32[]{:S(2)}, u32[]{:S(2)}) async-start(bf16[128,4,1536]{2,1,0:T(4,128)(2,1)} %bitcast.116), calls=%async_computation.4 | async-start | bytes 3145728 | tf_op jit(solution)/shard_map/all_to_all | solution.py:236
  143.7 24.9 %all-to-all-done.4 = bf16[128,4,1536]{2,1,0:T(4,128)(2,1)S(1)} async-done(((bf16[128,4,1536]{2,1,0:T(4,128)(2,1)}), bf16[128,4,1536]{2,1,0:T(4,128)(2,1)S(1)}, u32[]{:S(2)}, u32[]{:S(2)}) %all-to-all-start.4) | async-done | bytes 1572896 | tf_op jit(solution)/shard_map/all_to_all | solution.py:236
  (95 shorter events, 16.3 us)
Async XLA Ops:
  0.0 120.1 %copy-start = (bf16[288,1536]{1,0:T(8,128)(2,1)S(1)}, bf16[288,1536]{1,0:T(8,128)(2,1)}, u32[]{:S(2)}) copy-start(bf16[288,1536]{1,0:T(8,128)(2,1)} %param.27) | copy-start | bytes 2654212
  0.0 18.5 %copy-start.4 = (f32[1536]{0:T(1024)S(1)}, f32[1536]{0:T(1024)}, u32[]{:S(2)}) copy-start(f32[1536]{0:T(1024)} %param.20) | copy-start | bytes 18436
  0.0 18.5 %copy-start.3 = (bf16[1536,256]{1,0:T(8,128)(2,1)S(1)}, bf16[1536,256]{1,0:T(8,128)(2,1)}, u32[]{:S(2)}) copy-start(bf16[1536,256]{1,0:T(8,128)(2,1)} %param.22) | copy-start | bytes 2359300
  7.4 10.8 %all-to-all-start = ((bf16[4,8,1,1536]{3,0,2,1:T(4,128)(2,1)}), bf16[4,8,1,1536]{3,0,2,1:T(4,128)(2,1)S(1)}, u32[]{:S(2)}, u32[]{:S(2)}) async-start(bf16[4,8,1,1536]{3,0,2,1:T(4,128)(2,1)} %copy.102), calls=%async_computation | async-start | bytes 196608 | tf_op jit(solution)/shard_map/all_to_all | solution.py:150
  23.2 18.8 %all-to-all-start.1 = ((bf16[8,4,8,1792]{3,2,1,0:T(8,128)(2,1)}), bf16[8,4,8,1792]{3,2,1,0:T(8,128)(2,1)S(1)}, u32[]{:S(2)}, u32[]{:S(2)}) async-start(bf16[8,4,8,1792]{3,2,1,0:T(8,128)(2,1)} %broadcast_in_dim.336), calls=%async_computation.1 | async-start | bytes 1835008 | tf_op jit(solution)/shard_map/all_to_all | solution.py:164
  84.2 3.8 %copy-start.5 = (f32[1536]{0:T(1024)S(1)}, f32[1536]{0:T(1024)}, u32[]{:S(2)}) copy-start(f32[1536]{0:T(1024)} %param.24) | copy-start | bytes 18436
  89.9 25.6 %all-to-all-start.3 = ((bf16[16,8,4,1536]{3,2,1,0:T(4,128)(2,1)}), bf16[16,8,4,1536]{3,2,1,0:T(4,128)(2,1)S(1)}, u32[]{:S(2)}, u32[]{:S(2)}) async-start(bf16[16,8,4,1536]{3,2,1,0:T(4,128)(2,1)} %broadcast_in_dim.360), calls=%async_computation.3 | async-start | bytes 3145728 | tf_op jit(solution)/shard_map/all_to_all | solution.py:223
  95.6 24.5 %copy-start.2 = (bf16[1536,288]{0,1:T(8,128)(2,1)S(1)}, bf16[1536,288]{0,1:T(8,128)(2,1)}, u32[]{:S(2)}) copy-start(bf16[1536,288]{0,1:T(8,128)(2,1)} %param.26) | copy-start | bytes 2654212
  116.8 3.2 %copy-start.1 = (bf16[512,1536]{1,0:T(8,128)(2,1)S(1)}, bf16[512,1536]{1,0:T(8,128)(2,1)}, u32[]{:S(2)}) copy-start(bf16[512,1536]{1,0:T(8,128)(2,1)} %reshape.427) | copy-start | bytes 4718596
  134.9 33.8 %all-to-all-start.4 = ((bf16[128,4,1536]{2,1,0:T(4,128)(2,1)}), bf16[128,4,1536]{2,1,0:T(4,128)(2,1)S(1)}, u32[]{:S(2)}, u32[]{:S(2)}) async-start(bf16[128,4,1536]{2,1,0:T(4,128)(2,1)} %bitcast.116), calls=%async_computation.4 | async-start | bytes 3145728 | tf_op jit(solution)/shard_map/all_to_all | solution.py:236

commit v8 on v7

--- a/solution.py
+++ b/solution.py
@@ -219,20 +219,26 @@
         current.astype(jnp.float32)
         + jnp.dot(attended_own.reshape(steps * rows, qwidth), w_out, preferred_element_type=jnp.float32)
     ).astype(jnp.bfloat16)
-    mlp_own = jnp.swapaxes(rms_round(residual, norm_mlp).reshape(steps, rows, width), 0, 1)
+    by_req = jnp.swapaxes(residual.reshape(steps, rows, width), 0, 1).reshape(rows * steps, width)
+    mlp_own = rms_round(by_req, norm_mlp)
     mlp_in = lax.all_to_all(
         jnp.broadcast_to(mlp_own[None], (kv_count,) + mlp_own.shape), KV, 0, 0, tiled=True
-    ).reshape(kv_count * steps * rows, width)
+    ).reshape(kv_count * rows * steps, width)
     gate = jnp.dot(mlp_in, w_gate, preferred_element_type=jnp.float32)
     upward = jnp.dot(mlp_in, w_up, preferred_element_type=jnp.float32)
     hidden = (jax.nn.gelu(gate, approximate=True) * upward).astype(jnp.bfloat16)
-    terms = jnp.dot(hidden, w_down, preferred_element_type=jnp.float32)
-    terms = terms.reshape(kv_count, rows, steps, width)
-    own_rows = jnp.swapaxes(residual.astype(jnp.float32).reshape(steps, rows, width), 0, 1)
-    own_rows = lax.dynamic_index_in_dim(terms, member, 0, keepdims=False) + own_rows
-    terms = lax.dynamic_update_index_in_dim(terms, own_rows, member, 0).astype(jnp.bfloat16)
-
-    leaving = terms.reshape(kv_count * req_count, steps, width)
+    own_row = jnp.arange(kv_count * rows * steps, dtype=jnp.int32)
+    select = (
+        (own_row[:, None] // (rows * steps) == member)
+        & (own_row[:, None] % (rows * steps) == jnp.arange(rows * steps, dtype=jnp.int32)[None, :])
+    ).astype(jnp.bfloat16)
+    terms = jnp.dot(
+        jnp.concatenate([hidden, select], axis=1),
+        jnp.concatenate([w_down, by_req], axis=0),
+        preferred_element_type=jnp.float32,
+    ).astype(jnp.bfloat16)
+
+    leaving = terms
     arrived_sums = lax.all_to_all(leaving, KV + ("req",), 0, 0, tiled=True).reshape(
         kv_count, req_count, steps, width
     )

time: 171 us -> 155 us (0.906)
  local copies, waits for them, and re-layouts: 32.9 us -> 26.4 us
  matrix products: 14.5 us -> 9.32 us
  other arithmetic: 9.86 us -> 6.08 us
    reshape x2 -> x1, local copies, waits for them, and re-layouts: 6.15 us -> 0.03 us  [on_device(): jnp.swapaxes(residual.reshape(steps, rows, width), 0, 1)]
    convert_element_type x1 -> x2, other arithmetic: 3.71 us -> 0.11 us  [the longest x1 0.09 us: rms_round(): return (wide * lax.rsqrt(mean_square + EPSILON) * gain).astype(jnp.bfloat16)]
    dot_general x1 -> x2, matrix products: 4.39 us -> 1.7 us  [the longest x1 1 us: on_device(): jnp.dot(jnp.concatenate([hidden, select], axis=1), jnp.concatenate([w_dow...]
    dot_general x1, matrix products: 3.22 us -> 0.64 us  [on_device(): gate = jnp.dot(mlp_in, w_gate, preferred_element_type=jnp.float32)]
where the time goes in v8:
time: 155 us
  waiting for transfers between devices  50.6 us (33%)
  local copies, waits for them, and re-layouts  26.4 us (17%)
  starting transfers between devices  25.3 us (16%)
  Pallas kernels  22.6 us (15%)
  blocking collectives  14 us (9%)
  matrix products  9.32 us (6%)
  other arithmetic  6.08 us (4%)
    all_to_all x1, waiting for transfers between devices, on_device(): lax.all_to_all(leaving, KV + ('req',), 0, 0, tiled=True)  24.9 us
    pallas_call x1, Pallas kernels, attend(): pl.pallas_call(attend_kernel, grid_spec=pltpu.PrefetchScalarGridSpec(num_...  22.6 us
    all_to_all x1, waiting for transfers between devices, on_device(): lax.all_to_all(jnp.broadcast_to(mlp_own[None], (kv_count,) + mlp_own.shap...  19.9 us
    all_to_all x1, blocking collectives, on_device(): lax.all_to_all(attended, HALF, split_axis=0, concat_axis=0, tiled=True)  14 us
    all_to_all x1, starting transfers between devices, on_device(): lax.all_to_all(leaving, KV + ('req',), 0, 0, tiled=True)  8.31 us
    gather x1, local copies, waits for them, and re-layouts, on_device(): pool[table[offset_of] - device * pool.shape[0]]  7.82 us
    all_to_all x1, starting transfers between devices, on_device(): lax.all_to_all(outgoing, 'req', split_axis=1, concat_axis=1, tiled=True)  5.8 us
    all_to_all x1, starting transfers between devices, on_device(): lax.all_to_all(jnp.broadcast_to(mlp_own[None], (kv_count,) + mlp_own.shap...  5.69 us
  transfers between devices with their start and end apart: 4, of which 4 were waited for; matrix products, arithmetic and copies ran while one was open for 8% of the time, Pallas kernels for 0%

profile of v8, /device:TPU:1, one launch (start us, length us, event | category | flops | bytes accessed | tf_op | source)
XLA Modules:
  0.0 154.7 jit_solution(8276521147275225324)
XLA Ops:
  2.6 1.3 gather_fusion.3
  3.9 1.0 sort.17
  4.9 1.7 %gather_fusion = bf16[8,4,1536]{2,0,1:T(8,128)(2,1)S(1)} fusion(bf16[4,8,1536]{2,1,0:T(8,128)(2,1)} %param.14, s32[1024]{0:T(1024)S(1)} %pad_clamp_fusion.3), kind=kCustom, calls=%fused_computation | custom fusion | bytes 196640 | tf_op jit(solution)/shard_map/gather | solution.py:149
  7.4 5.8 %all-to-all-start = ((bf16[4,8,1,1536]{3,0,2,1:T(4,128)(2,1)}), bf16[4,8,1,1536]{3,0,2,1:T(4,128)(2,1)S(1)}, u32[]{:S(2)}, u32[]{:S(2)}) async-start(bf16[4,8,1,1536]{3,0,2,1:T(4,128)(2,1)} %copy.93), calls=%async_computation | async-start | bytes 196608 | tf_op jit(solution)/shard_map/all_to_all | solution.py:150
  15.9 2.2 %all-to-all-done = bf16[4,8,1,1536]{3,0,2,1:T(4,128)(2,1)S(1)} async-done(((bf16[4,8,1,1536]{3,0,2,1:T(4,128)(2,1)}), bf16[4,8,1,1536]{3,0,2,1:T(4,128)(2,1)S(1)}, u32[]{:S(2)}, u32[]{:S(2)}) %all-to-all-start) | async-done | bytes 98336 | tf_op jit(solution)/shard_map/all_to_all | solution.py:150
  18.5 3.4 %convolution_convert_fusion.1 = bf16[32,1536]{1,0:T(8,128)(2,1)S(1)} fusion(bf16[1536,1536]{1,0:T(8,128)(2,1)} %param.21, f32[4,8,1,1536]{3,0,2,1:T(4,128)S(1)} %convert_element_type.110, f32[1536]{0:T(1024)S(1)} %copy-done.3, f32[32]{0:T(128)S(1)} %rsqrt.23), kind=kOutput, calls=%fused_computation.10 | convolution fusion | flops 151191552 | bytes 5019776 | tf_op jit(solution)/shard_map/dot_general | solution.py:161
  22.2 1.0 broadcast_in_dim.335
  23.2 5.5 %all-to-all-start.1 = ((bf16[8,4,8,1792]{3,2,1,0:T(8,128)(2,1)}), bf16[8,4,8,1792]{3,2,1,0:T(8,128)(2,1)S(1)}, u32[]{:S(2)}, u32[]{:S(2)}) async-start(bf16[8,4,8,1792]{3,2,1,0:T(8,128)(2,1)} %broadcast_in_dim.335), calls=%async_computation.1 | async-start | bytes 1835008 | tf_op jit(solution)/shard_map/all_to_all | solution.py:164
  29.7 7.8 %gather_fusion.5 = bf16[72,128,256]{2,1,0:T(8,128)(2,1)} fusion(bf16[72,128,256]{2,1,0:T(8,128)(2,1)} %param.19, s32[1024]{0:T(1024)S(1)} %pad_clamp_fusion), kind=kCustom, calls=%fused_computation.5 | custom fusion | bytes 9437472 | tf_op jit(solution)/shard_map/gather | solution.py:193
  38.3 3.7 %all-to-all-done.1 = bf16[8,4,8,1792]{3,2,1,0:T(8,128)(2,1)S(1)} async-done(((bf16[8,4,8,1792]{3,2,1,0:T(8,128)(2,1)}), bf16[8,4,8,1792]{3,2,1,0:T(8,128)(2,1)S(1)}, u32[]{:S(2)}, u32[]{:S(2)}) %all-to-all-start.1) | async-done | bytes 917536 | tf_op jit(solution)/shard_map/all_to_all | solution.py:164
  43.0 0.9 copy.126
  44.1 1.0 copy.105.q_ref
  45.1 22.6 %shard_map.136 = bf16[8,4,96,128]{3,2,1,0:T(8,128)(2,1)} custom-call(s32[64]{0:T(128)} %reshape.512.bounds_ref, bf16[8,4,96,128]{3,2,1,0:T(8,128)(2,1)} %copy.105.q_ref, bf16[8,1152,256]{2,1,0:T(8,128)(2,1)} %bitcast.103, bf16[8,4,32,256]{3,2,1,0:T(8,128)(2,1)} %bitcast.106, f32[4,96,32]{2,1,0:T(8,128)} %and_convert_fusion.pick_ref), custom_call_target="tpu_custom_call" | custom-call | flops 1862270976 | bytes 6815744 | tf_op jit(solution)/shard_map/pallas_call | solution.py:85
  67.6 2.0 %reshape.517 = bf16[8,4,8,1536]{3,2,1,0:T(8,128)(2,1)S(1)} reshape(bf16[8,4,96,128]{3,2,1,0:T(8,128)(2,1)} %shard_map.136) | data formatting | bytes 1572864 | tf_op jit(solution)/shard_map/reshape | solution.py:211
  70.3 14.0 %all_to_all.29 = bf16[8,4,8,1536]{3,1,2,0:T(4,128)(2,1)S(1)} all-to-all(bf16[8,4,8,1536]{3,1,2,0:T(4,128)(2,1)S(1)} %bitcast_select_fusion), channel_id=1, replica_groups=mesh['req'=8,'y'=4,'zhi'=2,'zlo'=2] {'y','zlo'}, dimensions={0} | all-to-all | bytes 1572864 | tf_op jit(solution)/shard_map/all_to_all | solution.py:214
  84.7 3.3 %multiply_reduce_fusion = (f32[8,4]{0,1:T(4,128)S(1)}, bf16[8,4,1536]{2,0,1:T(8,128)(2,1)S(1)}) fusion(bf16[1536,1536]{1,0:T(8,128)(2,1)} %param.23, bf16[4,8,1536]{2,0,1:T(4,128)(2,1)S(1)} %reduce_sum.302, f32[4,8,1,1536]{3,0,2,1:T(4,128)S(1)} %convert_element_type.110), kind=kOutput, calls=%fused_computation.48 | convolution fusion | flops 151240672 | bytes 5111936 | tf_op jit(solution)/shard_map/dot_general | solution.py:220
  88.4 1.3 broadcast_in_dim.359
  89.7 5.7 %all-to-all-start.3 = ((bf16[16,32,1536]{2,1,0:T(8,128)(2,1)}), bf16[16,32,1536]{2,1,0:T(8,128)(2,1)S(1)}, u32[]{:S(2)}, u32[]{:S(2)}) async-start(bf16[16,32,1536]{2,1,0:T(8,128)(2,1)} %broadcast_in_dim.359), calls=%async_computation.3 | async-start | bytes 3145728 | tf_op jit(solution)/shard_map/all_to_all | solution.py:224
  95.4 19.9 %all-to-all-done.3 = bf16[16,32,1536]{2,1,0:T(8,128)(2,1)S(1)} async-done(((bf16[16,32,1536]{2,1,0:T(8,128)(2,1)}), bf16[16,32,1536]{2,1,0:T(8,128)(2,1)S(1)}, u32[]{:S(2)}, u32[]{:S(2)}) %all-to-all-start.3) | async-done | bytes 1572896 | tf_op jit(solution)/shard_map/all_to_all | solution.py:224
  117.6 1.0 convolution_convert_fusion
  118.6 1.4 all_to_all.22
  120.0 8.3 %all-to-all-start.4 = ((bf16[128,4,1536]{2,1,0:T(4,128)(2,1)}), bf16[128,4,1536]{2,1,0:T(4,128)(2,1)S(1)}, u32[]{:S(2)}, u32[]{:S(2)}) async-start(bf16[128,4,1536]{2,1,0:T(4,128)(2,1)} %all_to_all.22), calls=%async_computation.4 | async-start | bytes 3145728 | tf_op jit(solution)/shard_map/all_to_all | solution.py:242
  128.3 24.9 %all-to-all-done.4 = bf16[128,4,1536]{2,1,0:T(4,128)(2,1)S(1)} async-done(((bf16[128,4,1536]{2,1,0:T(4,128)(2,1)}), bf16[128,4,1536]{2,1,0:T(4,128)(2,1)S(1)}, u32[]{:S(2)}, u32[]{:S(2)}) %all-to-all-start.4) | async-done | bytes 1572896 | tf_op jit(solution)/shard_map/all_to_all | solution.py:242
  153.9 0.8 select_reduce_fusion
  (99 shorter events, 13.8 us)
Async XLA Ops:
  0.0 115.3 %copy-start = (bf16[1536,288]{0,1:T(8,128)(2,1)S(1)}, bf16[1536,288]{0,1:T(8,128)(2,1)}, u32[]{:S(2)}) copy-start(bf16[1536,288]{0,1:T(8,128)(2,1)} %param.25) | copy-start | bytes 2654212
  0.0 15.0 %copy-start.2 = (s32[8,9]{1,0:T(8,128)S(1)}, s32[8,9]{1,0:T(8,128)}, u32[]{:S(2)}) copy-start(s32[8,9]{1,0:T(8,128)} %param.18) | copy-start | bytes 868
  0.0 18.5 %copy-start.3 = (f32[1536]{0:T(1024)S(1)}, f32[1536]{0:T(1024)}, u32[]{:S(2)}) copy-start(f32[1536]{0:T(1024)} %param.20) | copy-start | bytes 18436
  7.4 10.8 %all-to-all-start = ((bf16[4,8,1,1536]{3,0,2,1:T(4,128)(2,1)}), bf16[4,8,1,1536]{3,0,2,1:T(4,128)(2,1)S(1)}, u32[]{:S(2)}, u32[]{:S(2)}) async-start(bf16[4,8,1,1536]{3,0,2,1:T(4,128)(2,1)} %copy.93), calls=%async_computation | async-start | bytes 196608 | tf_op jit(solution)/shard_map/all_to_all | solution.py:150
  18.5 3.4 %copy-start.1 = (bf16[1536,256]{1,0:T(8,128)(2,1)S(1)}, bf16[1536,256]{1,0:T(8,128)(2,1)}, u32[]{:S(2)}) copy-start(bf16[1536,256]{1,0:T(8,128)(2,1)} %param.22) | copy-start | bytes 2359300
  23.2 18.8 %all-to-all-start.1 = ((bf16[8,4,8,1792]{3,2,1,0:T(8,128)(2,1)}), bf16[8,4,8,1792]{3,2,1,0:T(8,128)(2,1)S(1)}, u32[]{:S(2)}, u32[]{:S(2)}) async-start(bf16[8,4,8,1792]{3,2,1,0:T(8,128)(2,1)} %broadcast_in_dim.335), calls=%async_computation.1 | async-start | bytes 1835008 | tf_op jit(solution)/shard_map/all_to_all | solution.py:164
  84.7 3.6 %copy-start.4 = (f32[1536]{0:T(1024)S(1)}, f32[1536]{0:T(1024)}, u32[]{:S(2)}) copy-start(f32[1536]{0:T(1024)} %param.24) | copy-start | bytes 18436
  89.7 25.6 %all-to-all-start.3 = ((bf16[16,32,1536]{2,1,0:T(8,128)(2,1)}), bf16[16,32,1536]{2,1,0:T(8,128)(2,1)S(1)}, u32[]{:S(2)}, u32[]{:S(2)}) async-start(bf16[16,32,1536]{2,1,0:T(8,128)(2,1)} %broadcast_in_dim.359), calls=%async_computation.3 | async-start | bytes 3145728 | tf_op jit(solution)/shard_map/all_to_all | solution.py:224
  115.3 1.2 copy-start.5
  116.5 1.2 copy-start.6
  120.0 33.2 %all-to-all-start.4 = ((bf16[128,4,1536]{2,1,0:T(4,128)(2,1)}), bf16[128,4,1536]{2,1,0:T(4,128)(2,1)S(1)}, u32[]{:S(2)}, u32[]{:S(2)}) async-start(bf16[128,4,1536]{2,1,0:T(4,128)(2,1)} %all_to_all.22), calls=%async_computation.4 | async-start | bytes 3145728 | tf_op jit(solution)/shard_map/all_to_all | solution.py:242

commit v9 on v8

--- a/solution.py
+++ b/solution.py
@@ -135,6 +135,10 @@
     per_group = halves * rows
     group_rows = kv_count * rows
     quota = rows // req_count
+    swap = [(0, 1), (1, 0)]
+    gate_w = jnp.concatenate([w_gate, lax.ppermute(w_gate, "zhi", swap)], axis=1)
+    up_w = jnp.concatenate([w_up, lax.ppermute(w_up, "zhi", swap)], axis=1)
+    down_w = jnp.concatenate([w_down, lax.ppermute(w_down, "zhi", swap)], axis=0)
 
     offsets = jnp.arange(rows, dtype=jnp.int32)
     slot_ids = group * per_group + half * rows + offsets
@@ -222,25 +226,24 @@
     by_req = jnp.swapaxes(residual.reshape(steps, rows, width), 0, 1).reshape(rows * steps, width)
     mlp_own = rms_round(by_req, norm_mlp)
     mlp_in = lax.all_to_all(
-        jnp.broadcast_to(mlp_own[None], (kv_count,) + mlp_own.shape), KV, 0, 0, tiled=True
-    ).reshape(kv_count * rows * steps, width)
-    gate = jnp.dot(mlp_in, w_gate, preferred_element_type=jnp.float32)
-    upward = jnp.dot(mlp_in, w_up, preferred_element_type=jnp.float32)
+        jnp.broadcast_to(mlp_own[None], (BEAMS,) + mlp_own.shape), HALF, 0, 0, tiled=True
+    ).reshape(BEAMS * rows * steps, width)
+    gate = jnp.dot(mlp_in, gate_w, preferred_element_type=jnp.float32)
+    upward = jnp.dot(mlp_in, up_w, preferred_element_type=jnp.float32)
     hidden = (jax.nn.gelu(gate, approximate=True) * upward).astype(jnp.bfloat16)
-    own_row = jnp.arange(kv_count * rows * steps, dtype=jnp.int32)
+    own_row = jnp.arange(BEAMS * rows * steps, dtype=jnp.int32)
     select = (
-        (own_row[:, None] // (rows * steps) == member)
+        (own_row[:, None] // (rows * steps) == beam)
         & (own_row[:, None] % (rows * steps) == jnp.arange(rows * steps, dtype=jnp.int32)[None, :])
     ).astype(jnp.bfloat16)
     terms = jnp.dot(
         jnp.concatenate([hidden, select], axis=1),
-        jnp.concatenate([w_down, by_req], axis=0),
+        jnp.concatenate([down_w, by_req], axis=0),
         preferred_element_type=jnp.float32,
     ).astype(jnp.bfloat16)
 
-    leaving = terms
-    arrived_sums = lax.all_to_all(leaving, KV + ("req",), 0, 0, tiled=True).reshape(
-        kv_count, req_count, steps, width
+    arrived_sums = lax.all_to_all(terms, HALF + ("req",), 0, 0, tiled=True).reshape(
+        BEAMS, req_count, steps, width
     )
     per_group_sum = jnp.sum(arrived_sums.astype(jnp.float32), axis=0)
     served_by = slot_req[:, half, :] == group

time: 155 us -> 181 us (1.17)
  waiting for transfers between devices: 50.6 us -> 77.3 us
  blocking collectives: 14 us -> 0 us
  starting transfers between devices: 25.3 us -> 34.9 us
  matrix products: 9.32 us -> 12.9 us
    ppermute x0 -> x3, waiting for transfers between devices: none -> 47.8 us  [the longest x1 17.5 us: on_device(): lax.ppermute(w_gate, 'zhi', swap)]
    all_to_all x2 -> x3, waiting for transfers between devices: 44.7 us -> 24.3 us  [the longest x1 15.3 us: on_device(): lax.all_to_all(terms, HALF + ('req',), 0, 0, tiled=True)]
    all_to_all x1 -> x0, blocking collectives: 14 us -> none  [on_device(): lax.all_to_all(attended, HALF, split_axis=0, concat_axis=0, tiled=True)]
    ppermute x0 -> x3, starting transfers between devices: none -> 6.96 us  [the longest x1 3.38 us: on_device(): up_w = jnp.concatenate([w_up, lax.ppermute(w_up, 'zhi', swap)], axis=1)]
    dot_general x3, matrix products: 2.35 us -> 5.94 us  [the longest x1 2.16 us: on_device(): gate = jnp.dot(mlp_in, gate_w, preferred_element_type=jnp.float32)]
    all_to_all x2 -> x3, starting transfers between devices: 14 us -> 16.6 us  [the longest x1 8.59 us: on_device(): lax.all_to_all(terms, HALF + ('req',), 0, 0, tiled=True)]
  transfers between devices with their start and end apart: 4 -> 8, of which waited for: 4 -> 8; matrix products, arithmetic and copies ran while one was open for 8% -> 12% of each run, Pallas kernels for 0% -> 0%
where the time goes in v9:
time: 181 us; the launch traced here: 180 us
  waiting for transfers between devices  77.3 us (43%)
  starting transfers between devices  34.9 us (19%)
  local copies, waits for them, and re-layouts  25.5 us (14%)
  Pallas kernels  22.6 us (12%)
  matrix products  12.9 us (7%)
  other arithmetic  6.67 us (4%)
    pallas_call x1, Pallas kernels, attend(): pl.pallas_call(attend_kernel, grid_spec=pltpu.PrefetchScalarGridSpec(num_...  22.6 us
    ppermute x1, waiting for transfers between devices, on_device(): lax.ppermute(w_gate, 'zhi', swap)  17.5 us
    ppermute x1, waiting for transfers between devices, on_device(): lax.ppermute(w_down, 'zhi', swap)  16.8 us
    all_to_all x1, waiting for transfers between devices, on_device(): lax.all_to_all(terms, HALF + ('req',), 0, 0, tiled=True)  15.3 us
    ppermute x1, waiting for transfers between devices, on_device(): up_w = jnp.concatenate([w_up, lax.ppermute(w_up, 'zhi', swap)], axis=1)  13.5 us
    all_to_all x1, starting transfers between devices, on_device(): lax.all_to_all(terms, HALF + ('req',), 0, 0, tiled=True)  8.59 us
    gather x1, local copies, waits for them, and re-layouts, on_device(): pool[table[offset_of] - device * pool.shape[0]]  7.82 us
    all_to_all x1, waiting for transfers between devices, on_device(): lax.all_to_all(attended, HALF, split_axis=0, concat_axis=0, tiled=True)  7.25 us
  transfers between devices with their start and end apart: 8, of which 8 were waited for; matrix products, arithmetic and copies ran while one was open for 12% of the time, Pallas kernels for 0%

profile of v9, /device:TPU:1, one launch (start us, length us, event | category | flops | bytes accessed | tf_op | source)
XLA Modules:
  0.0 180.2 jit_solution(13318946639836328786)
XLA Ops:
  4.9 1.7 gather_fusion
  7.4 5.8 %all-to-all-start = ((bf16[4,8,1,1536]{3,0,2,1:T(4,128)(2,1)}), bf16[4,8,1,1536]{3,0,2,1:T(4,128)(2,1)S(1)}, u32[]{:S(2)}, u32[]{:S(2)}) async-start(bf16[4,8,1,1536]{3,0,2,1:T(4,128)(2,1)} %copy.93), calls=%async_computation | async-start | bytes 196608 | tf_op jit(solution)/shard_map/all_to_all | solution.py:154
  18.5 3.3 %convolution_convert_fusion.1 = bf16[32,1536]{1,0:T(8,128)(2,1)S(1)} fusion(bf16[1536,1536]{1,0:T(8,128)(2,1)} %param.21, f32[4,8,1,1536]{3,0,2,1:T(4,128)S(1)} %convert_element_type.110, f32[1536]{0:T(1024)} %param.20, f32[32]{0:T(128)S(1)} %rsqrt.23), kind=kOutput, calls=%fused_computation.9 | convolution fusion | flops 151191552 | bytes 5019776 | tf_op jit(solution)/shard_map/dot_general | solution.py:165
  23.1 5.5 %all-to-all-start.1 = ((bf16[8,4,8,1792]{3,2,1,0:T(8,128)(2,1)}), bf16[8,4,8,1792]{3,2,1,0:T(8,128)(2,1)S(1)}, u32[]{:S(2)}, u32[]{:S(2)}) async-start(bf16[8,4,8,1792]{3,2,1,0:T(8,128)(2,1)} %broadcast_in_dim.335), calls=%async_computation.1 | async-start | bytes 1835008 | tf_op jit(solution)/shard_map/all_to_all | solution.py:168
  29.6 7.8 %gather_fusion.5 = bf16[72,128,256]{2,1,0:T(8,128)(2,1)} fusion(bf16[72,128,256]{2,1,0:T(8,128)(2,1)} %param.19, s32[1024]{0:T(1024)S(1)} %pad_clamp_fusion), kind=kCustom, calls=%fused_computation.5 | custom fusion | bytes 9437472 | tf_op jit(solution)/shard_map/gather | solution.py:197
  38.2 3.7 %all-to-all-done.1 = bf16[8,4,8,1792]{3,2,1,0:T(8,128)(2,1)S(1)} async-done(((bf16[8,4,8,1792]{3,2,1,0:T(8,128)(2,1)}), bf16[8,4,8,1792]{3,2,1,0:T(8,128)(2,1)S(1)}, u32[]{:S(2)}, u32[]{:S(2)}) %all-to-all-start.1) | async-done | bytes 917536 | tf_op jit(solution)/shard_map/all_to_all | solution.py:168
  45.0 22.6 %shard_map.136 = bf16[8,4,96,128]{3,2,1,0:T(8,128)(2,1)} custom-call(s32[64]{0:T(128)} %reshape.512.bounds_ref, bf16[8,4,96,128]{3,2,1,0:T(8,128)(2,1)} %copy.105.q_ref, bf16[8,1152,256]{2,1,0:T(8,128)(2,1)} %bitcast.101, bf16[8,4,32,256]{3,2,1,0:T(8,128)(2,1)} %bitcast.104, f32[4,96,32]{2,1,0:T(8,128)} %and_convert_fusion.pick_ref), custom_call_target="tpu_custom_call" | custom-call | flops 1862270976 | bytes 6815744 | tf_op jit(solution)/shard_map/pallas_call | solution.py:85
  67.6 2.1 %reshape.517 = bf16[8,4,8,1536]{3,2,1,0:T(8,128)(2,1)S(1)} reshape(bf16[8,4,96,128]{3,2,1,0:T(8,128)(2,1)} %shard_map.136) | data formatting | bytes 1572864 | tf_op jit(solution)/shard_map/reshape | solution.py:215
  69.7 1.6 bitcast_select_fusion
  71.2 3.5 %all-to-all-start.2 = ((bf16[8,4,8,1536]{3,1,2,0:T(4,128)(2,1)}), bf16[8,4,8,1536]{3,1,2,0:T(4,128)(2,1)S(1)}, u32[]{:S(2)}, u32[]{:S(2)}) async-start(bf16[8,4,8,1536]{3,1,2,0:T(4,128)(2,1)} %bitcast_select_fusion), calls=%async_computation.2 | async-start | bytes 1572864 | tf_op jit(solution)/shard_map/all_to_all | solution.py:218
  74.8 3.4 %collective-permute-start.1 = (bf16[1536,288]{0,1:T(8,128)(2,1)S(1)}, bf16[1536,288]{0,1:T(8,128)(2,1)}, u32[]{:S(2)}, u32[]{:S(2)}) collective-permute-start(bf16[1536,288]{0,1:T(8,128)(2,1)S(1)} %copy-done.3), channel_id=1, source_target_pairs={{0,2},{2,0},{1,3},{3,1},{4,6},{6,4},{5,7},{7,5},{8,10},{10,8},{9,1... | collective-permute-start | bytes 2654216 | tf_op jit(solution)/shard_map/ppermute | solution.py:140
  78.2 7.2 %all-to-all-done.2 = bf16[8,4,8,1536]{3,1,2,0:T(4,128)(2,1)S(1)} async-done(((bf16[8,4,8,1536]{3,1,2,0:T(4,128)(2,1)}), bf16[8,4,8,1536]{3,1,2,0:T(4,128)(2,1)S(1)}, u32[]{:S(2)}, u32[]{:S(2)}) %all-to-all-start.2) | async-done | bytes 786464 | tf_op jit(solution)/shard_map/all_to_all | solution.py:218
  85.8 3.3 %multiply_reduce_fusion = (f32[8,4]{0,1:T(4,128)S(1)}, bf16[8,4,1536]{2,0,1:T(8,128)(2,1)S(1)}) fusion(bf16[1536,1536]{1,0:T(8,128)(2,1)} %param.23, bf16[4,8,1536]{2,0,1:T(4,128)(2,1)S(1)} %reduce_sum.302, f32[4,8,1,1536]{3,0,2,1:T(4,128)S(1)} %convert_element_type.110), kind=kOutput, calls=%fused_computation.58 | convolution fusion | flops 151240672 | bytes 5111936 | tf_op jit(solution)/shard_map/dot_general | solution.py:224
  90.5 4.5 %all-to-all-start.3 = ((bf16[8,32,1536]{2,1,0:T(8,128)(2,1)}), bf16[8,32,1536]{2,1,0:T(8,128)(2,1)S(1)}, u32[]{:S(2)}, u32[]{:S(2)}) async-start(bf16[8,32,1536]{2,1,0:T(8,128)(2,1)} %broadcast_in_dim.359), calls=%async_computation.3 | async-start | bytes 1572864 | tf_op jit(solution)/shard_map/all_to_all | solution.py:228
  94.9 3.3 %collective-permute-start = (bf16[1536,288]{0,1:T(8,128)(2,1)}, bf16[1536,288]{0,1:T(8,128)(2,1)}, u32[]{:S(2)}, u32[]{:S(2)}) collective-permute-start(bf16[1536,288]{0,1:T(8,128)(2,1)} %param.25), channel_id=1, source_target_pairs={{0,2},{2,0},{1,3},{3,1},{4,6},{6,4},{5,7},{7,5},{8,10},{10,8},{9,1... | collective-permute-start | bytes 2654216 | tf_op jit(solution)/shard_map/ppermute | solution.py:139
  98.5 13.5 %collective-permute-done.1 = bf16[1536,288]{0,1:T(8,128)(2,1)} collective-permute-done((bf16[1536,288]{0,1:T(8,128)(2,1)S(1)}, bf16[1536,288]{0,1:T(8,128)(2,1)}, u32[]{:S(2)}, u32[]{:S(2)}) %collective-permute-start.1) | collective-permute-done | bytes 884768 | tf_op jit(solution)/shard_map/ppermute | solution.py:140
  112.1 1.8 all-to-all-done.3
  113.8 1.8 %fusion.11 = f32[256,576]{0,1:T(8,128)S(1)} fusion(bf16[256,1536]{1,0:T(8,128)(2,1)S(1)} %bitcast.105, bf16[1536,288]{0,1:T(8,128)(2,1)} %collective-permute-done.1, bf16[1536,288]{0,1:T(8,128)(2,1)S(1)} %copy-done.3), kind=kOutput, calls=%fused_computation.20 | convolution fusion | flops 456523776 | bytes 3145728 | tf_op jit(solution)/shard_map/dot_general | solution.py:232
  115.7 17.5 %collective-permute-done = bf16[1536,288]{0,1:T(8,128)(2,1)} collective-permute-done((bf16[1536,288]{0,1:T(8,128)(2,1)}, bf16[1536,288]{0,1:T(8,128)(2,1)}, u32[]{:S(2)}, u32[]{:S(2)}) %collective-permute-start) | collective-permute-done | bytes 884768 | tf_op jit(solution)/shard_map/ppermute | solution.py:139
  133.1 2.2 %fusion.27 = bf16[256,576]{0,1:T(8,128)(2,1)S(1)} fusion(f32[256,576]{0,1:T(8,128)S(1)} %fusion.11, bf16[256,1536]{1,0:T(8,128)(2,1)S(1)} %bitcast.106, bf16[1536,288]{0,1:T(8,128)(2,1)} %collective-permute-done, bf16[1536,288]{0,1:T(8,128)(2,1)} %param.25), kind=kOutput, calls=%fused_computation.38 | convolution fusion | flops 457998336 | bytes 3440640 | tf_op jit(solution)/shard_map/dot_general | solution.py:231
  135.3 16.8 %collective-permute-done.2 = bf16[288,1536]{1,0:T(8,128)(2,1)} collective-permute-done((bf16[288,1536]{1,0:T(8,128)(2,1)}, bf16[288,1536]{1,0:T(8,128)(2,1)}, u32[]{:S(2)}, u32[]{:S(2)}) %collective-permute-start.2) | collective-permute-done | bytes 884768 | tf_op jit(solution)/shard_map/ppermute | solution.py:141
  152.1 2.0 %convolution_convert_fusion = bf16[256,1536]{1,0:T(8,128)(2,1)S(1)} fusion(bf16[32,1536]{1,0:T(8,128)(2,1)S(1)} %reshape.520, bf16[288,1536]{1,0:T(8,128)(2,1)} %collective-permute-done.2, bf16[288,1536]{1,0:T(8,128)(2,1)S(1)} %copy-done.4, bf16[256,32]{0,1:T(8,128)(2,1)S(1)} %fusion.38, bf16[256,576]{0,1:T(8,128)(2,1)S(1)} %fusion.27), kind=kOutput, calls=%fused_computation.6 | convolution fusion | flops 484769792 | bytes 2965504 | tf_op jit(solution)/shard_map/dot_general | solution.py:239
  155.1 8.6 %all-to-all-start.4 = ((bf16[64,4,1536]{2,1,0:T(4,128)(2,1)}), bf16[64,4,1536]{2,1,0:T(4,128)(2,1)S(1)}, u32[]{:S(2)}, u32[]{:S(2)}) async-start(bf16[64,4,1536]{2,1,0:T(4,128)(2,1)} %all_to_all.22), calls=%async_computation.4 | async-start | bytes 1572864 | tf_op jit(solution)/shard_map/all_to_all | solution.py:245
  163.8 15.3 %all-to-all-done.4 = bf16[64,4,1536]{2,1,0:T(4,128)(2,1)S(1)} async-done(((bf16[64,4,1536]{2,1,0:T(4,128)(2,1)}), bf16[64,4,1536]{2,1,0:T(4,128)(2,1)S(1)}, u32[]{:S(2)}, u32[]{:S(2)}) %all-to-all-start.4) | async-done | bytes 786464 | tf_op jit(solution)/shard_map/all_to_all | solution.py:245
  (102 shorter events, 21.0 us)
Async XLA Ops:
  0.0 21.8 %copy-start = (bf16[1536,256]{1,0:T(8,128)(2,1)S(1)}, bf16[1536,256]{1,0:T(8,128)(2,1)}, u32[]{:S(2)}) copy-start(bf16[1536,256]{1,0:T(8,128)(2,1)} %param.22) | copy-start | bytes 2359300
  4.9 16.9 %copy-start.1 = (f32[1536]{0:T(1024)S(1)}, f32[1536]{0:T(1024)}, u32[]{:S(2)}) copy-start(f32[1536]{0:T(1024)} %param.20) | copy-start | bytes 18436
  7.4 10.8 %all-to-all-start = ((bf16[4,8,1,1536]{3,0,2,1:T(4,128)(2,1)}), bf16[4,8,1,1536]{3,0,2,1:T(4,128)(2,1)S(1)}, u32[]{:S(2)}, u32[]{:S(2)}) async-start(bf16[4,8,1,1536]{3,0,2,1:T(4,128)(2,1)} %copy.93), calls=%async_computation | async-start | bytes 196608 | tf_op jit(solution)/shard_map/all_to_all | solution.py:154
  23.1 18.8 %all-to-all-start.1 = ((bf16[8,4,8,1792]{3,2,1,0:T(8,128)(2,1)}), bf16[8,4,8,1792]{3,2,1,0:T(8,128)(2,1)S(1)}, u32[]{:S(2)}, u32[]{:S(2)}) async-start(bf16[8,4,8,1792]{3,2,1,0:T(8,128)(2,1)} %broadcast_in_dim.335), calls=%async_computation.1 | async-start | bytes 1835008 | tf_op jit(solution)/shard_map/all_to_all | solution.py:168
  67.6 7.2 %copy-start.3 = (bf16[1536,288]{0,1:T(8,128)(2,1)S(1)}, bf16[1536,288]{0,1:T(8,128)(2,1)}, u32[]{:S(2)}) copy-start(bf16[1536,288]{0,1:T(8,128)(2,1)} %param.26) | copy-start | bytes 2654212
  71.2 14.2 %all-to-all-start.2 = ((bf16[8,4,8,1536]{3,1,2,0:T(4,128)(2,1)}), bf16[8,4,8,1536]{3,1,2,0:T(4,128)(2,1)S(1)}, u32[]{:S(2)}, u32[]{:S(2)}) async-start(bf16[8,4,8,1536]{3,1,2,0:T(4,128)(2,1)} %bitcast_select_fusion), calls=%async_computation.2 | async-start | bytes 1572864 | tf_op jit(solution)/shard_map/all_to_all | solution.py:218
  74.8 14.6 %copy-start.2 = (f32[1536]{0:T(1024)S(1)}, f32[1536]{0:T(1024)}, u32[]{:S(2)}) copy-start(f32[1536]{0:T(1024)} %param.24) | copy-start | bytes 18436
  74.8 37.3 %collective-permute-start.1 = (bf16[1536,288]{0,1:T(8,128)(2,1)S(1)}, bf16[1536,288]{0,1:T(8,128)(2,1)}, u32[]{:S(2)}, u32[]{:S(2)}) collective-permute-start(bf16[1536,288]{0,1:T(8,128)(2,1)S(1)} %copy-done.3), channel_id=1, source_target_pairs={{0,2},{2,0},{1,3},{3,1},{4,6},{6,4},{5,7},{7,5},{8,10},{10,8},{9,1... | collective-permute-start | bytes 2654216 | tf_op jit(solution)/shard_map/ppermute | solution.py:140
  90.5 23.4 %all-to-all-start.3 = ((bf16[8,32,1536]{2,1,0:T(8,128)(2,1)}), bf16[8,32,1536]{2,1,0:T(8,128)(2,1)S(1)}, u32[]{:S(2)}, u32[]{:S(2)}) async-start(bf16[8,32,1536]{2,1,0:T(8,128)(2,1)} %broadcast_in_dim.359), calls=%async_computation.3 | async-start | bytes 1572864 | tf_op jit(solution)/shard_map/all_to_all | solution.py:228
  94.9 38.2 %collective-permute-start = (bf16[1536,288]{0,1:T(8,128)(2,1)}, bf16[1536,288]{0,1:T(8,128)(2,1)}, u32[]{:S(2)}, u32[]{:S(2)}) collective-permute-start(bf16[1536,288]{0,1:T(8,128)(2,1)} %param.25), channel_id=1, source_target_pairs={{0,2},{2,0},{1,3},{3,1},{4,6},{6,4},{5,7},{7,5},{8,10},{10,8},{9,1... | collective-permute-start | bytes 2654216 | tf_op jit(solution)/shard_map/ppermute | solution.py:139
  98.2 53.9 %collective-permute-start.2 = (bf16[288,1536]{1,0:T(8,128)(2,1)}, bf16[288,1536]{1,0:T(8,128)(2,1)}, u32[]{:S(2)}, u32[]{:S(2)}) collective-permute-start(bf16[288,1536]{1,0:T(8,128)(2,1)} %param.27), channel_id=1, source_target_pairs={{0,2},{2,0},{1,3},{3,1},{4,6},{6,4},{5,7},{7,5},{8,10},{10,8},{9,1... | collective-permute-start | bytes 2654216 | tf_op jit(solution)/shard_map/ppermute | solution.py:141
  115.7 36.4 %copy-start.4 = (bf16[288,1536]{1,0:T(8,128)(2,1)S(1)}, bf16[288,1536]{1,0:T(8,128)(2,1)}, u32[]{:S(2)}) copy-start(bf16[288,1536]{1,0:T(8,128)(2,1)} %param.27) | copy-start | bytes 2654212
  155.1 23.9 %all-to-all-start.4 = ((bf16[64,4,1536]{2,1,0:T(4,128)(2,1)}), bf16[64,4,1536]{2,1,0:T(4,128)(2,1)S(1)}, u32[]{:S(2)}, u32[]{:S(2)}) async-start(bf16[64,4,1536]{2,1,0:T(4,128)(2,1)} %all_to_all.22), calls=%async_computation.4 | async-start | bytes 1572864 | tf_op jit(solution)/shard_map/all_to_all | solution.py:245

commit v10 on v9

--- a/solution.py
+++ b/solution.py
@@ -136,9 +136,7 @@
     group_rows = kv_count * rows
     quota = rows // req_count
     swap = [(0, 1), (1, 0)]
-    gate_w = jnp.concatenate([w_gate, lax.ppermute(w_gate, "zhi", swap)], axis=1)
-    up_w = jnp.concatenate([w_up, lax.ppermute(w_up, "zhi", swap)], axis=1)
-    down_w = jnp.concatenate([w_down, lax.ppermute(w_down, "zhi", swap)], axis=0)
+    partner = [lax.ppermute(w, "zhi", swap) for w in (w_gate, w_up, w_down)]
 
     offsets = jnp.arange(rows, dtype=jnp.int32)
     slot_ids = group * per_group + half * rows + offsets
@@ -195,6 +193,10 @@
     first_page = jnp.maximum(length - WINDOW + 1, 0) // PAGE
     device = group * kv_count + member
     pages = pool[table[offset_of] - device * pool.shape[0]].reshape(rows, span, 2 * head_dim)
+    pages, partner = lax.optimization_barrier((pages, partner))
+    gate_w = jnp.concatenate([w_gate, partner[0]], axis=1)
+    up_w = jnp.concatenate([w_up, partner[1]], axis=1)
+    down_w = jnp.concatenate([w_down, partner[2]], axis=0)
     scale = head_dim ** (-0.5)
     step_ids = jnp.arange(steps, dtype=jnp.int32)
     base = first_page * PAGE

time: 181 us -> 181 us (level)
  blocking collectives: 0 us -> 15.8 us
  waiting for transfers between devices: 77.3 us -> 67.3 us
  starting transfers between devices: 34.9 us -> 29.6 us
    all_to_all x0 -> x1, blocking collectives: none -> 15.8 us  [on_device(): lax.all_to_all(attended, HALF, split_axis=0, concat_axis=0, tiled=True)]
    ppermute x3, waiting for transfers between devices: 47.8 us -> 39.2 us  [on_device(): partner = [lax.ppermute(w, 'zhi', swap) for w in (w_gate, w_up, w_down)]]
    all_to_all x1, waiting for transfers between devices: 1.77 us -> 9.84 us  [on_device(): lax.all_to_all(jnp.broadcast_to(mlp_own[None], (BEAMS,) + mlp_own.shape),...]
    all_to_all x1 -> x0, waiting for transfers between devices: 7.25 us -> none  [on_device(): lax.all_to_all(attended, HALF, split_axis=0, concat_axis=0, tiled=True)]
    all_to_all x1 -> x0, starting transfers between devices: 3.55 us -> none  [on_device(): lax.all_to_all(attended, HALF, split_axis=0, concat_axis=0, tiled=True)]
  transfers between devices with their start and end apart: 8 -> 7, of which waited for: 8 -> 5; matrix products, arithmetic and copies ran while one was open for 12% -> 10% of each run, Pallas kernels for 0% -> 0%
where the time goes in v10:
time: 181 us
  waiting for transfers between devices  67.3 us (37%)
  starting transfers between devices  29.6 us (16%)
  local copies, waits for them, and re-layouts  25.5 us (14%)
  Pallas kernels  22.6 us (12%)
  blocking collectives  15.8 us (9%)
  matrix products  13.7 us (8%)
  other arithmetic  5.75 us (3%)
    ppermute x3, waiting for transfers between devices, on_device(): partner = [lax.ppermute(w, 'zhi', swap) for w in (w_gate, w_up, w_down)]  39.2 us
    pallas_call x1, Pallas kernels, attend(): pl.pallas_call(attend_kernel, grid_spec=pltpu.PrefetchScalarGridSpec(num_...  22.6 us
    all_to_all x1, blocking collectives, on_device(): lax.all_to_all(attended, HALF, split_axis=0, concat_axis=0, tiled=True)  15.8 us
    all_to_all x1, waiting for transfers between devices, on_device(): lax.all_to_all(terms, HALF + ('req',), 0, 0, tiled=True)  15.3 us
    all_to_all x1, waiting for transfers between devices, on_device(): lax.all_to_all(jnp.broadcast_to(mlp_own[None], (BEAMS,) + mlp_own.shape),...  9.84 us
    all_to_all x1, starting transfers between devices, on_device(): lax.all_to_all(terms, HALF + ('req',), 0, 0, tiled=True)  8.83 us
    gather x1, local copies, waits for them, and re-layouts, on_device(): pool[table[offset_of] - device * pool.shape[0]]  7.86 us
    ppermute x3, starting transfers between devices, on_device(): partner = [lax.ppermute(w, 'zhi', swap) for w in (w_gate, w_up, w_down)]  6.58 us
  transfers between devices with their start and end apart: 7, of which 5 were waited for; matrix products, arithmetic and copies ran while one was open for 10% of the time, Pallas kernels for 0%

profile of v10, /device:TPU:1, one launch (start us, length us, event | category | flops | bytes accessed | tf_op | source)
XLA Modules:
  0.0 180.6 jit_solution(2002678471602413691)
XLA Ops:
  3.6 1.3 gather_fusion.3
  4.9 1.7 gather_fusion
  7.3 5.8 %all-to-all-start = ((bf16[4,8,1,1536]{3,0,2,1:T(4,128)(2,1)}), bf16[4,8,1,1536]{3,0,2,1:T(4,128)(2,1)S(1)}, u32[]{:S(2)}, u32[]{:S(2)}) async-start(bf16[4,8,1,1536]{3,0,2,1:T(4,128)(2,1)} %copy.93), calls=%async_computation | async-start | bytes 196608 | tf_op jit(solution)/shard_map/all_to_all | solution.py:152
  13.1 3.6 %collective-permute-start = (bf16[1536,288]{0,1:T(8,128)(2,1)}, bf16[1536,288]{0,1:T(8,128)(2,1)S(1)}, u32[]{:S(2)}, u32[]{:S(2)}) collective-permute-start(bf16[1536,288]{0,1:T(8,128)(2,1)} %param.25), channel_id=1, source_target_pairs={{0,2},{2,0},{1,3},{3,1},{4,6},{6,4},{5,7},{7,5},{8,10},{10,8},{9,1... | collective-permute-start | bytes 2654216 | tf_op jit(solution)/shard_map/ppermute | solution.py:139
  16.8 3.0 %collective-permute-start.2 = (bf16[288,1536]{1,0:T(8,128)(2,1)}, bf16[288,1536]{1,0:T(8,128)(2,1)}, u32[]{:S(2)}, u32[]{:S(2)}) collective-permute-start(bf16[288,1536]{1,0:T(8,128)(2,1)} %param.27), channel_id=1, source_target_pairs={{0,2},{2,0},{1,3},{3,1},{4,6},{6,4},{5,7},{7,5},{8,10},{10,8},{9,1... | collective-permute-start | bytes 2654216 | tf_op jit(solution)/shard_map/ppermute | solution.py:139
  19.8 1.2 gather_fusion.4
  24.6 3.3 %convolution_convert_fusion.1 = bf16[32,1536]{1,0:T(8,128)(2,1)S(1)} fusion(bf16[1536,1536]{1,0:T(8,128)(2,1)} %param.21, f32[4,8,1,1536]{3,0,2,1:T(4,128)S(1)} %convert_element_type.110, f32[1536]{0:T(1024)S(1)} %copy-done.1, f32[32]{0:T(128)S(1)} %rsqrt.23), kind=kOutput, calls=%fused_computation.9 | convolution fusion | flops 151191552 | bytes 5019776 | tf_op jit(solution)/shard_map/dot_general | solution.py:163
  28.9 4.6 %all-to-all-start.1 = ((bf16[8,4,8,1792]{3,2,1,0:T(8,128)(2,1)}), bf16[8,4,8,1792]{3,2,1,0:T(8,128)(2,1)S(1)}, u32[]{:S(2)}, u32[]{:S(2)}) async-start(bf16[8,4,8,1792]{3,2,1,0:T(8,128)(2,1)} %broadcast_in_dim.335), calls=%async_computation.1 | async-start | bytes 1835008 | tf_op jit(solution)/shard_map/all_to_all | solution.py:166
  34.5 7.9 %gather_fusion.5 = bf16[72,128,256]{2,1,0:T(8,128)(2,1)} fusion(bf16[72,128,256]{2,1,0:T(8,128)(2,1)} %param.19, s32[1024]{0:T(1024)S(1)} %pad_clamp_fusion), kind=kCustom, calls=%fused_computation.5 | custom fusion | bytes 9437472 | tf_op jit(solution)/shard_map/gather | solution.py:195
  43.1 20.3 %collective-permute-done.1 = bf16[1536,288]{0,1:T(8,128)(2,1)} collective-permute-done((bf16[1536,288]{0,1:T(8,128)(2,1)}, bf16[1536,288]{0,1:T(8,128)(2,1)}, u32[]{:S(2)}, u32[]{:S(2)}) %collective-permute-start.1) | collective-permute-done | bytes 884768 | tf_op jit(solution)/shard_map/ppermute | solution.py:139
  63.4 19.0 %collective-permute-done.2 = bf16[288,1536]{1,0:T(8,128)(2,1)} collective-permute-done((bf16[288,1536]{1,0:T(8,128)(2,1)}, bf16[288,1536]{1,0:T(8,128)(2,1)}, u32[]{:S(2)}, u32[]{:S(2)}) %collective-permute-start.2) | collective-permute-done | bytes 884768 | tf_op jit(solution)/shard_map/ppermute | solution.py:139
  82.4 2.9 %all-to-all-done.1 = bf16[8,4,8,1792]{3,2,1,0:T(8,128)(2,1)S(1)} async-done(((bf16[8,4,8,1792]{3,2,1,0:T(8,128)(2,1)}), bf16[8,4,8,1792]{3,2,1,0:T(8,128)(2,1)S(1)}, u32[]{:S(2)}, u32[]{:S(2)}) %all-to-all-start.1) | async-done | bytes 917536 | tf_op jit(solution)/shard_map/all_to_all | solution.py:166
  88.4 22.6 %shard_map.136 = bf16[8,4,96,128]{3,2,1,0:T(8,128)(2,1)} custom-call(s32[64]{0:T(128)} %reshape.512.bounds_ref, bf16[8,4,96,128]{3,2,1,0:T(8,128)(2,1)} %copy.105.q_ref, bf16[8,1152,256]{2,1,0:T(8,128)(2,1)} %bitcast.101, bf16[8,4,32,256]{3,2,1,0:T(8,128)(2,1)} %bitcast.104, f32[4,96,32]{2,1,0:T(8,128)} %and_convert_fusion.pick_ref), custom_call_target="tpu_custom_call" | custom-call | flops 1862270976 | bytes 6815744 | tf_op jit(solution)/shard_map/pallas_call | solution.py:85
  110.9 2.0 %reshape.517 = bf16[8,4,8,1536]{3,2,1,0:T(8,128)(2,1)S(1)} reshape(bf16[8,4,96,128]{3,2,1,0:T(8,128)(2,1)} %shard_map.136) | data formatting | bytes 1572864 | tf_op jit(solution)/shard_map/reshape | solution.py:217
  113.6 15.8 %all_to_all.29 = bf16[8,4,8,1536]{3,1,2,0:T(4,128)(2,1)S(1)} all-to-all(bf16[8,4,8,1536]{3,1,2,0:T(4,128)(2,1)S(1)} %bitcast_select_fusion), channel_id=1, replica_groups=mesh['req'=8,'y'=4,'zhi'=2,'zlo'=2] {'y','zlo'}, dimensions={0} | all-to-all | bytes 1572864 | tf_op jit(solution)/shard_map/all_to_all | solution.py:220
  129.8 3.4 %multiply_reduce_fusion = (f32[8,4]{0,1:T(4,128)S(1)}, bf16[8,4,1536]{2,0,1:T(8,128)(2,1)S(1)}) fusion(bf16[1536,1536]{1,0:T(8,128)(2,1)} %param.23, bf16[4,8,1536]{2,0,1:T(4,128)(2,1)S(1)} %reduce_sum.302, f32[4,8,1,1536]{3,0,2,1:T(4,128)S(1)} %convert_element_type.110), kind=kOutput, calls=%fused_computation.58 | convolution fusion | flops 151240672 | bytes 5111936 | tf_op jit(solution)/shard_map/dot_general | solution.py:226
  134.6 3.7 %all-to-all-start.3 = ((bf16[8,32,1536]{2,1,0:T(8,128)(2,1)}), bf16[8,32,1536]{2,1,0:T(8,128)(2,1)S(1)}, u32[]{:S(2)}, u32[]{:S(2)}) async-start(bf16[8,32,1536]{2,1,0:T(8,128)(2,1)} %broadcast_in_dim.359), calls=%async_computation.3 | async-start | bytes 1572864 | tf_op jit(solution)/shard_map/all_to_all | solution.py:230
  138.3 9.8 %all-to-all-done.3 = bf16[8,32,1536]{2,1,0:T(8,128)(2,1)S(1)} async-done(((bf16[8,32,1536]{2,1,0:T(8,128)(2,1)}), bf16[8,32,1536]{2,1,0:T(8,128)(2,1)S(1)}, u32[]{:S(2)}, u32[]{:S(2)}) %all-to-all-start.3) | async-done | bytes 786464 | tf_op jit(solution)/shard_map/all_to_all | solution.py:230
  148.2 1.8 %fusion.11 = f32[256,576]{0,1:T(8,128)S(1)} fusion(bf16[256,1536]{1,0:T(8,128)(2,1)S(1)} %bitcast.105, bf16[1536,288]{0,1:T(8,128)(2,1)} %collective-permute-done.1, bf16[1536,288]{0,1:T(8,128)(2,1)S(1)} %copy-done.3), kind=kOutput, calls=%fused_computation.20 | convolution fusion | flops 456523776 | bytes 3145728 | tf_op jit(solution)/shard_map/dot_general | solution.py:234
  150.0 2.2 %fusion.27 = bf16[256,576]{0,1:T(8,128)(2,1)S(1)} fusion(f32[256,576]{0,1:T(8,128)S(1)} %fusion.11, bf16[256,1536]{1,0:T(8,128)(2,1)S(1)} %bitcast.106, bf16[1536,288]{0,1:T(8,128)(2,1)} %copy-done.5, bf16[1536,288]{0,1:T(8,128)(2,1)} %param.25), kind=kOutput, calls=%fused_computation.38 | convolution fusion | flops 457998336 | bytes 3440640 | tf_op jit(solution)/shard_map/dot_general | solution.py:233
  152.3 2.0 %convolution_convert_fusion = bf16[256,1536]{1,0:T(8,128)(2,1)S(1)} fusion(bf16[32,1536]{1,0:T(8,128)(2,1)S(1)} %reshape.520, bf16[288,1536]{1,0:T(8,128)(2,1)} %collective-permute-done.2, bf16[288,1536]{1,0:T(8,128)(2,1)S(1)} %copy-done.4, bf16[256,32]{0,1:T(8,128)(2,1)S(1)} %fusion.38, bf16[256,576]{0,1:T(8,128)(2,1)S(1)} %fusion.27), kind=kOutput, calls=%fused_computation.6 | convolution fusion | flops 484769792 | bytes 2965504 | tf_op jit(solution)/shard_map/dot_general | solution.py:241
  154.2 1.1 all_to_all.22
  155.3 8.8 %all-to-all-start.4 = ((bf16[64,4,1536]{2,1,0:T(4,128)(2,1)}), bf16[64,4,1536]{2,1,0:T(4,128)(2,1)S(1)}, u32[]{:S(2)}, u32[]{:S(2)}) async-start(bf16[64,4,1536]{2,1,0:T(4,128)(2,1)} %all_to_all.22), calls=%async_computation.4 | async-start | bytes 1572864 | tf_op jit(solution)/shard_map/all_to_all | solution.py:247
  164.2 15.3 %all-to-all-done.4 = bf16[64,4,1536]{2,1,0:T(4,128)(2,1)S(1)} async-done(((bf16[64,4,1536]{2,1,0:T(4,128)(2,1)}), bf16[64,4,1536]{2,1,0:T(4,128)(2,1)S(1)}, u32[]{:S(2)}, u32[]{:S(2)}) %all-to-all-start.4) | async-done | bytes 786464 | tf_op jit(solution)/shard_map/all_to_all | solution.py:247
  (103 shorter events, 17.1 us)
Async XLA Ops:
  0.0 23.6 %copy-start = (bf16[1536,256]{1,0:T(8,128)(2,1)S(1)}, bf16[1536,256]{1,0:T(8,128)(2,1)}, u32[]{:S(2)}) copy-start(bf16[1536,256]{1,0:T(8,128)(2,1)} %param.22) | copy-start | bytes 2359300
  0.0 24.6 %copy-start.1 = (f32[1536]{0:T(1024)S(1)}, f32[1536]{0:T(1024)}, u32[]{:S(2)}) copy-start(f32[1536]{0:T(1024)} %param.20) | copy-start | bytes 18436
  7.3 15.9 %all-to-all-start = ((bf16[4,8,1,1536]{3,0,2,1:T(4,128)(2,1)}), bf16[4,8,1,1536]{3,0,2,1:T(4,128)(2,1)S(1)}, u32[]{:S(2)}, u32[]{:S(2)}) async-start(bf16[4,8,1,1536]{3,0,2,1:T(4,128)(2,1)} %copy.93), calls=%async_computation | async-start | bytes 196608 | tf_op jit(solution)/shard_map/all_to_all | solution.py:152
  13.1 30.0 %collective-permute-start = (bf16[1536,288]{0,1:T(8,128)(2,1)}, bf16[1536,288]{0,1:T(8,128)(2,1)S(1)}, u32[]{:S(2)}, u32[]{:S(2)}) collective-permute-start(bf16[1536,288]{0,1:T(8,128)(2,1)} %param.25), channel_id=1, source_target_pairs={{0,2},{2,0},{1,3},{3,1},{4,6},{6,4},{5,7},{7,5},{8,10},{10,8},{9,1... | collective-permute-start | bytes 2654216 | tf_op jit(solution)/shard_map/ppermute | solution.py:139
  16.7 46.7 %collective-permute-start.1 = (bf16[1536,288]{0,1:T(8,128)(2,1)}, bf16[1536,288]{0,1:T(8,128)(2,1)}, u32[]{:S(2)}, u32[]{:S(2)}) collective-permute-start(bf16[1536,288]{0,1:T(8,128)(2,1)} %param.26), channel_id=1, source_target_pairs={{0,2},{2,0},{1,3},{3,1},{4,6},{6,4},{5,7},{7,5},{8,10},{10,8},{9,1... | collective-permute-start | bytes 2654216 | tf_op jit(solution)/shard_map/ppermute | solution.py:139
  16.8 65.6 %collective-permute-start.2 = (bf16[288,1536]{1,0:T(8,128)(2,1)}, bf16[288,1536]{1,0:T(8,128)(2,1)}, u32[]{:S(2)}, u32[]{:S(2)}) collective-permute-start(bf16[288,1536]{1,0:T(8,128)(2,1)} %param.27), channel_id=1, source_target_pairs={{0,2},{2,0},{1,3},{3,1},{4,6},{6,4},{5,7},{7,5},{8,10},{10,8},{9,1... | collective-permute-start | bytes 2654216 | tf_op jit(solution)/shard_map/ppermute | solution.py:139
  28.9 56.3 %all-to-all-start.1 = ((bf16[8,4,8,1792]{3,2,1,0:T(8,128)(2,1)}), bf16[8,4,8,1792]{3,2,1,0:T(8,128)(2,1)S(1)}, u32[]{:S(2)}, u32[]{:S(2)}) async-start(bf16[8,4,8,1792]{3,2,1,0:T(8,128)(2,1)} %broadcast_in_dim.335), calls=%async_computation.1 | async-start | bytes 1835008 | tf_op jit(solution)/shard_map/all_to_all | solution.py:166
  43.1 44.3 %copy-start.5 = (bf16[1536,288]{0,1:T(8,128)(2,1)}, bf16[1536,288]{0,1:T(8,128)(2,1)S(1)}, u32[]{:S(2)}) copy-start(bf16[1536,288]{0,1:T(8,128)(2,1)S(1)} %collective-permute-done) | copy-start | bytes 2654212
  129.4 4.1 %copy-start.2 = (f32[1536]{0:T(1024)S(1)}, f32[1536]{0:T(1024)}, u32[]{:S(2)}) copy-start(f32[1536]{0:T(1024)} %param.24) | copy-start | bytes 18436
  129.8 18.4 %copy-start.3 = (bf16[1536,288]{0,1:T(8,128)(2,1)S(1)}, bf16[1536,288]{0,1:T(8,128)(2,1)}, u32[]{:S(2)}) copy-start(bf16[1536,288]{0,1:T(8,128)(2,1)} %param.26) | copy-start | bytes 2654212
  134.6 13.6 %all-to-all-start.3 = ((bf16[8,32,1536]{2,1,0:T(8,128)(2,1)}), bf16[8,32,1536]{2,1,0:T(8,128)(2,1)S(1)}, u32[]{:S(2)}, u32[]{:S(2)}) async-start(bf16[8,32,1536]{2,1,0:T(8,128)(2,1)} %broadcast_in_dim.359), calls=%async_computation.3 | async-start | bytes 1572864 | tf_op jit(solution)/shard_map/all_to_all | solution.py:230
  150.0 2.3 %copy-start.4 = (bf16[288,1536]{1,0:T(8,128)(2,1)S(1)}, bf16[288,1536]{1,0:T(8,128)(2,1)}, u32[]{:S(2)}) copy-start(bf16[288,1536]{1,0:T(8,128)(2,1)} %param.27) | copy-start | bytes 2654212
  155.3 24.2 %all-to-all-start.4 = ((bf16[64,4,1536]{2,1,0:T(4,128)(2,1)}), bf16[64,4,1536]{2,1,0:T(4,128)(2,1)S(1)}, u32[]{:S(2)}, u32[]{:S(2)}) async-start(bf16[64,4,1536]{2,1,0:T(4,128)(2,1)} %all_to_all.22), calls=%async_computation.4 | async-start | bytes 1572864 | tf_op jit(solution)/shard_map/all_to_all | solution.py:247

commit v11 on v8

--- a/solution.py
+++ b/solution.py
@@ -41,67 +41,75 @@
     return jnp.sum(jnp.where(picks[..., None], table[None, :, :, :], 0), axis=1).astype(table.dtype)
 
 
-def attend_kernel(bounds_ref, q_ref, kv_ref, new_ref, pick_ref, out_ref):
+def attend_kernel(count_ref, q_ref, lo_ref, hi_ref, kv_ref, new_ref, pick_ref, out_ref):
     r = pl.program_id(0)
-    steps = q_ref.shape[1]
+    chunks = q_ref.shape[1]
     head_dim = q_ref.shape[3]
     scale = head_dim ** (-0.5)
     keys = kv_ref[0, :, :head_dim]
     values = kv_ref[0, :, head_dim:]
     pos = lax.broadcasted_iota(jnp.int32, (1, kv_ref.shape[1]), 1)
     contract = (((1,), (1,)), ((), ()))
-    for t in range(steps):
-        lo = bounds_ref[(r * steps + t) * 2]
-        hi = bounds_ref[(r * steps + t) * 2 + 1]
-        query = q_ref[0, t]
-        scores = lax.dot_general(query, keys, contract, preferred_element_type=jnp.float32) * scale
-        allowed = (pos > lo) & (pos < hi)
-        scores = jnp.where(allowed, scores, NEGATIVE)
-        high_c = jnp.max(scores, axis=1, keepdims=True)
-        weights = jnp.exp(scores - high_c).astype(jnp.bfloat16)
-        total_c = jnp.sum(weights.astype(jnp.float32), axis=1, keepdims=True)
-        sum_c = jnp.dot(weights, values, preferred_element_type=jnp.float32)
-        entries = new_ref[0, t]
-        fresh = lax.dot_general(
-            query, entries[:, :head_dim], contract, preferred_element_type=jnp.float32
-        ) * scale
-        fresh = jnp.where(pick_ref[t] > 0, fresh, NEGATIVE)
-        high_n = jnp.max(fresh, axis=1, keepdims=True)
-        fresh_w = jnp.exp(fresh - high_n).astype(jnp.bfloat16)
-        total_n = jnp.sum(fresh_w.astype(jnp.float32), axis=1, keepdims=True)
-        sum_n = jnp.dot(fresh_w, entries[:, head_dim:], preferred_element_type=jnp.float32)
-        highest = jnp.maximum(high_c, high_n)
-        scale_c = jnp.exp(high_c - highest)
-        scale_n = jnp.exp(high_n - highest)
-        totals = total_c * scale_c + total_n * scale_n
-        weighted = sum_c * scale_c + sum_n * scale_n
-        out_ref[0, t] = (weighted / totals).astype(out_ref.dtype)
-
-
-def attend(bounds, queries, pages, entries, pick):
-    rows, steps, count, head_dim = queries.shape
+    for c in range(chunks):
+
+        @pl.when(c < count_ref[r])
+        def _(c=c):
+            query = q_ref[0, c]
+            scores = lax.dot_general(query, keys, contract, preferred_element_type=jnp.float32) * scale
+            allowed = (pos > lo_ref[0, c]) & (pos < hi_ref[0, c])
+            scores = jnp.where(allowed, scores, NEGATIVE)
+            high_c = jnp.max(scores, axis=1, keepdims=True)
+            weights = jnp.exp(scores - high_c).astype(jnp.bfloat16)
+            total_c = jnp.sum(weights.astype(jnp.float32), axis=1, keepdims=True)
+            sum_c = jnp.dot(weights, values, preferred_element_type=jnp.float32)
+            entries = new_ref[0, c]
+            fresh = lax.dot_general(
+                query, entries[:, :head_dim], contract, preferred_element_type=jnp.float32
+            ) * scale
+            fresh = jnp.where(pick_ref[0, c] > 0, fresh, NEGATIVE)
+            high_n = jnp.max(fresh, axis=1, keepdims=True)
+            fresh_w = jnp.exp(fresh - high_n).astype(jnp.bfloat16)
+            total_n = jnp.sum(fresh_w.astype(jnp.float32), axis=1, keepdims=True)
+            sum_n = jnp.dot(fresh_w, entries[:, head_dim:], preferred_element_type=jnp.float32)
+            highest = jnp.maximum(high_c, high_n)
+            scale_c = jnp.exp(high_c - highest)
+            scale_n = jnp.exp(high_n - highest)
+            totals = total_c * scale_c + total_n * scale_n
+            weighted = sum_c * scale_c + sum_n * scale_n
+            out_ref[0, c] = (weighted / totals).astype(out_ref.dtype)
+
+        @pl.when(c >= count_ref[r])
+        def _(c=c):
+            out_ref[0, c] = jnp.zeros(out_ref.shape[2:], out_ref.dtype)
+
+
+def attend(count, queries, lo, hi, pages, entries, pick):
+    rows, chunks, count_rows, head_dim = queries.shape
     span = pages.shape[1]
-    flops = 4 * rows * steps * count * (span + entries.shape[2]) * head_dim
+    flops = 4 * rows * chunks * count_rows * (span + entries.shape[2]) * head_dim
+    block = lambda *shape: pl.BlockSpec((1,) + shape, lambda r, n: (r,) + (0,) * len(shape))
     return pl.pallas_call(
         attend_kernel,
         grid_spec=pltpu.PrefetchScalarGridSpec(
             num_scalar_prefetch=1,
             grid=(rows,),
             in_specs=[
-                pl.BlockSpec((1, steps, count, head_dim), lambda r, b: (r, 0, 0, 0)),
-                pl.BlockSpec((1, span, pages.shape[2]), lambda r, b: (r, 0, 0)),
-                pl.BlockSpec((1,) + entries.shape[1:], lambda r, b: (r, 0, 0, 0)),
-                pl.BlockSpec(pick.shape, lambda r, b: (0, 0, 0)),
+                block(chunks, count_rows, head_dim),
+                block(chunks, count_rows, 1),
+                block(chunks, count_rows, 1),
+                block(span, pages.shape[2]),
+                block(*entries.shape[1:]),
+                block(*pick.shape[1:]),
             ],
-            out_specs=pl.BlockSpec((1, steps, count, head_dim), lambda r, b: (r, 0, 0, 0)),
+            out_specs=block(chunks, count_rows, head_dim),
         ),
         out_shape=jax.ShapeDtypeStruct(queries.shape, jnp.bfloat16),
         cost_estimate=pl.CostEstimate(
-            flops=flops,
-            transcendentals=rows * steps * count * span,
-            bytes_accessed=pages.size * 2 + queries.size * 4 + entries.size * 2,
+            flops=flops // 3,
+            transcendentals=rows * chunks * count_rows * span // 3,
+            bytes_accessed=pages.size * 2 + queries.size * 4 + entries.size * 2 + pick.size * 4,
         ),
-    )(bounds, queries, pages, entries, pick)
+    )(count, queries, lo, hi, pages, entries, pick)
 
 
 def on_device(
@@ -196,19 +204,40 @@
     base = first_page * PAGE
     lo = length[:, None] + step_ids[None, :] - WINDOW - base[:, None]
     hi = jnp.broadcast_to((length - base)[:, None], (rows, steps))
-    bounds = jnp.stack([lo, hi], axis=-1).reshape(rows * steps * 2)
-    by_row = jnp.transpose(queries, (2, 1, 0, 3, 4)).reshape(rows, steps, BEAMS * heads, head_dim)
-    entries_by_row = jnp.transpose(listed, (3, 0, 1, 2, 4)).reshape(
-        rows, steps, steps * BEAMS, 2 * head_dim
-    )
-    row_beam = jnp.arange(BEAMS * heads, dtype=jnp.int32) // heads
+    pairs = steps * BEAMS
+    held_by_row = jnp.transpose(held, (2, 1, 0)).reshape(rows, pairs)
+    pair_ids = jnp.arange(pairs, dtype=jnp.int32)
+    order = jnp.argsort(jnp.where(held_by_row, pair_ids[None, :], pair_ids[None, :] + pairs), axis=1)
+    place = jnp.argsort(order, axis=1)
+    count = (jnp.sum(held_by_row.astype(jnp.int32), axis=1) + BEAMS - 1) // BEAMS
+    pair_step = order // BEAMS
+    q_by = jnp.transpose(queries, (2, 1, 0, 3, 4)).reshape(rows, pairs, heads * head_dim)
+    q_c = jnp.take_along_axis(q_by, order[:, :, None], axis=1).reshape(
+        rows, steps, BEAMS * heads, head_dim
+    )
+    lo_c = jnp.take_along_axis(lo, pair_step, axis=1)
+    hi_c = jnp.take_along_axis(hi, pair_step, axis=1)
+    lo_c = jnp.broadcast_to(lo_c[:, :, None], (rows, pairs, heads)).reshape(rows, steps, BEAMS * heads, 1)
+    hi_c = jnp.broadcast_to(hi_c[:, :, None], (rows, pairs, heads)).reshape(rows, steps, BEAMS * heads, 1)
+    entries_by = jnp.transpose(listed, (3, 0, 2, 1, 4)).reshape(rows, pairs, steps, 2 * head_dim)
+    entries_c = jnp.take_along_axis(entries_by, order[:, :, None, None], axis=1)
+    entries_c = jnp.transpose(
+        entries_c.reshape(rows, steps, BEAMS, steps, 2 * head_dim), (0, 1, 3, 2, 4)
+    ).reshape(rows, steps, steps * BEAMS, 2 * head_dim)
+    slot_in_chunk = pair_ids % BEAMS
     column = jnp.arange(steps * BEAMS, dtype=jnp.int32)
     pick = (
-        (column[None, None, :] % BEAMS == row_beam[None, :, None])
-        & (column[None, None, :] // BEAMS <= step_ids[:, None, None])
-    ).astype(jnp.float32)
-    attended = attend(bounds, by_row, pages, entries_by_row, pick)
-    attended = jnp.transpose(attended.reshape(rows, steps, BEAMS, qwidth), (2, 1, 0, 3))
+        (column[None, None, None, :] % BEAMS == slot_in_chunk[None, :, None, None])
+        & (column[None, None, None, :] // BEAMS <= pair_step[:, :, None, None])
+    )
+    pick = jnp.broadcast_to(pick, (rows, pairs, heads, steps * BEAMS)).astype(jnp.float32).reshape(
+        rows, steps, BEAMS * heads, steps * BEAMS
+    )
+    out_c = attend(count, q_c, lo_c, hi_c, pages, entries_c, pick).reshape(rows, pairs, qwidth)
+    attended = jnp.take_along_axis(out_c, place[:, :, None], axis=1).reshape(
+        rows, steps, BEAMS, qwidth
+    )
+    attended = jnp.transpose(attended, (2, 1, 0, 3))
     attended = jnp.where(held[..., None], attended, jnp.zeros_like(attended))
 
     received = lax.all_to_all(attended, HALF, split_axis=0, concat_axis=0, tiled=True)

time: 155 us -> 168 us (1.084)
  local copies, waits for them, and re-layouts: 26.4 us -> 45.8 us
  Pallas kernels: 22.6 us -> 11.8 us
  blocking collectives: 14 us -> 18.1 us
  waiting for transfers between devices: 50.6 us -> 48 us
  other arithmetic: 6.08 us -> 8.46 us
    gather x0 -> x18, local copies, waits for them, and re-layouts: none -> 14.2 us  [the longest x3 3.68 us: on_device(): jnp.take_along_axis(q_by, order[:, :, None], axis=1)]
    pallas_call x1, Pallas kernels: 22.6 us -> 11.8 us  [attend(): pl.pallas_call(attend_kernel, grid_spec=pltpu.PrefetchScalarGridSpec(num_...]
    reshape x3 -> x6, local copies, waits for them, and re-layouts: 3.66 us -> 8.96 us  [the longest x1 2 us: on_device(): attend(count, q_c, lo_c, hi_c, pages, entries_c, pick)]
    all_to_all x1, blocking collectives: 14 us -> 18.1 us  [on_device(): lax.all_to_all(attended, HALF, split_axis=0, concat_axis=0, tiled=True)]
    all_to_all x1, waiting for transfers between devices: 3.69 us -> 0.68 us  [on_device(): lax.all_to_all(jnp.broadcast_to(packed[None], (BEAMS,) + packed.shape), H...]
    all_to_all x1, waiting for transfers between devices: 19.9 us -> 22.4 us  [on_device(): lax.all_to_all(jnp.broadcast_to(mlp_own[None], (kv_count,) + mlp_own.shap...]
    all_to_all x1, waiting for transfers between devices: 2.21 us -> 0.01 us  [on_device(): lax.all_to_all(outgoing, 'req', split_axis=1, concat_axis=1, tiled=True)]
  transfers between devices with their start and end apart: 4 -> 4, of which waited for: 4 -> 3; matrix products, arithmetic and copies ran while one was open for 8% -> 13% of each run, Pallas kernels for 0% -> 0%
where the time goes in v11:
time: 168 us; the launch traced here: 167 us
  waiting for transfers between devices  48 us (29%)
  local copies, waits for them, and re-layouts  45.8 us (27%)
  starting transfers between devices  25.1 us (15%)
  blocking collectives  18.1 us (11%)
  Pallas kernels  11.8 us (7%)
  matrix products  9.33 us (6%)
  other arithmetic  8.46 us (5%)
    all_to_all x1, waiting for transfers between devices, on_device(): lax.all_to_all(leaving, KV + ('req',), 0, 0, tiled=True)  24.9 us
    all_to_all x1, waiting for transfers between devices, on_device(): lax.all_to_all(jnp.broadcast_to(mlp_own[None], (kv_count,) + mlp_own.shap...  22.4 us
    all_to_all x1, blocking collectives, on_device(): lax.all_to_all(attended, HALF, split_axis=0, concat_axis=0, tiled=True)  18.1 us
    pallas_call x1, Pallas kernels, attend(): pl.pallas_call(attend_kernel, grid_spec=pltpu.PrefetchScalarGridSpec(num_...  11.8 us
    all_to_all x1, starting transfers between devices, on_device(): lax.all_to_all(leaving, KV + ('req',), 0, 0, tiled=True)  8.01 us
    gather x1, local copies, waits for them, and re-layouts, on_device(): pool[table[offset_of] - device * pool.shape[0]]  7.82 us
    all_to_all x1, starting transfers between devices, on_device(): lax.all_to_all(outgoing, 'req', split_axis=1, concat_axis=1, tiled=True)  5.8 us
    all_to_all x1, starting transfers between devices, on_device(): lax.all_to_all(jnp.broadcast_to(mlp_own[None], (kv_count,) + mlp_own.shap...  5.77 us
  transfers between devices with their start and end apart: 4, of which 3 were waited for; matrix products, arithmetic and copies ran while one was open for 13% of the time, Pallas kernels for 0%

profile of v11, /device:TPU:1, one launch (start us, length us, event | category | flops | bytes accessed | tf_op | source)
XLA Modules:
  0.0 167.2 jit_solution(8167081353967908874)
XLA Ops:
  5.4 1.7 %gather_fusion = bf16[8,4,1536]{2,0,1:T(8,128)(2,1)S(1)} fusion(bf16[4,8,1536]{2,1,0:T(8,128)(2,1)} %param.18, s32[1024]{0:T(1024)S(1)} %pad_clamp_fusion.3), kind=kCustom, calls=%fused_computation.4 | custom fusion | bytes 196640 | tf_op jit(solution)/shard_map/gather | solution.py:157
  7.9 5.8 %all-to-all-start = ((bf16[4,8,1,1536]{3,0,2,1:T(4,128)(2,1)}), bf16[4,8,1,1536]{3,0,2,1:T(4,128)(2,1)S(1)}, u32[]{:S(2)}, u32[]{:S(2)}) async-start(bf16[4,8,1,1536]{3,0,2,1:T(4,128)(2,1)} %copy.159), calls=%async_computation | async-start | bytes 196608 | tf_op jit(solution)/shard_map/all_to_all | solution.py:158
  17.7 1.4 gather_fusion.9
  19.3 1.4 gather_fusion.8
  21.5 3.4 %convolution_convert_fusion.1 = bf16[32,1536]{1,0:T(8,128)(2,1)S(1)} fusion(bf16[1536,1536]{1,0:T(8,128)(2,1)} %param.25, f32[4,8,1,1536]{3,0,2,1:T(4,128)S(1)} %convert_element_type.116, f32[1536]{0:T(1024)S(1)} %copy-done.4, f32[32]{0:T(128)S(1)} %rsqrt.23), kind=kOutput, calls=%fused_computation.15 | convolution fusion | flops 151191552 | bytes 5019776 | tf_op jit(solution)/shard_map/dot_general | solution.py:169
  26.2 5.5 %all-to-all-start.1 = ((bf16[8,4,8,1792]{3,2,1,0:T(8,128)(2,1)}), bf16[8,4,8,1792]{3,2,1,0:T(8,128)(2,1)S(1)}, u32[]{:S(2)}, u32[]{:S(2)}) async-start(bf16[8,4,8,1792]{3,2,1,0:T(8,128)(2,1)} %broadcast_in_dim.401), calls=%async_computation.1 | async-start | bytes 1835008 | tf_op jit(solution)/shard_map/all_to_all | solution.py:172
  32.4 1.5 copy.186.pick_ref
  34.1 1.6 reshape.636.lo_ref
  35.9 1.6 reshape.637.hi_ref
  37.8 7.8 %gather_fusion.5 = bf16[72,128,256]{2,1,0:T(8,128)(2,1)} fusion(bf16[72,128,256]{2,1,0:T(8,128)(2,1)} %param.23, s32[1024]{0:T(1024)S(1)} %pad_clamp_fusion), kind=kCustom, calls=%fused_computation.9 | custom fusion | bytes 9437472 | tf_op jit(solution)/shard_map/gather | solution.py:201
  48.0 2.3 %gather_fusion.6 = bf16[256,4,256]{2,1,0:T(4,128)(2,1)} fusion(bf16[8,32,4,256]{3,2,1,0:T(4,128)(2,1)S(1)} %copy.181, s32[256]{0:T(256)S(1)} %reshape.593), kind=kCustom, calls=%fused_computation.10 | custom fusion | bytes 1050624 | tf_op jit(solution)/shard_map/jit(take_along_axis)/gather | solution.py:223
  51.9 3.5 %gather_fusion.7 = bf16[256,1536]{1,0:T(8,128)(2,1)S(1)} fusion(bf16[8,32,1536]{2,1,0:T(8,128)(2,1)S(1)} %bitcast.152, s32[256]{0:T(256)S(1)} %reshape.618), kind=kCustom, calls=%fused_computation.clone | custom fusion | bytes 1574912 | tf_op jit(solution)/shard_map/jit(take_along_axis)/gather | solution.py:215
  55.6 1.8 %reshape.504.q_ref = bf16[8,4,96,128]{3,2,1,0:T(8,128)(2,1)} reshape(bf16[8,32,1536]{2,1,0:T(8,128)(2,1)S(1)} %broadcast_select_fusion) | data formatting | bytes 1572864 | tf_op jit(solution)/shard_map/reshape | solution.py:215
  58.4 11.8 %shard_map.136 = bf16[8,4,96,128]{3,2,1,0:T(8,128)(2,1)} custom-call(s32[8]{0:T(128)} %get-tuple-element.61.count_ref, bf16[8,4,96,128]{3,2,1,0:T(8,128)(2,1)} %reshape.504.q_ref, s32[8,4,96,1]{3,2,1,0:T(8,128)} %reshape.636.lo_ref, s32[8,4,96,1]{3,2,1,0:T(8,128)} %reshape.637.hi_ref, bf16[8,1152,256]{2,1,0:T(8,128)(2,1)} %bitcast.153, ...), custom_call_target="tpu_custom_call" | custom-call | flops 620756992 | bytes 7208960 | tf_op jit(solution)/shard_map/pallas_call | solution.py:91
  70.2 2.0 %reshape.512 = bf16[8,32,1536]{2,1,0:T(8,128)(2,1)S(1)} reshape(bf16[8,4,96,128]{3,2,1,0:T(8,128)(2,1)} %shard_map.136) | data formatting | bytes 1572864 | tf_op jit(solution)/shard_map/reshape | solution.py:236
  72.2 3.5 %gather_fusion.10 = bf16[256,1536]{1,0:T(8,128)(2,1)S(1)} fusion(bf16[8,32,1536]{2,1,0:T(8,128)(2,1)S(1)} %reshape.512, s32[256]{0:T(256)S(1)} %reshape.632), kind=kCustom, calls=%fused_computation.2.clone | custom fusion | bytes 1574912 | tf_op jit(solution)/shard_map/jit(take_along_axis)/gather | solution.py:237
  76.3 18.1 %all_to_all.29 = bf16[8,4,8,1536]{3,1,2,0:T(4,128)(2,1)S(1)} all-to-all(bf16[8,4,8,1536]{3,1,2,0:T(4,128)(2,1)S(1)} %copy.188), channel_id=1, replica_groups=mesh['req'=8,'y'=4,'zhi'=2,'zlo'=2] {'y','zlo'}, dimensions={0} | all-to-all | bytes 1572864 | tf_op jit(solution)/shard_map/all_to_all | solution.py:243
  94.9 3.3 %multiply_reduce_fusion = (f32[8,4]{0,1:T(4,128)S(1)}, bf16[8,4,1536]{2,0,1:T(8,128)(2,1)S(1)}) fusion(bf16[1536,1536]{1,0:T(8,128)(2,1)} %param.27, bf16[4,8,1536]{2,0,1:T(4,128)(2,1)S(1)} %reduce_sum.312, f32[4,8,1,1536]{3,0,2,1:T(4,128)S(1)} %convert_element_type.116), kind=kOutput, calls=%fused_computation.57 | convolution fusion | flops 151240672 | bytes 5111936 | tf_op jit(solution)/shard_map/dot_general | solution.py:249
  98.6 1.3 broadcast_in_dim.436
  99.9 5.8 %all-to-all-start.3 = ((bf16[16,32,1536]{2,1,0:T(8,128)(2,1)}), bf16[16,32,1536]{2,1,0:T(8,128)(2,1)S(1)}, u32[]{:S(2)}, u32[]{:S(2)}) async-start(bf16[16,32,1536]{2,1,0:T(8,128)(2,1)} %broadcast_in_dim.436), calls=%async_computation.3 | async-start | bytes 3145728 | tf_op jit(solution)/shard_map/all_to_all | solution.py:253
  105.7 22.4 %all-to-all-done.3 = bf16[16,32,1536]{2,1,0:T(8,128)(2,1)S(1)} async-done(((bf16[16,32,1536]{2,1,0:T(8,128)(2,1)}), bf16[16,32,1536]{2,1,0:T(8,128)(2,1)S(1)}, u32[]{:S(2)}, u32[]{:S(2)}) %all-to-all-start.3) | async-done | bytes 1572896 | tf_op jit(solution)/shard_map/all_to_all | solution.py:253
  131.4 1.4 all_to_all.22
  132.8 8.0 %all-to-all-start.4 = ((bf16[128,4,1536]{2,1,0:T(4,128)(2,1)}), bf16[128,4,1536]{2,1,0:T(4,128)(2,1)S(1)}, u32[]{:S(2)}, u32[]{:S(2)}) async-start(bf16[128,4,1536]{2,1,0:T(4,128)(2,1)} %all_to_all.22), calls=%async_computation.4 | async-start | bytes 3145728 | tf_op jit(solution)/shard_map/all_to_all | solution.py:271
  140.8 24.9 %all-to-all-done.4 = bf16[128,4,1536]{2,1,0:T(4,128)(2,1)S(1)} async-done(((bf16[128,4,1536]{2,1,0:T(4,128)(2,1)}), bf16[128,4,1536]{2,1,0:T(4,128)(2,1)S(1)}, u32[]{:S(2)}, u32[]{:S(2)}) %all-to-all-start.4) | async-done | bytes 1572896 | tf_op jit(solution)/shard_map/all_to_all | solution.py:271
  (143 shorter events, 24.7 us)
Async XLA Ops:
  0.0 128.1 %copy-start = (bf16[1536,288]{0,1:T(8,128)(2,1)S(1)}, bf16[1536,288]{0,1:T(8,128)(2,1)}, u32[]{:S(2)}) copy-start(bf16[1536,288]{0,1:T(8,128)(2,1)} %param.29) | copy-start | bytes 2654212
  0.0 15.4 %copy-start.3 = (s32[8,9]{1,0:T(8,128)S(1)}, s32[8,9]{1,0:T(8,128)}, u32[]{:S(2)}) copy-start(s32[8,9]{1,0:T(8,128)} %param.22) | copy-start | bytes 868
  0.0 17.0 %copy-start.1 = (s32[128]{0:T(128)S(1)}, s32[128]{0:T(128)}, u32[]{:S(2)}) copy-start(s32[128]{0:T(128)} %param.19) | copy-start | bytes 1540
  7.9 13.3 %all-to-all-start = ((bf16[4,8,1,1536]{3,0,2,1:T(4,128)(2,1)}), bf16[4,8,1,1536]{3,0,2,1:T(4,128)(2,1)S(1)}, u32[]{:S(2)}, u32[]{:S(2)}) async-start(bf16[4,8,1,1536]{3,0,2,1:T(4,128)(2,1)} %copy.159), calls=%async_computation | async-start | bytes 196608 | tf_op jit(solution)/shard_map/all_to_all | solution.py:158
  19.3 2.2 %copy-start.4 = (f32[1536]{0:T(1024)S(1)}, f32[1536]{0:T(1024)}, u32[]{:S(2)}) copy-start(f32[1536]{0:T(1024)} %param.24) | copy-start | bytes 18436
  21.5 3.4 %copy-start.2 = (bf16[1536,256]{1,0:T(8,128)(2,1)S(1)}, bf16[1536,256]{1,0:T(8,128)(2,1)}, u32[]{:S(2)}) copy-start(bf16[1536,256]{1,0:T(8,128)(2,1)} %param.26) | copy-start | bytes 2359300
  26.2 20.2 %all-to-all-start.1 = ((bf16[8,4,8,1792]{3,2,1,0:T(8,128)(2,1)}), bf16[8,4,8,1792]{3,2,1,0:T(8,128)(2,1)S(1)}, u32[]{:S(2)}, u32[]{:S(2)}) async-start(bf16[8,4,8,1792]{3,2,1,0:T(8,128)(2,1)} %broadcast_in_dim.401), calls=%async_computation.1 | async-start | bytes 1835008 | tf_op jit(solution)/shard_map/all_to_all | solution.py:172
  94.8 3.6 %copy-start.5 = (f32[1536]{0:T(1024)S(1)}, f32[1536]{0:T(1024)}, u32[]{:S(2)}) copy-start(f32[1536]{0:T(1024)} %param.28) | copy-start | bytes 18436
  99.9 28.2 %all-to-all-start.3 = ((bf16[16,32,1536]{2,1,0:T(8,128)(2,1)}), bf16[16,32,1536]{2,1,0:T(8,128)(2,1)S(1)}, u32[]{:S(2)}, u32[]{:S(2)}) async-start(bf16[16,32,1536]{2,1,0:T(8,128)(2,1)} %broadcast_in_dim.436), calls=%async_computation.3 | async-start | bytes 3145728 | tf_op jit(solution)/shard_map/all_to_all | solution.py:253
  128.1 1.2 copy-start.6
  129.3 1.2 copy-start.7
  132.8 32.9 %all-to-all-start.4 = ((bf16[128,4,1536]{2,1,0:T(4,128)(2,1)}), bf16[128,4,1536]{2,1,0:T(4,128)(2,1)S(1)}, u32[]{:S(2)}, u32[]{:S(2)}) async-start(bf16[128,4,1536]{2,1,0:T(4,128)(2,1)} %all_to_all.22), calls=%async_computation.4 | async-start | bytes 3145728 | tf_op jit(solution)/shard_map/all_to_all | solution.py:271

commit v12 on v8

--- a/solution.py
+++ b/solution.py
@@ -41,7 +41,7 @@
     return jnp.sum(jnp.where(picks[..., None], table[None, :, :, :], 0), axis=1).astype(table.dtype)
 
 
-def attend_kernel(bounds_ref, q_ref, kv_ref, new_ref, pick_ref, out_ref):
+def attend_kernel(bounds_ref, used_ref, q_ref, kv_ref, new_ref, pick_ref, out_ref):
     r = pl.program_id(0)
     steps = q_ref.shape[1]
     head_dim = q_ref.shape[3]
@@ -51,49 +51,56 @@
     pos = lax.broadcasted_iota(jnp.int32, (1, kv_ref.shape[1]), 1)
     contract = (((1,), (1,)), ((), ()))
     for t in range(steps):
-        lo = bounds_ref[(r * steps + t) * 2]
-        hi = bounds_ref[(r * steps + t) * 2 + 1]
-        query = q_ref[0, t]
-        scores = lax.dot_general(query, keys, contract, preferred_element_type=jnp.float32) * scale
-        allowed = (pos > lo) & (pos < hi)
-        scores = jnp.where(allowed, scores, NEGATIVE)
-        high_c = jnp.max(scores, axis=1, keepdims=True)
-        weights = jnp.exp(scores - high_c).astype(jnp.bfloat16)
-        total_c = jnp.sum(weights.astype(jnp.float32), axis=1, keepdims=True)
-        sum_c = jnp.dot(weights, values, preferred_element_type=jnp.float32)
-        entries = new_ref[0, t]
-        fresh = lax.dot_general(
-            query, entries[:, :head_dim], contract, preferred_element_type=jnp.float32
-        ) * scale
-        fresh = jnp.where(pick_ref[t] > 0, fresh, NEGATIVE)
-        high_n = jnp.max(fresh, axis=1, keepdims=True)
-        fresh_w = jnp.exp(fresh - high_n).astype(jnp.bfloat16)
-        total_n = jnp.sum(fresh_w.astype(jnp.float32), axis=1, keepdims=True)
-        sum_n = jnp.dot(fresh_w, entries[:, head_dim:], preferred_element_type=jnp.float32)
-        highest = jnp.maximum(high_c, high_n)
-        scale_c = jnp.exp(high_c - highest)
-        scale_n = jnp.exp(high_n - highest)
-        totals = total_c * scale_c + total_n * scale_n
-        weighted = sum_c * scale_c + sum_n * scale_n
-        out_ref[0, t] = (weighted / totals).astype(out_ref.dtype)
-
-
-def attend(bounds, queries, pages, entries, pick):
+
+        @pl.when(used_ref[r * steps + t] != 0)
+        def _(t=t):
+            lo = bounds_ref[(r * steps + t) * 2]
+            hi = bounds_ref[(r * steps + t) * 2 + 1]
+            query = q_ref[0, t]
+            scores = lax.dot_general(query, keys, contract, preferred_element_type=jnp.float32) * scale
+            allowed = (pos > lo) & (pos < hi)
+            scores = jnp.where(allowed, scores, NEGATIVE)
+            high_c = jnp.max(scores, axis=1, keepdims=True)
+            weights = jnp.exp(scores - high_c).astype(jnp.bfloat16)
+            total_c = jnp.sum(weights.astype(jnp.float32), axis=1, keepdims=True)
+            sum_c = jnp.dot(weights, values, preferred_element_type=jnp.float32)
+            entries = new_ref[0, t]
+            fresh = lax.dot_general(
+                query, entries[:, :head_dim], contract, preferred_element_type=jnp.float32
+            ) * scale
+            fresh = jnp.where(pick_ref[t] > 0, fresh, NEGATIVE)
+            high_n = jnp.max(fresh, axis=1, keepdims=True)
+            fresh_w = jnp.exp(fresh - high_n).astype(jnp.bfloat16)
+            total_n = jnp.sum(fresh_w.astype(jnp.float32), axis=1, keepdims=True)
+            sum_n = jnp.dot(fresh_w, entries[:, head_dim:], preferred_element_type=jnp.float32)
+            highest = jnp.maximum(high_c, high_n)
+            scale_c = jnp.exp(high_c - highest)
+            scale_n = jnp.exp(high_n - highest)
+            totals = total_c * scale_c + total_n * scale_n
+            weighted = sum_c * scale_c + sum_n * scale_n
+            out_ref[0, t] = (weighted / totals).astype(out_ref.dtype)
+
+        @pl.when(used_ref[r * steps + t] == 0)
+        def _(t=t):
+            out_ref[0, t] = jnp.zeros(out_ref.shape[2:], out_ref.dtype)
+
+
+def attend(bounds, used, queries, pages, entries, pick):
     rows, steps, count, head_dim = queries.shape
     span = pages.shape[1]
     flops = 4 * rows * steps * count * (span + entries.shape[2]) * head_dim
     return pl.pallas_call(
         attend_kernel,
         grid_spec=pltpu.PrefetchScalarGridSpec(
-            num_scalar_prefetch=1,
+            num_scalar_prefetch=2,
             grid=(rows,),
             in_specs=[
-                pl.BlockSpec((1, steps, count, head_dim), lambda r, b: (r, 0, 0, 0)),
-                pl.BlockSpec((1, span, pages.shape[2]), lambda r, b: (r, 0, 0)),
-                pl.BlockSpec((1,) + entries.shape[1:], lambda r, b: (r, 0, 0, 0)),
-                pl.BlockSpec(pick.shape, lambda r, b: (0, 0, 0)),
+                pl.BlockSpec((1, steps, count, head_dim), lambda r, b, u: (r, 0, 0, 0)),
+                pl.BlockSpec((1, span, pages.shape[2]), lambda r, b, u: (r, 0, 0)),
+                pl.BlockSpec((1,) + entries.shape[1:], lambda r, b, u: (r, 0, 0, 0)),
+                pl.BlockSpec(pick.shape, lambda r, b, u: (0, 0, 0)),
             ],
-            out_specs=pl.BlockSpec((1, steps, count, head_dim), lambda r, b: (r, 0, 0, 0)),
+            out_specs=pl.BlockSpec((1, steps, count, head_dim), lambda r, b, u: (r, 0, 0, 0)),
         ),
         out_shape=jax.ShapeDtypeStruct(queries.shape, jnp.bfloat16),
         cost_estimate=pl.CostEstimate(
@@ -101,7 +108,7 @@
             transcendentals=rows * steps * count * span,
             bytes_accessed=pages.size * 2 + queries.size * 4 + entries.size * 2,
         ),
-    )(bounds, queries, pages, entries, pick)
+    )(bounds, used, queries, pages, entries, pick)
 
 
 def on_device(
@@ -207,7 +214,8 @@
         (column[None, None, :] % BEAMS == row_beam[None, :, None])
         & (column[None, None, :] // BEAMS <= step_ids[:, None, None])
     ).astype(jnp.float32)
-    attended = attend(bounds, by_row, pages, entries_by_row, pick)
+    used = jnp.any(held, axis=0).T.astype(jnp.int32).reshape(rows * steps)
+    attended = attend(bounds, used, by_row, pages, entries_by_row, pick)
     attended = jnp.transpose(attended.reshape(rows, steps, BEAMS, qwidth), (2, 1, 0, 3))
     attended = jnp.where(held[..., None], attended, jnp.zeros_like(attended))
 

time: 155 us -> 155 us (level)
  starting transfers between devices: 25.3 us -> 29.5 us
  waiting for transfers between devices: 50.6 us -> 49 us
  blocking collectives: 14 us -> 12.4 us
    all_to_all x1, starting transfers between devices: 8.31 us -> 12.8 us  [on_device(): lax.all_to_all(leaving, KV + ('req',), 0, 0, tiled=True)]
    all_to_all x1, blocking collectives: 14 us -> 12.4 us  [on_device(): lax.all_to_all(attended, HALF, split_axis=0, concat_axis=0, tiled=True)]
where the time goes in v12:
time: 155 us
  waiting for transfers between devices  49 us (32%)
  starting transfers between devices  29.5 us (19%)
  local copies, waits for them, and re-layouts  27 us (17%)
  Pallas kernels  21.5 us (14%)
  blocking collectives  12.4 us (8%)
  matrix products  9.32 us (6%)
  other arithmetic  6.1 us (4%)
    all_to_all x1, waiting for transfers between devices, on_device(): lax.all_to_all(leaving, KV + ('req',), 0, 0, tiled=True)  24.9 us
    pallas_call x1, Pallas kernels, attend(): pl.pallas_call(attend_kernel, grid_spec=pltpu.PrefetchScalarGridSpec(num_...  21.5 us
    all_to_all x1, waiting for transfers between devices, on_device(): lax.all_to_all(jnp.broadcast_to(mlp_own[None], (kv_count,) + mlp_own.shap...  18.9 us
    all_to_all x1, starting transfers between devices, on_device(): lax.all_to_all(leaving, KV + ('req',), 0, 0, tiled=True)  12.8 us
    all_to_all x1, blocking collectives, on_device(): lax.all_to_all(attended, HALF, split_axis=0, concat_axis=0, tiled=True)  12.4 us
    gather x1, local copies, waits for them, and re-layouts, on_device(): pool[table[offset_of] - device * pool.shape[0]]  7.82 us
    all_to_all x1, starting transfers between devices, on_device(): lax.all_to_all(outgoing, 'req', split_axis=1, concat_axis=1, tiled=True)  5.8 us
    all_to_all x1, starting transfers between devices, on_device(): lax.all_to_all(jnp.broadcast_to(packed[None], (BEAMS,) + packed.shape), H...  5.55 us
  transfers between devices with their start and end apart: 4, of which 4 were waited for; matrix products, arithmetic and copies ran while one was open for 8% of the time, Pallas kernels for 0%

profile of v12, /device:TPU:1, one launch (start us, length us, event | category | flops | bytes accessed | tf_op | source)
XLA Modules:
  0.0 155.3 jit_solution(5376313012792240071)
XLA Ops:
  2.6 1.3 gather_fusion.3
  3.9 1.0 sort.17
  4.9 1.7 %gather_fusion = bf16[8,4,1536]{2,0,1:T(8,128)(2,1)S(1)} fusion(bf16[4,8,1536]{2,1,0:T(8,128)(2,1)} %param.14, s32[1024]{0:T(1024)S(1)} %pad_clamp_fusion.3), kind=kCustom, calls=%fused_computation | custom fusion | bytes 196640 | tf_op jit(solution)/shard_map/gather | solution.py:156
  7.4 5.8 %all-to-all-start = ((bf16[4,8,1,1536]{3,0,2,1:T(4,128)(2,1)}), bf16[4,8,1,1536]{3,0,2,1:T(4,128)(2,1)S(1)}, u32[]{:S(2)}, u32[]{:S(2)}) async-start(bf16[4,8,1,1536]{3,0,2,1:T(4,128)(2,1)} %copy.96), calls=%async_computation | async-start | bytes 196608 | tf_op jit(solution)/shard_map/all_to_all | solution.py:157
  16.0 2.2 %all-to-all-done = bf16[4,8,1,1536]{3,0,2,1:T(4,128)(2,1)S(1)} async-done(((bf16[4,8,1,1536]{3,0,2,1:T(4,128)(2,1)}), bf16[4,8,1,1536]{3,0,2,1:T(4,128)(2,1)S(1)}, u32[]{:S(2)}, u32[]{:S(2)}) %all-to-all-start) | async-done | bytes 98336 | tf_op jit(solution)/shard_map/all_to_all | solution.py:157
  18.5 3.4 %convolution_convert_fusion.1 = bf16[32,1536]{1,0:T(8,128)(2,1)S(1)} fusion(bf16[1536,1536]{1,0:T(8,128)(2,1)} %param.21, f32[4,8,1,1536]{3,0,2,1:T(4,128)S(1)} %convert_element_type.115, f32[1536]{0:T(1024)S(1)} %copy-done.3, f32[32]{0:T(128)S(1)} %rsqrt.23), kind=kOutput, calls=%fused_computation.10 | convolution fusion | flops 151191552 | bytes 5019776 | tf_op jit(solution)/shard_map/dot_general | solution.py:168
  22.2 1.0 broadcast_in_dim.335
  23.2 5.5 %all-to-all-start.1 = ((bf16[8,4,8,1792]{3,2,1,0:T(8,128)(2,1)}), bf16[8,4,8,1792]{3,2,1,0:T(8,128)(2,1)S(1)}, u32[]{:S(2)}, u32[]{:S(2)}) async-start(bf16[8,4,8,1792]{3,2,1,0:T(8,128)(2,1)} %broadcast_in_dim.335), calls=%async_computation.1 | async-start | bytes 1835008 | tf_op jit(solution)/shard_map/all_to_all | solution.py:171
  30.4 7.8 %gather_fusion.5 = bf16[72,128,256]{2,1,0:T(8,128)(2,1)} fusion(bf16[72,128,256]{2,1,0:T(8,128)(2,1)} %param.19, s32[1024]{0:T(1024)S(1)} %pad_clamp_fusion), kind=kCustom, calls=%fused_computation.5 | custom fusion | bytes 9437472 | tf_op jit(solution)/shard_map/gather | solution.py:200
  38.9 3.0 %all-to-all-done.1 = bf16[8,4,8,1792]{3,2,1,0:T(8,128)(2,1)S(1)} async-done(((bf16[8,4,8,1792]{3,2,1,0:T(8,128)(2,1)}), bf16[8,4,8,1792]{3,2,1,0:T(8,128)(2,1)S(1)}, u32[]{:S(2)}, u32[]{:S(2)}) %all-to-all-start.1) | async-done | bytes 917536 | tf_op jit(solution)/shard_map/all_to_all | solution.py:171
  43.0 0.9 copy.130
  44.1 1.0 copy.109.q_ref
  45.1 21.5 %shard_map.136 = bf16[8,4,96,128]{3,2,1,0:T(8,128)(2,1)} custom-call(s32[64]{0:T(128)} %reshape.517.bounds_ref, s32[32]{0:T(128)} %reshape.531.used_ref, bf16[8,4,96,128]{3,2,1,0:T(8,128)(2,1)} %copy.109.q_ref, bf16[8,1152,256]{2,1,0:T(8,128)(2,1)} %bitcast.105, bf16[8,4,32,256]{3,2,1,0:T(8,128)(2,1)} %bitcast.108, f32[4,96,32]{2,1,0:T(8,128)} %and_convert_fusion.pick_ref), custom_call_target="tpu_custom_call" | custom-call | flops 1862270976 | bytes 6815744 | tf_op jit(solution)/shard_map/pallas_call | solution.py:92
  66.6 2.0 %reshape.524 = bf16[8,4,8,1536]{3,2,1,0:T(8,128)(2,1)S(1)} reshape(bf16[8,4,96,128]{3,2,1,0:T(8,128)(2,1)} %shard_map.136) | data formatting | bytes 1572864 | tf_op jit(solution)/shard_map/reshape | solution.py:219
  69.3 12.4 %all_to_all.29 = bf16[8,4,8,1536]{3,1,2,0:T(4,128)(2,1)S(1)} all-to-all(bf16[8,4,8,1536]{3,1,2,0:T(4,128)(2,1)S(1)} %bitcast_select_fusion), channel_id=1, replica_groups=mesh['req'=8,'y'=4,'zhi'=2,'zlo'=2] {'y','zlo'}, dimensions={0} | all-to-all | bytes 1572864 | tf_op jit(solution)/shard_map/all_to_all | solution.py:222
  82.1 3.3 %multiply_reduce_fusion = (f32[8,4]{0,1:T(4,128)S(1)}, bf16[8,4,1536]{2,0,1:T(8,128)(2,1)S(1)}) fusion(bf16[1536,1536]{1,0:T(8,128)(2,1)} %param.23, bf16[4,8,1536]{2,0,1:T(4,128)(2,1)S(1)} %reduce_sum.302, f32[4,8,1,1536]{3,0,2,1:T(4,128)S(1)} %convert_element_type.115), kind=kOutput, calls=%fused_computation.48 | convolution fusion | flops 151240672 | bytes 5111936 | tf_op jit(solution)/shard_map/dot_general | solution.py:228
  85.8 1.3 broadcast_in_dim.359
  87.1 5.4 %all-to-all-start.3 = ((bf16[16,32,1536]{2,1,0:T(8,128)(2,1)}), bf16[16,32,1536]{2,1,0:T(8,128)(2,1)S(1)}, u32[]{:S(2)}, u32[]{:S(2)}) async-start(bf16[16,32,1536]{2,1,0:T(8,128)(2,1)} %broadcast_in_dim.359), calls=%async_computation.3 | async-start | bytes 3145728 | tf_op jit(solution)/shard_map/all_to_all | solution.py:232
  92.5 18.9 %all-to-all-done.3 = bf16[16,32,1536]{2,1,0:T(8,128)(2,1)S(1)} async-done(((bf16[16,32,1536]{2,1,0:T(8,128)(2,1)}), bf16[16,32,1536]{2,1,0:T(8,128)(2,1)S(1)}, u32[]{:S(2)}, u32[]{:S(2)}) %all-to-all-start.3) | async-done | bytes 1572896 | tf_op jit(solution)/shard_map/all_to_all | solution.py:232
  113.7 1.0 convolution_convert_fusion
  114.8 1.4 all_to_all.22
  116.1 12.8 %all-to-all-start.4 = ((bf16[128,4,1536]{2,1,0:T(4,128)(2,1)}), bf16[128,4,1536]{2,1,0:T(4,128)(2,1)S(1)}, u32[]{:S(2)}, u32[]{:S(2)}) async-start(bf16[128,4,1536]{2,1,0:T(4,128)(2,1)} %all_to_all.22), calls=%async_computation.4 | async-start | bytes 3145728 | tf_op jit(solution)/shard_map/all_to_all | solution.py:250
  128.9 24.9 %all-to-all-done.4 = bf16[128,4,1536]{2,1,0:T(4,128)(2,1)S(1)} async-done(((bf16[128,4,1536]{2,1,0:T(4,128)(2,1)}), bf16[128,4,1536]{2,1,0:T(4,128)(2,1)S(1)}, u32[]{:S(2)}, u32[]{:S(2)}) %all-to-all-start.4) | async-done | bytes 1572896 | tf_op jit(solution)/shard_map/all_to_all | solution.py:250
  154.5 0.8 select_reduce_fusion
  (102 shorter events, 14.5 us)
Async XLA Ops:
  0.0 111.4 %copy-start = (bf16[1536,288]{0,1:T(8,128)(2,1)S(1)}, bf16[1536,288]{0,1:T(8,128)(2,1)}, u32[]{:S(2)}) copy-start(bf16[1536,288]{0,1:T(8,128)(2,1)} %param.25) | copy-start | bytes 2654212
  0.0 15.0 %copy-start.2 = (s32[8,9]{1,0:T(8,128)S(1)}, s32[8,9]{1,0:T(8,128)}, u32[]{:S(2)}) copy-start(s32[8,9]{1,0:T(8,128)} %param.18) | copy-start | bytes 868
  0.0 18.5 %copy-start.3 = (f32[1536]{0:T(1024)S(1)}, f32[1536]{0:T(1024)}, u32[]{:S(2)}) copy-start(f32[1536]{0:T(1024)} %param.20) | copy-start | bytes 18436
  7.4 10.8 %all-to-all-start = ((bf16[4,8,1,1536]{3,0,2,1:T(4,128)(2,1)}), bf16[4,8,1,1536]{3,0,2,1:T(4,128)(2,1)S(1)}, u32[]{:S(2)}, u32[]{:S(2)}) async-start(bf16[4,8,1,1536]{3,0,2,1:T(4,128)(2,1)} %copy.96), calls=%async_computation | async-start | bytes 196608 | tf_op jit(solution)/shard_map/all_to_all | solution.py:157
  18.5 3.4 %copy-start.1 = (bf16[1536,256]{1,0:T(8,128)(2,1)S(1)}, bf16[1536,256]{1,0:T(8,128)(2,1)}, u32[]{:S(2)}) copy-start(bf16[1536,256]{1,0:T(8,128)(2,1)} %param.22) | copy-start | bytes 2359300
  23.2 18.8 %all-to-all-start.1 = ((bf16[8,4,8,1792]{3,2,1,0:T(8,128)(2,1)}), bf16[8,4,8,1792]{3,2,1,0:T(8,128)(2,1)S(1)}, u32[]{:S(2)}, u32[]{:S(2)}) async-start(bf16[8,4,8,1792]{3,2,1,0:T(8,128)(2,1)} %broadcast_in_dim.335), calls=%async_computation.1 | async-start | bytes 1835008 | tf_op jit(solution)/shard_map/all_to_all | solution.py:171
  82.1 3.6 %copy-start.4 = (f32[1536]{0:T(1024)S(1)}, f32[1536]{0:T(1024)}, u32[]{:S(2)}) copy-start(f32[1536]{0:T(1024)} %param.24) | copy-start | bytes 18436
  87.1 24.3 %all-to-all-start.3 = ((bf16[16,32,1536]{2,1,0:T(8,128)(2,1)}), bf16[16,32,1536]{2,1,0:T(8,128)(2,1)S(1)}, u32[]{:S(2)}, u32[]{:S(2)}) async-start(bf16[16,32,1536]{2,1,0:T(8,128)(2,1)} %broadcast_in_dim.359), calls=%async_computation.3 | async-start | bytes 3145728 | tf_op jit(solution)/shard_map/all_to_all | solution.py:232
  111.4 1.2 copy-start.5
  112.6 1.2 copy-start.6
  116.1 37.7 %all-to-all-start.4 = ((bf16[128,4,1536]{2,1,0:T(4,128)(2,1)}), bf16[128,4,1536]{2,1,0:T(4,128)(2,1)S(1)}, u32[]{:S(2)}, u32[]{:S(2)}) async-start(bf16[128,4,1536]{2,1,0:T(4,128)(2,1)} %all_to_all.22), calls=%async_computation.4 | async-start | bytes 3145728 | tf_op jit(solution)/shard_map/all_to_all | solution.py:250

commit v13 on v12

--- a/solution.py
+++ b/solution.py
@@ -151,26 +151,28 @@
         jnp.where(placed == slot_ids[None, :], jnp.arange(req_count, dtype=jnp.int32)[:, None], 0),
         axis=0,
     )
-    anchor = serving // per_group
-    send_order = jnp.argsort(target * rows + offsets)
-    outgoing = x_steps[:, send_order].reshape(steps, req_count, quota, width)
-    arrived = lax.all_to_all(outgoing, "req", split_axis=1, concat_axis=1, tiled=True).reshape(
-        steps, rows, width
-    )
     slot_req = perm.reshape(req_count, halves, rows) // (halves * rows)
     mine_req = slot_req[:, half, :][group]
     offset_of = jnp.sum(
         jnp.where(mine_req[None, :] == offsets[:, None], offsets[None, :], 0), axis=1
     )
-    inputs = arrived
-
-    normed = rms_round(inputs.reshape(steps * rows, width), norm_attn)
+
+    normed = rms_round(x_steps.reshape(steps * rows, width), norm_attn)
     query = jnp.dot(normed, w_query, preferred_element_type=jnp.float32).astype(jnp.bfloat16)
     fresh = jnp.dot(normed, w_keyval, preferred_element_type=jnp.float32).astype(jnp.bfloat16)
-    packed = jnp.concatenate([query, fresh], axis=-1).reshape(steps, rows, qwidth + 2 * head_dim)
-    mine = lax.all_to_all(
-        jnp.broadcast_to(packed[None], (BEAMS,) + packed.shape), HALF, 0, 0, tiled=True
-    )
+    packed = jnp.concatenate(
+        [x_steps.reshape(steps * rows, width), query, fresh], axis=-1
+    ).reshape(steps, rows, width + qwidth + 2 * head_dim)
+    send_slot = jnp.sum(
+        jnp.where(target[None, :] == offsets[:, None], offsets[None, :], 0), axis=1
+    )
+    sending = jnp.swapaxes(jnp.take(packed, send_slot, axis=1), 0, 1)
+    sending = jnp.broadcast_to(sending[:, None], (req_count, BEAMS) + sending.shape[1:])
+    arrived = lax.all_to_all(
+        sending.reshape((req_count * BEAMS,) + sending.shape[2:]), ("req",) + HALF, 0, 0, tiled=True
+    ).reshape((req_count, BEAMS) + sending.shape[2:])
+    inputs = jnp.swapaxes(lax.dynamic_index_in_dim(arrived, beam, 1, keepdims=False)[..., :width], 0, 1)
+    mine = jnp.transpose(arrived[..., width:], (1, 2, 0, 3))
     queries = mine[..., :qwidth].reshape(BEAMS, steps, rows, heads, head_dim)
     entries = mine[..., qwidth:]
 

time: 155 us -> 165 us (1.065); the launches traced: 155 us -> 163 us
  waiting for transfers between devices: 49 us -> 65 us
  blocking collectives: 12.4 us -> 0 us
  Pallas kernels: 21.5 us -> 13.4 us
  starting transfers between devices: 29.5 us -> 36.6 us
  local copies, waits for them, and re-layouts: 27 us -> 29.7 us
    all_to_all x2, waiting for transfers between devices: 5.23 us -> 19.7 us  [the longest x1 10.3 us: on_device(): lax.all_to_all(sending.reshape((req_count * BEAMS,) + sending.shape[2:]),...]
    all_to_all x1 -> x0, blocking collectives: 12.4 us -> none  [on_device(): lax.all_to_all(attended, HALF, split_axis=0, concat_axis=0, tiled=True)]
    all_to_all x2, starting transfers between devices: 11.3 us -> 19.8 us  [the longest x1 10.5 us: on_device(): lax.all_to_all(sending.reshape((req_count * BEAMS,) + sending.shape[2:]),...]
    pallas_call x1, Pallas kernels: 21.5 us -> 13.4 us  [attend(): pl.pallas_call(attend_kernel, grid_spec=pltpu.PrefetchScalarGridSpec(num_...]
    all_to_all x1, starting transfers between devices: 12.8 us -> 10.4 us  [on_device(): lax.all_to_all(leaving, KV + ('req',), 0, 0, tiled=True)]
    unnamed x15 -> x17, local copies, waits for them, and re-layouts: 1.01 us -> 3.02 us
    dynamic_slice x0 -> x1, local copies, waits for them, and re-layouts: none -> 1.89 us  [on_device(): lax.dynamic_index_in_dim(arrived, beam, 1, keepdims=False)[..., :width]]
  transfers between devices with their start and end apart: 4 -> 4, of which waited for: 4 -> 4; matrix products, arithmetic and copies ran while one was open for 8% -> 10% of each run, Pallas kernels for 0% -> 0%
where the time goes in v13:
time: 165 us; the launch traced here: 163 us
  waiting for transfers between devices  65 us (39%)
  starting transfers between devices  36.6 us (22%)
  local copies, waits for them, and re-layouts  29.7 us (18%)
  Pallas kernels  13.4 us (8%)
  matrix products  10.5 us (6%)
  other arithmetic  7.28 us (4%)
    all_to_all x1, waiting for transfers between devices, on_device(): lax.all_to_all(leaving, KV + ('req',), 0, 0, tiled=True)  24.9 us
    all_to_all x1, waiting for transfers between devices, on_device(): lax.all_to_all(jnp.broadcast_to(mlp_own[None], (kv_count,) + mlp_own.shap...  20.4 us
    pallas_call x1, Pallas kernels, attend(): pl.pallas_call(attend_kernel, grid_spec=pltpu.PrefetchScalarGridSpec(num_...  13.4 us
    all_to_all x1, starting transfers between devices, on_device(): lax.all_to_all(sending.reshape((req_count * BEAMS,) + sending.shape[2:]),...  10.5 us
    all_to_all x1, starting transfers between devices, on_device(): lax.all_to_all(leaving, KV + ('req',), 0, 0, tiled=True)  10.4 us
    all_to_all x1, waiting for transfers between devices, on_device(): lax.all_to_all(sending.reshape((req_count * BEAMS,) + sending.shape[2:]),...  10.3 us
    all_to_all x1, waiting for transfers between devices, on_device(): lax.all_to_all(attended, HALF, split_axis=0, concat_axis=0, tiled=True)  9.34 us
    all_to_all x1, starting transfers between devices, on_device(): lax.all_to_all(attended, HALF, split_axis=0, concat_axis=0, tiled=True)  9.32 us
  transfers between devices with their start and end apart: 4, of which 4 were waited for; matrix products, arithmetic and copies ran while one was open for 10% of the time, Pallas kernels for 0%

profile of v13, /device:TPU:1, one launch (start us, length us, event | category | flops | bytes accessed | tf_op | source)
XLA Modules:
  0.0 163.1 jit_solution(635845855506475337)
XLA Ops:
  1.6 1.0 fusion.21
  4.0 1.5 fusion.4
  5.5 3.4 %fusion.1 = bf16[4,8,1536]{2,1,0:T(8,128)(2,1)S(1)} fusion(bf16[1536,1536]{1,0:T(8,128)(2,1)} %param.21, bf16[4,8,1536]{2,1,0:T(8,128)(2,1)} %param.14, f32[1536]{0:T(1024)} %param.20, f32[32]{0:T(128)S(1)} %rsqrt.23), kind=kOutput, calls=%fused_computation.11 | convolution fusion | flops 151240704 | bytes 4921472 | tf_op jit(solution)/shard_map/dot_general | solution.py:161
  10.0 1.7 %broadcast_in_dim.346 = bf16[8,8,4,3328]{3,2,1,0:T(4,128)(2,1)} broadcast(bf16[8,4,3328]{2,1,0:T(4,128)(2,1)S(1)} %broadcast_select_fusion), dimensions={0,2,3} | broadcast | bytes 1916928 | tf_op jit(solution)/shard_map/broadcast_in_dim | solution.py:170
  11.6 10.5 %all-to-all-start = ((bf16[64,4,3328]{2,1,0:T(4,128)(2,1)}), bf16[64,4,3328]{2,1,0:T(4,128)(2,1)S(1)}, u32[]{:S(2)}, u32[]{:S(2)}) async-start(bf16[64,4,3328]{2,1,0:T(4,128)(2,1)} %bitcast.124), calls=%async_computation | async-start | bytes 3407872 | tf_op jit(solution)/shard_map/all_to_all | solution.py:171
  28.0 7.8 %gather_fusion.5 = bf16[72,128,256]{2,1,0:T(8,128)(2,1)} fusion(bf16[72,128,256]{2,1,0:T(8,128)(2,1)} %param.19, s32[1024]{0:T(1024)S(1)} %pad_clamp_fusion), kind=kCustom, calls=%fused_computation.5 | custom fusion | bytes 9437472 | tf_op jit(solution)/shard_map/gather | solution.py:202
  36.7 10.3 %all-to-all-done = bf16[64,4,3328]{2,1,0:T(4,128)(2,1)S(1)} async-done(((bf16[64,4,3328]{2,1,0:T(4,128)(2,1)}), bf16[64,4,3328]{2,1,0:T(4,128)(2,1)S(1)}, u32[]{:S(2)}, u32[]{:S(2)}) %all-to-all-start) | async-done | bytes 1703968 | tf_op jit(solution)/shard_map/all_to_all | solution.py:171
  47.4 1.0 copy-done.2
  48.7 1.0 copy.129.q_ref
  50.8 1.0 copy.152
  51.8 13.4 %shard_map.136 = bf16[8,4,96,128]{3,2,1,0:T(8,128)(2,1)} custom-call(s32[64]{0:T(128)} %reshape.550.bounds_ref, s32[32]{0:T(128)} %reshape.565.used_ref, bf16[8,4,96,128]{3,2,1,0:T(8,128)(2,1)} %copy.129.q_ref, bf16[8,1152,256]{2,1,0:T(8,128)(2,1)} %bitcast.123, bf16[8,4,32,256]{3,2,1,0:T(8,128)(2,1)} %bitcast.130, f32[4,96,32]{2,1,0:T(8,128)} %and_convert_fusion.pick_ref), custom_call_target="tpu_custom_call" | custom-call | flops 1862270976 | bytes 6815744 | tf_op jit(solution)/shard_map/pallas_call | solution.py:92
  65.2 2.0 %reshape.557 = bf16[8,4,8,1536]{3,2,1,0:T(8,128)(2,1)S(1)} reshape(bf16[8,4,96,128]{3,2,1,0:T(8,128)(2,1)} %shard_map.136) | data formatting | bytes 1572864 | tf_op jit(solution)/shard_map/reshape | solution.py:221
  67.2 1.6 bitcast_select_fusion
  68.8 9.3 %all-to-all-start.1 = ((bf16[8,4,8,1536]{3,1,2,0:T(4,128)(2,1)}), bf16[8,4,8,1536]{3,1,2,0:T(4,128)(2,1)S(1)}, u32[]{:S(2)}, u32[]{:S(2)}) async-start(bf16[8,4,8,1536]{3,1,2,0:T(4,128)(2,1)} %bitcast_select_fusion), calls=%async_computation.1 | async-start | bytes 1572864 | tf_op jit(solution)/shard_map/all_to_all | solution.py:224
  78.1 1.9 %constant_dynamic-slice_fusion.3 = bf16[8,1,4,3328]{3,1,0,2:T(2,128)(2,1)S(1)} fusion(bf16[8,8,4,3328]{3,1,0,2:T(8,128)(2,1)} %bitcast.127, s32[]{:T(128)S(6)} %select_n.248), kind=kLoop, calls=%fused_computation.143 | loop fusion | bytes 425988 | tf_op jit(solution)/shard_map/jit(dynamic_index_in_dim)/dynamic_slice | solution.py:174
  80.0 9.3 %all-to-all-done.1 = bf16[8,4,8,1536]{3,1,2,0:T(4,128)(2,1)S(1)} async-done(((bf16[8,4,8,1536]{3,1,2,0:T(4,128)(2,1)}), bf16[8,4,8,1536]{3,1,2,0:T(4,128)(2,1)S(1)}, u32[]{:S(2)}, u32[]{:S(2)}) %all-to-all-start.1) | async-done | bytes 786464 | tf_op jit(solution)/shard_map/all_to_all | solution.py:224
  89.8 3.3 %multiply_reduce_fusion = (f32[8,4]{0,1:T(4,128)S(1)}, bf16[8,4,1536]{2,0,1:T(8,128)(2,1)S(1)}) fusion(bf16[1536,1536]{1,0:T(8,128)(2,1)} %param.23, bf16[4,8,1536]{2,0,1:T(4,128)(2,1)S(1)} %reduce_sum.315, bf16[8,4,3328]{2,0,1:T(8,128)(2,1)S(1)} %bitcast.133), kind=kOutput, calls=%fused_computation.58 | convolution fusion | flops 151289824 | bytes 5013632 | tf_op jit(solution)/shard_map/dot_general | solution.py:230
  93.5 1.3 broadcast_in_dim.378
  94.8 6.3 %all-to-all-start.2 = ((bf16[16,32,1536]{2,1,0:T(8,128)(2,1)}), bf16[16,32,1536]{2,1,0:T(8,128)(2,1)S(1)}, u32[]{:S(2)}, u32[]{:S(2)}) async-start(bf16[16,32,1536]{2,1,0:T(8,128)(2,1)} %broadcast_in_dim.378), calls=%async_computation.2 | async-start | bytes 3145728 | tf_op jit(solution)/shard_map/all_to_all | solution.py:234
  101.2 20.4 %all-to-all-done.2 = bf16[16,32,1536]{2,1,0:T(8,128)(2,1)S(1)} async-done(((bf16[16,32,1536]{2,1,0:T(8,128)(2,1)}), bf16[16,32,1536]{2,1,0:T(8,128)(2,1)S(1)}, u32[]{:S(2)}, u32[]{:S(2)}) %all-to-all-start.2) | async-done | bytes 1572896 | tf_op jit(solution)/shard_map/all_to_all | solution.py:234
  123.9 1.0 convolution_convert_fusion
  124.9 1.4 all_to_all.18
  126.3 10.4 %all-to-all-start.3 = ((bf16[128,4,1536]{2,1,0:T(4,128)(2,1)}), bf16[128,4,1536]{2,1,0:T(4,128)(2,1)S(1)}, u32[]{:S(2)}, u32[]{:S(2)}) async-start(bf16[128,4,1536]{2,1,0:T(4,128)(2,1)} %all_to_all.18), calls=%async_computation.3 | async-start | bytes 3145728 | tf_op jit(solution)/shard_map/all_to_all | solution.py:252
  136.8 24.9 %all-to-all-done.3 = bf16[128,4,1536]{2,1,0:T(4,128)(2,1)S(1)} async-done(((bf16[128,4,1536]{2,1,0:T(4,128)(2,1)}), bf16[128,4,1536]{2,1,0:T(4,128)(2,1)S(1)}, u32[]{:S(2)}, u32[]{:S(2)}) %all-to-all-start.3) | async-done | bytes 1572896 | tf_op jit(solution)/shard_map/all_to_all | solution.py:252
  (113 shorter events, 16.8 us)
Async XLA Ops:
  0.0 121.6 %copy-start = (bf16[1536,288]{0,1:T(8,128)(2,1)S(1)}, bf16[1536,288]{0,1:T(8,128)(2,1)}, u32[]{:S(2)}) copy-start(bf16[1536,288]{0,1:T(8,128)(2,1)} %param.25) | copy-start | bytes 2654212
  11.6 11.3 %copy-start.1 = (s32[128]{0:T(128)S(1)}, s32[128]{0:T(128)}, u32[]{:S(2)}) copy-start(s32[128]{0:T(128)} %param.15) | copy-start | bytes 1540
  11.6 12.0 %copy-start.3 = (s32[8,9]{1,0:T(8,128)S(1)}, s32[8,9]{1,0:T(8,128)}, u32[]{:S(2)}) copy-start(s32[8,9]{1,0:T(8,128)} %param.18) | copy-start | bytes 868
  11.6 35.4 %all-to-all-start = ((bf16[64,4,3328]{2,1,0:T(4,128)(2,1)}), bf16[64,4,3328]{2,1,0:T(4,128)(2,1)S(1)}, u32[]{:S(2)}, u32[]{:S(2)}) async-start(bf16[64,4,3328]{2,1,0:T(4,128)(2,1)} %bitcast.124), calls=%async_computation | async-start | bytes 3407872 | tf_op jit(solution)/shard_map/all_to_all | solution.py:171
  47.2 1.2 copy-start.2
  68.8 20.6 %all-to-all-start.1 = ((bf16[8,4,8,1536]{3,1,2,0:T(4,128)(2,1)}), bf16[8,4,8,1536]{3,1,2,0:T(4,128)(2,1)S(1)}, u32[]{:S(2)}, u32[]{:S(2)}) async-start(bf16[8,4,8,1536]{3,1,2,0:T(4,128)(2,1)} %bitcast_select_fusion), calls=%async_computation.1 | async-start | bytes 1572864 | tf_op jit(solution)/shard_map/all_to_all | solution.py:224
  89.8 3.6 %copy-start.4 = (f32[1536]{0:T(1024)S(1)}, f32[1536]{0:T(1024)}, u32[]{:S(2)}) copy-start(f32[1536]{0:T(1024)} %param.24) | copy-start | bytes 18436
  94.8 26.8 %all-to-all-start.2 = ((bf16[16,32,1536]{2,1,0:T(8,128)(2,1)}), bf16[16,32,1536]{2,1,0:T(8,128)(2,1)S(1)}, u32[]{:S(2)}, u32[]{:S(2)}) async-start(bf16[16,32,1536]{2,1,0:T(8,128)(2,1)} %broadcast_in_dim.378), calls=%async_computation.2 | async-start | bytes 3145728 | tf_op jit(solution)/shard_map/all_to_all | solution.py:234
  121.6 1.2 copy-start.5
  122.7 1.2 copy-start.6
  126.3 35.4 %all-to-all-start.3 = ((bf16[128,4,1536]{2,1,0:T(4,128)(2,1)}), bf16[128,4,1536]{2,1,0:T(4,128)(2,1)S(1)}, u32[]{:S(2)}, u32[]{:S(2)}) async-start(bf16[128,4,1536]{2,1,0:T(4,128)(2,1)} %all_to_all.18), calls=%async_computation.3 | async-start | bytes 3145728 | tf_op jit(solution)/shard_map/all_to_all | solution.py:252

commit v14 on v13

--- a/solution.py
+++ b/solution.py
@@ -160,19 +160,20 @@
     normed = rms_round(x_steps.reshape(steps * rows, width), norm_attn)
     query = jnp.dot(normed, w_query, preferred_element_type=jnp.float32).astype(jnp.bfloat16)
     fresh = jnp.dot(normed, w_keyval, preferred_element_type=jnp.float32).astype(jnp.bfloat16)
-    packed = jnp.concatenate(
-        [x_steps.reshape(steps * rows, width), query, fresh], axis=-1
-    ).reshape(steps, rows, width + qwidth + 2 * head_dim)
+    packed = jnp.concatenate([query, fresh], axis=-1).reshape(steps, rows, qwidth + 2 * head_dim)
     send_slot = jnp.sum(
         jnp.where(target[None, :] == offsets[:, None], offsets[None, :], 0), axis=1
     )
+    inputs = lax.all_to_all(
+        jnp.take(x_steps, send_slot, axis=1), "req", split_axis=1, concat_axis=1, tiled=True
+    )
+    inputs, packed = lax.optimization_barrier((inputs, packed))
     sending = jnp.swapaxes(jnp.take(packed, send_slot, axis=1), 0, 1)
     sending = jnp.broadcast_to(sending[:, None], (req_count, BEAMS) + sending.shape[1:])
     arrived = lax.all_to_all(
         sending.reshape((req_count * BEAMS,) + sending.shape[2:]), ("req",) + HALF, 0, 0, tiled=True
     ).reshape((req_count, BEAMS) + sending.shape[2:])
-    inputs = jnp.swapaxes(lax.dynamic_index_in_dim(arrived, beam, 1, keepdims=False)[..., :width], 0, 1)
-    mine = jnp.transpose(arrived[..., width:], (1, 2, 0, 3))
+    mine = jnp.transpose(arrived, (1, 2, 0, 3))
     queries = mine[..., :qwidth].reshape(BEAMS, steps, rows, heads, head_dim)
     entries = mine[..., qwidth:]
 

time: 165 us -> 164 us (level)
  Pallas kernels: 13.4 us -> 18.7 us
  waiting for transfers between devices: 65 us -> 62.7 us
  local copies, waits for them, and re-layouts: 29.7 us -> 27.5 us
    all_to_all x0 -> x1, starting transfers between devices: none -> 5.8 us  [on_device(): lax.all_to_all(jnp.take(x_steps, send_slot, axis=1), 'req', split_axis=1,...]
    all_to_all x1, starting transfers between devices: 9.32 us -> 3.55 us  [on_device(): lax.all_to_all(attended, HALF, split_axis=0, concat_axis=0, tiled=True)]
    pallas_call x1, Pallas kernels: 13.4 us -> 18.7 us  [attend(): pl.pallas_call(attend_kernel, grid_spec=pltpu.PrefetchScalarGridSpec(num_...]
    all_to_all x1, waiting for transfers between devices: 10.3 us -> 6.28 us  [on_device(): lax.all_to_all(sending.reshape((req_count * BEAMS,) + sending.shape[2:]),...]
    unnamed x17 -> x19, local copies, waits for them, and re-layouts: 3.02 us -> 1.02 us
    dynamic_slice x1 -> x0, local copies, waits for them, and re-layouts: 1.89 us -> none  [on_device(): lax.dynamic_index_in_dim(arrived, beam, 1, keepdims=False)[..., :width]]
    all_to_all x1, waiting for transfers between devices: 9.34 us -> 11.2 us  [on_device(): lax.all_to_all(attended, HALF, split_axis=0, concat_axis=0, tiled=True)]
    gather x0 -> x1, local copies, waits for them, and re-layouts: none -> 1.73 us  [on_device(): jnp.take(x_steps, send_slot, axis=1)]
  transfers between devices with their start and end apart: 4 -> 5, of which waited for: 4 -> 4; matrix products, arithmetic and copies ran while one was open for 10% -> 12% of each run, Pallas kernels for 0% -> 0%
where the time goes in v14:
time: 164 us; the launch traced here: 163 us
  waiting for transfers between devices  62.7 us (38%)
  starting transfers between devices  37.1 us (23%)
  local copies, waits for them, and re-layouts  27.5 us (17%)
  Pallas kernels  18.7 us (11%)
  matrix products  9.38 us (6%)
  other arithmetic  7.22 us (4%)
    all_to_all x1, waiting for transfers between devices, on_device(): lax.all_to_all(leaving, KV + ('req',), 0, 0, tiled=True)  24.9 us
    all_to_all x1, waiting for transfers between devices, on_device(): lax.all_to_all(jnp.broadcast_to(mlp_own[None], (kv_count,) + mlp_own.shap...  20.3 us
    pallas_call x1, Pallas kernels, attend(): pl.pallas_call(attend_kernel, grid_spec=pltpu.PrefetchScalarGridSpec(num_...  18.7 us
    all_to_all x1, waiting for transfers between devices, on_device(): lax.all_to_all(attended, HALF, split_axis=0, concat_axis=0, tiled=True)  11.2 us
    all_to_all x1, starting transfers between devices, on_device(): lax.all_to_all(leaving, KV + ('req',), 0, 0, tiled=True)  11.1 us
    all_to_all x1, starting transfers between devices, on_device(): lax.all_to_all(sending.reshape((req_count * BEAMS,) + sending.shape[2:]),...  9.35 us
    gather x1, local copies, waits for them, and re-layouts, on_device(): pool[table[offset_of] - device * pool.shape[0]]  7.81 us
    all_to_all x1, starting transfers between devices, on_device(): lax.all_to_all(jnp.broadcast_to(mlp_own[None], (kv_count,) + mlp_own.shap...  7.27 us
  transfers between devices with their start and end apart: 5, of which 4 were waited for; matrix products, arithmetic and copies ran while one was open for 12% of the time, Pallas kernels for 0%

profile of v14, /device:TPU:1, one launch (start us, length us, event | category | flops | bytes accessed | tf_op | source)
XLA Modules:
  0.0 163.2 jit_solution(4240740938003118762)
XLA Ops:
  2.0 1.7 %gather_fusion = bf16[8,4,1536]{2,0,1:T(8,128)(2,1)S(1)} fusion(bf16[4,8,1536]{2,1,0:T(8,128)(2,1)} %param.14, s32[1024]{0:T(1024)S(1)} %pad_clamp_fusion.3), kind=kCustom, calls=%fused_computation | custom fusion | bytes 196640 | tf_op jit(solution)/shard_map/jit(_take)/gather | solution.py:168
  4.5 5.8 %all-to-all-start = ((bf16[4,8,1536]{2,0,1:T(4,128)(2,1)}), bf16[4,8,1536]{2,0,1:T(4,128)(2,1)S(1)}, u32[]{:S(2)}, u32[]{:S(2)}) async-start(bf16[4,8,1536]{2,0,1:T(4,128)(2,1)} %copy.105), calls=%async_computation | async-start | bytes 196608 | tf_op jit(solution)/shard_map/all_to_all | solution.py:167
  10.3 1.0 fusion.19
  11.5 3.4 %convolution_convert_fusion.1 = bf16[32,1536]{1,0:T(8,128)(2,1)S(1)} fusion(bf16[1536,1536]{1,0:T(8,128)(2,1)} %param.21, bf16[4,8,1536]{2,1,0:T(8,128)(2,1)} %param.14, f32[1536]{0:T(1024)} %param.20, f32[32]{0:T(128)S(1)} %rsqrt.23), kind=kOutput, calls=%fused_computation.11 | convolution fusion | flops 151240704 | bytes 4921472 | tf_op jit(solution)/shard_map/dot_general | solution.py:161
  20.3 1.2 broadcast_in_dim.366
  21.5 9.3 %all-to-all-start.1 = ((bf16[64,4,1792]{2,1,0:T(4,128)(2,1)}), bf16[64,4,1792]{2,1,0:T(4,128)(2,1)S(1)}, u32[]{:S(2)}, u32[]{:S(2)}) async-start(bf16[64,4,1792]{2,1,0:T(4,128)(2,1)} %bitcast.23), calls=%async_computation.1 | async-start | bytes 1835008 | tf_op jit(solution)/shard_map/all_to_all | solution.py:173
  32.5 7.8 %gather_fusion.6 = bf16[72,128,256]{2,1,0:T(8,128)(2,1)} fusion(bf16[72,128,256]{2,1,0:T(8,128)(2,1)} %param.19, s32[1024]{0:T(1024)S(1)} %pad_clamp_fusion), kind=kCustom, calls=%fused_computation.6 | custom fusion | bytes 9437472 | tf_op jit(solution)/shard_map/gather | solution.py:203
  41.1 6.3 %all-to-all-done.1 = bf16[64,4,1792]{2,1,0:T(4,128)(2,1)S(1)} async-done(((bf16[64,4,1792]{2,1,0:T(4,128)(2,1)}), bf16[64,4,1792]{2,1,0:T(4,128)(2,1)S(1)}, u32[]{:S(2)}, u32[]{:S(2)}) %all-to-all-start.1) | async-done | bytes 917536 | tf_op jit(solution)/shard_map/all_to_all | solution.py:173
  48.6 0.9 copy.146
  49.9 1.0 copy.124.q_ref
  50.9 18.7 %shard_map.136 = bf16[8,4,96,128]{3,2,1,0:T(8,128)(2,1)} custom-call(s32[64]{0:T(128)} %reshape.546.bounds_ref, s32[32]{0:T(128)} %reshape.563.used_ref, bf16[8,4,96,128]{3,2,1,0:T(8,128)(2,1)} %copy.124.q_ref, bf16[8,1152,256]{2,1,0:T(8,128)(2,1)} %bitcast.118, bf16[8,4,32,256]{3,2,1,0:T(8,128)(2,1)} %bitcast.124, f32[4,96,32]{2,1,0:T(8,128)} %and_convert_fusion.pick_ref), custom_call_target="tpu_custom_call" | custom-call | flops 1862270976 | bytes 6815744 | tf_op jit(solution)/shard_map/pallas_call | solution.py:92
  69.6 2.0 %reshape.555 = bf16[8,4,8,1536]{3,2,1,0:T(8,128)(2,1)S(1)} reshape(bf16[8,4,96,128]{3,2,1,0:T(8,128)(2,1)} %shard_map.136) | data formatting | bytes 1572864 | tf_op jit(solution)/shard_map/reshape | solution.py:222
  71.6 1.6 bitcast_select_fusion
  73.1 3.5 %all-to-all-start.2 = ((bf16[8,4,8,1536]{3,1,2,0:T(4,128)(2,1)}), bf16[8,4,8,1536]{3,1,2,0:T(4,128)(2,1)S(1)}, u32[]{:S(2)}, u32[]{:S(2)}) async-start(bf16[8,4,8,1536]{3,1,2,0:T(4,128)(2,1)} %bitcast_select_fusion), calls=%async_computation.2 | async-start | bytes 1572864 | tf_op jit(solution)/shard_map/all_to_all | solution.py:225
  76.7 11.2 %all-to-all-done.2 = bf16[8,4,8,1536]{3,1,2,0:T(4,128)(2,1)S(1)} async-done(((bf16[8,4,8,1536]{3,1,2,0:T(4,128)(2,1)}), bf16[8,4,8,1536]{3,1,2,0:T(4,128)(2,1)S(1)}, u32[]{:S(2)}, u32[]{:S(2)}) %all-to-all-start.2) | async-done | bytes 786464 | tf_op jit(solution)/shard_map/all_to_all | solution.py:225
  88.3 3.3 %multiply_reduce_fusion = (f32[8,4]{0,1:T(4,128)S(1)}, bf16[8,4,1536]{2,0,1:T(8,128)(2,1)S(1)}) fusion(bf16[1536,1536]{1,0:T(8,128)(2,1)} %param.23, bf16[4,8,1536]{2,0,1:T(4,128)(2,1)S(1)} %reduce_sum.315, f32[4,8,1536]{2,0,1:T(4,128)S(1)} %convert_element_type.123), kind=kOutput, calls=%fused_computation.53 | convolution fusion | flops 151240672 | bytes 5111936 | tf_op jit(solution)/shard_map/dot_general | solution.py:231
  92.0 1.3 broadcast_in_dim.390
  93.4 7.3 %all-to-all-start.3 = ((bf16[16,32,1536]{2,1,0:T(8,128)(2,1)}), bf16[16,32,1536]{2,1,0:T(8,128)(2,1)S(1)}, u32[]{:S(2)}, u32[]{:S(2)}) async-start(bf16[16,32,1536]{2,1,0:T(8,128)(2,1)} %broadcast_in_dim.390), calls=%async_computation.3 | async-start | bytes 3145728 | tf_op jit(solution)/shard_map/all_to_all | solution.py:235
  100.7 20.3 %all-to-all-done.3 = bf16[16,32,1536]{2,1,0:T(8,128)(2,1)S(1)} async-done(((bf16[16,32,1536]{2,1,0:T(8,128)(2,1)}), bf16[16,32,1536]{2,1,0:T(8,128)(2,1)S(1)}, u32[]{:S(2)}, u32[]{:S(2)}) %all-to-all-start.3) | async-done | bytes 1572896 | tf_op jit(solution)/shard_map/all_to_all | solution.py:235
  123.3 1.0 convolution_convert_fusion
  124.3 1.4 all_to_all.22
  125.7 11.1 %all-to-all-start.4 = ((bf16[128,4,1536]{2,1,0:T(4,128)(2,1)}), bf16[128,4,1536]{2,1,0:T(4,128)(2,1)S(1)}, u32[]{:S(2)}, u32[]{:S(2)}) async-start(bf16[128,4,1536]{2,1,0:T(4,128)(2,1)} %all_to_all.22), calls=%async_computation.4 | async-start | bytes 3145728 | tf_op jit(solution)/shard_map/all_to_all | solution.py:253
  136.9 24.9 %all-to-all-done.4 = bf16[128,4,1536]{2,1,0:T(4,128)(2,1)S(1)} async-done(((bf16[128,4,1536]{2,1,0:T(4,128)(2,1)}), bf16[128,4,1536]{2,1,0:T(4,128)(2,1)S(1)}, u32[]{:S(2)}, u32[]{:S(2)}) %all-to-all-start.4) | async-done | bytes 1572896 | tf_op jit(solution)/shard_map/all_to_all | solution.py:253
  162.4 0.8 select_reduce_fusion
  (118 shorter events, 15.6 us)
Async XLA Ops:
  0.0 121.0 %copy-start = (bf16[1536,288]{0,1:T(8,128)(2,1)S(1)}, bf16[1536,288]{0,1:T(8,128)(2,1)}, u32[]{:S(2)}) copy-start(bf16[1536,288]{0,1:T(8,128)(2,1)} %param.25) | copy-start | bytes 2654212
  4.5 15.0 %all-to-all-start = ((bf16[4,8,1536]{2,0,1:T(4,128)(2,1)}), bf16[4,8,1536]{2,0,1:T(4,128)(2,1)S(1)}, u32[]{:S(2)}, u32[]{:S(2)}) async-start(bf16[4,8,1536]{2,0,1:T(4,128)(2,1)} %copy.105), calls=%async_computation | async-start | bytes 196608 | tf_op jit(solution)/shard_map/all_to_all | solution.py:167
  11.4 3.5 %copy-start.2 = (bf16[4,8,1536]{2,1,0:T(8,128)(2,1)S(1)}, bf16[4,8,1536]{2,1,0:T(8,128)(2,1)}, u32[]{:S(2)}) copy-start(bf16[4,8,1536]{2,1,0:T(8,128)(2,1)} %param.14) | copy-start | bytes 294916
  11.4 3.5 %copy-start.3 = (bf16[1536,256]{1,0:T(8,128)(2,1)S(1)}, bf16[1536,256]{1,0:T(8,128)(2,1)}, u32[]{:S(2)}) copy-start(bf16[1536,256]{1,0:T(8,128)(2,1)} %param.22) | copy-start | bytes 2359300
  11.4 3.5 %copy-start.5 = (f32[1536]{0:T(1024)S(1)}, f32[1536]{0:T(1024)}, u32[]{:S(2)}) copy-start(f32[1536]{0:T(1024)} %param.20) | copy-start | bytes 18436
  11.5 5.8 %copy-start.4 = (s32[8,9]{1,0:T(8,128)S(1)}, s32[8,9]{1,0:T(8,128)}, u32[]{:S(2)}) copy-start(s32[8,9]{1,0:T(8,128)} %param.18) | copy-start | bytes 868
  14.9 3.8 %copy-start.1 = (s32[128]{0:T(128)S(1)}, s32[128]{0:T(128)}, u32[]{:S(2)}) copy-start(s32[128]{0:T(128)} %param.15) | copy-start | bytes 1540
  21.5 25.9 %all-to-all-start.1 = ((bf16[64,4,1792]{2,1,0:T(4,128)(2,1)}), bf16[64,4,1792]{2,1,0:T(4,128)(2,1)S(1)}, u32[]{:S(2)}, u32[]{:S(2)}) async-start(bf16[64,4,1792]{2,1,0:T(4,128)(2,1)} %bitcast.23), calls=%async_computation.1 | async-start | bytes 1835008 | tf_op jit(solution)/shard_map/all_to_all | solution.py:173
  73.1 14.8 %all-to-all-start.2 = ((bf16[8,4,8,1536]{3,1,2,0:T(4,128)(2,1)}), bf16[8,4,8,1536]{3,1,2,0:T(4,128)(2,1)S(1)}, u32[]{:S(2)}, u32[]{:S(2)}) async-start(bf16[8,4,8,1536]{3,1,2,0:T(4,128)(2,1)} %bitcast_select_fusion), calls=%async_computation.2 | async-start | bytes 1572864 | tf_op jit(solution)/shard_map/all_to_all | solution.py:225
  88.3 3.6 %copy-start.6 = (f32[1536]{0:T(1024)S(1)}, f32[1536]{0:T(1024)}, u32[]{:S(2)}) copy-start(f32[1536]{0:T(1024)} %param.24) | copy-start | bytes 18436
  93.4 27.6 %all-to-all-start.3 = ((bf16[16,32,1536]{2,1,0:T(8,128)(2,1)}), bf16[16,32,1536]{2,1,0:T(8,128)(2,1)S(1)}, u32[]{:S(2)}, u32[]{:S(2)}) async-start(bf16[16,32,1536]{2,1,0:T(8,128)(2,1)} %broadcast_in_dim.390), calls=%async_computation.3 | async-start | bytes 3145728 | tf_op jit(solution)/shard_map/all_to_all | solution.py:235
  121.0 1.2 copy-start.7
  122.2 1.2 copy-start.8
  125.7 36.0 %all-to-all-start.4 = ((bf16[128,4,1536]{2,1,0:T(4,128)(2,1)}), bf16[128,4,1536]{2,1,0:T(4,128)(2,1)S(1)}, u32[]{:S(2)}, u32[]{:S(2)}) async-start(bf16[128,4,1536]{2,1,0:T(4,128)(2,1)} %all_to_all.22), calls=%async_computation.4 | async-start | bytes 3145728 | tf_op jit(solution)/shard_map/all_to_all | solution.py:253

commit v15 on v12

--- a/solution.py
+++ b/solution.py
@@ -152,8 +152,10 @@
         axis=0,
     )
     anchor = serving // per_group
-    send_order = jnp.argsort(target * rows + offsets)
-    outgoing = x_steps[:, send_order].reshape(steps, req_count, quota, width)
+    send_slot = jnp.sum(
+        jnp.where(target[None, :] == offsets[:, None], offsets[None, :], 0), axis=1
+    )
+    outgoing = jnp.take(x_steps, send_slot, axis=1).reshape(steps, req_count, quota, width)
     arrived = lax.all_to_all(outgoing, "req", split_axis=1, concat_axis=1, tiled=True).reshape(
         steps, rows, width
     )

time: 155 us -> 155 us (level); the launches traced: 155 us -> 152 us
  starting transfers between devices: 29.5 us -> 34.9 us
  waiting for transfers between devices: 49 us -> 43.7 us
  Pallas kernels: 21.5 us -> 19.7 us
    all_to_all x1, starting transfers between devices: 12.8 us -> 17.3 us  [on_device(): lax.all_to_all(leaving, KV + ('req',), 0, 0, tiled=True)]
    all_to_all x1, waiting for transfers between devices: 18.9 us -> 15.1 us  [on_device(): lax.all_to_all(jnp.broadcast_to(mlp_own[None], (kv_count,) + mlp_own.shap...]
    pallas_call x1, Pallas kernels: 21.5 us -> 19.7 us  [attend(): pl.pallas_call(attend_kernel, grid_spec=pltpu.PrefetchScalarGridSpec(num_...]
  transfers between devices with their start and end apart: 4 -> 4, of which waited for: 4 -> 4; matrix products, arithmetic and copies ran while one was open for 8% -> 9% of each run, Pallas kernels for 0% -> 0%
where the time goes in v15:
time: 155 us; the launch traced here: 152 us
  waiting for transfers between devices  43.7 us (28%)
  starting transfers between devices  34.9 us (23%)
  local copies, waits for them, and re-layouts  26.3 us (17%)
  Pallas kernels  19.7 us (13%)
  blocking collectives  12.4 us (8%)
  matrix products  9.33 us (6%)
  other arithmetic  5.37 us (3%)
    all_to_all x1, waiting for transfers between devices, on_device(): lax.all_to_all(leaving, KV + ('req',), 0, 0, tiled=True)  24.9 us
    pallas_call x1, Pallas kernels, attend(): pl.pallas_call(attend_kernel, grid_spec=pltpu.PrefetchScalarGridSpec(num_...  19.7 us
    all_to_all x1, starting transfers between devices, on_device(): lax.all_to_all(leaving, KV + ('req',), 0, 0, tiled=True)  17.3 us
    all_to_all x1, waiting for transfers between devices, on_device(): lax.all_to_all(jnp.broadcast_to(mlp_own[None], (kv_count,) + mlp_own.shap...  15.1 us
    all_to_all x1, blocking collectives, on_device(): lax.all_to_all(attended, HALF, split_axis=0, concat_axis=0, tiled=True)  12.4 us
    gather x1, local copies, waits for them, and re-layouts, on_device(): pool[table[offset_of] - device * pool.shape[0]]  7.81 us
    all_to_all x1, starting transfers between devices, on_device(): lax.all_to_all(jnp.broadcast_to(mlp_own[None], (kv_count,) + mlp_own.shap...  6.24 us
    all_to_all x1, starting transfers between devices, on_device(): lax.all_to_all(outgoing, 'req', split_axis=1, concat_axis=1, tiled=True)  5.8 us
  transfers between devices with their start and end apart: 4, of which 4 were waited for; matrix products, arithmetic and copies ran while one was open for 9% of the time, Pallas kernels for 0%

profile of v15, /device:TPU:1, one launch (start us, length us, event | category | flops | bytes accessed | tf_op | source)
XLA Modules:
  0.0 152.3 jit_solution(3063819448270775115)
XLA Ops:
  0.0 0.8 reshape.537
  0.8 0.7 reshape.536
  2.0 1.7 %gather_fusion = bf16[8,4,1536]{2,0,1:T(8,128)(2,1)S(1)} fusion(bf16[4,8,1536]{2,1,0:T(8,128)(2,1)} %param.14, s32[1024]{0:T(1024)S(1)} %pad_clamp_fusion.3), kind=kCustom, calls=%fused_computation | custom fusion | bytes 196640 | tf_op jit(solution)/shard_map/jit(_take)/gather | solution.py:158
  4.5 5.8 %all-to-all-start = ((bf16[4,8,1,1536]{3,0,2,1:T(4,128)(2,1)}), bf16[4,8,1,1536]{3,0,2,1:T(4,128)(2,1)S(1)}, u32[]{:S(2)}, u32[]{:S(2)}) async-start(bf16[4,8,1,1536]{3,0,2,1:T(4,128)(2,1)} %copy.96), calls=%async_computation | async-start | bytes 196608 | tf_op jit(solution)/shard_map/all_to_all | solution.py:159
  15.7 3.4 %convolution_convert_fusion.1 = bf16[32,1536]{1,0:T(8,128)(2,1)S(1)} fusion(bf16[1536,1536]{1,0:T(8,128)(2,1)} %param.21, f32[4,8,1,1536]{3,0,2,1:T(4,128)S(1)} %convert_element_type.115, f32[1536]{0:T(1024)S(1)} %copy-done.4, f32[32]{0:T(128)S(1)} %rsqrt.23), kind=kOutput, calls=%fused_computation.10 | convolution fusion | flops 151191552 | bytes 5019776 | tf_op jit(solution)/shard_map/dot_general | solution.py:170
  19.4 1.0 broadcast_in_dim.356
  20.4 5.5 %all-to-all-start.1 = ((bf16[8,4,8,1792]{3,2,1,0:T(8,128)(2,1)}), bf16[8,4,8,1792]{3,2,1,0:T(8,128)(2,1)S(1)}, u32[]{:S(2)}, u32[]{:S(2)}) async-start(bf16[8,4,8,1792]{3,2,1,0:T(8,128)(2,1)} %broadcast_in_dim.356), calls=%async_computation.1 | async-start | bytes 1835008 | tf_op jit(solution)/shard_map/all_to_all | solution.py:173
  27.5 7.8 %gather_fusion.5 = bf16[72,128,256]{2,1,0:T(8,128)(2,1)} fusion(bf16[72,128,256]{2,1,0:T(8,128)(2,1)} %param.19, s32[1024]{0:T(1024)S(1)} %pad_clamp_fusion), kind=kCustom, calls=%fused_computation.5 | custom fusion | bytes 9437472 | tf_op jit(solution)/shard_map/gather | solution.py:202
  36.2 3.0 %all-to-all-done.1 = bf16[8,4,8,1792]{3,2,1,0:T(8,128)(2,1)S(1)} async-done(((bf16[8,4,8,1792]{3,2,1,0:T(8,128)(2,1)}), bf16[8,4,8,1792]{3,2,1,0:T(8,128)(2,1)S(1)}, u32[]{:S(2)}, u32[]{:S(2)}) %all-to-all-start.1) | async-done | bytes 917536 | tf_op jit(solution)/shard_map/all_to_all | solution.py:173
  39.2 0.8 select_reduce_fusion.10
  40.2 0.9 copy.130
  41.2 1.0 copy.109.q_ref
  42.3 19.7 %shard_map.136 = bf16[8,4,96,128]{3,2,1,0:T(8,128)(2,1)} custom-call(s32[64]{0:T(128)} %reshape.540.bounds_ref, s32[32]{0:T(128)} %reshape.554.used_ref, bf16[8,4,96,128]{3,2,1,0:T(8,128)(2,1)} %copy.109.q_ref, bf16[8,1152,256]{2,1,0:T(8,128)(2,1)} %bitcast.110, bf16[8,4,32,256]{3,2,1,0:T(8,128)(2,1)} %bitcast.113, f32[4,96,32]{2,1,0:T(8,128)} %and_convert_fusion.pick_ref), custom_call_target="tpu_custom_call" | custom-call | flops 1862270976 | bytes 6815744 | tf_op jit(solution)/shard_map/pallas_call | solution.py:92
  62.0 2.0 %reshape.547 = bf16[8,4,8,1536]{3,2,1,0:T(8,128)(2,1)S(1)} reshape(bf16[8,4,96,128]{3,2,1,0:T(8,128)(2,1)} %shard_map.136) | data formatting | bytes 1572864 | tf_op jit(solution)/shard_map/reshape | solution.py:221
  64.6 12.4 %all_to_all.29 = bf16[8,4,8,1536]{3,1,2,0:T(4,128)(2,1)S(1)} all-to-all(bf16[8,4,8,1536]{3,1,2,0:T(4,128)(2,1)S(1)} %bitcast_select_fusion), channel_id=1, replica_groups=mesh['req'=8,'y'=4,'zhi'=2,'zlo'=2] {'y','zlo'}, dimensions={0} | all-to-all | bytes 1572864 | tf_op jit(solution)/shard_map/all_to_all | solution.py:224
  77.4 3.3 %multiply_reduce_fusion = (f32[8,4]{0,1:T(4,128)S(1)}, bf16[8,4,1536]{2,0,1:T(8,128)(2,1)S(1)}) fusion(bf16[1536,1536]{1,0:T(8,128)(2,1)} %param.23, bf16[4,8,1536]{2,0,1:T(4,128)(2,1)S(1)} %reduce_sum.315, f32[4,8,1,1536]{3,0,2,1:T(4,128)S(1)} %convert_element_type.115), kind=kOutput, calls=%fused_computation.48 | convolution fusion | flops 151240672 | bytes 5111936 | tf_op jit(solution)/shard_map/dot_general | solution.py:230
  81.1 1.3 broadcast_in_dim.380
  82.4 6.2 %all-to-all-start.3 = ((bf16[16,32,1536]{2,1,0:T(8,128)(2,1)}), bf16[16,32,1536]{2,1,0:T(8,128)(2,1)S(1)}, u32[]{:S(2)}, u32[]{:S(2)}) async-start(bf16[16,32,1536]{2,1,0:T(8,128)(2,1)} %broadcast_in_dim.380), calls=%async_computation.3 | async-start | bytes 3145728 | tf_op jit(solution)/shard_map/all_to_all | solution.py:234
  88.7 15.1 %all-to-all-done.3 = bf16[16,32,1536]{2,1,0:T(8,128)(2,1)S(1)} async-done(((bf16[16,32,1536]{2,1,0:T(8,128)(2,1)}), bf16[16,32,1536]{2,1,0:T(8,128)(2,1)S(1)}, u32[]{:S(2)}, u32[]{:S(2)}) %all-to-all-start.3) | async-done | bytes 1572896 | tf_op jit(solution)/shard_map/all_to_all | solution.py:234
  106.2 1.0 convolution_convert_fusion
  107.2 1.4 all_to_all.22
  108.5 17.3 %all-to-all-start.4 = ((bf16[128,4,1536]{2,1,0:T(4,128)(2,1)}), bf16[128,4,1536]{2,1,0:T(4,128)(2,1)S(1)}, u32[]{:S(2)}, u32[]{:S(2)}) async-start(bf16[128,4,1536]{2,1,0:T(4,128)(2,1)} %all_to_all.22), calls=%async_computation.4 | async-start | bytes 3145728 | tf_op jit(solution)/shard_map/all_to_all | solution.py:252
  125.9 24.9 %all-to-all-done.4 = bf16[128,4,1536]{2,1,0:T(4,128)(2,1)S(1)} async-done(((bf16[128,4,1536]{2,1,0:T(4,128)(2,1)}), bf16[128,4,1536]{2,1,0:T(4,128)(2,1)S(1)}, u32[]{:S(2)}, u32[]{:S(2)}) %all-to-all-start.4) | async-done | bytes 1572896 | tf_op jit(solution)/shard_map/all_to_all | solution.py:252
  151.5 0.8 select_reduce_fusion
  (107 shorter events, 13.7 us)
Async XLA Ops:
  0.0 103.8 %copy-start = (bf16[1536,288]{0,1:T(8,128)(2,1)S(1)}, bf16[1536,288]{0,1:T(8,128)(2,1)}, u32[]{:S(2)}) copy-start(bf16[1536,288]{0,1:T(8,128)(2,1)} %param.25) | copy-start | bytes 2654212
  0.0 12.4 %copy-start.3 = (s32[8,9]{1,0:T(8,128)S(1)}, s32[8,9]{1,0:T(8,128)}, u32[]{:S(2)}) copy-start(s32[8,9]{1,0:T(8,128)} %param.18) | copy-start | bytes 868
  0.0 13.9 %copy-start.1 = (s32[128]{0:T(128)S(1)}, s32[128]{0:T(128)}, u32[]{:S(2)}) copy-start(s32[128]{0:T(128)} %param.15) | copy-start | bytes 1540
  0.0 15.7 %copy-start.4 = (f32[1536]{0:T(1024)S(1)}, f32[1536]{0:T(1024)}, u32[]{:S(2)}) copy-start(f32[1536]{0:T(1024)} %param.20) | copy-start | bytes 18436
  4.5 10.8 %all-to-all-start = ((bf16[4,8,1,1536]{3,0,2,1:T(4,128)(2,1)}), bf16[4,8,1,1536]{3,0,2,1:T(4,128)(2,1)S(1)}, u32[]{:S(2)}, u32[]{:S(2)}) async-start(bf16[4,8,1,1536]{3,0,2,1:T(4,128)(2,1)} %copy.96), calls=%async_computation | async-start | bytes 196608 | tf_op jit(solution)/shard_map/all_to_all | solution.py:159
  15.7 3.4 %copy-start.2 = (bf16[1536,256]{1,0:T(8,128)(2,1)S(1)}, bf16[1536,256]{1,0:T(8,128)(2,1)}, u32[]{:S(2)}) copy-start(bf16[1536,256]{1,0:T(8,128)(2,1)} %param.22) | copy-start | bytes 2359300
  20.4 18.8 %all-to-all-start.1 = ((bf16[8,4,8,1792]{3,2,1,0:T(8,128)(2,1)}), bf16[8,4,8,1792]{3,2,1,0:T(8,128)(2,1)S(1)}, u32[]{:S(2)}, u32[]{:S(2)}) async-start(bf16[8,4,8,1792]{3,2,1,0:T(8,128)(2,1)} %broadcast_in_dim.356), calls=%async_computation.1 | async-start | bytes 1835008 | tf_op jit(solution)/shard_map/all_to_all | solution.py:173
  77.4 3.6 %copy-start.5 = (f32[1536]{0:T(1024)S(1)}, f32[1536]{0:T(1024)}, u32[]{:S(2)}) copy-start(f32[1536]{0:T(1024)} %param.24) | copy-start | bytes 18436
  82.4 21.4 %all-to-all-start.3 = ((bf16[16,32,1536]{2,1,0:T(8,128)(2,1)}), bf16[16,32,1536]{2,1,0:T(8,128)(2,1)S(1)}, u32[]{:S(2)}, u32[]{:S(2)}) async-start(bf16[16,32,1536]{2,1,0:T(8,128)(2,1)} %broadcast_in_dim.380), calls=%async_computation.3 | async-start | bytes 3145728 | tf_op jit(solution)/shard_map/all_to_all | solution.py:234
  103.8 1.2 copy-start.6
  105.0 1.2 copy-start.7
  108.5 42.2 %all-to-all-start.4 = ((bf16[128,4,1536]{2,1,0:T(4,128)(2,1)}), bf16[128,4,1536]{2,1,0:T(4,128)(2,1)S(1)}, u32[]{:S(2)}, u32[]{:S(2)}) async-start(bf16[128,4,1536]{2,1,0:T(4,128)(2,1)} %all_to_all.22), calls=%async_computation.4 | async-start | bytes 3145728 | tf_op jit(solution)/shard_map/all_to_all | solution.py:252

commit v16 on v15

--- a/solution.py
+++ b/solution.py
@@ -47,7 +47,9 @@
     head_dim = q_ref.shape[3]
     scale = head_dim ** (-0.5)
     keys = kv_ref[0, :, :head_dim]
-    values = kv_ref[0, :, head_dim:]
+    values = jnp.concatenate(
+        [kv_ref[0, :, head_dim:], jnp.ones((kv_ref.shape[1], head_dim), kv_ref.dtype)], axis=1
+    )
     pos = lax.broadcasted_iota(jnp.int32, (1, kv_ref.shape[1]), 1)
     contract = (((1,), (1,)), ((), ()))
     for t in range(steps):
@@ -62,8 +64,9 @@
             scores = jnp.where(allowed, scores, NEGATIVE)
             high_c = jnp.max(scores, axis=1, keepdims=True)
             weights = jnp.exp(scores - high_c).astype(jnp.bfloat16)
-            total_c = jnp.sum(weights.astype(jnp.float32), axis=1, keepdims=True)
-            sum_c = jnp.dot(weights, values, preferred_element_type=jnp.float32)
+            both = jnp.dot(weights, values, preferred_element_type=jnp.float32)
+            sum_c = both[:, :head_dim]
+            total_c = both[:, head_dim : head_dim + 1]
             entries = new_ref[0, t]
             fresh = lax.dot_general(
                 query, entries[:, :head_dim], contract, preferred_element_type=jnp.float32

time: 155 us -> 156 us (level)
  waiting for transfers between devices: 43.7 us -> 50.7 us
  starting transfers between devices: 34.9 us -> 28.6 us
    all_to_all x1, starting transfers between devices: 17.3 us -> 6.41 us  [on_device(): lax.all_to_all(leaving, KV + ('req',), 0, 0, tiled=True)]
    all_to_all x1, waiting for transfers between devices: 15.1 us -> 21.9 us  [on_device(): lax.all_to_all(jnp.broadcast_to(mlp_own[None], (kv_count,) + mlp_own.shap...]
    all_to_all x1, starting transfers between devices: 6.24 us -> 10.8 us  [on_device(): lax.all_to_all(jnp.broadcast_to(mlp_own[None], (kv_count,) + mlp_own.shap...]
where the time goes in v16:
time: 156 us; the launch traced here: 155 us
  waiting for transfers between devices  50.7 us (32%)
  starting transfers between devices  28.6 us (18%)
  local copies, waits for them, and re-layouts  26.3 us (17%)
  Pallas kernels  20.6 us (13%)
  blocking collectives  13.3 us (9%)
  matrix products  9.33 us (6%)
  other arithmetic  5.37 us (3%)
    all_to_all x1, waiting for transfers between devices, on_device(): lax.all_to_all(leaving, KV + ('req',), 0, 0, tiled=True)  25 us
    all_to_all x1, waiting for transfers between devices, on_device(): lax.all_to_all(jnp.broadcast_to(mlp_own[None], (kv_count,) + mlp_own.shap...  21.9 us
    pallas_call x1, Pallas kernels, attend(): pl.pallas_call(attend_kernel, grid_spec=pltpu.PrefetchScalarGridSpec(num_...  20.6 us
    all_to_all x1, blocking collectives, on_device(): lax.all_to_all(attended, HALF, split_axis=0, concat_axis=0, tiled=True)  13.3 us
    all_to_all x1, starting transfers between devices, on_device(): lax.all_to_all(jnp.broadcast_to(mlp_own[None], (kv_count,) + mlp_own.shap...  10.8 us
    gather x1, local copies, waits for them, and re-layouts, on_device(): pool[table[offset_of] - device * pool.shape[0]]  7.81 us
    all_to_all x1, starting transfers between devices, on_device(): lax.all_to_all(leaving, KV + ('req',), 0, 0, tiled=True)  6.41 us
    all_to_all x1, starting transfers between devices, on_device(): lax.all_to_all(outgoing, 'req', split_axis=1, concat_axis=1, tiled=True)  5.8 us
  transfers between devices with their start and end apart: 4, of which 4 were waited for; matrix products, arithmetic and copies ran while one was open for 9% of the time, Pallas kernels for 0%

profile of v16, /device:TPU:1, one launch (start us, length us, event | category | flops | bytes accessed | tf_op | source)
XLA Modules:
  0.0 154.8 jit_solution(6750001998069520027)
XLA Ops:
  0.0 0.8 reshape.537
  0.8 0.7 reshape.536
  2.0 1.7 %gather_fusion = bf16[8,4,1536]{2,0,1:T(8,128)(2,1)S(1)} fusion(bf16[4,8,1536]{2,1,0:T(8,128)(2,1)} %param.14, s32[1024]{0:T(1024)S(1)} %pad_clamp_fusion.3), kind=kCustom, calls=%fused_computation | custom fusion | bytes 196640 | tf_op jit(solution)/shard_map/jit(_take)/gather | solution.py:161
  4.5 5.8 %all-to-all-start = ((bf16[4,8,1,1536]{3,0,2,1:T(4,128)(2,1)}), bf16[4,8,1,1536]{3,0,2,1:T(4,128)(2,1)S(1)}, u32[]{:S(2)}, u32[]{:S(2)}) async-start(bf16[4,8,1,1536]{3,0,2,1:T(4,128)(2,1)} %copy.96), calls=%async_computation | async-start | bytes 196608 | tf_op jit(solution)/shard_map/all_to_all | solution.py:162
  15.7 3.4 %convolution_convert_fusion.1 = bf16[32,1536]{1,0:T(8,128)(2,1)S(1)} fusion(bf16[1536,1536]{1,0:T(8,128)(2,1)} %param.21, f32[4,8,1,1536]{3,0,2,1:T(4,128)S(1)} %convert_element_type.115, f32[1536]{0:T(1024)S(1)} %copy-done.4, f32[32]{0:T(128)S(1)} %rsqrt.23), kind=kOutput, calls=%fused_computation.10 | convolution fusion | flops 151191552 | bytes 5019776 | tf_op jit(solution)/shard_map/dot_general | solution.py:173
  19.4 1.0 broadcast_in_dim.356
  20.4 5.5 %all-to-all-start.1 = ((bf16[8,4,8,1792]{3,2,1,0:T(8,128)(2,1)}), bf16[8,4,8,1792]{3,2,1,0:T(8,128)(2,1)S(1)}, u32[]{:S(2)}, u32[]{:S(2)}) async-start(bf16[8,4,8,1792]{3,2,1,0:T(8,128)(2,1)} %broadcast_in_dim.356), calls=%async_computation.1 | async-start | bytes 1835008 | tf_op jit(solution)/shard_map/all_to_all | solution.py:176
  27.5 7.8 %gather_fusion.5 = bf16[72,128,256]{2,1,0:T(8,128)(2,1)} fusion(bf16[72,128,256]{2,1,0:T(8,128)(2,1)} %param.19, s32[1024]{0:T(1024)S(1)} %pad_clamp_fusion), kind=kCustom, calls=%fused_computation.5 | custom fusion | bytes 9437472 | tf_op jit(solution)/shard_map/gather | solution.py:205
  36.2 3.0 %all-to-all-done.1 = bf16[8,4,8,1792]{3,2,1,0:T(8,128)(2,1)S(1)} async-done(((bf16[8,4,8,1792]{3,2,1,0:T(8,128)(2,1)}), bf16[8,4,8,1792]{3,2,1,0:T(8,128)(2,1)S(1)}, u32[]{:S(2)}, u32[]{:S(2)}) %all-to-all-start.1) | async-done | bytes 917536 | tf_op jit(solution)/shard_map/all_to_all | solution.py:176
  39.2 0.8 select_reduce_fusion.10
  40.2 0.9 copy.130
  41.2 1.0 copy.109.q_ref
  42.3 20.6 %shard_map.136 = bf16[8,4,96,128]{3,2,1,0:T(8,128)(2,1)} custom-call(s32[64]{0:T(128)} %reshape.540.bounds_ref, s32[32]{0:T(128)} %reshape.554.used_ref, bf16[8,4,96,128]{3,2,1,0:T(8,128)(2,1)} %copy.109.q_ref, bf16[8,1152,256]{2,1,0:T(8,128)(2,1)} %bitcast.110, bf16[8,4,32,256]{3,2,1,0:T(8,128)(2,1)} %bitcast.113, f32[4,96,32]{2,1,0:T(8,128)} %and_convert_fusion.pick_ref), custom_call_target="tpu_custom_call" | custom-call | flops 1862270976 | bytes 6815744 | tf_op jit(solution)/shard_map/pallas_call | solution.py:95
  62.8 2.0 %reshape.547 = bf16[8,4,8,1536]{3,2,1,0:T(8,128)(2,1)S(1)} reshape(bf16[8,4,96,128]{3,2,1,0:T(8,128)(2,1)} %shard_map.136) | data formatting | bytes 1572864 | tf_op jit(solution)/shard_map/reshape | solution.py:224
  65.5 13.3 %all_to_all.29 = bf16[8,4,8,1536]{3,1,2,0:T(4,128)(2,1)S(1)} all-to-all(bf16[8,4,8,1536]{3,1,2,0:T(4,128)(2,1)S(1)} %bitcast_select_fusion), channel_id=1, replica_groups=mesh['req'=8,'y'=4,'zhi'=2,'zlo'=2] {'y','zlo'}, dimensions={0} | all-to-all | bytes 1572864 | tf_op jit(solution)/shard_map/all_to_all | solution.py:227
  79.3 3.3 %multiply_reduce_fusion = (f32[8,4]{0,1:T(4,128)S(1)}, bf16[8,4,1536]{2,0,1:T(8,128)(2,1)S(1)}) fusion(bf16[1536,1536]{1,0:T(8,128)(2,1)} %param.23, bf16[4,8,1536]{2,0,1:T(4,128)(2,1)S(1)} %reduce_sum.315, f32[4,8,1,1536]{3,0,2,1:T(4,128)S(1)} %convert_element_type.115), kind=kOutput, calls=%fused_computation.48 | convolution fusion | flops 151240672 | bytes 5111936 | tf_op jit(solution)/shard_map/dot_general | solution.py:233
  83.0 1.3 broadcast_in_dim.380
  84.3 10.8 %all-to-all-start.3 = ((bf16[16,32,1536]{2,1,0:T(8,128)(2,1)}), bf16[16,32,1536]{2,1,0:T(8,128)(2,1)S(1)}, u32[]{:S(2)}, u32[]{:S(2)}) async-start(bf16[16,32,1536]{2,1,0:T(8,128)(2,1)} %broadcast_in_dim.380), calls=%async_computation.3 | async-start | bytes 3145728 | tf_op jit(solution)/shard_map/all_to_all | solution.py:237
  95.1 21.9 %all-to-all-done.3 = bf16[16,32,1536]{2,1,0:T(8,128)(2,1)S(1)} async-done(((bf16[16,32,1536]{2,1,0:T(8,128)(2,1)}), bf16[16,32,1536]{2,1,0:T(8,128)(2,1)S(1)}, u32[]{:S(2)}, u32[]{:S(2)}) %all-to-all-start.3) | async-done | bytes 1572896 | tf_op jit(solution)/shard_map/all_to_all | solution.py:237
  119.4 1.0 convolution_convert_fusion
  120.4 1.4 all_to_all.22
  121.8 6.4 %all-to-all-start.4 = ((bf16[128,4,1536]{2,1,0:T(4,128)(2,1)}), bf16[128,4,1536]{2,1,0:T(4,128)(2,1)S(1)}, u32[]{:S(2)}, u32[]{:S(2)}) async-start(bf16[128,4,1536]{2,1,0:T(4,128)(2,1)} %all_to_all.22), calls=%async_computation.4 | async-start | bytes 3145728 | tf_op jit(solution)/shard_map/all_to_all | solution.py:255
  128.2 25.0 %all-to-all-done.4 = bf16[128,4,1536]{2,1,0:T(4,128)(2,1)S(1)} async-done(((bf16[128,4,1536]{2,1,0:T(4,128)(2,1)}), bf16[128,4,1536]{2,1,0:T(4,128)(2,1)S(1)}, u32[]{:S(2)}, u32[]{:S(2)}) %all-to-all-start.4) | async-done | bytes 1572896 | tf_op jit(solution)/shard_map/all_to_all | solution.py:255
  153.9 0.8 select_reduce_fusion
  (107 shorter events, 13.7 us)
Async XLA Ops:
  0.0 117.1 %copy-start = (bf16[1536,288]{0,1:T(8,128)(2,1)S(1)}, bf16[1536,288]{0,1:T(8,128)(2,1)}, u32[]{:S(2)}) copy-start(bf16[1536,288]{0,1:T(8,128)(2,1)} %param.25) | copy-start | bytes 2654212
  0.0 12.4 %copy-start.3 = (s32[8,9]{1,0:T(8,128)S(1)}, s32[8,9]{1,0:T(8,128)}, u32[]{:S(2)}) copy-start(s32[8,9]{1,0:T(8,128)} %param.18) | copy-start | bytes 868
  0.0 13.9 %copy-start.1 = (s32[128]{0:T(128)S(1)}, s32[128]{0:T(128)}, u32[]{:S(2)}) copy-start(s32[128]{0:T(128)} %param.15) | copy-start | bytes 1540
  0.0 15.7 %copy-start.4 = (f32[1536]{0:T(1024)S(1)}, f32[1536]{0:T(1024)}, u32[]{:S(2)}) copy-start(f32[1536]{0:T(1024)} %param.20) | copy-start | bytes 18436
  4.5 10.8 %all-to-all-start = ((bf16[4,8,1,1536]{3,0,2,1:T(4,128)(2,1)}), bf16[4,8,1,1536]{3,0,2,1:T(4,128)(2,1)S(1)}, u32[]{:S(2)}, u32[]{:S(2)}) async-start(bf16[4,8,1,1536]{3,0,2,1:T(4,128)(2,1)} %copy.96), calls=%async_computation | async-start | bytes 196608 | tf_op jit(solution)/shard_map/all_to_all | solution.py:162
  15.7 3.4 %copy-start.2 = (bf16[1536,256]{1,0:T(8,128)(2,1)S(1)}, bf16[1536,256]{1,0:T(8,128)(2,1)}, u32[]{:S(2)}) copy-start(bf16[1536,256]{1,0:T(8,128)(2,1)} %param.22) | copy-start | bytes 2359300
  20.4 18.8 %all-to-all-start.1 = ((bf16[8,4,8,1792]{3,2,1,0:T(8,128)(2,1)}), bf16[8,4,8,1792]{3,2,1,0:T(8,128)(2,1)S(1)}, u32[]{:S(2)}, u32[]{:S(2)}) async-start(bf16[8,4,8,1792]{3,2,1,0:T(8,128)(2,1)} %broadcast_in_dim.356), calls=%async_computation.1 | async-start | bytes 1835008 | tf_op jit(solution)/shard_map/all_to_all | solution.py:176
  79.3 3.6 %copy-start.5 = (f32[1536]{0:T(1024)S(1)}, f32[1536]{0:T(1024)}, u32[]{:S(2)}) copy-start(f32[1536]{0:T(1024)} %param.24) | copy-start | bytes 18436
  84.3 32.8 %all-to-all-start.3 = ((bf16[16,32,1536]{2,1,0:T(8,128)(2,1)}), bf16[16,32,1536]{2,1,0:T(8,128)(2,1)S(1)}, u32[]{:S(2)}, u32[]{:S(2)}) async-start(bf16[16,32,1536]{2,1,0:T(8,128)(2,1)} %broadcast_in_dim.380), calls=%async_computation.3 | async-start | bytes 3145728 | tf_op jit(solution)/shard_map/all_to_all | solution.py:237
  117.1 1.2 copy-start.6
  118.3 1.2 copy-start.7
  121.8 31.5 %all-to-all-start.4 = ((bf16[128,4,1536]{2,1,0:T(4,128)(2,1)}), bf16[128,4,1536]{2,1,0:T(4,128)(2,1)S(1)}, u32[]{:S(2)}, u32[]{:S(2)}) async-start(bf16[128,4,1536]{2,1,0:T(4,128)(2,1)} %all_to_all.22), calls=%async_computation.4 | async-start | bytes 3145728 | tf_op jit(solution)/shard_map/all_to_all | solution.py:255

commit v17 on v15

--- a/solution.py
+++ b/solution.py
@@ -78,7 +78,11 @@
             scale_n = jnp.exp(high_n - highest)
             totals = total_c * scale_c + total_n * scale_n
             weighted = sum_c * scale_c + sum_n * scale_n
-            out_ref[0, t] = (weighted / totals).astype(out_ref.dtype)
+            attended = weighted / totals
+            for h in range(out_ref.shape[3] // head_dim):
+                out_ref[0, t, :, h * head_dim : (h + 1) * head_dim] = attended[
+                    h * out_ref.shape[2] : (h + 1) * out_ref.shape[2]
+                ].astype(out_ref.dtype)
 
         @pl.when(used_ref[r * steps + t] == 0)
         def _(t=t):
@@ -87,6 +91,8 @@
 
 def attend(bounds, used, queries, pages, entries, pick):
     rows, steps, count, head_dim = queries.shape
+    out_rows = BEAMS
+    out_width = count // BEAMS * head_dim
     span = pages.shape[1]
     flops = 4 * rows * steps * count * (span + entries.shape[2]) * head_dim
     return pl.pallas_call(
@@ -100,9 +106,9 @@
                 pl.BlockSpec((1,) + entries.shape[1:], lambda r, b, u: (r, 0, 0, 0)),
                 pl.BlockSpec(pick.shape, lambda r, b, u: (0, 0, 0)),
             ],
-            out_specs=pl.BlockSpec((1, steps, count, head_dim), lambda r, b, u: (r, 0, 0, 0)),
+            out_specs=pl.BlockSpec((1, steps, out_rows, out_width), lambda r, b, u: (r, 0, 0, 0)),
         ),
-        out_shape=jax.ShapeDtypeStruct(queries.shape, jnp.bfloat16),
+        out_shape=jax.ShapeDtypeStruct((rows, steps, out_rows, out_width), jnp.bfloat16),
         cost_estimate=pl.CostEstimate(
             flops=flops,
             transcendentals=rows * steps * count * span,
@@ -206,11 +212,11 @@
     lo = length[:, None] + step_ids[None, :] - WINDOW - base[:, None]
     hi = jnp.broadcast_to((length - base)[:, None], (rows, steps))
     bounds = jnp.stack([lo, hi], axis=-1).reshape(rows * steps * 2)
-    by_row = jnp.transpose(queries, (2, 1, 0, 3, 4)).reshape(rows, steps, BEAMS * heads, head_dim)
+    by_row = jnp.transpose(queries, (2, 1, 3, 0, 4)).reshape(rows, steps, heads * BEAMS, head_dim)
     entries_by_row = jnp.transpose(listed, (3, 0, 1, 2, 4)).reshape(
         rows, steps, steps * BEAMS, 2 * head_dim
     )
-    row_beam = jnp.arange(BEAMS * heads, dtype=jnp.int32) // heads
+    row_beam = jnp.arange(BEAMS * heads, dtype=jnp.int32) % BEAMS
     column = jnp.arange(steps * BEAMS, dtype=jnp.int32)
     pick = (
         (column[None, None, :] % BEAMS == row_beam[None, :, None])
@@ -218,7 +224,7 @@
     ).astype(jnp.float32)
     used = jnp.any(held, axis=0).T.astype(jnp.int32).reshape(rows * steps)
     attended = attend(bounds, used, by_row, pages, entries_by_row, pick)
-    attended = jnp.transpose(attended.reshape(rows, steps, BEAMS, qwidth), (2, 1, 0, 3))
+    attended = jnp.transpose(attended, (2, 1, 0, 3))
     attended = jnp.where(held[..., None], attended, jnp.zeros_like(attended))
 
     received = lax.all_to_all(attended, HALF, split_axis=0, concat_axis=0, tiled=True)

time: 155 us -> 157 us (1.013); the launches traced: 152 us -> 157 us
  Pallas kernels: 19.7 us -> 16.1 us
  blocking collectives: 12.4 us -> 15.9 us
  waiting for transfers between devices: 43.7 us -> 46.8 us
  starting transfers between devices: 34.9 us -> 37.7 us
    all_to_all x1, starting transfers between devices: 17.3 us -> 21.3 us  [on_device(): lax.all_to_all(leaving, KV + ('req',), 0, 0, tiled=True)]
    all_to_all x1, blocking collectives: 12.4 us -> 15.9 us  [on_device(): lax.all_to_all(attended, HALF, split_axis=0, concat_axis=0, tiled=True)]
    pallas_call x1, Pallas kernels: 19.7 us -> 16.1 us  [attend(): pl.pallas_call(attend_kernel, grid_spec=pltpu.PrefetchScalarGridSpec(num_...]
    reshape x2 -> x0, local copies, waits for them, and re-layouts: 3.03 us -> none  [the longest x1 2 us: on_device(): attended.reshape(rows, steps, BEAMS, qwidth)]
    all_to_all x1, waiting for transfers between devices: 15.1 us -> 18.1 us  [on_device(): lax.all_to_all(jnp.broadcast_to(mlp_own[None], (kv_count,) + mlp_own.shap...]
where the time goes in v17:
time: 157 us
  waiting for transfers between devices  46.8 us (30%)
  starting transfers between devices  37.7 us (24%)
  local copies, waits for them, and re-layouts  25 us (16%)
  Pallas kernels  16.1 us (10%)
  blocking collectives  15.9 us (10%)
  matrix products  9.33 us (6%)
  other arithmetic  5.96 us (4%)
    all_to_all x1, waiting for transfers between devices, on_device(): lax.all_to_all(leaving, KV + ('req',), 0, 0, tiled=True)  24.9 us
    all_to_all x1, starting transfers between devices, on_device(): lax.all_to_all(leaving, KV + ('req',), 0, 0, tiled=True)  21.3 us
    all_to_all x1, waiting for transfers between devices, on_device(): lax.all_to_all(jnp.broadcast_to(mlp_own[None], (kv_count,) + mlp_own.shap...  18.1 us
    pallas_call x1, Pallas kernels, attend(): pl.pallas_call(attend_kernel, grid_spec=pltpu.PrefetchScalarGridSpec(num_...  16.1 us
    all_to_all x1, blocking collectives, on_device(): lax.all_to_all(attended, HALF, split_axis=0, concat_axis=0, tiled=True)  15.9 us
    gather x1, local copies, waits for them, and re-layouts, on_device(): pool[table[offset_of] - device * pool.shape[0]]  7.81 us
    all_to_all x1, starting transfers between devices, on_device(): lax.all_to_all(outgoing, 'req', split_axis=1, concat_axis=1, tiled=True)  5.8 us
    all_to_all x1, starting transfers between devices, on_device(): lax.all_to_all(jnp.broadcast_to(packed[None], (BEAMS,) + packed.shape), H...  5.54 us
  transfers between devices with their start and end apart: 4, of which 4 were waited for; matrix products, arithmetic and copies ran while one was open for 9% of the time, Pallas kernels for 0%

profile of v17, /device:TPU:1, one launch (start us, length us, event | category | flops | bytes accessed | tf_op | source)
XLA Modules:
  0.0 157.5 jit_solution(11694215106846238408)
XLA Ops:
  0.0 0.8 reshape.530
  0.8 0.7 reshape.529
  2.0 1.7 %gather_fusion = bf16[8,4,1536]{2,0,1:T(8,128)(2,1)S(1)} fusion(bf16[4,8,1536]{2,1,0:T(8,128)(2,1)} %param.14, s32[1024]{0:T(1024)S(1)} %pad_clamp_fusion.3), kind=kCustom, calls=%fused_computation | custom fusion | bytes 196640 | tf_op jit(solution)/shard_map/jit(_take)/gather | solution.py:164
  4.5 5.8 %all-to-all-start = ((bf16[4,8,1,1536]{3,0,2,1:T(4,128)(2,1)}), bf16[4,8,1,1536]{3,0,2,1:T(4,128)(2,1)S(1)}, u32[]{:S(2)}, u32[]{:S(2)}) async-start(bf16[4,8,1,1536]{3,0,2,1:T(4,128)(2,1)} %copy.86), calls=%async_computation | async-start | bytes 196608 | tf_op jit(solution)/shard_map/all_to_all | solution.py:165
  15.7 3.4 %convolution_convert_fusion.1 = bf16[32,1536]{1,0:T(8,128)(2,1)S(1)} fusion(bf16[1536,1536]{1,0:T(8,128)(2,1)} %param.21, f32[4,8,1,1536]{3,0,2,1:T(4,128)S(1)} %convert_element_type.115, f32[1536]{0:T(1024)S(1)} %copy-done.4, f32[32]{0:T(128)S(1)} %rsqrt.23), kind=kOutput, calls=%fused_computation.10 | convolution fusion | flops 151191552 | bytes 5019776 | tf_op jit(solution)/shard_map/dot_general | solution.py:176
  19.4 1.0 broadcast_in_dim.356
  20.4 5.5 %all-to-all-start.1 = ((bf16[8,4,8,1792]{3,2,1,0:T(8,128)(2,1)}), bf16[8,4,8,1792]{3,2,1,0:T(8,128)(2,1)S(1)}, u32[]{:S(2)}, u32[]{:S(2)}) async-start(bf16[8,4,8,1792]{3,2,1,0:T(8,128)(2,1)} %broadcast_in_dim.356), calls=%async_computation.1 | async-start | bytes 1835008 | tf_op jit(solution)/shard_map/all_to_all | solution.py:179
  27.5 7.8 %gather_fusion.5 = bf16[72,128,256]{2,1,0:T(8,128)(2,1)} fusion(bf16[72,128,256]{2,1,0:T(8,128)(2,1)} %param.19, s32[1024]{0:T(1024)S(1)} %pad_clamp_fusion), kind=kCustom, calls=%fused_computation.5 | custom fusion | bytes 9437472 | tf_op jit(solution)/shard_map/gather | solution.py:208
  36.1 3.0 %all-to-all-done.1 = bf16[8,4,8,1792]{3,2,1,0:T(8,128)(2,1)S(1)} async-done(((bf16[8,4,8,1792]{3,2,1,0:T(8,128)(2,1)}), bf16[8,4,8,1792]{3,2,1,0:T(8,128)(2,1)S(1)}, u32[]{:S(2)}, u32[]{:S(2)}) %all-to-all-start.1) | async-done | bytes 917536 | tf_op jit(solution)/shard_map/all_to_all | solution.py:179
  39.2 0.8 select_reduce_fusion.10
  40.2 0.9 copy.120
  41.2 1.4 copy.119
  42.6 16.1 %shard_map.136 = bf16[8,4,8,1536]{3,2,1,0:T(8,128)(2,1)} custom-call(s32[64]{0:T(128)} %reshape.533.bounds_ref, s32[32]{0:T(128)} %reshape.546.used_ref, bf16[8,4,96,128]{3,2,1,0:T(8,128)(2,1)} %bitcast.112, bf16[8,1152,256]{2,1,0:T(8,128)(2,1)} %bitcast.110, bf16[8,4,32,256]{3,2,1,0:T(8,128)(2,1)} %bitcast.113, f32[4,96,32]{2,1,0:T(8,128)} %and_convert_fusion.pick_ref), custom_call_target="tpu_custom_call" | custom-call | flops 1862270976 | bytes 6815744 | tf_op jit(solution)/shard_map/pallas_call | solution.py:98
  58.7 1.3 bitcast_select_fusion
  60.4 15.9 %all_to_all.29 = bf16[8,4,8,1536]{3,1,2,0:T(4,128)(2,1)S(1)} all-to-all(bf16[8,4,8,1536]{3,1,2,0:T(4,128)(2,1)S(1)} %copy.99), channel_id=1, replica_groups=mesh['req'=8,'y'=4,'zhi'=2,'zlo'=2] {'y','zlo'}, dimensions={0} | all-to-all | bytes 1572864 | tf_op jit(solution)/shard_map/all_to_all | solution.py:230
  76.8 3.3 %multiply_reduce_fusion = (f32[8,4]{0,1:T(4,128)S(1)}, bf16[8,4,1536]{2,0,1:T(8,128)(2,1)S(1)}) fusion(bf16[1536,1536]{1,0:T(8,128)(2,1)} %param.23, bf16[4,8,1536]{2,0,1:T(4,128)(2,1)S(1)} %reduce_sum.315, f32[4,8,1,1536]{3,0,2,1:T(4,128)S(1)} %convert_element_type.115), kind=kOutput, calls=%fused_computation.49 | convolution fusion | flops 151240672 | bytes 5111936 | tf_op jit(solution)/shard_map/dot_general | solution.py:236
  80.5 1.3 broadcast_in_dim.380
  81.8 5.1 %all-to-all-start.3 = ((bf16[16,32,1536]{2,1,0:T(8,128)(2,1)}), bf16[16,32,1536]{2,1,0:T(8,128)(2,1)S(1)}, u32[]{:S(2)}, u32[]{:S(2)}) async-start(bf16[16,32,1536]{2,1,0:T(8,128)(2,1)} %broadcast_in_dim.380), calls=%async_computation.3 | async-start | bytes 3145728 | tf_op jit(solution)/shard_map/all_to_all | solution.py:240
  86.9 18.1 %all-to-all-done.3 = bf16[16,32,1536]{2,1,0:T(8,128)(2,1)S(1)} async-done(((bf16[16,32,1536]{2,1,0:T(8,128)(2,1)}), bf16[16,32,1536]{2,1,0:T(8,128)(2,1)S(1)}, u32[]{:S(2)}, u32[]{:S(2)}) %all-to-all-start.3) | async-done | bytes 1572896 | tf_op jit(solution)/shard_map/all_to_all | solution.py:240
  107.4 1.0 convolution_convert_fusion
  108.4 1.4 all_to_all.22
  109.7 21.3 %all-to-all-start.4 = ((bf16[128,4,1536]{2,1,0:T(4,128)(2,1)}), bf16[128,4,1536]{2,1,0:T(4,128)(2,1)S(1)}, u32[]{:S(2)}, u32[]{:S(2)}) async-start(bf16[128,4,1536]{2,1,0:T(4,128)(2,1)} %all_to_all.22), calls=%async_computation.4 | async-start | bytes 3145728 | tf_op jit(solution)/shard_map/all_to_all | solution.py:258
  131.1 24.9 %all-to-all-done.4 = bf16[128,4,1536]{2,1,0:T(4,128)(2,1)S(1)} async-done(((bf16[128,4,1536]{2,1,0:T(4,128)(2,1)}), bf16[128,4,1536]{2,1,0:T(4,128)(2,1)S(1)}, u32[]{:S(2)}, u32[]{:S(2)}) %all-to-all-start.4) | async-done | bytes 1572896 | tf_op jit(solution)/shard_map/all_to_all | solution.py:258
  156.6 0.8 select_reduce_fusion
  (106 shorter events, 13.4 us)
Async XLA Ops:
  0.0 105.0 %copy-start = (bf16[1536,288]{0,1:T(8,128)(2,1)S(1)}, bf16[1536,288]{0,1:T(8,128)(2,1)}, u32[]{:S(2)}) copy-start(bf16[1536,288]{0,1:T(8,128)(2,1)} %param.25) | copy-start | bytes 2654212
  0.0 12.4 %copy-start.3 = (s32[8,9]{1,0:T(8,128)S(1)}, s32[8,9]{1,0:T(8,128)}, u32[]{:S(2)}) copy-start(s32[8,9]{1,0:T(8,128)} %param.18) | copy-start | bytes 868
  0.0 13.9 %copy-start.1 = (s32[128]{0:T(128)S(1)}, s32[128]{0:T(128)}, u32[]{:S(2)}) copy-start(s32[128]{0:T(128)} %param.15) | copy-start | bytes 1540
  0.0 15.7 %copy-start.4 = (f32[1536]{0:T(1024)S(1)}, f32[1536]{0:T(1024)}, u32[]{:S(2)}) copy-start(f32[1536]{0:T(1024)} %param.20) | copy-start | bytes 18436
  4.5 10.8 %all-to-all-start = ((bf16[4,8,1,1536]{3,0,2,1:T(4,128)(2,1)}), bf16[4,8,1,1536]{3,0,2,1:T(4,128)(2,1)S(1)}, u32[]{:S(2)}, u32[]{:S(2)}) async-start(bf16[4,8,1,1536]{3,0,2,1:T(4,128)(2,1)} %copy.86), calls=%async_computation | async-start | bytes 196608 | tf_op jit(solution)/shard_map/all_to_all | solution.py:165
  15.7 3.4 %copy-start.2 = (bf16[1536,256]{1,0:T(8,128)(2,1)S(1)}, bf16[1536,256]{1,0:T(8,128)(2,1)}, u32[]{:S(2)}) copy-start(bf16[1536,256]{1,0:T(8,128)(2,1)} %param.22) | copy-start | bytes 2359300
  20.4 18.8 %all-to-all-start.1 = ((bf16[8,4,8,1792]{3,2,1,0:T(8,128)(2,1)}), bf16[8,4,8,1792]{3,2,1,0:T(8,128)(2,1)S(1)}, u32[]{:S(2)}, u32[]{:S(2)}) async-start(bf16[8,4,8,1792]{3,2,1,0:T(8,128)(2,1)} %broadcast_in_dim.356), calls=%async_computation.1 | async-start | bytes 1835008 | tf_op jit(solution)/shard_map/all_to_all | solution.py:179
  76.7 3.6 %copy-start.5 = (f32[1536]{0:T(1024)S(1)}, f32[1536]{0:T(1024)}, u32[]{:S(2)}) copy-start(f32[1536]{0:T(1024)} %param.24) | copy-start | bytes 18436
  81.8 23.3 %all-to-all-start.3 = ((bf16[16,32,1536]{2,1,0:T(8,128)(2,1)}), bf16[16,32,1536]{2,1,0:T(8,128)(2,1)S(1)}, u32[]{:S(2)}, u32[]{:S(2)}) async-start(bf16[16,32,1536]{2,1,0:T(8,128)(2,1)} %broadcast_in_dim.380), calls=%async_computation.3 | async-start | bytes 3145728 | tf_op jit(solution)/shard_map/all_to_all | solution.py:240
  105.0 1.2 copy-start.6
  106.2 1.2 copy-start.7
  109.7 46.2 %all-to-all-start.4 = ((bf16[128,4,1536]{2,1,0:T(4,128)(2,1)}), bf16[128,4,1536]{2,1,0:T(4,128)(2,1)S(1)}, u32[]{:S(2)}, u32[]{:S(2)}) async-start(bf16[128,4,1536]{2,1,0:T(4,128)(2,1)} %all_to_all.22), calls=%async_computation.4 | async-start | bytes 3145728 | tf_op jit(solution)/shard_map/all_to_all | solution.py:258

commit v18 on v17

--- a/solution.py
+++ b/solution.py
@@ -41,7 +41,7 @@
     return jnp.sum(jnp.where(picks[..., None], table[None, :, :, :], 0), axis=1).astype(table.dtype)
 
 
-def attend_kernel(bounds_ref, used_ref, q_ref, kv_ref, new_ref, pick_ref, out_ref):
+def attend_kernel(bounds_ref, used_ref, q_ref, kv_ref, new_ref, pick_ref, held_ref, out_ref):
     r = pl.program_id(0)
     steps = q_ref.shape[1]
     head_dim = q_ref.shape[3]
@@ -79,17 +79,19 @@
             totals = total_c * scale_c + total_n * scale_n
             weighted = sum_c * scale_c + sum_n * scale_n
             attended = weighted / totals
+            kept = held_ref[0, t] > 0
             for h in range(out_ref.shape[3] // head_dim):
-                out_ref[0, t, :, h * head_dim : (h + 1) * head_dim] = attended[
-                    h * out_ref.shape[2] : (h + 1) * out_ref.shape[2]
-                ].astype(out_ref.dtype)
+                part = attended[h * out_ref.shape[2] : (h + 1) * out_ref.shape[2]]
+                out_ref[0, t, :, h * head_dim : (h + 1) * head_dim] = jnp.where(
+                    kept, part, 0.0
+                ).astype(out_ref.dtype)
 
         @pl.when(used_ref[r * steps + t] == 0)
         def _(t=t):
             out_ref[0, t] = jnp.zeros(out_ref.shape[2:], out_ref.dtype)
 
 
-def attend(bounds, used, queries, pages, entries, pick):
+def attend(bounds, used, queries, pages, entries, pick, held):
     rows, steps, count, head_dim = queries.shape
     out_rows = BEAMS
     out_width = count // BEAMS * head_dim
@@ -105,6 +107,7 @@
                 pl.BlockSpec((1, span, pages.shape[2]), lambda r, b, u: (r, 0, 0)),
                 pl.BlockSpec((1,) + entries.shape[1:], lambda r, b, u: (r, 0, 0, 0)),
                 pl.BlockSpec(pick.shape, lambda r, b, u: (0, 0, 0)),
+                pl.BlockSpec((1,) + held.shape[1:], lambda r, b, u: (r, 0, 0, 0)),
             ],
             out_specs=pl.BlockSpec((1, steps, out_rows, out_width), lambda r, b, u: (r, 0, 0, 0)),
         ),
@@ -114,7 +117,7 @@
             transcendentals=rows * steps * count * span,
             bytes_accessed=pages.size * 2 + queries.size * 4 + entries.size * 2,
         ),
-    )(bounds, used, queries, pages, entries, pick)
+    )(bounds, used, queries, pages, entries, pick, held)
 
 
 def on_device(
@@ -223,12 +226,13 @@
         & (column[None, None, :] // BEAMS <= step_ids[:, None, None])
     ).astype(jnp.float32)
     used = jnp.any(held, axis=0).T.astype(jnp.int32).reshape(rows * steps)
-    attended = attend(bounds, used, by_row, pages, entries_by_row, pick)
-    attended = jnp.transpose(attended, (2, 1, 0, 3))
-    attended = jnp.where(held[..., None], attended, jnp.zeros_like(attended))
-
-    received = lax.all_to_all(attended, HALF, split_axis=0, concat_axis=0, tiled=True)
-    attended_own = jnp.sum(received.astype(jnp.float32), axis=0).astype(jnp.bfloat16)
+    held_by_row = jnp.transpose(held, (2, 1, 0)).astype(jnp.float32)[..., None]
+    attended = attend(bounds, used, by_row, pages, entries_by_row, pick, held_by_row)
+
+    received = lax.all_to_all(attended, HALF, split_axis=2, concat_axis=2, tiled=True)
+    attended_own = jnp.swapaxes(
+        jnp.sum(received.astype(jnp.float32), axis=2).astype(jnp.bfloat16), 0, 1
+    )
 
     current = inputs.reshape(steps * rows, width)
     residual = (

time: 157 us -> 152 us (0.968)
  starting transfers between devices: 37.7 us -> 34.6 us
  Pallas kernels: 16.1 us -> 13.9 us
  local copies, waits for them, and re-layouts: 25 us -> 27.1 us
    all_to_all x1, starting transfers between devices: 21.3 us -> 11.4 us  [on_device(): lax.all_to_all(leaving, KV + ('req',), 0, 0, tiled=True)]
    all_to_all x1, starting transfers between devices: 5.09 us -> 11.8 us  [on_device(): lax.all_to_all(jnp.broadcast_to(mlp_own[None], (kv_count,) + mlp_own.shap...]
    pallas_call x1, Pallas kernels: 16.1 us -> 13.9 us  [attend(): pl.pallas_call(attend_kernel, grid_spec=pltpu.PrefetchScalarGridSpec(num_...]
    all_to_all x1, waiting for transfers between devices: 18.1 us -> 20.1 us  [on_device(): lax.all_to_all(jnp.broadcast_to(mlp_own[None], (kv_count,) + mlp_own.shap...]
  transfers between devices with their start and end apart: 4 -> 4, of which waited for: 4 -> 4; matrix products, arithmetic and copies ran while one was open for 9% -> 10% of each run, Pallas kernels for 0% -> 0%
where the time goes in v18:
time: 152 us; the launch traced here: 154 us
  waiting for transfers between devices  47.8 us (31%)
  starting transfers between devices  34.6 us (23%)
  local copies, waits for them, and re-layouts  27.1 us (18%)
  blocking collectives  15.6 us (10%)
  Pallas kernels  13.9 us (9%)
  matrix products  9.34 us (6%)
  other arithmetic  4.72 us (3%)
    all_to_all x1, waiting for transfers between devices, on_device(): lax.all_to_all(leaving, KV + ('req',), 0, 0, tiled=True)  24.9 us
    all_to_all x1, waiting for transfers between devices, on_device(): lax.all_to_all(jnp.broadcast_to(mlp_own[None], (kv_count,) + mlp_own.shap...  20.1 us
    all_to_all x1, blocking collectives, on_device(): lax.all_to_all(attended, HALF, split_axis=2, concat_axis=2, tiled=True)  15.6 us
    pallas_call x1, Pallas kernels, attend(): pl.pallas_call(attend_kernel, grid_spec=pltpu.PrefetchScalarGridSpec(num_...  13.9 us
    all_to_all x1, starting transfers between devices, on_device(): lax.all_to_all(jnp.broadcast_to(mlp_own[None], (kv_count,) + mlp_own.shap...  11.8 us
    all_to_all x1, starting transfers between devices, on_device(): lax.all_to_all(leaving, KV + ('req',), 0, 0, tiled=True)  11.4 us
    gather x1, local copies, waits for them, and re-layouts, on_device(): pool[table[offset_of] - device * pool.shape[0]]  7.81 us
    all_to_all x1, starting transfers between devices, on_device(): lax.all_to_all(outgoing, 'req', split_axis=1, concat_axis=1, tiled=True)  5.8 us
  transfers between devices with their start and end apart: 4, of which 4 were waited for; matrix products, arithmetic and copies ran while one was open for 10% of the time, Pallas kernels for 0%

profile of v18, /device:TPU:1, one launch (start us, length us, event | category | flops | bytes accessed | tf_op | source)
XLA Modules:
  0.0 153.6 jit_solution(2293159162893864509)
XLA Ops:
  0.0 0.8 reshape.497
  2.0 1.7 %gather_fusion = bf16[8,4,1536]{2,0,1:T(8,128)(2,1)S(1)} fusion(bf16[4,8,1536]{2,1,0:T(8,128)(2,1)} %param.14, s32[1024]{0:T(1024)S(1)} %pad_clamp_fusion.3), kind=kCustom, calls=%fused_computation | custom fusion | bytes 196640 | tf_op jit(solution)/shard_map/jit(_take)/gather | solution.py:167
  4.5 5.8 %all-to-all-start = ((bf16[4,8,1,1536]{3,0,2,1:T(4,128)(2,1)}), bf16[4,8,1,1536]{3,0,2,1:T(4,128)(2,1)S(1)}, u32[]{:S(2)}, u32[]{:S(2)}) async-start(bf16[4,8,1,1536]{3,0,2,1:T(4,128)(2,1)} %copy.77), calls=%async_computation | async-start | bytes 196608 | tf_op jit(solution)/shard_map/all_to_all | solution.py:168
  15.7 3.4 %convolution_convert_fusion.1 = bf16[32,1536]{1,0:T(8,128)(2,1)S(1)} fusion(bf16[1536,1536]{1,0:T(8,128)(2,1)} %param.21, f32[4,8,1,1536]{3,0,2,1:T(4,128)S(1)} %convert_element_type.120, f32[1536]{0:T(1024)S(1)} %copy-done.4, f32[32]{0:T(128)S(1)} %rsqrt.23), kind=kOutput, calls=%fused_computation.10 | convolution fusion | flops 151191552 | bytes 5019776 | tf_op jit(solution)/shard_map/dot_general | solution.py:179
  19.4 1.0 broadcast_in_dim.348
  20.4 5.5 %all-to-all-start.1 = ((bf16[8,4,8,1792]{3,2,1,0:T(8,128)(2,1)}), bf16[8,4,8,1792]{3,2,1,0:T(8,128)(2,1)S(1)}, u32[]{:S(2)}, u32[]{:S(2)}) async-start(bf16[8,4,8,1792]{3,2,1,0:T(8,128)(2,1)} %broadcast_in_dim.348), calls=%async_computation.1 | async-start | bytes 1835008 | tf_op jit(solution)/shard_map/all_to_all | solution.py:182
  25.9 0.9 copy.90.held_ref
  28.4 7.8 %gather_fusion.5 = bf16[72,128,256]{2,1,0:T(8,128)(2,1)} fusion(bf16[72,128,256]{2,1,0:T(8,128)(2,1)} %param.19, s32[1024]{0:T(1024)S(1)} %pad_clamp_fusion), kind=kCustom, calls=%fused_computation.5 | custom fusion | bytes 9437472 | tf_op jit(solution)/shard_map/gather | solution.py:211
  37.0 2.1 %all-to-all-done.1 = bf16[8,4,8,1792]{3,2,1,0:T(8,128)(2,1)S(1)} async-done(((bf16[8,4,8,1792]{3,2,1,0:T(8,128)(2,1)}), bf16[8,4,8,1792]{3,2,1,0:T(8,128)(2,1)S(1)}, u32[]{:S(2)}, u32[]{:S(2)}) %all-to-all-start.1) | async-done | bytes 917536 | tf_op jit(solution)/shard_map/all_to_all | solution.py:182
  39.2 0.8 select_reduce_fusion.10
  40.2 0.9 copy.114
  41.2 1.4 copy.113
  42.6 13.9 %shard_map.136 = bf16[8,4,8,1536]{3,2,1,0:T(8,128)(2,1)} custom-call(s32[64]{0:T(128)} %reshape.498.bounds_ref, s32[32]{0:T(128)} %reshape.513.used_ref, bf16[8,4,96,128]{3,2,1,0:T(8,128)(2,1)} %bitcast.115, bf16[8,1152,256]{2,1,0:T(8,128)(2,1)} %bitcast.113, bf16[8,4,32,256]{3,2,1,0:T(8,128)(2,1)} %bitcast.116, f32[4,96,32]{2,1,0:T(8,128)} %and_convert_fusion.pick_ref, ...), custom_call_target="tpu_custom_call" | custom-call | flops 1862270976 | bytes 6815744 | tf_op jit(solution)/shard_map/pallas_call | solution.py:100
  56.5 1.5 %copy.91 = bf16[8,4,8,1536]{3,1,0,2:T(4,128)(2,1)S(1)} copy(bf16[8,4,8,1536]{3,2,1,0:T(8,128)(2,1)} %shard_map.136) | data formatting | bytes 1572864 | tf_op jit(solution)/shard_map/pallas_call | solution.py:100
  58.0 15.6 %all_to_all.29 = bf16[8,4,8,1536]{3,1,0,2:T(4,128)(2,1)S(1)} all-to-all(bf16[8,4,8,1536]{3,1,0,2:T(4,128)(2,1)S(1)} %copy.91), channel_id=1, replica_groups=mesh['req'=8,'y'=4,'zhi'=2,'zlo'=2] {'y','zlo'}, dimensions={2} | all-to-all | bytes 1572864 | tf_op jit(solution)/shard_map/all_to_all | solution.py:232
  74.1 3.3 %multiply_reduce_fusion = (f32[8,4]{0,1:T(4,128)S(1)}, bf16[8,4,1536]{2,0,1:T(8,128)(2,1)S(1)}) fusion(bf16[1536,1536]{1,0:T(8,128)(2,1)} %param.23, bf16[4,8,1536]{2,0,1:T(4,128)(2,1)S(1)} %bitcast.119, f32[4,8,1,1536]{3,0,2,1:T(4,128)S(1)} %convert_element_type.120), kind=kOutput, calls=%fused_computation.48 | convolution fusion | flops 151240672 | bytes 5111936 | tf_op jit(solution)/shard_map/dot_general | solution.py:240
  77.8 1.3 broadcast_in_dim.373
  79.1 11.8 %all-to-all-start.3 = ((bf16[16,32,1536]{2,1,0:T(8,128)(2,1)}), bf16[16,32,1536]{2,1,0:T(8,128)(2,1)S(1)}, u32[]{:S(2)}, u32[]{:S(2)}) async-start(bf16[16,32,1536]{2,1,0:T(8,128)(2,1)} %broadcast_in_dim.373), calls=%async_computation.3 | async-start | bytes 3145728 | tf_op jit(solution)/shard_map/all_to_all | solution.py:244
  91.0 20.1 %all-to-all-done.3 = bf16[16,32,1536]{2,1,0:T(8,128)(2,1)S(1)} async-done(((bf16[16,32,1536]{2,1,0:T(8,128)(2,1)}), bf16[16,32,1536]{2,1,0:T(8,128)(2,1)S(1)}, u32[]{:S(2)}, u32[]{:S(2)}) %all-to-all-start.3) | async-done | bytes 1572896 | tf_op jit(solution)/shard_map/all_to_all | solution.py:244
  113.4 1.0 convolution_convert_fusion
  114.4 1.4 all_to_all.22
  115.8 11.4 %all-to-all-start.4 = ((bf16[128,4,1536]{2,1,0:T(4,128)(2,1)}), bf16[128,4,1536]{2,1,0:T(4,128)(2,1)S(1)}, u32[]{:S(2)}, u32[]{:S(2)}) async-start(bf16[128,4,1536]{2,1,0:T(4,128)(2,1)} %all_to_all.22), calls=%async_computation.4 | async-start | bytes 3145728 | tf_op jit(solution)/shard_map/all_to_all | solution.py:262
  127.2 24.9 %all-to-all-done.4 = bf16[128,4,1536]{2,1,0:T(4,128)(2,1)S(1)} async-done(((bf16[128,4,1536]{2,1,0:T(4,128)(2,1)}), bf16[128,4,1536]{2,1,0:T(4,128)(2,1)S(1)}, u32[]{:S(2)}, u32[]{:S(2)}) %all-to-all-start.4) | async-done | bytes 1572896 | tf_op jit(solution)/shard_map/all_to_all | solution.py:262
  152.8 0.8 select_reduce_fusion
  (106 shorter events, 13.7 us)
Async XLA Ops:
  0.0 111.1 %copy-start = (bf16[1536,288]{0,1:T(8,128)(2,1)S(1)}, bf16[1536,288]{0,1:T(8,128)(2,1)}, u32[]{:S(2)}) copy-start(bf16[1536,288]{0,1:T(8,128)(2,1)} %param.25) | copy-start | bytes 2654212
  0.0 12.4 %copy-start.3 = (s32[8,9]{1,0:T(8,128)S(1)}, s32[8,9]{1,0:T(8,128)}, u32[]{:S(2)}) copy-start(s32[8,9]{1,0:T(8,128)} %param.18) | copy-start | bytes 868
  0.0 13.9 %copy-start.1 = (s32[128]{0:T(128)S(1)}, s32[128]{0:T(128)}, u32[]{:S(2)}) copy-start(s32[128]{0:T(128)} %param.15) | copy-start | bytes 1540
  0.0 15.7 %copy-start.4 = (f32[1536]{0:T(1024)S(1)}, f32[1536]{0:T(1024)}, u32[]{:S(2)}) copy-start(f32[1536]{0:T(1024)} %param.20) | copy-start | bytes 18436
  4.5 10.8 %all-to-all-start = ((bf16[4,8,1,1536]{3,0,2,1:T(4,128)(2,1)}), bf16[4,8,1,1536]{3,0,2,1:T(4,128)(2,1)S(1)}, u32[]{:S(2)}, u32[]{:S(2)}) async-start(bf16[4,8,1,1536]{3,0,2,1:T(4,128)(2,1)} %copy.77), calls=%async_computation | async-start | bytes 196608 | tf_op jit(solution)/shard_map/all_to_all | solution.py:168
  15.7 3.4 %copy-start.2 = (bf16[1536,256]{1,0:T(8,128)(2,1)S(1)}, bf16[1536,256]{1,0:T(8,128)(2,1)}, u32[]{:S(2)}) copy-start(bf16[1536,256]{1,0:T(8,128)(2,1)} %param.22) | copy-start | bytes 2359300
  20.4 18.8 %all-to-all-start.1 = ((bf16[8,4,8,1792]{3,2,1,0:T(8,128)(2,1)}), bf16[8,4,8,1792]{3,2,1,0:T(8,128)(2,1)S(1)}, u32[]{:S(2)}, u32[]{:S(2)}) async-start(bf16[8,4,8,1792]{3,2,1,0:T(8,128)(2,1)} %broadcast_in_dim.348), calls=%async_computation.1 | async-start | bytes 1835008 | tf_op jit(solution)/shard_map/all_to_all | solution.py:182
  74.1 3.6 %copy-start.5 = (f32[1536]{0:T(1024)S(1)}, f32[1536]{0:T(1024)}, u32[]{:S(2)}) copy-start(f32[1536]{0:T(1024)} %param.24) | copy-start | bytes 18436
  79.1 31.9 %all-to-all-start.3 = ((bf16[16,32,1536]{2,1,0:T(8,128)(2,1)}), bf16[16,32,1536]{2,1,0:T(8,128)(2,1)S(1)}, u32[]{:S(2)}, u32[]{:S(2)}) async-start(bf16[16,32,1536]{2,1,0:T(8,128)(2,1)} %broadcast_in_dim.373), calls=%async_computation.3 | async-start | bytes 3145728 | tf_op jit(solution)/shard_map/all_to_all | solution.py:244
  111.1 1.2 copy-start.6
  112.2 1.2 copy-start.7
  115.8 36.4 %all-to-all-start.4 = ((bf16[128,4,1536]{2,1,0:T(4,128)(2,1)}), bf16[128,4,1536]{2,1,0:T(4,128)(2,1)S(1)}, u32[]{:S(2)}, u32[]{:S(2)}) async-start(bf16[128,4,1536]{2,1,0:T(4,128)(2,1)} %all_to_all.22), calls=%async_computation.4 | async-start | bytes 3145728 | tf_op jit(solution)/shard_map/all_to_all | solution.py:262

commit v19 on v17

--- a/solution.py
+++ b/solution.py
@@ -34,6 +34,14 @@
 def follow(index, table):
     picks = index[:, None, :] == jnp.arange(BEAMS, dtype=jnp.int32)[None, :, None]
     return jnp.sum(jnp.where(picks, table[None, :, :], 0), axis=1)
+
+
+def pick_by_row(index, table):
+    picks = index.T[:, :, None] == jnp.arange(BEAMS, dtype=jnp.int32)[None, None, :]
+    rows_first = jnp.swapaxes(table, 0, 1)
+    return jnp.sum(
+        jnp.where(picks[..., None], rows_first[:, None, :, :], 0), axis=2
+    ).astype(table.dtype)
 
 
 def pick_rows(index, table):
@@ -196,11 +204,11 @@
         cache_beam = follow(family[step_index], cache_beam)
         sources = [follow(family[step_index], source) for source in sources] + [own]
         cache_beams.append(cache_beam)
-        picked = [pick_rows(source, entries[:, s]) for s, source in enumerate(sources)]
+        picked = [pick_by_row(source, entries[:, s]) for s, source in enumerate(sources)]
         picked += [jnp.zeros_like(picked[0])] * (steps - 1 - step_index)
-        listed.append(jnp.stack(picked))
+        listed.append(jnp.stack(picked, axis=1))
     held = jnp.stack(cache_beams, axis=1) == beam
-    listed = jnp.stack(listed)
+    listed = jnp.stack(listed, axis=1)
 
     length = lengths[serving[offset_of]]
     first_page = jnp.maximum(length - WINDOW + 1, 0) // PAGE
@@ -213,9 +221,7 @@
     hi = jnp.broadcast_to((length - base)[:, None], (rows, steps))
     bounds = jnp.stack([lo, hi], axis=-1).reshape(rows * steps * 2)
     by_row = jnp.transpose(queries, (2, 1, 3, 0, 4)).reshape(rows, steps, heads * BEAMS, head_dim)
-    entries_by_row = jnp.transpose(listed, (3, 0, 1, 2, 4)).reshape(
-        rows, steps, steps * BEAMS, 2 * head_dim
-    )
+    entries_by_row = listed.reshape(rows, steps, steps * BEAMS, 2 * head_dim)
     row_beam = jnp.arange(BEAMS * heads, dtype=jnp.int32) % BEAMS
     column = jnp.arange(steps * BEAMS, dtype=jnp.int32)
     pick = (

time: 157 us -> 154 us (0.981); the launches traced: 157 us -> 152 us
  starting transfers between devices: 37.7 us -> 30.9 us
  blocking collectives: 15.9 us -> 18.1 us
  Pallas kernels: 16.1 us -> 14.2 us
  other arithmetic: 5.96 us -> 7.8 us
    all_to_all x1, starting transfers between devices: 21.3 us -> 12.7 us  [on_device(): lax.all_to_all(leaving, KV + ('req',), 0, 0, tiled=True)]
    all_to_all x1, blocking collectives: 15.9 us -> 18.1 us  [on_device(): lax.all_to_all(attended, HALF, split_axis=0, concat_axis=0, tiled=True)]
    pallas_call x1, Pallas kernels: 16.1 us -> 14.2 us  [attend(): pl.pallas_call(attend_kernel, grid_spec=pltpu.PrefetchScalarGridSpec(num_...]
    all_to_all x1, starting transfers between devices: 5.09 us -> 6.83 us  [on_device(): lax.all_to_all(jnp.broadcast_to(mlp_own[None], (kv_count,) + mlp_own.shap...]
  transfers between devices with their start and end apart: 4 -> 4, of which waited for: 4 -> 4; matrix products, arithmetic and copies ran while one was open for 9% -> 10% of each run, Pallas kernels for 0% -> 0%
where the time goes in v19:
time: 154 us; the launch traced here: 152 us
  waiting for transfers between devices  46.6 us (30%)
  starting transfers between devices  30.9 us (20%)
  local copies, waits for them, and re-layouts  24.6 us (16%)
  blocking collectives  18.1 us (12%)
  Pallas kernels  14.2 us (9%)
  matrix products  9.33 us (6%)
  other arithmetic  7.8 us (5%)
    all_to_all x1, waiting for transfers between devices, on_device(): lax.all_to_all(leaving, KV + ('req',), 0, 0, tiled=True)  24.9 us
    all_to_all x1, waiting for transfers between devices, on_device(): lax.all_to_all(jnp.broadcast_to(mlp_own[None], (kv_count,) + mlp_own.shap...  18.7 us
    all_to_all x1, blocking collectives, on_device(): lax.all_to_all(attended, HALF, split_axis=0, concat_axis=0, tiled=True)  18.1 us
    pallas_call x1, Pallas kernels, attend(): pl.pallas_call(attend_kernel, grid_spec=pltpu.PrefetchScalarGridSpec(num_...  14.2 us
    all_to_all x1, starting transfers between devices, on_device(): lax.all_to_all(leaving, KV + ('req',), 0, 0, tiled=True)  12.7 us
    gather x1, local copies, waits for them, and re-layouts, on_device(): pool[table[offset_of] - device * pool.shape[0]]  7.82 us
    all_to_all x1, starting transfers between devices, on_device(): lax.all_to_all(jnp.broadcast_to(mlp_own[None], (kv_count,) + mlp_own.shap...  6.83 us
    all_to_all x1, starting transfers between devices, on_device(): lax.all_to_all(outgoing, 'req', split_axis=1, concat_axis=1, tiled=True)  5.8 us
  transfers between devices with their start and end apart: 4, of which 4 were waited for; matrix products, arithmetic and copies ran while one was open for 10% of the time, Pallas kernels for 0%

profile of v19, /device:TPU:1, one launch (start us, length us, event | category | flops | bytes accessed | tf_op | source)
XLA Modules:
  0.0 152.0 jit_solution(5553084909537259523)
XLA Ops:
  0.0 0.8 reshape.541
  0.8 0.7 reshape.540
  2.0 1.7 %gather_fusion = bf16[8,4,1536]{2,0,1:T(8,128)(2,1)S(1)} fusion(bf16[4,8,1536]{2,1,0:T(8,128)(2,1)} %param.14, s32[1024]{0:T(1024)S(1)} %pad_clamp_fusion.3), kind=kCustom, calls=%fused_computation | custom fusion | bytes 196640 | tf_op jit(solution)/shard_map/jit(_take)/gather | solution.py:172
  4.5 5.8 %all-to-all-start = ((bf16[4,8,1,1536]{3,0,2,1:T(4,128)(2,1)}), bf16[4,8,1,1536]{3,0,2,1:T(4,128)(2,1)S(1)}, u32[]{:S(2)}, u32[]{:S(2)}) async-start(bf16[4,8,1,1536]{3,0,2,1:T(4,128)(2,1)} %copy.122), calls=%async_computation | async-start | bytes 196608 | tf_op jit(solution)/shard_map/all_to_all | solution.py:173
  15.7 3.4 %convolution_convert_fusion.1 = bf16[32,1536]{1,0:T(8,128)(2,1)S(1)} fusion(bf16[1536,1536]{1,0:T(8,128)(2,1)} %param.21, f32[4,8,1,1536]{3,0,2,1:T(4,128)S(1)} %convert_element_type.115, f32[1536]{0:T(1024)S(1)} %copy-done.4, f32[32]{0:T(128)S(1)} %rsqrt.23), kind=kOutput, calls=%fused_computation.10 | convolution fusion | flops 151191552 | bytes 5019776 | tf_op jit(solution)/shard_map/dot_general | solution.py:184
  19.4 1.0 broadcast_in_dim.365
  20.4 5.5 %all-to-all-start.1 = ((bf16[8,4,8,1792]{3,2,1,0:T(8,128)(2,1)}), bf16[8,4,8,1792]{3,2,1,0:T(8,128)(2,1)S(1)}, u32[]{:S(2)}, u32[]{:S(2)}) async-start(bf16[8,4,8,1792]{3,2,1,0:T(8,128)(2,1)} %broadcast_in_dim.365), calls=%async_computation.1 | async-start | bytes 1835008 | tf_op jit(solution)/shard_map/all_to_all | solution.py:187
  27.6 7.8 %gather_fusion.5 = bf16[72,128,256]{2,1,0:T(8,128)(2,1)} fusion(bf16[72,128,256]{2,1,0:T(8,128)(2,1)} %param.19, s32[1024]{0:T(1024)S(1)} %pad_clamp_fusion), kind=kCustom, calls=%fused_computation.5 | custom fusion | bytes 9437472 | tf_op jit(solution)/shard_map/gather | solution.py:216
  36.2 2.9 %all-to-all-done.1 = bf16[8,4,8,1792]{3,2,1,0:T(8,128)(2,1)S(1)} async-done(((bf16[8,4,8,1792]{3,2,1,0:T(8,128)(2,1)}), bf16[8,4,8,1792]{3,2,1,0:T(8,128)(2,1)S(1)}, u32[]{:S(2)}, u32[]{:S(2)}) %all-to-all-start.1) | async-done | bytes 917536 | tf_op jit(solution)/shard_map/all_to_all | solution.py:187
  39.3 1.4 copy.171
  40.7 1.4 select_reduce_fusion.10
  42.3 0.9 pad_maximum_fusion.new_ref
  43.1 14.2 %shard_map.136 = bf16[8,4,8,1536]{3,2,1,0:T(8,128)(2,1)} custom-call(s32[64]{0:T(128)} %reshape.544.bounds_ref, s32[32]{0:T(128)} %reshape.556.used_ref, bf16[8,4,96,128]{3,2,1,0:T(8,128)(2,1)} %bitcast.129, bf16[8,1152,256]{2,1,0:T(8,128)(2,1)} %bitcast.127, bf16[8,4,32,256]{3,2,1,0:T(8,128)(2,1)} %pad_maximum_fusion.new_ref, ...), custom_call_target="tpu_custom_call" | custom-call | flops 1862270976 | bytes 6815744 | tf_op jit(solution)/shard_map/pallas_call | solution.py:106
  57.3 1.3 bitcast_select_fusion
  59.0 18.1 %all_to_all.29 = bf16[8,4,8,1536]{3,1,2,0:T(4,128)(2,1)S(1)} all-to-all(bf16[8,4,8,1536]{3,1,2,0:T(4,128)(2,1)S(1)} %copy.150), channel_id=1, replica_groups=mesh['req'=8,'y'=4,'zhi'=2,'zlo'=2] {'y','zlo'}, dimensions={0} | all-to-all | bytes 1572864 | tf_op jit(solution)/shard_map/all_to_all | solution.py:236
  77.6 3.3 %multiply_reduce_fusion = (f32[8,4]{0,1:T(4,128)S(1)}, bf16[8,4,1536]{2,0,1:T(8,128)(2,1)S(1)}) fusion(bf16[1536,1536]{1,0:T(8,128)(2,1)} %param.23, bf16[4,8,1536]{2,0,1:T(4,128)(2,1)S(1)} %reduce_sum.315, f32[4,8,1,1536]{3,0,2,1:T(4,128)S(1)} %convert_element_type.115), kind=kOutput, calls=%fused_computation.48 | convolution fusion | flops 151240672 | bytes 5111936 | tf_op jit(solution)/shard_map/dot_general | solution.py:242
  81.3 1.3 broadcast_in_dim.385
  82.6 6.8 %all-to-all-start.3 = ((bf16[16,32,1536]{2,1,0:T(8,128)(2,1)}), bf16[16,32,1536]{2,1,0:T(8,128)(2,1)S(1)}, u32[]{:S(2)}, u32[]{:S(2)}) async-start(bf16[16,32,1536]{2,1,0:T(8,128)(2,1)} %broadcast_in_dim.385), calls=%async_computation.3 | async-start | bytes 3145728 | tf_op jit(solution)/shard_map/all_to_all | solution.py:246
  89.5 18.7 %all-to-all-done.3 = bf16[16,32,1536]{2,1,0:T(8,128)(2,1)S(1)} async-done(((bf16[16,32,1536]{2,1,0:T(8,128)(2,1)}), bf16[16,32,1536]{2,1,0:T(8,128)(2,1)S(1)}, u32[]{:S(2)}, u32[]{:S(2)}) %all-to-all-start.3) | async-done | bytes 1572896 | tf_op jit(solution)/shard_map/all_to_all | solution.py:246
  110.5 1.0 convolution_convert_fusion
  111.5 1.4 all_to_all.22
  112.9 12.7 %all-to-all-start.4 = ((bf16[128,4,1536]{2,1,0:T(4,128)(2,1)}), bf16[128,4,1536]{2,1,0:T(4,128)(2,1)S(1)}, u32[]{:S(2)}, u32[]{:S(2)}) async-start(bf16[128,4,1536]{2,1,0:T(4,128)(2,1)} %all_to_all.22), calls=%async_computation.4 | async-start | bytes 3145728 | tf_op jit(solution)/shard_map/all_to_all | solution.py:264
  125.6 24.9 %all-to-all-done.4 = bf16[128,4,1536]{2,1,0:T(4,128)(2,1)S(1)} async-done(((bf16[128,4,1536]{2,1,0:T(4,128)(2,1)}), bf16[128,4,1536]{2,1,0:T(4,128)(2,1)S(1)}, u32[]{:S(2)}, u32[]{:S(2)}) %all-to-all-start.4) | async-done | bytes 1572896 | tf_op jit(solution)/shard_map/all_to_all | solution.py:264
  151.2 0.8 select_reduce_fusion
  (117 shorter events, 13.5 us)
Async XLA Ops:
  0.0 108.2 %copy-start = (bf16[1536,288]{0,1:T(8,128)(2,1)S(1)}, bf16[1536,288]{0,1:T(8,128)(2,1)}, u32[]{:S(2)}) copy-start(bf16[1536,288]{0,1:T(8,128)(2,1)} %param.25) | copy-start | bytes 2654212
  0.0 13.1 %copy-start.3 = (s32[8,9]{1,0:T(8,128)S(1)}, s32[8,9]{1,0:T(8,128)}, u32[]{:S(2)}) copy-start(s32[8,9]{1,0:T(8,128)} %param.18) | copy-start | bytes 868
  0.0 14.5 %copy-start.1 = (s32[128]{0:T(128)S(1)}, s32[128]{0:T(128)}, u32[]{:S(2)}) copy-start(s32[128]{0:T(128)} %param.15) | copy-start | bytes 1540
  0.0 15.7 %copy-start.4 = (f32[1536]{0:T(1024)S(1)}, f32[1536]{0:T(1024)}, u32[]{:S(2)}) copy-start(f32[1536]{0:T(1024)} %param.20) | copy-start | bytes 18436
  4.5 10.8 %all-to-all-start = ((bf16[4,8,1,1536]{3,0,2,1:T(4,128)(2,1)}), bf16[4,8,1,1536]{3,0,2,1:T(4,128)(2,1)S(1)}, u32[]{:S(2)}, u32[]{:S(2)}) async-start(bf16[4,8,1,1536]{3,0,2,1:T(4,128)(2,1)} %copy.122), calls=%async_computation | async-start | bytes 196608 | tf_op jit(solution)/shard_map/all_to_all | solution.py:173
  15.7 3.4 %copy-start.2 = (bf16[1536,256]{1,0:T(8,128)(2,1)S(1)}, bf16[1536,256]{1,0:T(8,128)(2,1)}, u32[]{:S(2)}) copy-start(bf16[1536,256]{1,0:T(8,128)(2,1)} %param.22) | copy-start | bytes 2359300
  20.4 18.8 %all-to-all-start.1 = ((bf16[8,4,8,1792]{3,2,1,0:T(8,128)(2,1)}), bf16[8,4,8,1792]{3,2,1,0:T(8,128)(2,1)S(1)}, u32[]{:S(2)}, u32[]{:S(2)}) async-start(bf16[8,4,8,1792]{3,2,1,0:T(8,128)(2,1)} %broadcast_in_dim.365), calls=%async_computation.1 | async-start | bytes 1835008 | tf_op jit(solution)/shard_map/all_to_all | solution.py:187
  77.6 3.6 %copy-start.5 = (f32[1536]{0:T(1024)S(1)}, f32[1536]{0:T(1024)}, u32[]{:S(2)}) copy-start(f32[1536]{0:T(1024)} %param.24) | copy-start | bytes 18436
  82.6 25.6 %all-to-all-start.3 = ((bf16[16,32,1536]{2,1,0:T(8,128)(2,1)}), bf16[16,32,1536]{2,1,0:T(8,128)(2,1)S(1)}, u32[]{:S(2)}, u32[]{:S(2)}) async-start(bf16[16,32,1536]{2,1,0:T(8,128)(2,1)} %broadcast_in_dim.385), calls=%async_computation.3 | async-start | bytes 3145728 | tf_op jit(solution)/shard_map/all_to_all | solution.py:246
  108.2 1.2 copy-start.6
  109.3 1.2 copy-start.7
  112.9 37.6 %all-to-all-start.4 = ((bf16[128,4,1536]{2,1,0:T(4,128)(2,1)}), bf16[128,4,1536]{2,1,0:T(4,128)(2,1)S(1)}, u32[]{:S(2)}, u32[]{:S(2)}) async-start(bf16[128,4,1536]{2,1,0:T(4,128)(2,1)} %all_to_all.22), calls=%async_computation.4 | async-start | bytes 3145728 | tf_op jit(solution)/shard_map/all_to_all | solution.py:264

commit v20 on v19

--- a/solution.py
+++ b/solution.py
@@ -204,11 +204,14 @@
         cache_beam = follow(family[step_index], cache_beam)
         sources = [follow(family[step_index], source) for source in sources] + [own]
         cache_beams.append(cache_beam)
-        picked = [pick_by_row(source, entries[:, s]) for s, source in enumerate(sources)]
-        picked += [jnp.zeros_like(picked[0])] * (steps - 1 - step_index)
-        listed.append(jnp.stack(picked, axis=1))
+        listed.append(jnp.stack(sources + [jnp.full_like(own, -1)] * (steps - 1 - step_index)))
     held = jnp.stack(cache_beams, axis=1) == beam
-    listed = jnp.stack(listed, axis=1)
+    source_of = jnp.transpose(jnp.stack(listed), (3, 0, 1, 2))
+    chosen = source_of[..., None] == jnp.arange(BEAMS, dtype=jnp.int32)
+    by_source = jnp.transpose(entries, (2, 1, 0, 3))
+    listed = jnp.sum(
+        jnp.where(chosen[..., None], by_source[:, None, :, None, :, :], 0), axis=4
+    ).astype(entries.dtype)
 
     length = lengths[serving[offset_of]]
     first_page = jnp.maximum(length - WINDOW + 1, 0) // PAGE

time: 154 us -> 157 us (1.019)
  blocking collectives: 18.1 us -> 26 us
  starting transfers between devices: 30.9 us -> 26.8 us
  Pallas kernels: 14.2 us -> 12.5 us
    all_to_all x1, blocking collectives: 18.1 us -> 26 us  [on_device(): lax.all_to_all(attended, HALF, split_axis=0, concat_axis=0, tiled=True)]
    all_to_all x1, starting transfers between devices: 6.83 us -> 4.12 us  [on_device(): lax.all_to_all(jnp.broadcast_to(mlp_own[None], (kv_count,) + mlp_own.shap...]
    reduce_sum x1, other arithmetic: 1.4 us -> 3.26 us  [on_device(): jnp.sum(jnp.where(chosen[..., None], by_source[:, None, :, None, :, :], 0...]
    pallas_call x1, Pallas kernels: 14.2 us -> 12.5 us  [attend(): pl.pallas_call(attend_kernel, grid_spec=pltpu.PrefetchScalarGridSpec(num_...]
  transfers between devices with their start and end apart: 4 -> 4, of which waited for: 4 -> 3; matrix products, arithmetic and copies ran while one was open for 10% -> 10% of each run, Pallas kernels for 0% -> 0%
where the time goes in v20:
time: 157 us; the launch traced here: 156 us
  waiting for transfers between devices  47.8 us (30%)
  starting transfers between devices  26.8 us (17%)
  blocking collectives  26 us (17%)
  local copies, waits for them, and re-layouts  25 us (16%)
  Pallas kernels  12.5 us (8%)
  matrix products  9.33 us (6%)
  other arithmetic  8.48 us (5%)
    all_to_all x1, blocking collectives, on_device(): lax.all_to_all(attended, HALF, split_axis=0, concat_axis=0, tiled=True)  26 us
    all_to_all x1, waiting for transfers between devices, on_device(): lax.all_to_all(leaving, KV + ('req',), 0, 0, tiled=True)  24.9 us
    all_to_all x1, waiting for transfers between devices, on_device(): lax.all_to_all(jnp.broadcast_to(mlp_own[None], (kv_count,) + mlp_own.shap...  20.1 us
    pallas_call x1, Pallas kernels, attend(): pl.pallas_call(attend_kernel, grid_spec=pltpu.PrefetchScalarGridSpec(num_...  12.5 us
    all_to_all x1, starting transfers between devices, on_device(): lax.all_to_all(leaving, KV + ('req',), 0, 0, tiled=True)  11.3 us
    gather x1, local copies, waits for them, and re-layouts, on_device(): pool[table[offset_of] - device * pool.shape[0]]  7.81 us
    all_to_all x1, starting transfers between devices, on_device(): lax.all_to_all(outgoing, 'req', split_axis=1, concat_axis=1, tiled=True)  5.8 us
    all_to_all x1, starting transfers between devices, on_device(): lax.all_to_all(jnp.broadcast_to(packed[None], (BEAMS,) + packed.shape), H...  5.54 us
  transfers between devices with their start and end apart: 4, of which 3 were waited for; matrix products, arithmetic and copies ran while one was open for 10% of the time, Pallas kernels for 0%

profile of v20, /device:TPU:1, one launch (start us, length us, event | category | flops | bytes accessed | tf_op | source)
XLA Modules:
  0.0 156.3 jit_solution(10433727566353418139)
XLA Ops:
  0.0 0.8 reshape.502
  0.8 0.7 reshape.501
  2.0 1.7 %gather_fusion = bf16[8,4,1536]{2,0,1:T(8,128)(2,1)S(1)} fusion(bf16[4,8,1536]{2,1,0:T(8,128)(2,1)} %param.14, s32[1024]{0:T(1024)S(1)} %pad_clamp_fusion.3), kind=kCustom, calls=%fused_computation | custom fusion | bytes 196640 | tf_op jit(solution)/shard_map/jit(_take)/gather | solution.py:172
  4.5 5.8 %all-to-all-start = ((bf16[4,8,1,1536]{3,0,2,1:T(4,128)(2,1)}), bf16[4,8,1,1536]{3,0,2,1:T(4,128)(2,1)S(1)}, u32[]{:S(2)}, u32[]{:S(2)}) async-start(bf16[4,8,1,1536]{3,0,2,1:T(4,128)(2,1)} %copy.92), calls=%async_computation | async-start | bytes 196608 | tf_op jit(solution)/shard_map/all_to_all | solution.py:173
  12.2 1.2 gather_fusion.4
  15.7 3.4 %convolution_convert_fusion.1 = bf16[32,1536]{1,0:T(8,128)(2,1)S(1)} fusion(bf16[1536,1536]{1,0:T(8,128)(2,1)} %param.21, f32[4,8,1,1536]{3,0,2,1:T(4,128)S(1)} %convert_element_type.88, f32[1536]{0:T(1024)S(1)} %copy-done.3, f32[32]{0:T(128)S(1)} %rsqrt.23), kind=kOutput, calls=%fused_computation.11 | convolution fusion | flops 151191552 | bytes 5019776 | tf_op jit(solution)/shard_map/dot_general | solution.py:184
  19.4 1.0 broadcast_in_dim.239
  20.4 5.5 %all-to-all-start.1 = ((bf16[8,4,8,1792]{3,2,1,0:T(8,128)(2,1)}), bf16[8,4,8,1792]{3,2,1,0:T(8,128)(2,1)S(1)}, u32[]{:S(2)}, u32[]{:S(2)}) async-start(bf16[8,4,8,1792]{3,2,1,0:T(8,128)(2,1)} %broadcast_in_dim.239), calls=%async_computation.1 | async-start | bytes 1835008 | tf_op jit(solution)/shard_map/all_to_all | solution.py:187
  27.6 7.8 %gather_fusion.5 = bf16[72,128,256]{2,1,0:T(8,128)(2,1)} fusion(bf16[72,128,256]{2,1,0:T(8,128)(2,1)} %param.19, s32[1024]{0:T(1024)S(1)} %pad_clamp_fusion), kind=kCustom, calls=%fused_computation.5 | custom fusion | bytes 9437472 | tf_op jit(solution)/shard_map/gather | solution.py:219
  36.4 2.9 %all-to-all-done.1 = bf16[8,4,8,1792]{3,2,1,0:T(8,128)(2,1)S(1)} async-done(((bf16[8,4,8,1792]{3,2,1,0:T(8,128)(2,1)}), bf16[8,4,8,1792]{3,2,1,0:T(8,128)(2,1)S(1)}, u32[]{:S(2)}, u32[]{:S(2)}) %all-to-all-start.1) | async-done | bytes 917536 | tf_op jit(solution)/shard_map/all_to_all | solution.py:187
  39.4 1.4 copy.125
  40.8 3.3 %select_reduce_fusion = bf16[8,4,4,8,256]{4,3,2,1,0:T(8,128)(2,1)} fusion(pred[8,4,4,8,8]{4,3,2,1,0:T(8,128)(4,1)S(1)} %iota_compare_fusion, bf16[8,4,8,256]{3,2,1,0:T(8,128)(2,1)S(1)} %copy.105), kind=kLoop, calls=%fused_computation.6 | loop fusion | flops 3932160 | bytes 663552 | tf_op jit(solution)/shard_map/reduce_sum | solution.py:212
  44.1 12.5 %shard_map.136 = bf16[8,4,8,1536]{3,2,1,0:T(8,128)(2,1)} custom-call(s32[64]{0:T(128)} %reshape.505.bounds_ref, s32[32]{0:T(128)} %reshape.518.used_ref, bf16[8,4,96,128]{3,2,1,0:T(8,128)(2,1)} %bitcast.100, bf16[8,1152,256]{2,1,0:T(8,128)(2,1)} %bitcast.98, bf16[8,4,32,256]{3,2,1,0:T(8,128)(2,1)} %bitcast.101, f32[4,96,32]{2,1,0:T(8,128)} %and_convert_fusion.pick_ref), custom_call_target="tpu_custom_call" | custom-call | flops 1862270976 | bytes 6815744 | tf_op jit(solution)/shard_map/pallas_call | solution.py:106
  56.5 1.3 bitcast_select_fusion
  58.2 26.0 %all_to_all.29 = bf16[8,4,8,1536]{3,1,2,0:T(4,128)(2,1)S(1)} all-to-all(bf16[8,4,8,1536]{3,1,2,0:T(4,128)(2,1)S(1)} %copy.106), channel_id=1, replica_groups=mesh['req'=8,'y'=4,'zhi'=2,'zlo'=2] {'y','zlo'}, dimensions={0} | all-to-all | bytes 1572864 | tf_op jit(solution)/shard_map/all_to_all | solution.py:239
  84.6 3.3 %multiply_reduce_fusion = (f32[8,4]{0,1:T(4,128)S(1)}, bf16[8,4,1536]{2,0,1:T(8,128)(2,1)S(1)}) fusion(bf16[1536,1536]{1,0:T(8,128)(2,1)} %param.23, bf16[4,8,1536]{2,0,1:T(4,128)(2,1)S(1)} %reduce_sum.198, f32[4,8,1,1536]{3,0,2,1:T(4,128)S(1)} %convert_element_type.88), kind=kOutput, calls=%fused_computation.39 | convolution fusion | flops 151240672 | bytes 5111936 | tf_op jit(solution)/shard_map/dot_general | solution.py:245
  88.3 1.3 broadcast_in_dim.250
  89.6 4.1 %all-to-all-start.3 = ((bf16[16,32,1536]{2,1,0:T(8,128)(2,1)}), bf16[16,32,1536]{2,1,0:T(8,128)(2,1)S(1)}, u32[]{:S(2)}, u32[]{:S(2)}) async-start(bf16[16,32,1536]{2,1,0:T(8,128)(2,1)} %broadcast_in_dim.250), calls=%async_computation.3 | async-start | bytes 3145728 | tf_op jit(solution)/shard_map/all_to_all | solution.py:249
  93.8 20.1 %all-to-all-done.3 = bf16[16,32,1536]{2,1,0:T(8,128)(2,1)S(1)} async-done(((bf16[16,32,1536]{2,1,0:T(8,128)(2,1)}), bf16[16,32,1536]{2,1,0:T(8,128)(2,1)S(1)}, u32[]{:S(2)}, u32[]{:S(2)}) %all-to-all-start.3) | async-done | bytes 1572896 | tf_op jit(solution)/shard_map/all_to_all | solution.py:249
  116.2 1.0 convolution_convert_fusion
  117.2 1.4 all_to_all.22
  118.6 11.3 %all-to-all-start.4 = ((bf16[128,4,1536]{2,1,0:T(4,128)(2,1)}), bf16[128,4,1536]{2,1,0:T(4,128)(2,1)S(1)}, u32[]{:S(2)}, u32[]{:S(2)}) async-start(bf16[128,4,1536]{2,1,0:T(4,128)(2,1)} %all_to_all.22), calls=%async_computation.4 | async-start | bytes 3145728 | tf_op jit(solution)/shard_map/all_to_all | solution.py:267
  129.9 24.9 %all-to-all-done.4 = bf16[128,4,1536]{2,1,0:T(4,128)(2,1)S(1)} async-done(((bf16[128,4,1536]{2,1,0:T(4,128)(2,1)}), bf16[128,4,1536]{2,1,0:T(4,128)(2,1)S(1)}, u32[]{:S(2)}, u32[]{:S(2)}) %all-to-all-start.4) | async-done | bytes 1572896 | tf_op jit(solution)/shard_map/all_to_all | solution.py:267
  155.5 0.8 select_reduce_fusion.1
  (103 shorter events, 12.3 us)
Async XLA Ops:
  0.0 113.9 %copy-start = (bf16[1536,288]{0,1:T(8,128)(2,1)S(1)}, bf16[1536,288]{0,1:T(8,128)(2,1)}, u32[]{:S(2)}) copy-start(bf16[1536,288]{0,1:T(8,128)(2,1)} %param.25) | copy-start | bytes 2654212
  0.0 14.5 %copy-start.1 = (s32[128]{0:T(128)S(1)}, s32[128]{0:T(128)}, u32[]{:S(2)}) copy-start(s32[128]{0:T(128)} %param.15) | copy-start | bytes 1540
  0.0 15.7 %copy-start.3 = (f32[1536]{0:T(1024)S(1)}, f32[1536]{0:T(1024)}, u32[]{:S(2)}) copy-start(f32[1536]{0:T(1024)} %param.20) | copy-start | bytes 18436
  4.5 10.8 %all-to-all-start = ((bf16[4,8,1,1536]{3,0,2,1:T(4,128)(2,1)}), bf16[4,8,1,1536]{3,0,2,1:T(4,128)(2,1)S(1)}, u32[]{:S(2)}, u32[]{:S(2)}) async-start(bf16[4,8,1,1536]{3,0,2,1:T(4,128)(2,1)} %copy.92), calls=%async_computation | async-start | bytes 196608 | tf_op jit(solution)/shard_map/all_to_all | solution.py:173
  15.7 3.4 %copy-start.2 = (bf16[1536,256]{1,0:T(8,128)(2,1)S(1)}, bf16[1536,256]{1,0:T(8,128)(2,1)}, u32[]{:S(2)}) copy-start(bf16[1536,256]{1,0:T(8,128)(2,1)} %param.22) | copy-start | bytes 2359300
  20.4 18.8 %all-to-all-start.1 = ((bf16[8,4,8,1792]{3,2,1,0:T(8,128)(2,1)}), bf16[8,4,8,1792]{3,2,1,0:T(8,128)(2,1)S(1)}, u32[]{:S(2)}, u32[]{:S(2)}) async-start(bf16[8,4,8,1792]{3,2,1,0:T(8,128)(2,1)} %broadcast_in_dim.239), calls=%async_computation.1 | async-start | bytes 1835008 | tf_op jit(solution)/shard_map/all_to_all | solution.py:187
  84.6 3.6 %copy-start.4 = (f32[1536]{0:T(1024)S(1)}, f32[1536]{0:T(1024)}, u32[]{:S(2)}) copy-start(f32[1536]{0:T(1024)} %param.24) | copy-start | bytes 18436
  89.6 24.3 %all-to-all-start.3 = ((bf16[16,32,1536]{2,1,0:T(8,128)(2,1)}), bf16[16,32,1536]{2,1,0:T(8,128)(2,1)S(1)}, u32[]{:S(2)}, u32[]{:S(2)}) async-start(bf16[16,32,1536]{2,1,0:T(8,128)(2,1)} %broadcast_in_dim.250), calls=%async_computation.3 | async-start | bytes 3145728 | tf_op jit(solution)/shard_map/all_to_all | solution.py:249
  113.9 1.2 copy-start.5
  115.1 1.2 copy-start.6
  118.6 36.2 %all-to-all-start.4 = ((bf16[128,4,1536]{2,1,0:T(4,128)(2,1)}), bf16[128,4,1536]{2,1,0:T(4,128)(2,1)S(1)}, u32[]{:S(2)}, u32[]{:S(2)}) async-start(bf16[128,4,1536]{2,1,0:T(4,128)(2,1)} %all_to_all.22), calls=%async_computation.4 | async-start | bytes 3145728 | tf_op jit(solution)/shard_map/all_to_all | solution.py:267

commit v21 on v19

--- a/solution.py
+++ b/solution.py
@@ -231,10 +231,13 @@
     used = jnp.any(held, axis=0).T.astype(jnp.int32).reshape(rows * steps)
     attended = attend(bounds, used, by_row, pages, entries_by_row, pick)
     attended = jnp.transpose(attended, (2, 1, 0, 3))
-    attended = jnp.where(held[..., None], attended, jnp.zeros_like(attended))
 
     received = lax.all_to_all(attended, HALF, split_axis=0, concat_axis=0, tiled=True)
-    attended_own = jnp.sum(received.astype(jnp.float32), axis=0).astype(jnp.bfloat16)
+    own_cache = lax.dynamic_index_in_dim(jnp.stack(cache_beams), beam, 1, keepdims=False)
+    from_holder = own_cache[None] == jnp.arange(BEAMS, dtype=jnp.int32)[:, None, None]
+    attended_own = jnp.sum(
+        jnp.where(from_holder[..., None], received.astype(jnp.float32), 0.0), axis=0
+    ).astype(jnp.bfloat16)
 
     current = inputs.reshape(steps * rows, width)
     residual = (

time: 154 us -> 158 us (1.026); the launches traced: 152 us -> 158 us
  blocking collectives: 18.1 us -> 0 us
  waiting for transfers between devices: 46.6 us -> 62.9 us
  starting transfers between devices: 30.9 us -> 37.6 us
  local copies, waits for them, and re-layouts: 24.6 us -> 27.2 us
    all_to_all x1 -> x0, blocking collectives: 18.1 us -> none  [on_device(): lax.all_to_all(attended, HALF, split_axis=0, concat_axis=0, tiled=True)]
    all_to_all x0 -> x1, waiting for transfers between devices: none -> 11.6 us  [on_device(): lax.all_to_all(attended, HALF, split_axis=0, concat_axis=0, tiled=True)]
    all_to_all x0 -> x1, starting transfers between devices: none -> 10.2 us  [on_device(): lax.all_to_all(attended, HALF, split_axis=0, concat_axis=0, tiled=True)]
    all_to_all x1, starting transfers between devices: 12.7 us -> 7.7 us  [on_device(): lax.all_to_all(leaving, KV + ('req',), 0, 0, tiled=True)]
    all_to_all x1, waiting for transfers between devices: 18.7 us -> 23.3 us  [on_device(): lax.all_to_all(jnp.broadcast_to(mlp_own[None], (kv_count,) + mlp_own.shap...]
    transpose x0 -> x1, local copies, waits for them, and re-layouts: none -> 2.41 us  [on_device(): attended = jnp.transpose(attended, (2, 1, 0, 3))]
  transfers between devices with their start and end apart: 4 -> 5, of which waited for: 4 -> 5; matrix products, arithmetic and copies ran while one was open for 10% -> 10% of each run, Pallas kernels for 0% -> 0%
where the time goes in v21:
time: 158 us
  waiting for transfers between devices  62.9 us (40%)
  starting transfers between devices  37.6 us (24%)
  local copies, waits for them, and re-layouts  27.2 us (17%)
  Pallas kernels  14 us (9%)
  matrix products  9.32 us (6%)
  other arithmetic  6.26 us (4%)
    all_to_all x1, waiting for transfers between devices, on_device(): lax.all_to_all(leaving, KV + ('req',), 0, 0, tiled=True)  24.9 us
    all_to_all x1, waiting for transfers between devices, on_device(): lax.all_to_all(jnp.broadcast_to(mlp_own[None], (kv_count,) + mlp_own.shap...  23.3 us
    pallas_call x1, Pallas kernels, attend(): pl.pallas_call(attend_kernel, grid_spec=pltpu.PrefetchScalarGridSpec(num_...  14 us
    all_to_all x1, waiting for transfers between devices, on_device(): lax.all_to_all(attended, HALF, split_axis=0, concat_axis=0, tiled=True)  11.6 us
    all_to_all x1, starting transfers between devices, on_device(): lax.all_to_all(attended, HALF, split_axis=0, concat_axis=0, tiled=True)  10.2 us
    all_to_all x1, starting transfers between devices, on_device(): lax.all_to_all(jnp.broadcast_to(mlp_own[None], (kv_count,) + mlp_own.shap...  8.32 us
    gather x1, local copies, waits for them, and re-layouts, on_device(): pool[table[offset_of] - device * pool.shape[0]]  7.81 us
    all_to_all x1, starting transfers between devices, on_device(): lax.all_to_all(leaving, KV + ('req',), 0, 0, tiled=True)  7.7 us
  transfers between devices with their start and end apart: 5, of which 5 were waited for; matrix products, arithmetic and copies ran while one was open for 10% of the time, Pallas kernels for 0%

profile of v21, /device:TPU:1, one launch (start us, length us, event | category | flops | bytes accessed | tf_op | source)
XLA Modules:
  0.0 157.8 jit_solution(4759476646181324849)
XLA Ops:
  0.0 0.8 reshape.513
  0.8 0.7 reshape.512
  1.9 1.7 %gather_fusion = bf16[8,4,1536]{2,0,1:T(8,128)(2,1)S(1)} fusion(bf16[4,8,1536]{2,1,0:T(8,128)(2,1)} %param.14, s32[1024]{0:T(1024)S(1)} %pad_clamp_fusion.3), kind=kCustom, calls=%fused_computation | custom fusion | bytes 196640 | tf_op jit(solution)/shard_map/jit(_take)/gather | solution.py:172
  4.4 5.8 %all-to-all-start = ((bf16[4,8,1,1536]{3,0,2,1:T(4,128)(2,1)}), bf16[4,8,1,1536]{3,0,2,1:T(4,128)(2,1)S(1)}, u32[]{:S(2)}, u32[]{:S(2)}) async-start(bf16[4,8,1,1536]{3,0,2,1:T(4,128)(2,1)} %copy.131), calls=%async_computation | async-start | bytes 196608 | tf_op jit(solution)/shard_map/all_to_all | solution.py:173
  15.6 3.4 %convolution_convert_fusion.1 = bf16[32,1536]{1,0:T(8,128)(2,1)S(1)} fusion(bf16[1536,1536]{1,0:T(8,128)(2,1)} %param.21, f32[4,8,1,1536]{3,0,2,1:T(4,128)S(1)} %convert_element_type.126, f32[1536]{0:T(1024)S(1)} %copy-done.4, f32[32]{0:T(128)S(1)} %rsqrt.23), kind=kOutput, calls=%fused_computation.10 | convolution fusion | flops 151191552 | bytes 5019776 | tf_op jit(solution)/shard_map/dot_general | solution.py:184
  19.3 1.0 broadcast_in_dim.366
  20.3 5.5 %all-to-all-start.1 = ((bf16[8,4,8,1792]{3,2,1,0:T(8,128)(2,1)}), bf16[8,4,8,1792]{3,2,1,0:T(8,128)(2,1)S(1)}, u32[]{:S(2)}, u32[]{:S(2)}) async-start(bf16[8,4,8,1792]{3,2,1,0:T(8,128)(2,1)} %broadcast_in_dim.366), calls=%async_computation.1 | async-start | bytes 1835008 | tf_op jit(solution)/shard_map/all_to_all | solution.py:187
  27.4 7.8 %gather_fusion.5 = bf16[72,128,256]{2,1,0:T(8,128)(2,1)} fusion(bf16[72,128,256]{2,1,0:T(8,128)(2,1)} %param.19, s32[1024]{0:T(1024)S(1)} %pad_clamp_fusion), kind=kCustom, calls=%fused_computation.5 | custom fusion | bytes 9437472 | tf_op jit(solution)/shard_map/gather | solution.py:216
  36.1 3.0 %all-to-all-done.1 = bf16[8,4,8,1792]{3,2,1,0:T(8,128)(2,1)S(1)} async-done(((bf16[8,4,8,1792]{3,2,1,0:T(8,128)(2,1)}), bf16[8,4,8,1792]{3,2,1,0:T(8,128)(2,1)S(1)}, u32[]{:S(2)}, u32[]{:S(2)}) %all-to-all-start.1) | async-done | bytes 917536 | tf_op jit(solution)/shard_map/all_to_all | solution.py:187
  39.2 1.4 copy.183
  40.7 1.4 select_reduce_fusion.11
  42.2 0.9 pad_maximum_fusion.new_ref
  43.1 14.0 %shard_map.136 = bf16[8,4,8,1536]{3,2,1,0:T(8,128)(2,1)} custom-call(s32[64]{0:T(128)} %reshape.516.bounds_ref, s32[32]{0:T(128)} %reshape.527.used_ref, bf16[8,4,96,128]{3,2,1,0:T(8,128)(2,1)} %bitcast.133, bf16[8,1152,256]{2,1,0:T(8,128)(2,1)} %bitcast.131, bf16[8,4,32,256]{3,2,1,0:T(8,128)(2,1)} %pad_maximum_fusion.new_ref, ...), custom_call_target="tpu_custom_call" | custom-call | flops 1862270976 | bytes 6815744 | tf_op jit(solution)/shard_map/pallas_call | solution.py:106
  57.1 2.4 %copy.159 = bf16[8,4,8,1536]{3,1,2,0:T(4,128)(2,1)} copy(bf16[8,4,8,1536]{3,0,1,2:T(8,128)(2,1)} %bitcast.134) | data formatting | bytes 1572864 | tf_op jit(solution)/shard_map/transpose | solution.py:233
  59.5 10.2 %all-to-all-start.2 = ((bf16[8,4,8,1536]{3,1,2,0:T(4,128)(2,1)}), bf16[8,4,8,1536]{3,1,2,0:T(4,128)(2,1)S(1)}, u32[]{:S(2)}, u32[]{:S(2)}) async-start(bf16[8,4,8,1536]{3,1,2,0:T(4,128)(2,1)} %copy.159), calls=%async_computation.2 | async-start | bytes 1572864 | tf_op jit(solution)/shard_map/all_to_all | solution.py:235
  69.8 11.6 %all-to-all-done.2 = bf16[8,4,8,1536]{3,1,2,0:T(4,128)(2,1)S(1)} async-done(((bf16[8,4,8,1536]{3,1,2,0:T(4,128)(2,1)}), bf16[8,4,8,1536]{3,1,2,0:T(4,128)(2,1)S(1)}, u32[]{:S(2)}, u32[]{:S(2)}) %all-to-all-start.2) | async-done | bytes 786464 | tf_op jit(solution)/shard_map/all_to_all | solution.py:235
  82.0 3.3 %multiply_reduce_fusion = (f32[8,4]{0,1:T(4,128)S(1)}, bf16[8,4,1536]{2,0,1:T(8,128)(2,1)S(1)}) fusion(bf16[1536,1536]{1,0:T(8,128)(2,1)} %param.23, bf16[4,8,1536]{2,0,1:T(4,128)(2,1)S(1)} %select_reduce_fusion.1, f32[4,8,1,1536]{3,0,2,1:T(4,128)S(1)} %convert_element_type.126), kind=kOutput, calls=%fused_computation.48 | convolution fusion | flops 151240672 | bytes 5111936 | tf_op jit(solution)/shard_map/dot_general | solution.py:245
  85.7 1.3 broadcast_in_dim.386
  87.0 8.3 %all-to-all-start.3 = ((bf16[16,32,1536]{2,1,0:T(8,128)(2,1)}), bf16[16,32,1536]{2,1,0:T(8,128)(2,1)S(1)}, u32[]{:S(2)}, u32[]{:S(2)}) async-start(bf16[16,32,1536]{2,1,0:T(8,128)(2,1)} %broadcast_in_dim.386), calls=%async_computation.3 | async-start | bytes 3145728 | tf_op jit(solution)/shard_map/all_to_all | solution.py:249
  95.4 23.3 %all-to-all-done.3 = bf16[16,32,1536]{2,1,0:T(8,128)(2,1)S(1)} async-done(((bf16[16,32,1536]{2,1,0:T(8,128)(2,1)}), bf16[16,32,1536]{2,1,0:T(8,128)(2,1)S(1)}, u32[]{:S(2)}, u32[]{:S(2)}) %all-to-all-start.3) | async-done | bytes 1572896 | tf_op jit(solution)/shard_map/all_to_all | solution.py:249
  121.0 1.0 convolution_convert_fusion
  122.1 1.4 all_to_all.22
  123.4 7.7 %all-to-all-start.4 = ((bf16[128,4,1536]{2,1,0:T(4,128)(2,1)}), bf16[128,4,1536]{2,1,0:T(4,128)(2,1)S(1)}, u32[]{:S(2)}, u32[]{:S(2)}) async-start(bf16[128,4,1536]{2,1,0:T(4,128)(2,1)} %all_to_all.22), calls=%async_computation.4 | async-start | bytes 3145728 | tf_op jit(solution)/shard_map/all_to_all | solution.py:267
  131.2 24.9 %all-to-all-done.4 = bf16[128,4,1536]{2,1,0:T(4,128)(2,1)S(1)} async-done(((bf16[128,4,1536]{2,1,0:T(4,128)(2,1)}), bf16[128,4,1536]{2,1,0:T(4,128)(2,1)S(1)}, u32[]{:S(2)}, u32[]{:S(2)}) %all-to-all-start.4) | async-done | bytes 1572896 | tf_op jit(solution)/shard_map/all_to_all | solution.py:267
  (120 shorter events, 14.3 us)
Async XLA Ops:
  0.0 118.7 %copy-start = (bf16[1536,288]{0,1:T(8,128)(2,1)S(1)}, bf16[1536,288]{0,1:T(8,128)(2,1)}, u32[]{:S(2)}) copy-start(bf16[1536,288]{0,1:T(8,128)(2,1)} %param.25) | copy-start | bytes 2654212
  0.0 13.0 %copy-start.3 = (s32[8,9]{1,0:T(8,128)S(1)}, s32[8,9]{1,0:T(8,128)}, u32[]{:S(2)}) copy-start(s32[8,9]{1,0:T(8,128)} %param.18) | copy-start | bytes 868
  0.0 14.5 %copy-start.1 = (s32[128]{0:T(128)S(1)}, s32[128]{0:T(128)}, u32[]{:S(2)}) copy-start(s32[128]{0:T(128)} %param.15) | copy-start | bytes 1540
  0.0 15.6 %copy-start.4 = (f32[1536]{0:T(1024)S(1)}, f32[1536]{0:T(1024)}, u32[]{:S(2)}) copy-start(f32[1536]{0:T(1024)} %param.20) | copy-start | bytes 18436
  4.4 10.8 %all-to-all-start = ((bf16[4,8,1,1536]{3,0,2,1:T(4,128)(2,1)}), bf16[4,8,1,1536]{3,0,2,1:T(4,128)(2,1)S(1)}, u32[]{:S(2)}, u32[]{:S(2)}) async-start(bf16[4,8,1,1536]{3,0,2,1:T(4,128)(2,1)} %copy.131), calls=%async_computation | async-start | bytes 196608 | tf_op jit(solution)/shard_map/all_to_all | solution.py:173
  15.6 3.4 %copy-start.2 = (bf16[1536,256]{1,0:T(8,128)(2,1)S(1)}, bf16[1536,256]{1,0:T(8,128)(2,1)}, u32[]{:S(2)}) copy-start(bf16[1536,256]{1,0:T(8,128)(2,1)} %param.22) | copy-start | bytes 2359300
  20.3 18.8 %all-to-all-start.1 = ((bf16[8,4,8,1792]{3,2,1,0:T(8,128)(2,1)}), bf16[8,4,8,1792]{3,2,1,0:T(8,128)(2,1)S(1)}, u32[]{:S(2)}, u32[]{:S(2)}) async-start(bf16[8,4,8,1792]{3,2,1,0:T(8,128)(2,1)} %broadcast_in_dim.366), calls=%async_computation.1 | async-start | bytes 1835008 | tf_op jit(solution)/shard_map/all_to_all | solution.py:187
  59.5 21.9 %all-to-all-start.2 = ((bf16[8,4,8,1536]{3,1,2,0:T(4,128)(2,1)}), bf16[8,4,8,1536]{3,1,2,0:T(4,128)(2,1)S(1)}, u32[]{:S(2)}, u32[]{:S(2)}) async-start(bf16[8,4,8,1536]{3,1,2,0:T(4,128)(2,1)} %copy.159), calls=%async_computation.2 | async-start | bytes 1572864 | tf_op jit(solution)/shard_map/all_to_all | solution.py:235
  82.0 3.6 %copy-start.5 = (f32[1536]{0:T(1024)S(1)}, f32[1536]{0:T(1024)}, u32[]{:S(2)}) copy-start(f32[1536]{0:T(1024)} %param.24) | copy-start | bytes 18436
  87.0 31.7 %all-to-all-start.3 = ((bf16[16,32,1536]{2,1,0:T(8,128)(2,1)}), bf16[16,32,1536]{2,1,0:T(8,128)(2,1)S(1)}, u32[]{:S(2)}, u32[]{:S(2)}) async-start(bf16[16,32,1536]{2,1,0:T(8,128)(2,1)} %broadcast_in_dim.386), calls=%async_computation.3 | async-start | bytes 3145728 | tf_op jit(solution)/shard_map/all_to_all | solution.py:249
  118.7 1.2 copy-start.6
  119.9 1.2 copy-start.7
  123.4 32.6 %all-to-all-start.4 = ((bf16[128,4,1536]{2,1,0:T(4,128)(2,1)}), bf16[128,4,1536]{2,1,0:T(4,128)(2,1)S(1)}, u32[]{:S(2)}, u32[]{:S(2)}) async-start(bf16[128,4,1536]{2,1,0:T(4,128)(2,1)} %all_to_all.22), calls=%async_computation.4 | async-start | bytes 3145728 | tf_op jit(solution)/shard_map/all_to_all | solution.py:267
